TPU v7x, 32 devices: a whole 2x2x4 slice. The times are simulated.
32 devices in a mesh: req: 8 (over z, y), tp: 4 (over x, core).
Axes of the slice: x: 2, y: 2, z: 4, core: 2. Of those that a mesh axis runs over, the one named last changes fastest.
Arguments:
- hidden: bfloat16 [32, 128, 2304], P('req', None, 'tp')
- qkv: bfloat16 [32, 128, 4, 1024], P('req', None, 'tp')
- page_store: bfloat16 [16, 128, 4, 512], P('req', None, 'tp')
- page_owner: int32 [8], replicated, may hold values from 0 to 7, as said below
- page_slot: int32 [8], replicated, may hold values from 0 to 1
- lengths: int32 [32], replicated, may hold values from 1 to 128, 2048 in all
- request_perm: int32 [32], replicated, may hold values from 0 to 31, each once
- w_out: bfloat16 [2048, 2304], P(None, 'tp')
- post_gain: float32 [2304], P('tp'), may hold values from 0.25 to 1.75
Outputs:
- result: bfloat16 [32, 128, 2304], P('req', None, 'tp')
Inputs may be any that keep to these rules, and one draw needn't show every extreme that they name: Page p lies in slot page_slot[p] of the device with index page_owner[p] along req; no two pages share an owner.
All inputs are finite; a program needn't handle non-finite values.
Results may differ from a plain program's by a relative error of at most 0.0043.
Values may be sent and summed in bfloat16 or wider, within the bound.
No kernel may reach another device: no remote copies, remote signals or barrier semaphores. Data moves between devices by JAX's collectives and lax.ppermute only.
A program may use at most 64 MiB of HBM per device.

v0:
```python
import jax
import jax.numpy as jnp
from jax import lax
from jax.sharding import PartitionSpec as P

D = 2304
HD = 256


EPSILON = 1e-06
SOFT_CAP = 50.0


def tables(positions, width):
    half_width = width // 2
    frequency = 10000.0 ** (-(jnp.arange(half_width, dtype=jnp.float32) * 2.0 / width))
    angles = positions.astype(jnp.float32)[:, None] * frequency[None, :]
    return (jnp.cos(angles), jnp.sin(angles))


def rotate(values, cosine, sine):
    half_width = values.shape[-1] // 2
    first = values[..., :half_width]
    second = values[..., half_width:]
    return jnp.concatenate([first * cosine - second * sine, second * cosine + first * sine], -1)


def capped_exp(scores):
    return jnp.exp(SOFT_CAP * jnp.tanh(scores / SOFT_CAP))


def on_device(
    hidden, qkv, page_store, page_owner, page_slot, lengths, request_perm, w_out, post_gain
):
    requests, slots, local_width = hidden.shape
    groups = qkv.shape[2]
    per_group = qkv.shape[3] // HD - 2
    token_rows = requests * slots
    device_row = lax.axis_index("req")
    my_requests = lax.dynamic_slice_in_dim(request_perm, device_row * requests, requests)
    matches = my_requests[:, None] == jnp.arange(lengths.shape[0], dtype=jnp.int32)[None, :]
    my_lengths = jnp.sum(jnp.where(matches, lengths[None, :], 0), 1)
    position = jnp.arange(slots, dtype=jnp.int32)
    live_mask = (position[None, :] < my_lengths[:, None]).astype(jnp.float32)
    source = hidden.astype(jnp.float32)
    projections = qkv.astype(jnp.float32).reshape(requests, slots, groups, per_group + 2, HD)
    page_count = page_owner.shape[0]
    prefix_len = page_store.shape[1] * page_count
    cosine, sine = tables(prefix_len + position, HD)
    queries = (
        rotate(
            projections[:, :, :, :per_group],
            cosine[None, :, None, None, :],
            sine[None, :, None, None, :],
        )
        * HD ** (-0.5)
    ).astype(jnp.bfloat16)
    fresh_keys = rotate(
        projections[:, :, :, per_group], cosine[None, :, None, :], sine[None, :, None, :]
    ).astype(jnp.bfloat16)
    fresh_values = projections[:, :, :, per_group + 1].astype(jnp.bfloat16)
    picked = page_store[page_slot]
    held_here = page_owner == device_row
    offered = jnp.where(held_here[:, None, None, None], picked.astype(jnp.float32), 0.0)
    prefix = lax.psum(offered, "req").astype(jnp.bfloat16)
    prefix = prefix.reshape(prefix_len, groups, 2 * HD)
    prefix_keys = prefix[:, :, :HD]
    prefix_values = prefix[:, :, HD:]
    prefix_weights = capped_exp(
        jnp.einsum("rsgqh,tgh->rsgqt", queries, prefix_keys, preferred_element_type=jnp.float32)
    )
    allowed = (position[None, None, :] <= position[None, :, None]) & (
        position[None, None, :] < my_lengths[:, None, None]
    )
    suffix_raw = capped_exp(
        jnp.einsum("rsgqh,rtgh->rsgqt", queries, fresh_keys, preferred_element_type=jnp.float32)
    )
    suffix_weights = jnp.where(allowed[:, :, None, None, :], suffix_raw, 0.0)
    totals = jnp.sum(prefix_weights, -1) + jnp.sum(suffix_weights, -1)
    prefix_probs = (prefix_weights / totals[..., None]).astype(jnp.bfloat16)
    suffix_probs = (suffix_weights / totals[..., None]).astype(jnp.bfloat16)
    attended = jnp.einsum(
        "rsgqt,tgh->rsgqh", prefix_probs, prefix_values, preferred_element_type=jnp.float32
    )
    attended = attended + jnp.einsum(
        "rsgqt,rtgh->rsgqh", suffix_probs, fresh_values, preferred_element_type=jnp.float32
    )
    attended = attended.astype(jnp.bfloat16).reshape(token_rows, groups * per_group * HD)
    projected = jnp.dot(
        lax.all_gather(attended, "tp", axis=1, tiled=True),
        w_out,
        preferred_element_type=jnp.float32,
    )
    projected = projected.reshape(requests, slots, local_width)
    branch_total = lax.psum(jnp.sum(projected * projected, -1), "tp")
    branch = projected * lax.rsqrt(branch_total / D + EPSILON)[..., None] * post_gain
    return ((source + branch) * live_mask[..., None]).astype(jnp.bfloat16)


def solution(mesh):
    placed = (
        P("req", None, "tp"),
        P("req", None, "tp", None),
        P("req", None, "tp", None),
        P(),
        P(),
        P(),
        P(),
        P(None, "tp"),
        P("tp"),
    )
    return jax.shard_map(
        on_device, mesh=mesh, in_specs=placed, out_specs=P("req", None, "tp"), check_vma=False
    )
```

profile of v0, /device:TPU:0, one launch (start us, length us, event | category | flops | bytes accessed | tf_op | source)
XLA Modules:
  0.0 157.9 jit_solution(3614587715875364756)
XLA Ops:
  6.6 0.8 broadcast_compare_fusion
  7.4 0.7 compare_select_fusion
  8.1 0.7 dynamic_slice.3
  8.8 0.8 select_reduce_fusion
  9.7 1.6 gather_fusion
  11.3 1.7 %convert_select_fusion = f32[8,128,1,512]{3,1,0,2:T(8,128)} fusion(bf16[8,128,512]{2,1,0:T(8,128)(2,1)S(1)} %gather_fusion, pred[8]{0:T(512)(128)(4,1)S(1)} %broadcast_compare_fusion), kind=kLoop, calls=%fused_computation.5 | loop fusion | flops 1048576 | bytes 3145736 | tf_op jit(solution)/shard_map/jit(_where)/select_n | solution.py:64
  13.0 95.0 %all-reduce.1 = bf16[8,128,1,512]{3,1,0,2:T(8,128)(2,1)} all-reduce(f32[8,128,1,512]{3,1,0,2:T(8,128)} %convert_select_fusion), channel_id=1, replica_groups=mesh['req'=8,'tp'=4] {'req'}, use_global_device_ids=true, to_apply=%region_0.1 | all-reduce | flops 524288 | bytes 3145728 | tf_op jit(solution)/shard_map/psum | solution.py:65
  108.0 1.3 copy.24
  109.3 1.5 copy.25
  110.8 0.2 reshape.303
  111.0 0.3 multiply_cosine_fusion
  111.4 0.1 subtract_bitcast_fusion
  111.6 0.1 broadcast_and_fusion
  111.7 0.5 copy-done.1
  112.2 1.3 bitcast_reduce_fusion
  113.6 0.4 fusion.37
  114.0 1.5 fusion.6
  115.5 1.2 fusion.10
  116.7 0.5 copy.31
  117.2 0.9 copy.43
  118.1 21.8 %all-gather.2.cloned.1.call-done = bf16[512,2048]{1,0:T(8,128)(2,1)} async-done(((bf16[512,512]{1,0:T(8,128)(2,1)}), bf16[512,2048]{1,0:T(8,128)(2,1)}) %all-gather.2.cloned.1.call-update) | async-done | bytes 2097168 | tf_op jit(solution)/shard_map/all_gather | solution.py:90
  139.9 3.0 %multiply_reduce_fusion = (f32[512]{0:T(512)S(1)}, f32[512,576]{0,1:T(8,128)S(1)}) fusion(bf16[512,2048]{1,0:T(8,128)(2,1)} %all-gather.2.cloned.1.call-done, bf16[2048,576]{0,1:T(8,128)(2,1)S(1)} %copy-done), kind=kOutput, calls=%fused_computation.24 | convolution fusion | flops 1208548864 | bytes 5638144 | tf_op jit(solution)/shard_map/dot_general | solution.py:89
  143.0 5.9 %psum.15 = f32[4,128]{1,0:T(4,128)S(1)} all-reduce(f32[4,128]{1,0:T(4,128)S(1)} %bitcast.112), channel_id=1, replica_groups=mesh['req'=8,'tp'=4] {'tp'}, use_global_device_ids=true, to_apply=%region_5.6 | all-reduce | flops 512 | bytes 4096 | tf_op jit(solution)/shard_map/psum | solution.py:95
  148.9 2.2 %fusion.18 = bf16[4,128,576]{1,2,0:T(8,128)(2,1)} fusion(bf16[4,128,576]{1,2,0:T(8,128)(2,1)} %param.9, f32[4,128]{1,0:T(4,128)S(1)} %get-tuple-element.11, f32[576]{0:T(1024)S(1)} %copy-done.3, f32[4,128]{1,0:T(4,128)S(1)} %add_rsqrt_fusion, f32[512,576]{0,1:T(8,128)S(1)} %get-tuple-element.18), kind=kLoop, calls=%fused_computation.23 | loop fusion | flops 1769472 | bytes 2365696 | tf_op jit(solution)/shard_map/convert_element_type | solution.py:97
  (18 shorter events, 0.3 us)
Async XLA Ops:
  6.5 133.4 %copy-start = (bf16[2048,576]{0,1:T(8,128)(2,1)S(1)}, bf16[2048,576]{0,1:T(8,128)(2,1)}, u32[]{:S(2)}) copy-start(bf16[2048,576]{0,1:T(8,128)(2,1)} %param.16) | copy-start | bytes 7077892
  6.5 133.4 %all-gather.2.cloned.1.call-start = ((), (), s32[]{:S(2)}) async-start(), calls=%async_computation | async-start | bytes 2621440 | tf_op jit(solution)/shard_map/all_gather | solution.py:90
  13.0 95.0 %copy-start.2 = (bf16[4,128,1,1024]{3,1,2,0:T(8,128)(2,1)S(1)}, bf16[4,128,1,1024]{3,1,2,0:T(8,128)(2,1)}, u32[]{:S(2)}) copy-start(bf16[4,128,1,1024]{3,1,2,0:T(8,128)(2,1)} %param.10) | copy-start | bytes 3145732
  111.0 1.2 copy-start.1
  118.1 30.8 %copy-start.3 = (f32[576]{0:T(1024)S(1)}, f32[576]{0:T(1024)}, u32[]{:S(2)}) copy-start(f32[576]{0:T(1024)} %param.17) | copy-start | bytes 6916
Sparse Core Ops, SparseCore 0:
  118.2 21.6 all-gather.1
where the time goes:
time: 158 us
  blocking collectives  101 us (64%)
  waiting for transfers between devices  21.9 us (14%)
  between operations  13.5 us (9%)
  matrix products  7.48 us (5%)
  other arithmetic  7.23 us (5%)
  local copies, waits for them, and re-layouts  6.97 us (4%)
    psum x1, blocking collectives, on_device(): prefix = lax.psum(offered, 'req').astype(jnp.bfloat16)  95 us
    all_gather x1, waiting for transfers between devices, on_device(): lax.all_gather(attended, 'tp', axis=1, tiled=True)  21.8 us
    psum x1, blocking collectives, on_device(): branch_total = lax.psum(jnp.sum(projected * projected, -1), 'tp')  5.89 us
  transfers between devices with their start and end apart: 1, of which 1 were waited for; matrix products, arithmetic and copies ran while one was open for 0% of the time, Pallas kernels for 0%

commit v1 on v0

v1 whole, which is shorter than its diff:
```python
import jax
import jax.numpy as jnp
from jax import lax
from jax.sharding import PartitionSpec as P

D = 2304
HD = 256


EPSILON = 1e-06
SOFT_CAP = 50.0


def tables(positions, width):
    half_width = width // 2
    frequency = 10000.0 ** (-(jnp.arange(half_width, dtype=jnp.float32) * 2.0 / width))
    angles = positions.astype(jnp.float32)[:, None] * frequency[None, :]
    return (jnp.cos(angles), jnp.sin(angles))


def rotate(values, cosine, sine):
    half_width = values.shape[-1] // 2
    first = values[..., :half_width]
    second = values[..., half_width:]
    return jnp.concatenate([first * cosine - second * sine, second * cosine + first * sine], -1)


def capped_exp(scores):
    return jnp.exp(SOFT_CAP * jnp.tanh(scores / SOFT_CAP))


def shifted(value, axis, size, shift):
    return lax.ppermute(value, axis, [(i, (i + shift) % size) for i in range(size)])


def swapped(value, axis, size, mask):
    return lax.ppermute(value, axis, [(i, i ^ mask) for i in range(size)])


def gather_prefix(page_store, page_owner, page_slot, n_req):
    device_row = lax.axis_index("req")
    page_count = page_owner.shape[0]
    if n_req <= page_count:
        mine = page_owner == device_row
        slot = jnp.sum(jnp.where(mine, page_slot, 0))
        own = lax.dynamic_index_in_dim(page_store, slot, 0, keepdims=False)[:, 0]
        blocks = [own]
        sources = [device_row]
        for shift in range(1, n_req):
            blocks.append(shifted(own, "req", n_req, shift))
            sources.append((device_row - shift) % n_req)
        sources = jnp.stack(sources)
        valid = jnp.any(page_owner[None, :] == sources[:, None], 1)
        return jnp.stack(blocks), valid
    picked = page_store[page_slot][:, :, 0]
    held_here = page_owner == device_row
    offered = jnp.where(held_here[:, None, None], picked, jnp.zeros_like(picked))
    prefix = lax.psum(offered, "req")
    return prefix, jnp.ones((page_count,), jnp.bool_)


def on_device(
    hidden, qkv, page_store, page_owner, page_slot, lengths, request_perm, w_out, post_gain,
    *, n_req, n_tp
):
    requests, slots, local_width = hidden.shape
    per_group = qkv.shape[3] // HD - 2
    token_rows = requests * slots
    tp_index = lax.axis_index("tp")

    blocks, valid = gather_prefix(page_store, page_owner, page_slot, n_req)
    block_count, page_len = blocks.shape[0], blocks.shape[1]
    prefix_keys = blocks[:, :, :HD].reshape(block_count * page_len, HD)
    prefix_values = blocks[:, :, HD:].reshape(block_count * page_len, HD)
    key_valid = jnp.repeat(valid, page_len)

    device_row = lax.axis_index("req")
    my_requests = lax.dynamic_slice_in_dim(request_perm, device_row * requests, requests)
    matches = my_requests[:, None] == jnp.arange(lengths.shape[0], dtype=jnp.int32)[None, :]
    my_lengths = jnp.sum(jnp.where(matches, lengths[None, :], 0), 1)
    position = jnp.arange(slots, dtype=jnp.int32)
    live_mask = (position[None, :] < my_lengths[:, None]).astype(jnp.float32)

    projections = qkv[:, :, 0].astype(jnp.float32).reshape(requests, slots, per_group + 2, HD)
    prefix_len = page_store.shape[1] * page_owner.shape[0]
    cosine, sine = tables(prefix_len + position, HD)
    queries = (
        rotate(projections[:, :, :per_group], cosine[None, :, None, :], sine[None, :, None, :])
        * HD ** (-0.5)
    ).astype(jnp.bfloat16)
    fresh_keys = rotate(projections[:, :, per_group], cosine[None], sine[None]).astype(jnp.bfloat16)
    fresh_values = projections[:, :, per_group + 1].astype(jnp.bfloat16)

    prefix_weights = capped_exp(
        jnp.einsum("rsqh,th->rsqt", queries, prefix_keys, preferred_element_type=jnp.float32)
    )
    prefix_weights = jnp.where(key_valid[None, None, None, :], prefix_weights, 0.0)
    allowed = (position[None, None, :] <= position[None, :, None]) & (
        position[None, None, :] < my_lengths[:, None, None]
    )
    suffix_raw = capped_exp(
        jnp.einsum("rsqh,rth->rsqt", queries, fresh_keys, preferred_element_type=jnp.float32)
    )
    suffix_weights = jnp.where(allowed[:, :, None, :], suffix_raw, 0.0)
    totals = jnp.sum(prefix_weights, -1) + jnp.sum(suffix_weights, -1)
    prefix_probs = (prefix_weights / totals[..., None]).astype(jnp.bfloat16)
    suffix_probs = (suffix_weights / totals[..., None]).astype(jnp.bfloat16)
    attended = jnp.einsum(
        "rsqt,th->rsqh", prefix_probs, prefix_values, preferred_element_type=jnp.float32
    )
    attended = attended + jnp.einsum(
        "rsqt,rth->rsqh", suffix_probs, fresh_values, preferred_element_type=jnp.float32
    )
    own = attended.astype(jnp.bfloat16).reshape(token_rows, per_group * HD)

    group_width = per_group * HD
    w_blocks = w_out.reshape(n_tp, group_width, local_width)
    if n_tp == 4:
        near = swapped(own, "tp", n_tp, 1)
        far = swapped(own, "tp", n_tp, 2)
        farther = swapped(far, "tp", n_tp, 1)
        parts = [(own, tp_index), (near, tp_index ^ 1), (far, tp_index ^ 2), (farther, tp_index ^ 3)]
    else:
        parts = [(own, tp_index)]
        for shift in range(1, n_tp):
            parts.append((shifted(own, "tp", n_tp, shift), (tp_index - shift) % n_tp))
    projected = None
    for block, group in parts:
        rows = lax.dynamic_index_in_dim(w_blocks, group, 0, keepdims=False)
        term = jnp.dot(block, rows, preferred_element_type=jnp.float32)
        projected = term if projected is None else projected + term
    projected = projected.reshape(requests, slots, local_width)

    squares = jnp.sum(projected * projected, -1)
    branch_total = squares
    for shift in range(1, n_tp):
        branch_total = branch_total + shifted(squares, "tp", n_tp, shift)
    branch = projected * lax.rsqrt(branch_total / D + EPSILON)[..., None] * post_gain
    source = hidden.astype(jnp.float32)
    return ((source + branch) * live_mask[..., None]).astype(jnp.bfloat16)


def solution(mesh):
    placed = (
        P("req", None, "tp"),
        P("req", None, "tp", None),
        P("req", None, "tp", None),
        P(),
        P(),
        P(),
        P(),
        P(None, "tp"),
        P("tp"),
    )
    body = lambda *args: on_device(*args, n_req=mesh.shape["req"], n_tp=mesh.shape["tp"])
    return jax.shard_map(
        body, mesh=mesh, in_specs=placed, out_specs=P("req", None, "tp"), check_vma=False
    )
```

time: 158 us -> 64.1 us (0.41)
  blocking collectives: 101 us -> 0 us
  starting transfers between devices: 0.01 us -> 17.5 us
  local copies, waits for them, and re-layouts: 6.97 us -> 21.5 us
  between operations: 13.5 us -> 2.43 us
  waiting for transfers between devices: 21.9 us -> 11.3 us
  other arithmetic: 7.23 us -> 4.44 us
    psum x2 -> x0, blocking collectives: 101 us -> none  [the longest x1 95 us: on_device(): prefix = lax.psum(offered, 'req').astype(jnp.bfloat16)]
    all_gather x1 -> x0, waiting for transfers between devices: 21.8 us -> none  [on_device(): lax.all_gather(attended, 'tp', axis=1, tiled=True)]
    ppermute x0 -> x13, starting transfers between devices: none -> 17.5 us  [the longest x10 15.9 us: shifted(): lax.ppermute(value, axis, [(i, (i + shift) % size) for i in range(size)])]
    ppermute x0 -> x13, waiting for transfers between devices: none -> 11.3 us  [the longest x3 8.23 us: swapped(): return lax.ppermute(value, axis, [(i, i ^ mask) for i in range(size)])]
    unnamed x10 -> x25, local copies, waits for them, and re-layouts: 2.71 us -> 8.54 us
    dynamic_slice x0 -> x1, local copies, waits for them, and re-layouts: none -> 4.89 us  [on_device(): rows = lax.dynamic_index_in_dim(w_blocks, group, 0, keepdims=False)]
    reshape x1, local copies, waits for them, and re-layouts: 1.48 us -> 5.08 us  [on_device(): w_blocks = w_out.reshape(n_tp, group_width, local_width)]
    select_n x2 -> x0, other arithmetic: 2.37 us -> none  [the longest x1 1.72 us: on_device(): jnp.where(held_here[:, None, None, None], picked.astype(jnp.float32), 0.0)]
  transfers between devices with their start and end apart: 1 -> 13, of which waited for: 1 -> 4; matrix products, arithmetic and copies ran while one was open for 0% -> 36% of each run, Pallas kernels for 0% -> 0%
where the time goes in v1:
time: 64.1 us; the launch traced here: 63.7 us
  local copies, waits for them, and re-layouts  21.5 us (34%)
  starting transfers between devices  17.5 us (27%)
  waiting for transfers between devices  11.3 us (18%)
  matrix products  6.49 us (10%)
  other arithmetic  4.44 us (7%)
  between operations  2.43 us (4%)
    ppermute x10, starting transfers between devices, shifted(): lax.ppermute(value, axis, [(i, (i + shift) % size) for i in range(size)])  15.9 us
    unnamed x25, local copies, waits for them, and re-layouts  8.54 us
    ppermute x3, waiting for transfers between devices, swapped(): return lax.ppermute(value, axis, [(i, i ^ mask) for i in range(size)])  8.23 us
    reshape x1, local copies, waits for them, and re-layouts, on_device(): w_blocks = w_out.reshape(n_tp, group_width, local_width)  5.08 us
    dynamic_slice x1, local copies, waits for them, and re-layouts, on_device(): rows = lax.dynamic_index_in_dim(w_blocks, group, 0, keepdims=False)  4.89 us
    ppermute x10, waiting for transfers between devices, shifted(): lax.ppermute(value, axis, [(i, (i + shift) % size) for i in range(size)])  3.07 us
    dot_general x4, matrix products, on_device(): term = jnp.dot(block, rows, preferred_element_type=jnp.float32)  2.05 us
    ppermute x3, starting transfers between devices, swapped(): return lax.ppermute(value, axis, [(i, i ^ mask) for i in range(size)])  1.63 us
  transfers between devices with their start and end apart: 13, of which 4 were waited for; matrix products, arithmetic and copies ran while one was open for 36% of the time, Pallas kernels for 0%

profile of v1, /device:TPU:0, one launch (start us, length us, event | category | flops | bytes accessed | tf_op | source)
XLA Modules:
  0.0 63.7 jit_solution(7620274276886833961)
XLA Ops:
  0.0 1.3 %fusion.29 = s32[]{:T(128)} fusion(s32[8]{0:T(128)} %param.13, s32[8]{0:T(128)} %param.12, s32[]{:T(128)} %axis_index.27), kind=kLoop, calls=%fused_computation.68 | loop fusion | flops 23 | bytes 72 | tf_op jit(solution)/shard_map/reduce_sum | solution.py:45
  3.2 0.9 %dynamic-slice_bitcast_fusion = bf16[128,512]{1,0:T(8,128)(2,1)S(1)} fusion(bf16[2,128,1,512]{3,1,2,0:T(8,128)(2,1)} %param.11, s32[]{:T(128)S(6)} %select_n.75), kind=kLoop, calls=%fused_computation.52 | loop fusion | bytes 262148 | tf_op jit(solution)/shard_map/squeeze | solution.py:46
  4.2 3.0 %collective-permute-start = (bf16[128,512]{1,0:T(8,128)(2,1)S(1)}, bf16[128,512]{1,0:T(8,128)(2,1)}, u32[]{:S(2)}, u32[]{:S(2)}) collective-permute-start(bf16[128,512]{1,0:T(8,128)(2,1)S(1)} %dynamic-slice_bitcast_fusion), channel_id=1, source_target_pairs={{0,4},{4,8},{8,12},{12,16},{16,20},{20,24},{24,28},{28,0},{1,5},{5... | collective-permute-start | bytes 393224 | tf_op jit(solution)/shard_map/ppermute | solution.py:33
  7.2 1.6 %collective-permute-start.1 = (bf16[128,512]{1,0:T(8,128)(2,1)S(1)}, bf16[128,512]{1,0:T(8,128)(2,1)}, u32[]{:S(2)}, u32[]{:S(2)}) collective-permute-start(bf16[128,512]{1,0:T(8,128)(2,1)S(1)} %dynamic-slice_bitcast_fusion), channel_id=1, source_target_pairs={{0,8},{4,12},{8,16},{12,20},{16,24},{20,28},{24,0},{28,4},{1,9},{5... | collective-permute-start | bytes 393224 | tf_op jit(solution)/shard_map/ppermute | solution.py:33
  8.8 2.5 %collective-permute-start.2 = (bf16[128,512]{1,0:T(8,128)(2,1)S(1)}, bf16[128,512]{1,0:T(8,128)(2,1)}, u32[]{:S(2)}, u32[]{:S(2)}) collective-permute-start(bf16[128,512]{1,0:T(8,128)(2,1)S(1)} %dynamic-slice_bitcast_fusion), channel_id=1, source_target_pairs={{0,12},{4,16},{8,20},{12,24},{16,28},{20,0},{24,4},{28,8},{1,13},{... | collective-permute-start | bytes 393224 | tf_op jit(solution)/shard_map/ppermute | solution.py:33
  11.3 1.2 %collective-permute-start.3 = (bf16[128,512]{1,0:T(8,128)(2,1)S(1)}, bf16[128,512]{1,0:T(8,128)(2,1)}, u32[]{:S(2)}, u32[]{:S(2)}) collective-permute-start(bf16[128,512]{1,0:T(8,128)(2,1)S(1)} %dynamic-slice_bitcast_fusion), channel_id=1, source_target_pairs={{0,16},{4,20},{8,24},{12,28},{16,0},{20,4},{24,8},{28,12},{1,17},{... | collective-permute-start | bytes 393224 | tf_op jit(solution)/shard_map/ppermute | solution.py:33
  12.6 2.6 %collective-permute-start.4 = (bf16[128,512]{1,0:T(8,128)(2,1)S(1)}, bf16[128,512]{1,0:T(8,128)(2,1)}, u32[]{:S(2)}, u32[]{:S(2)}) collective-permute-start(bf16[128,512]{1,0:T(8,128)(2,1)S(1)} %dynamic-slice_bitcast_fusion), channel_id=1, source_target_pairs={{0,20},{4,24},{8,28},{12,0},{16,4},{20,8},{24,12},{28,16},{1,21},{... | collective-permute-start | bytes 393224 | tf_op jit(solution)/shard_map/ppermute | solution.py:33
  17.0 1.6 %copy.24 = bf16[4,128,1,1024]{1,3,0,2:T(8,128)(2,1)S(1)} copy(bf16[4,128,1,1024]{3,1,2,0:T(8,128)(2,1)} %param.10) | data formatting | bytes 2097152 | tf_op args[1]
  20.7 1.2 %fusion.40 = (f32[4,128,2]{1,2,0:T(2,128)S(1)}, f32[4,128,2,128]{1,3,2,0:T(8,128)}) fusion(bf16[4,128,128]{2,1,0:T(8,128)(2,1)S(1)} %get-tuple-element.14, bf16[4,128,128]{2,1,0:T(8,128)(2,1)S(1)} %get-tuple-element.13, f32[4,128,2,128]{3,1,2,0:T(8,128)S(1)} %get-tuple-element.10, f32[4,128,2,128]{3,1,2,0:T(8,128)S(1)} %get-tuple-element.9, ...), kind=kOutput, calls=%fused_computation.81 | convolution fusion | flops 68942848 | bytes 1904640 | tf_op jit(solution)/shard_map/rsqh,rth->rsqt/dot_general | solution.py:102
  22.0 5.1 %reshape.216 = bf16[4,512,576]{1,0,2:T(4,128)(2,1)S(1)} reshape(bf16[2048,576]{0,1:T(8,128)(2,1)} %param.16) | data formatting | bytes 4718592 | tf_op jit(solution)/shard_map/reshape | solution.py:117
  27.1 0.9 %bitcast_dynamic-update-slice_fusion.7 = bf16[8,128,512]{2,1,0:T(8,128)(2,1)S(1)} fusion(bf16[2,128,1,512]{3,1,2,0:T(8,128)(2,1)} %param.11, s32[]{:T(128)S(6)} %select_n.75), kind=kLoop, calls=%fused_computation.50 | loop fusion | bytes 262148
  28.0 1.4 %collective-permute-start.5 = (bf16[128,512]{1,0:T(8,128)(2,1)S(1)}, bf16[128,512]{1,0:T(8,128)(2,1)S(1)}, u32[]{:S(2)}, u32[]{:S(2)}) collective-permute-start(bf16[128,512]{1,0:T(8,128)(2,1)S(1)} %dynamic-slice_bitcast_fusion), channel_id=1, source_target_pairs={{0,24},{4,28},{8,0},{12,4},{16,8},{20,12},{24,16},{28,20},{1,25},{... | collective-permute-start | bytes 393224 | tf_op jit(solution)/shard_map/ppermute | solution.py:33
  30.3 1.6 %collective-permute-start.6 = (bf16[128,512]{1,0:T(8,128)(2,1)S(1)}, bf16[128,512]{1,0:T(8,128)(2,1)S(1)}, u32[]{:S(2)}, u32[]{:S(2)}) collective-permute-start(bf16[128,512]{1,0:T(8,128)(2,1)S(1)} %dynamic-slice_bitcast_fusion), channel_id=1, source_target_pairs={{0,28},{4,0},{8,4},{12,8},{16,12},{20,16},{24,20},{28,24},{1,29},{... | collective-permute-start | bytes 393224 | tf_op jit(solution)/shard_map/ppermute | solution.py:33
  32.9 0.9 %bitcast_dynamic-update-slice_fusion.4 = bf16[8,128,512]{2,1,0:T(8,128)(2,1)S(1)} fusion(bf16[8,128,512]{2,1,0:T(8,128)(2,1)S(1)} %bitcast_dynamic-update-slice_fusion.5, bf16[128,512]{1,0:T(8,128)(2,1)} %collective-permute-done.2), kind=kLoop, calls=%fused_computation.47 | loop fusion | bytes 262144
  33.8 0.9 %bitcast_dynamic-update-slice_fusion.3 = bf16[8,128,512]{2,1,0:T(8,128)(2,1)S(1)} fusion(bf16[8,128,512]{2,1,0:T(8,128)(2,1)S(1)} %bitcast_dynamic-update-slice_fusion.4, bf16[128,512]{1,0:T(8,128)(2,1)} %collective-permute-done.3), kind=kLoop, calls=%fused_computation.46 | loop fusion | bytes 262144
  34.8 0.9 %bitcast_dynamic-update-slice_fusion.2 = bf16[8,128,512]{2,1,0:T(8,128)(2,1)S(1)} fusion(bf16[8,128,512]{2,1,0:T(8,128)(2,1)S(1)} %bitcast_dynamic-update-slice_fusion.3, bf16[128,512]{1,0:T(8,128)(2,1)} %collective-permute-done.4), kind=kLoop, calls=%fused_computation.45 | loop fusion | bytes 262144
  36.9 1.5 %fusion = (f32[4,128,2]{1,2,0:T(2,128)S(1)}, f32[4,128,2,1024]{3,1,2,0:T(8,128)S(1)}) fusion(pred[1024]{0:T(1024)(128)(4,1)S(1)} %broadcast_bitcast_fusion, bf16[1024,256,1,1]{1,0,3,2:T(8,128)(2,1)S(1)} %bitcast.102, f32[4,128,2,128]{3,1,2,0:T(8,128)S(1)} %copy-done.4, f32[4,128,2,128]{3,1,2,0:T(8,128)S(1)} %copy-done.2), kind=kOutput, calls=%fused_computation.2 | convolution fusion | flops 541850624 | bytes 5772288 | tf_op jit(solution)/shard_map/rsqh,th->rsqt/dot_general | solution.py:95
  38.8 1.4 %fusion.3 = bf16[4,128,2,256]{3,1,2,0:T(8,128)(2,1)S(1)} fusion(f32[4,128,2,256]{3,1,2,0:T(8,128)S(1)} %fusion.22, bf16[1024,256,1,1]{1,0,3,2:T(8,128)(2,1)S(1)} %bitcast.101, f32[4,128,2,1024]{3,1,2,0:T(8,128)S(1)} %get-tuple-element.20, f32[4,128,2]{1,2,0:T(2,128)S(1)} %add.129, pred[1024]{0:T(1024)(128)(4,1)S(1)} %broadcast_bitcast_fusion), kind=kOutput, calls=%fused_computation.8 | convolution fusion | flops 542638080 | bytes 6296576 | tf_op jit(solution)/shard_map/rsqt,th->rsqh/dot_general | solution.py:108
  40.9 1.6 %collective-permute-start.8 = (bf16[512,512]{1,0:T(8,128)(2,1)S(1)}, bf16[512,512]{1,0:T(8,128)(2,1)S(1)}, u32[]{:S(2)}, u32[]{:S(2)}) collective-permute-start(bf16[512,512]{1,0:T(8,128)(2,1)S(1)} %bitcast.99), channel_id=1, source_target_pairs={{0,2},{1,3},{2,0},{3,1},{4,6},{5,7},{6,4},{7,5},{8,10},{9,11},{10,... | collective-permute-start | bytes 1572872 | tf_op jit(solution)/shard_map/ppermute | solution.py:37
  42.5 4.9 %constant_dynamic-slice_fusion = (bf16[1,512,576]{1,0,2:T(2,128)(2,1)S(1)}, bf16[1,512,576]{1,0,2:T(2,128)(2,1)S(1)}, bf16[1,512,576]{1,0,2:T(2,128)(2,1)S(1)}, bf16[1,512,576]{1,0,2:T(2,128)(2,1)S(1)}) fusion(bf16[4,512,576]{1,0,2:T(4,128)(2,1)S(1)} %reshape.216, s32[]{:T(128)S(6)} %select_n.83, s32[]{:T(128)S(6)} %select_n.82, s32[]{:T(128)S(6)} %select_n.81, ...), kind=kLoop, calls=%fused_computation.64 | loop fusion | bytes 4718608 | tf_op jit(solution)/shard_map/jit(dynamic_index_in_dim)/dynamic_slice | solution.py:129
  47.9 7.4 %collective-permute-done.8 = bf16[512,512]{1,0:T(8,128)(2,1)S(1)} collective-permute-done((bf16[512,512]{1,0:T(8,128)(2,1)S(1)}, bf16[512,512]{1,0:T(8,128)(2,1)S(1)}, u32[]{:S(2)}, u32[]{:S(2)}) %collective-permute-start.8) | collective-permute-done | bytes 524320 | tf_op jit(solution)/shard_map/ppermute | solution.py:37
  57.7 1.3 %collective-permute-start.12 = (f32[4,128]{1,0:T(4,128)S(1)}, f32[4,128]{1,0:T(4,128)S(1)}, u32[]{:S(2)}, u32[]{:S(2)}) collective-permute-start(f32[4,128]{1,0:T(4,128)S(1)} %bitcast.103), channel_id=1, source_target_pairs={{0,3},{1,0},{2,1},{3,2},{4,7},{5,4},{6,5},{7,6},{8,11},{9,8},{10,9... | collective-permute-start | bytes 6152 | tf_op jit(solution)/shard_map/ppermute | solution.py:33
  60.3 2.3 %collective-permute-done.11 = f32[4,128]{1,0:T(4,128)S(1)} collective-permute-done((f32[4,128]{1,0:T(4,128)S(1)}, f32[4,128]{1,0:T(4,128)S(1)}, u32[]{:S(2)}, u32[]{:S(2)}) %collective-permute-start.11) | collective-permute-done | bytes 2080 | tf_op jit(solution)/shard_map/ppermute | solution.py:33
  62.6 1.1 %fusion.11 = bf16[4,128,576]{1,2,0:T(8,128)(2,1)} fusion(bf16[4,128,576]{1,2,0:T(8,128)(2,1)S(1)} %copy-done, f32[4,128]{1,0:T(4,128)S(1)} %get-tuple-element.17, f32[576]{0:T(1024)S(1)} %copy-done.5, f32[4,128]{1,0:T(4,128)S(1)} %add_rsqrt_fusion, f32[512,576]{0,1:T(8,128)S(1)} %get-tuple-element.24), kind=kLoop, calls=%fused_computation.18 | loop fusion | flops 1769472 | bytes 2365696 | tf_op jit(solution)/shard_map/convert_element_type | solution.py:140
  (61 shorter events, 12.0 us)
Async XLA Ops:
  4.2 23.8 %collective-permute-start = (bf16[128,512]{1,0:T(8,128)(2,1)S(1)}, bf16[128,512]{1,0:T(8,128)(2,1)}, u32[]{:S(2)}, u32[]{:S(2)}) collective-permute-start(bf16[128,512]{1,0:T(8,128)(2,1)S(1)} %dynamic-slice_bitcast_fusion), channel_id=1, source_target_pairs={{0,4},{4,8},{8,12},{12,16},{16,20},{20,24},{24,28},{28,0},{1,5},{5... | collective-permute-start | bytes 393224 | tf_op jit(solution)/shard_map/ppermute | solution.py:33
  7.2 23.1 %collective-permute-start.1 = (bf16[128,512]{1,0:T(8,128)(2,1)S(1)}, bf16[128,512]{1,0:T(8,128)(2,1)}, u32[]{:S(2)}, u32[]{:S(2)}) collective-permute-start(bf16[128,512]{1,0:T(8,128)(2,1)S(1)} %dynamic-slice_bitcast_fusion), channel_id=1, source_target_pairs={{0,8},{4,12},{8,16},{12,20},{16,24},{20,28},{24,0},{28,4},{1,9},{5... | collective-permute-start | bytes 393224 | tf_op jit(solution)/shard_map/ppermute | solution.py:33
  8.8 24.1 %collective-permute-start.2 = (bf16[128,512]{1,0:T(8,128)(2,1)S(1)}, bf16[128,512]{1,0:T(8,128)(2,1)}, u32[]{:S(2)}, u32[]{:S(2)}) collective-permute-start(bf16[128,512]{1,0:T(8,128)(2,1)S(1)} %dynamic-slice_bitcast_fusion), channel_id=1, source_target_pairs={{0,12},{4,16},{8,20},{12,24},{16,28},{20,0},{24,4},{28,8},{1,13},{... | collective-permute-start | bytes 393224 | tf_op jit(solution)/shard_map/ppermute | solution.py:33
  11.3 22.5 %collective-permute-start.3 = (bf16[128,512]{1,0:T(8,128)(2,1)S(1)}, bf16[128,512]{1,0:T(8,128)(2,1)}, u32[]{:S(2)}, u32[]{:S(2)}) collective-permute-start(bf16[128,512]{1,0:T(8,128)(2,1)S(1)} %dynamic-slice_bitcast_fusion), channel_id=1, source_target_pairs={{0,16},{4,20},{8,24},{12,28},{16,0},{20,4},{24,8},{28,12},{1,17},{... | collective-permute-start | bytes 393224 | tf_op jit(solution)/shard_map/ppermute | solution.py:33
  12.6 22.2 %collective-permute-start.4 = (bf16[128,512]{1,0:T(8,128)(2,1)S(1)}, bf16[128,512]{1,0:T(8,128)(2,1)}, u32[]{:S(2)}, u32[]{:S(2)}) collective-permute-start(bf16[128,512]{1,0:T(8,128)(2,1)S(1)} %dynamic-slice_bitcast_fusion), channel_id=1, source_target_pairs={{0,20},{4,24},{8,28},{12,0},{16,4},{20,8},{24,12},{28,16},{1,21},{... | collective-permute-start | bytes 393224 | tf_op jit(solution)/shard_map/ppermute | solution.py:33
  19.7 0.7 %copy-start.6 = (s32[8]{0:T(128)S(1)}, s32[8]{0:T(128)}, u32[]{:S(2)}) copy-start(s32[8]{0:T(128)} %param.12) | copy-start | bytes 100
  19.9 2.0 %copy-start.1 = (f32[4,128,2,128]{3,1,2,0:T(8,128)}, f32[4,128,2,128]{3,1,2,0:T(8,128)S(1)}, u32[]{:S(2)}) copy-start(f32[4,128,2,128]{3,1,2,0:T(8,128)S(1)} %get-tuple-element.9) | copy-start | bytes 1572868
  19.9 2.0 %copy-start.3 = (f32[4,128,2,128]{3,1,2,0:T(8,128)}, f32[4,128,2,128]{3,1,2,0:T(8,128)S(1)}, u32[]{:S(2)}) copy-start(f32[4,128,2,128]{3,1,2,0:T(8,128)S(1)} %get-tuple-element.10) | copy-start | bytes 1572868
  28.0 7.7 %collective-permute-start.5 = (bf16[128,512]{1,0:T(8,128)(2,1)S(1)}, bf16[128,512]{1,0:T(8,128)(2,1)S(1)}, u32[]{:S(2)}, u32[]{:S(2)}) collective-permute-start(bf16[128,512]{1,0:T(8,128)(2,1)S(1)} %dynamic-slice_bitcast_fusion), channel_id=1, source_target_pairs={{0,24},{4,28},{8,0},{12,4},{16,8},{20,12},{24,16},{28,20},{1,25},{... | collective-permute-start | bytes 393224 | tf_op jit(solution)/shard_map/ppermute | solution.py:33
  30.3 5.4 %collective-permute-start.6 = (bf16[128,512]{1,0:T(8,128)(2,1)S(1)}, bf16[128,512]{1,0:T(8,128)(2,1)S(1)}, u32[]{:S(2)}, u32[]{:S(2)}) collective-permute-start(bf16[128,512]{1,0:T(8,128)(2,1)S(1)} %dynamic-slice_bitcast_fusion), channel_id=1, source_target_pairs={{0,28},{4,0},{8,4},{12,8},{16,12},{20,16},{24,20},{28,24},{1,29},{... | collective-permute-start | bytes 393224 | tf_op jit(solution)/shard_map/ppermute | solution.py:33
  35.7 1.0 %copy-start.2 = (f32[4,128,2,128]{3,1,2,0:T(8,128)S(1)}, f32[4,128,2,128]{3,1,2,0:T(8,128)}, u32[]{:S(2)}) copy-start(f32[4,128,2,128]{3,1,2,0:T(8,128)} %copy-done.1) | copy-start | bytes 1572868
  35.7 1.2 %copy-start.4 = (f32[4,128,2,128]{3,1,2,0:T(8,128)S(1)}, f32[4,128,2,128]{3,1,2,0:T(8,128)}, u32[]{:S(2)}) copy-start(f32[4,128,2,128]{3,1,2,0:T(8,128)} %copy-done.3) | copy-start | bytes 1572868
  36.9 1.5 %copy-start.7 = (f32[4,128,2,128]{1,3,2,0:T(8,128)S(1)}, f32[4,128,2,128]{1,3,2,0:T(8,128)}, u32[]{:S(2)}) copy-start(f32[4,128,2,128]{1,3,2,0:T(8,128)} %get-tuple-element.22) | copy-start | bytes 1572868
  40.9 14.4 %collective-permute-start.7 = (bf16[512,512]{1,0:T(8,128)(2,1)S(1)}, bf16[512,512]{1,0:T(8,128)(2,1)S(1)}, u32[]{:S(2)}, u32[]{:S(2)}) collective-permute-start(bf16[512,512]{1,0:T(8,128)(2,1)S(1)} %bitcast.98), channel_id=1, source_target_pairs={{0,1},{1,0},{2,3},{3,2},{4,5},{5,4},{6,7},{7,6},{8,9},{9,8},{10,11... | collective-permute-start | bytes 1572872 | tf_op jit(solution)/shard_map/ppermute | solution.py:37
  40.9 14.3 %collective-permute-start.8 = (bf16[512,512]{1,0:T(8,128)(2,1)S(1)}, bf16[512,512]{1,0:T(8,128)(2,1)S(1)}, u32[]{:S(2)}, u32[]{:S(2)}) collective-permute-start(bf16[512,512]{1,0:T(8,128)(2,1)S(1)} %bitcast.99), channel_id=1, source_target_pairs={{0,2},{1,3},{2,0},{3,1},{4,6},{5,7},{6,4},{7,5},{8,10},{9,11},{10,... | collective-permute-start | bytes 1572872 | tf_op jit(solution)/shard_map/ppermute | solution.py:37
  55.3 1.9 %collective-permute-start.9 = (bf16[512,512]{1,0:T(8,128)(2,1)S(1)}, bf16[512,512]{1,0:T(8,128)(2,1)S(1)}, u32[]{:S(2)}, u32[]{:S(2)}) collective-permute-start(bf16[512,512]{1,0:T(8,128)(2,1)S(1)} %collective-permute-done.8), channel_id=1, source_target_pairs={{0,1},{1,0},{2,3},{3,2},{4,5},{5,4},{6,7},{7,6},{8,9},{9,8},{10,11... | collective-permute-start | bytes 1572872 | tf_op jit(solution)/shard_map/ppermute | solution.py:37
  57.2 5.4 %copy-start = (bf16[4,128,576]{1,2,0:T(8,128)(2,1)S(1)}, bf16[4,128,576]{1,2,0:T(8,128)(2,1)}, u32[]{:S(2)}) copy-start(bf16[4,128,576]{1,2,0:T(8,128)(2,1)} %param.9) | copy-start | bytes 1769476
  57.2 5.4 %copy-start.5 = (f32[576]{0:T(1024)S(1)}, f32[576]{0:T(1024)}, u32[]{:S(2)}) copy-start(f32[576]{0:T(1024)} %param.17) | copy-start | bytes 6916
  57.7 2.6 %collective-permute-start.12 = (f32[4,128]{1,0:T(4,128)S(1)}, f32[4,128]{1,0:T(4,128)S(1)}, u32[]{:S(2)}, u32[]{:S(2)}) collective-permute-start(f32[4,128]{1,0:T(4,128)S(1)} %bitcast.103), channel_id=1, source_target_pairs={{0,3},{1,0},{2,1},{3,2},{4,7},{5,4},{6,5},{7,6},{8,11},{9,8},{10,9... | collective-permute-start | bytes 6152 | tf_op jit(solution)/shard_map/ppermute | solution.py:33
  59.0 3.6 %collective-permute-start.11 = (f32[4,128]{1,0:T(4,128)S(1)}, f32[4,128]{1,0:T(4,128)S(1)}, u32[]{:S(2)}, u32[]{:S(2)}) collective-permute-start(f32[4,128]{1,0:T(4,128)S(1)} %bitcast.104), channel_id=1, source_target_pairs={{0,2},{1,3},{2,0},{3,1},{4,6},{5,7},{6,4},{7,5},{8,10},{9,11},{10,... | collective-permute-start | bytes 6152 | tf_op jit(solution)/shard_map/ppermute | solution.py:33
  59.5 3.1 %collective-permute-start.10 = (f32[4,128]{1,0:T(4,128)S(1)}, f32[4,128]{1,0:T(4,128)S(1)}, u32[]{:S(2)}, u32[]{:S(2)}) collective-permute-start(f32[4,128]{1,0:T(4,128)S(1)} %bitcast.105), channel_id=1, source_target_pairs={{0,1},{1,2},{2,3},{3,0},{4,5},{5,6},{6,7},{7,4},{8,9},{9,10},{10,1... | collective-permute-start | bytes 6152 | tf_op jit(solution)/shard_map/ppermute | solution.py:33

commit v2 on v1

--- a/solution.py
+++ b/solution.py
@@ -51,12 +51,12 @@
             sources.append((device_row - shift) % n_req)
         sources = jnp.stack(sources)
         valid = jnp.any(page_owner[None, :] == sources[:, None], 1)
-        return jnp.stack(blocks), valid
+        return blocks, valid
     picked = page_store[page_slot][:, :, 0]
     held_here = page_owner == device_row
     offered = jnp.where(held_here[:, None, None], picked, jnp.zeros_like(picked))
     prefix = lax.psum(offered, "req")
-    return prefix, jnp.ones((page_count,), jnp.bool_)
+    return [prefix[p] for p in range(page_count)], jnp.ones((page_count,), jnp.bool_)
 
 
 def on_device(
@@ -69,10 +69,6 @@
     tp_index = lax.axis_index("tp")
 
     blocks, valid = gather_prefix(page_store, page_owner, page_slot, n_req)
-    block_count, page_len = blocks.shape[0], blocks.shape[1]
-    prefix_keys = blocks[:, :, :HD].reshape(block_count * page_len, HD)
-    prefix_values = blocks[:, :, HD:].reshape(block_count * page_len, HD)
-    key_valid = jnp.repeat(valid, page_len)
 
     device_row = lax.axis_index("req")
     my_requests = lax.dynamic_slice_in_dim(request_perm, device_row * requests, requests)
@@ -91,10 +87,6 @@
     fresh_keys = rotate(projections[:, :, per_group], cosine[None], sine[None]).astype(jnp.bfloat16)
     fresh_values = projections[:, :, per_group + 1].astype(jnp.bfloat16)
 
-    prefix_weights = capped_exp(
-        jnp.einsum("rsqh,th->rsqt", queries, prefix_keys, preferred_element_type=jnp.float32)
-    )
-    prefix_weights = jnp.where(key_valid[None, None, None, :], prefix_weights, 0.0)
     allowed = (position[None, None, :] <= position[None, :, None]) & (
         position[None, None, :] < my_lengths[:, None, None]
     )
@@ -102,19 +94,25 @@
         jnp.einsum("rsqh,rth->rsqt", queries, fresh_keys, preferred_element_type=jnp.float32)
     )
     suffix_weights = jnp.where(allowed[:, :, None, :], suffix_raw, 0.0)
-    totals = jnp.sum(prefix_weights, -1) + jnp.sum(suffix_weights, -1)
-    prefix_probs = (prefix_weights / totals[..., None]).astype(jnp.bfloat16)
-    suffix_probs = (suffix_weights / totals[..., None]).astype(jnp.bfloat16)
+    totals = jnp.sum(suffix_weights, -1)
     attended = jnp.einsum(
-        "rsqt,th->rsqh", prefix_probs, prefix_values, preferred_element_type=jnp.float32
+        "rsqt,rth->rsqh", suffix_weights.astype(jnp.bfloat16), fresh_values,
+        preferred_element_type=jnp.float32,
     )
-    attended = attended + jnp.einsum(
-        "rsqt,rth->rsqh", suffix_probs, fresh_values, preferred_element_type=jnp.float32
-    )
+    for index, block in enumerate(blocks):
+        raw = capped_exp(
+            jnp.einsum("rsqh,th->rsqt", queries, block[:, :HD], preferred_element_type=jnp.float32)
+        )
+        weights = jnp.where(valid[index], raw, 0.0)
+        totals = totals + jnp.sum(weights, -1)
+        attended = attended + jnp.einsum(
+            "rsqt,th->rsqh", weights.astype(jnp.bfloat16), block[:, HD:],
+            preferred_element_type=jnp.float32,
+        )
+    attended = attended / totals[..., None]
     own = attended.astype(jnp.bfloat16).reshape(token_rows, per_group * HD)
 
     group_width = per_group * HD
-    w_blocks = w_out.reshape(n_tp, group_width, local_width)
     if n_tp == 4:
         near = swapped(own, "tp", n_tp, 1)
         far = swapped(own, "tp", n_tp, 2)
@@ -126,7 +124,7 @@
             parts.append((shifted(own, "tp", n_tp, shift), (tp_index - shift) % n_tp))
     projected = None
     for block, group in parts:
-        rows = lax.dynamic_index_in_dim(w_blocks, group, 0, keepdims=False)
+        rows = lax.dynamic_slice_in_dim(w_out, group * group_width, group_width, 0)
         term = jnp.dot(block, rows, preferred_element_type=jnp.float32)
         projected = term if projected is None else projected + term
     projected = projected.reshape(requests, slots, local_width)

time: 64.1 us -> 75.1 us (1.17)
  matrix products: 6.49 us -> 23.1 us
  local copies, waits for them, and re-layouts: 21.5 us -> 7.91 us
  other arithmetic: 4.44 us -> 10.3 us
  starting transfers between devices: 17.5 us -> 19.4 us
    dot_general x3 -> x17, matrix products: 3.28 us -> 19.6 us  [the longest x8 12.1 us: on_device(): jnp.einsum('rsqh,th->rsqt', queries, block[:, :HD], preferred_element_typ...]
    unnamed x25 -> x10, local copies, waits for them, and re-layouts: 8.54 us -> 2.38 us
    reshape x1 -> x0, local copies, waits for them, and re-layouts: 5.08 us -> none  [on_device(): w_blocks = w_out.reshape(n_tp, group_width, local_width)]
    dynamic_slice x1 -> x0, local copies, waits for them, and re-layouts: 4.89 us -> none  [on_device(): rows = lax.dynamic_index_in_dim(w_blocks, group, 0, keepdims=False)]
    ppermute x10, starting transfers between devices: 15.9 us -> 17.8 us  [shifted(): lax.ppermute(value, axis, [(i, (i + shift) % size) for i in range(size)])]
    ppermute x10, waiting for transfers between devices: 3.07 us -> 1.33 us  [shifted(): lax.ppermute(value, axis, [(i, (i + shift) % size) for i in range(size)])]
    ppermute x3, waiting for transfers between devices: 8.23 us -> 9.71 us  [swapped(): return lax.ppermute(value, axis, [(i, i ^ mask) for i in range(size)])]
    convert_element_type x1, other arithmetic: 0.22 us -> 1.58 us  [on_device(): qkv[:, :, 0].astype(jnp.float32).reshape(requests, slots, per_group + 2, HD)]
  transfers between devices with their start and end apart: 13 -> 13, of which waited for: 4 -> 3; matrix products, arithmetic and copies ran while one was open for 36% -> 39% of each run, Pallas kernels for 0% -> 0%
where the time goes in v2:
time: 75.1 us; the launch traced here: 74.1 us
  matrix products  23.1 us (31%)
  starting transfers between devices  19.4 us (26%)
  waiting for transfers between devices  11 us (15%)
  other arithmetic  10.3 us (14%)
  local copies, waits for them, and re-layouts  7.91 us (11%)
  between operations  2.44 us (3%)
    ppermute x10, starting transfers between devices, shifted(): lax.ppermute(value, axis, [(i, (i + shift) % size) for i in range(size)])  17.8 us
    dot_general x8, matrix products, on_device(): jnp.einsum('rsqh,th->rsqt', queries, block[:, :HD], preferred_element_typ...  12.1 us
    ppermute x3, waiting for transfers between devices, swapped(): return lax.ppermute(value, axis, [(i, i ^ mask) for i in range(size)])  9.71 us
    dot_general x8, matrix products, on_device(): jnp.einsum('rsqt,th->rsqh', weights.astype(jnp.bfloat16), block[:, HD:],...  7.14 us
    dot_general x4, matrix products, on_device(): term = jnp.dot(block, rows, preferred_element_type=jnp.float32)  3.08 us
    unnamed x10, local copies, waits for them, and re-layouts  2.38 us
    convert_element_type x1, other arithmetic, on_device(): qkv[:, :, 0].astype(jnp.float32).reshape(requests, slots, per_group + 2, HD)  1.58 us
    ppermute x3, starting transfers between devices, swapped(): return lax.ppermute(value, axis, [(i, i ^ mask) for i in range(size)])  1.55 us
  transfers between devices with their start and end apart: 13, of which 3 were waited for; matrix products, arithmetic and copies ran while one was open for 39% of the time, Pallas kernels for 0%

profile of v2, /device:TPU:0, one launch (start us, length us, event | category | flops | bytes accessed | tf_op | source)
XLA Modules:
  0.0 74.1 jit_solution(794698587951611524)
XLA Ops:
  0.0 1.5 %fusion.85 = s32[]{:T(128)} fusion(s32[8]{0:T(128)} %param.13, s32[8]{0:T(128)} %param.12, s32[]{:T(128)} %axis_index.27), kind=kLoop, calls=%fused_computation.137 | loop fusion | flops 23 | bytes 72 | tf_op jit(solution)/shard_map/reduce_sum | solution.py:45
  4.5 5.1 %collective-permute-start.5 = (bf16[128,512]{1,0:T(8,128)(2,1)S(1)}, bf16[128,512]{1,0:T(8,128)(2,1)}, u32[]{:S(2)}, u32[]{:S(2)}) collective-permute-start(bf16[128,512]{1,0:T(8,128)(2,1)S(1)} %dynamic-slice_bitcast_fusion), channel_id=1, source_target_pairs={{0,24},{4,28},{8,0},{12,4},{16,8},{20,12},{24,16},{28,20},{1,25},{... | collective-permute-start | bytes 393224 | tf_op jit(solution)/shard_map/ppermute | solution.py:33
  10.1 3.5 %collective-permute-start.3 = (bf16[128,512]{1,0:T(8,128)(2,1)S(1)}, bf16[128,512]{1,0:T(8,128)(2,1)}, u32[]{:S(2)}, u32[]{:S(2)}) collective-permute-start(bf16[128,512]{1,0:T(8,128)(2,1)S(1)} %dynamic-slice_bitcast_fusion), channel_id=1, source_target_pairs={{0,16},{4,20},{8,24},{12,28},{16,0},{20,4},{24,8},{28,12},{1,17},{... | collective-permute-start | bytes 393224 | tf_op jit(solution)/shard_map/ppermute | solution.py:33
  17.3 2.3 %copy.52 = bf16[4,128,1,1024]{1,3,0,2:T(8,128)(2,1)} copy(bf16[4,128,1,1024]{3,1,2,0:T(8,128)(2,1)} %param.10) | data formatting | bytes 2097152 | tf_op args[1]
  19.6 1.5 %copy.53 = bf16[4,128,4,256]{3,1,0,2:T(8,128)(2,1)S(1)} copy(bf16[4,128,4,256]{1,3,2,0:T(8,128)(2,1)} %bitcast.171) | data formatting | bytes 2097152 | tf_op jit(solution)/shard_map/convert_element_type | solution.py:80
  21.1 1.6 %convert_element_type.81 = f32[4,128,4,256]{3,1,0,2:T(8,128)} convert(bf16[4,128,4,256]{3,1,0,2:T(8,128)(2,1)S(1)} %copy.53) | non-fusion elementwise | flops 524288 | bytes 3145728 | tf_op jit(solution)/shard_map/convert_element_type | solution.py:80
  26.9 1.3 %multiply_subtract_fusion = (f32[4,128,2,128]{3,1,0,2:T(8,128)S(1)}, f32[4,128,2,128]{3,1,0,2:T(8,128)S(1)}) fusion(f32[4,128,4,256]{3,1,0,2:T(8,128)} %convert_element_type.81, f32[128,128]{1,0:T(8,128)S(1)} %get-tuple-element.10, f32[128,128]{1,0:T(8,128)S(1)} %get-tuple-element.9), kind=kLoop, calls=%fused_computation.73 | loop fusion | flops 786432 | bytes 2228224 | tf_op jit(solution)/shard_map/sub | solution.py:25
  30.6 1.6 %collective-permute-start = (bf16[128,512]{1,0:T(8,128)(2,1)S(1)}, bf16[128,512]{1,0:T(8,128)(2,1)S(1)}, u32[]{:S(2)}, u32[]{:S(2)}) collective-permute-start(bf16[128,512]{1,0:T(8,128)(2,1)S(1)} %dynamic-slice_bitcast_fusion), channel_id=1, source_target_pairs={{0,4},{4,8},{8,12},{12,16},{16,20},{20,24},{24,28},{28,0},{1,5},{5... | collective-permute-start | bytes 393224 | tf_op jit(solution)/shard_map/ppermute | solution.py:33
  32.2 1.9 %fusion.90 = (f32[4,128,2]{1,2,0:T(2,128)S(1)}, bf16[4,128,2,128]{1,3,2,0:T(8,128)(2,1)S(1)}) fusion(bf16[128,512]{1,0:T(8,128)(2,1)} %collective-permute-done.5, bf16[4,128,2,256]{3,1,0,2:T(8,128)(2,1)S(1)} %fusion.48, pred[]{:T(512)} %bitcast.46), kind=kOutput, calls=%fused_computation.144 | convolution fusion | flops 67763200 | bytes 856576 | tf_op jit(solution)/shard_map/rsqh,th->rsqt/dot_general | solution.py:104
  34.1 3.3 %collective-permute-start.6 = (bf16[128,512]{1,0:T(8,128)(2,1)S(1)}, bf16[128,512]{1,0:T(8,128)(2,1)S(1)}, u32[]{:S(2)}, u32[]{:S(2)}) collective-permute-start(bf16[128,512]{1,0:T(8,128)(2,1)S(1)} %dynamic-slice_bitcast_fusion), channel_id=1, source_target_pairs={{0,28},{4,0},{8,4},{12,8},{16,12},{20,16},{24,20},{28,24},{1,29},{... | collective-permute-start | bytes 393224 | tf_op jit(solution)/shard_map/ppermute | solution.py:33
  37.3 1.8 %fusion.91 = (f32[4,128,2]{1,2,0:T(2,128)S(1)}, bf16[4,128,2,128]{1,3,2,0:T(8,128)(2,1)S(1)}) fusion(bf16[128,512]{1,0:T(8,128)(2,1)} %collective-permute-done.4, bf16[4,128,2,256]{3,1,0,2:T(8,128)(2,1)S(1)} %fusion.48, pred[]{:T(512)} %bitcast.41), kind=kOutput, calls=%fused_computation.145 | convolution fusion | flops 67763200 | bytes 856576 | tf_op jit(solution)/shard_map/rsqh,th->rsqt/dot_general | solution.py:104
  39.1 1.8 %fusion.92 = (f32[4,128,2]{1,2,0:T(2,128)S(1)}, bf16[4,128,2,128]{1,3,2,0:T(8,128)(2,1)S(1)}) fusion(bf16[128,512]{1,0:T(8,128)(2,1)} %collective-permute-done.3, bf16[4,128,2,256]{3,1,0,2:T(8,128)(2,1)S(1)} %fusion.48, pred[]{:T(512)} %bitcast.36), kind=kOutput, calls=%fused_computation.146 | convolution fusion | flops 67763200 | bytes 856576 | tf_op jit(solution)/shard_map/rsqh,th->rsqt/dot_general | solution.py:104
  40.9 1.8 %fusion.93 = (f32[4,128,2]{1,2,0:T(2,128)S(1)}, bf16[4,128,2,128]{1,3,2,0:T(8,128)(2,1)S(1)}) fusion(bf16[128,512]{1,0:T(8,128)(2,1)} %collective-permute-done.2, bf16[4,128,2,256]{3,1,0,2:T(8,128)(2,1)S(1)} %fusion.48, pred[]{:T(512)} %bitcast.31), kind=kOutput, calls=%fused_computation.147 | convolution fusion | flops 67763200 | bytes 856576 | tf_op jit(solution)/shard_map/rsqh,th->rsqt/dot_general | solution.py:104
  42.8 1.9 %fusion.94 = (f32[4,128,2]{1,2,0:T(2,128)S(1)}, bf16[4,128,2,128]{1,3,2,0:T(8,128)(2,1)S(1)}) fusion(bf16[128,512]{1,0:T(8,128)(2,1)} %collective-permute-done.1, bf16[4,128,2,256]{3,1,0,2:T(8,128)(2,1)S(1)} %fusion.48, pred[]{:T(512)} %bitcast.26), kind=kOutput, calls=%fused_computation.148 | convolution fusion | flops 67763200 | bytes 856576 | tf_op jit(solution)/shard_map/rsqh,th->rsqt/dot_general | solution.py:104
  46.7 1.2 %fusion.59 = f32[4,128,2,256]{3,1,2,0:T(8,128)S(1)} fusion(bf16[4,128,2,128]{1,3,2,0:T(8,128)(2,1)S(1)} %get-tuple-element.24, bf16[128,512]{1,0:T(8,128)(2,1)} %collective-permute-done.5), kind=kOutput, calls=%fused_computation.81 | convolution fusion | flops 67108864 | bytes 1376256 | tf_op jit(solution)/shard_map/rsqt,th->rsqh/dot_general | solution.py:108
  47.9 1.2 %fusion.61 = f32[4,128,2,256]{3,1,2,0:T(8,128)S(1)} fusion(bf16[4,128,2,128]{1,3,2,0:T(8,128)(2,1)S(1)} %get-tuple-element.26, bf16[128,512]{1,0:T(8,128)(2,1)} %collective-permute-done.4), kind=kOutput, calls=%fused_computation.83 | convolution fusion | flops 67108864 | bytes 1376256 | tf_op jit(solution)/shard_map/rsqt,th->rsqh/dot_general | solution.py:108
  49.1 1.2 %fusion.63 = f32[4,128,2,256]{3,1,2,0:T(8,128)S(1)} fusion(bf16[4,128,2,128]{1,3,2,0:T(8,128)(2,1)S(1)} %get-tuple-element.28, bf16[128,512]{1,0:T(8,128)(2,1)} %collective-permute-done.3), kind=kOutput, calls=%fused_computation.85 | convolution fusion | flops 67108864 | bytes 1376256 | tf_op jit(solution)/shard_map/rsqt,th->rsqh/dot_general | solution.py:108
  50.2 1.2 %fusion.65 = f32[4,128,2,256]{3,1,2,0:T(8,128)S(1)} fusion(bf16[4,128,2,128]{1,3,2,0:T(8,128)(2,1)S(1)} %get-tuple-element.30, bf16[128,512]{1,0:T(8,128)(2,1)} %collective-permute-done.2), kind=kOutput, calls=%fused_computation.87 | convolution fusion | flops 67108864 | bytes 1376256 | tf_op jit(solution)/shard_map/rsqt,th->rsqh/dot_general | solution.py:108
  51.4 1.2 %fusion.67 = f32[4,128,2,256]{3,1,2,0:T(8,128)S(1)} fusion(bf16[4,128,2,128]{1,3,2,0:T(8,128)(2,1)S(1)} %get-tuple-element.32, bf16[128,512]{1,0:T(8,128)(2,1)} %collective-permute-done.1), kind=kOutput, calls=%fused_computation.89 | convolution fusion | flops 67108864 | bytes 1376256 | tf_op jit(solution)/shard_map/rsqt,th->rsqh/dot_general | solution.py:108
  54.2 1.5 %collective-permute-start.8 = (bf16[512,512]{1,0:T(8,128)(2,1)S(1)}, bf16[512,512]{1,0:T(8,128)(2,1)S(1)}, u32[]{:S(2)}, u32[]{:S(2)}) collective-permute-start(bf16[512,512]{1,0:T(8,128)(2,1)S(1)} %bitcast.172), channel_id=1, source_target_pairs={{0,2},{1,3},{2,0},{3,1},{4,6},{5,7},{6,4},{7,5},{8,10},{9,11},{10,... | collective-permute-start | bytes 1572872 | tf_op jit(solution)/shard_map/ppermute | solution.py:37
  56.3 9.7 %collective-permute-done.8 = bf16[512,512]{1,0:T(8,128)(2,1)S(1)} collective-permute-done((bf16[512,512]{1,0:T(8,128)(2,1)S(1)}, bf16[512,512]{1,0:T(8,128)(2,1)S(1)}, u32[]{:S(2)}, u32[]{:S(2)}) %collective-permute-start.8) | collective-permute-done | bytes 524320 | tf_op jit(solution)/shard_map/ppermute | solution.py:37
  66.0 1.5 %convolution_add_fusion.2 = f32[512,576]{0,1:T(8,128)S(1)} fusion(f32[512,576]{0,1:T(8,128)S(1)} %fusion.52, bf16[512,512]{1,0:T(8,128)(2,1)} %collective-permute-done.7, bf16[2048,576]{0,1:T(8,128)(2,1)S(1)} %copy-done, s32[]{:T(128)S(6)} %select_n.141), kind=kOutput, calls=%fused_computation.2 | convolution fusion | flops 302284800 | bytes 3473412 | tf_op jit(solution)/shard_map/dot_general | solution.py:128
  69.2 1.5 %collective-permute-start.11 = (f32[4,128]{1,0:T(4,128)S(1)}, f32[4,128]{1,0:T(4,128)S(1)}, u32[]{:S(2)}, u32[]{:S(2)}) collective-permute-start(f32[4,128]{1,0:T(4,128)S(1)} %bitcast.178), channel_id=1, source_target_pairs={{0,2},{1,3},{2,0},{3,1},{4,6},{5,7},{6,4},{7,5},{8,10},{9,11},{10,... | collective-permute-start | bytes 6152 | tf_op jit(solution)/shard_map/ppermute | solution.py:33
  73.0 1.1 %fusion.47 = bf16[4,128,576]{1,2,0:T(8,128)(2,1)} fusion(bf16[4,128,576]{1,2,0:T(8,128)(2,1)S(1)} %copy-done.1, f32[4,128]{1,0:T(4,128)S(1)} %copy-done.2, f32[576]{0:T(1024)S(1)} %copy-done.3, f32[4,128]{1,0:T(4,128)S(1)} %add_rsqrt_fusion, f32[512,576]{0,1:T(8,128)S(1)} %get-tuple-element.40), kind=kLoop, calls=%fused_computation.62 | loop fusion | flops 1769472 | bytes 2365696 | tf_op jit(solution)/shard_map/convert_element_type | solution.py:138
  (57 shorter events, 19.6 us)
Async XLA Ops:
  0.0 55.8 %copy-start = (bf16[2048,576]{0,1:T(8,128)(2,1)S(1)}, bf16[2048,576]{0,1:T(8,128)(2,1)}, u32[]{:S(2)}) copy-start(bf16[2048,576]{0,1:T(8,128)(2,1)} %param.16) | copy-start | bytes 7077892
  4.5 26.1 %collective-permute-start.5 = (bf16[128,512]{1,0:T(8,128)(2,1)S(1)}, bf16[128,512]{1,0:T(8,128)(2,1)}, u32[]{:S(2)}, u32[]{:S(2)}) collective-permute-start(bf16[128,512]{1,0:T(8,128)(2,1)S(1)} %dynamic-slice_bitcast_fusion), channel_id=1, source_target_pairs={{0,24},{4,28},{8,0},{12,4},{16,8},{20,12},{24,16},{28,20},{1,25},{... | collective-permute-start | bytes 393224 | tf_op jit(solution)/shard_map/ppermute | solution.py:33
  9.7 24.4 %collective-permute-start.4 = (bf16[128,512]{1,0:T(8,128)(2,1)S(1)}, bf16[128,512]{1,0:T(8,128)(2,1)}, u32[]{:S(2)}, u32[]{:S(2)}) collective-permute-start(bf16[128,512]{1,0:T(8,128)(2,1)S(1)} %dynamic-slice_bitcast_fusion), channel_id=1, source_target_pairs={{0,20},{4,24},{8,28},{12,0},{16,4},{20,8},{24,12},{28,16},{1,21},{... | collective-permute-start | bytes 393224 | tf_op jit(solution)/shard_map/ppermute | solution.py:33
  10.1 29.1 %collective-permute-start.3 = (bf16[128,512]{1,0:T(8,128)(2,1)S(1)}, bf16[128,512]{1,0:T(8,128)(2,1)}, u32[]{:S(2)}, u32[]{:S(2)}) collective-permute-start(bf16[128,512]{1,0:T(8,128)(2,1)S(1)} %dynamic-slice_bitcast_fusion), channel_id=1, source_target_pairs={{0,16},{4,20},{8,24},{12,28},{16,0},{20,4},{24,8},{28,12},{1,17},{... | collective-permute-start | bytes 393224 | tf_op jit(solution)/shard_map/ppermute | solution.py:33
  13.5 27.3 %collective-permute-start.2 = (bf16[128,512]{1,0:T(8,128)(2,1)S(1)}, bf16[128,512]{1,0:T(8,128)(2,1)}, u32[]{:S(2)}, u32[]{:S(2)}) collective-permute-start(bf16[128,512]{1,0:T(8,128)(2,1)S(1)} %dynamic-slice_bitcast_fusion), channel_id=1, source_target_pairs={{0,12},{4,16},{8,20},{12,24},{16,28},{20,0},{24,4},{28,8},{1,13},{... | collective-permute-start | bytes 393224 | tf_op jit(solution)/shard_map/ppermute | solution.py:33
  13.6 29.2 %collective-permute-start.1 = (bf16[128,512]{1,0:T(8,128)(2,1)S(1)}, bf16[128,512]{1,0:T(8,128)(2,1)}, u32[]{:S(2)}, u32[]{:S(2)}) collective-permute-start(bf16[128,512]{1,0:T(8,128)(2,1)S(1)} %dynamic-slice_bitcast_fusion), channel_id=1, source_target_pairs={{0,8},{4,12},{8,16},{12,20},{16,24},{20,28},{24,0},{28,4},{1,9},{5... | collective-permute-start | bytes 393224 | tf_op jit(solution)/shard_map/ppermute | solution.py:33
  30.6 14.0 %collective-permute-start = (bf16[128,512]{1,0:T(8,128)(2,1)S(1)}, bf16[128,512]{1,0:T(8,128)(2,1)S(1)}, u32[]{:S(2)}, u32[]{:S(2)}) collective-permute-start(bf16[128,512]{1,0:T(8,128)(2,1)S(1)} %dynamic-slice_bitcast_fusion), channel_id=1, source_target_pairs={{0,4},{4,8},{8,12},{12,16},{16,20},{20,24},{24,28},{28,0},{1,5},{5... | collective-permute-start | bytes 393224 | tf_op jit(solution)/shard_map/ppermute | solution.py:33
  34.1 11.7 %collective-permute-start.6 = (bf16[128,512]{1,0:T(8,128)(2,1)S(1)}, bf16[128,512]{1,0:T(8,128)(2,1)S(1)}, u32[]{:S(2)}, u32[]{:S(2)}) collective-permute-start(bf16[128,512]{1,0:T(8,128)(2,1)S(1)} %dynamic-slice_bitcast_fusion), channel_id=1, source_target_pairs={{0,28},{4,0},{8,4},{12,8},{16,12},{20,16},{24,20},{28,24},{1,29},{... | collective-permute-start | bytes 393224 | tf_op jit(solution)/shard_map/ppermute | solution.py:33
  54.2 11.8 %collective-permute-start.8 = (bf16[512,512]{1,0:T(8,128)(2,1)S(1)}, bf16[512,512]{1,0:T(8,128)(2,1)S(1)}, u32[]{:S(2)}, u32[]{:S(2)}) collective-permute-start(bf16[512,512]{1,0:T(8,128)(2,1)S(1)} %bitcast.172), channel_id=1, source_target_pairs={{0,2},{1,3},{2,0},{3,1},{4,6},{5,7},{6,4},{7,5},{8,10},{9,11},{10,... | collective-permute-start | bytes 1572872 | tf_op jit(solution)/shard_map/ppermute | solution.py:37
  55.8 10.2 %collective-permute-start.7 = (bf16[512,512]{1,0:T(8,128)(2,1)S(1)}, bf16[512,512]{1,0:T(8,128)(2,1)}, u32[]{:S(2)}, u32[]{:S(2)}) collective-permute-start(bf16[512,512]{1,0:T(8,128)(2,1)S(1)} %bitcast.173), channel_id=1, source_target_pairs={{0,1},{1,0},{2,3},{3,2},{4,5},{5,4},{6,7},{7,6},{8,9},{9,8},{10,11... | collective-permute-start | bytes 1572872 | tf_op jit(solution)/shard_map/ppermute | solution.py:37
  66.0 2.1 %collective-permute-start.9 = (bf16[512,512]{1,0:T(8,128)(2,1)S(1)}, bf16[512,512]{1,0:T(8,128)(2,1)S(1)}, u32[]{:S(2)}, u32[]{:S(2)}) collective-permute-start(bf16[512,512]{1,0:T(8,128)(2,1)S(1)} %collective-permute-done.8), channel_id=1, source_target_pairs={{0,1},{1,0},{2,3},{3,2},{4,5},{5,4},{6,7},{7,6},{8,9},{9,8},{10,11... | collective-permute-start | bytes 1572872 | tf_op jit(solution)/shard_map/ppermute | solution.py:37
  68.1 4.9 %copy-start.1 = (bf16[4,128,576]{1,2,0:T(8,128)(2,1)S(1)}, bf16[4,128,576]{1,2,0:T(8,128)(2,1)}, u32[]{:S(2)}) copy-start(bf16[4,128,576]{1,2,0:T(8,128)(2,1)} %param.9) | copy-start | bytes 1769476
  68.1 4.9 %copy-start.2 = (f32[4,128]{1,0:T(4,128)S(1)}, f32[4,128]{1,0:T(4,128)}, u32[]{:S(2)}) copy-start(f32[4,128]{1,0:T(4,128)} %get-tuple-element.11) | copy-start | bytes 6148
  68.1 4.9 %copy-start.3 = (f32[576]{0:T(1024)S(1)}, f32[576]{0:T(1024)}, u32[]{:S(2)}) copy-start(f32[576]{0:T(1024)} %param.17) | copy-start | bytes 6916
  68.6 3.1 %collective-permute-start.10 = (f32[4,128]{1,0:T(4,128)S(1)}, f32[4,128]{1,0:T(4,128)S(1)}, u32[]{:S(2)}, u32[]{:S(2)}) collective-permute-start(f32[4,128]{1,0:T(4,128)S(1)} %bitcast.177), channel_id=1, source_target_pairs={{0,1},{1,2},{2,3},{3,0},{4,5},{5,6},{6,7},{7,4},{8,9},{9,10},{10,1... | collective-permute-start | bytes 6152 | tf_op jit(solution)/shard_map/ppermute | solution.py:33
  69.2 3.6 %collective-permute-start.11 = (f32[4,128]{1,0:T(4,128)S(1)}, f32[4,128]{1,0:T(4,128)S(1)}, u32[]{:S(2)}, u32[]{:S(2)}) collective-permute-start(f32[4,128]{1,0:T(4,128)S(1)} %bitcast.178), channel_id=1, source_target_pairs={{0,2},{1,3},{2,0},{3,1},{4,6},{5,7},{6,4},{7,5},{8,10},{9,11},{10,... | collective-permute-start | bytes 6152 | tf_op jit(solution)/shard_map/ppermute | solution.py:33
  70.7 2.3 %collective-permute-start.12 = (f32[4,128]{1,0:T(4,128)S(1)}, f32[4,128]{1,0:T(4,128)S(1)}, u32[]{:S(2)}, u32[]{:S(2)}) collective-permute-start(f32[4,128]{1,0:T(4,128)S(1)} %bitcast.179), channel_id=1, source_target_pairs={{0,3},{1,0},{2,1},{3,2},{4,7},{5,4},{6,5},{7,6},{8,11},{9,8},{10,9... | collective-permute-start | bytes 6152 | tf_op jit(solution)/shard_map/ppermute | solution.py:33

commit v3 on v2

--- a/solution.py
+++ b/solution.py
@@ -1,6 +1,9 @@
+import numpy as np
 import jax
 import jax.numpy as jnp
 from jax import lax
+from jax.experimental import pallas as pl
+from jax.experimental.pallas import tpu as pltpu
 from jax.sharding import PartitionSpec as P
 
 D = 2304
@@ -9,20 +12,6 @@
 
 EPSILON = 1e-06
 SOFT_CAP = 50.0
-
-
-def tables(positions, width):
-    half_width = width // 2
-    frequency = 10000.0 ** (-(jnp.arange(half_width, dtype=jnp.float32) * 2.0 / width))
-    angles = positions.astype(jnp.float32)[:, None] * frequency[None, :]
-    return (jnp.cos(angles), jnp.sin(angles))
-
-
-def rotate(values, cosine, sine):
-    half_width = values.shape[-1] // 2
-    first = values[..., :half_width]
-    second = values[..., half_width:]
-    return jnp.concatenate([first * cosine - second * sine, second * cosine + first * sine], -1)
 
 
 def capped_exp(scores):
@@ -59,6 +48,81 @@
     return [prefix[p] for p in range(page_count)], jnp.ones((page_count,), jnp.bool_)
 
 
+def static_tables(positions, width):
+    half_width = width // 2
+    exponent = np.arange(half_width, dtype=np.float32) * np.float32(2.0) / np.float32(width)
+    frequency = np.power(np.float32(10000.0), -exponent).astype(np.float32)
+    angles = positions.astype(np.float32)[:, None] * frequency[None, :]
+    return np.cos(angles).astype(np.float32), np.sin(angles).astype(np.float32)
+
+
+def attention_kernel(length_ref, valid_ref, qkv_ref, cos_ref, sin_ref, *rest):
+    page_refs, out_ref = rest[:-1], rest[-1]
+    request = pl.program_id(0)
+    slots = qkv_ref.shape[1]
+    per_group = qkv_ref.shape[2] // HD - 2
+    half = HD // 2
+    cosine = cos_ref[...]
+    sine = sin_ref[...]
+    values_in = qkv_ref[0].astype(jnp.float32)
+
+    def rope(part):
+        first = part[:, :half]
+        second = part[:, half:]
+        return jnp.concatenate([first * cosine - second * sine, second * cosine + first * sine], -1)
+
+    queries = jnp.concatenate(
+        [(rope(values_in[:, q * HD:(q + 1) * HD]) * HD ** (-0.5)).astype(jnp.bfloat16)
+         for q in range(per_group)], 0)
+    fresh_keys = rope(values_in[:, per_group * HD:(per_group + 1) * HD]).astype(jnp.bfloat16)
+    fresh_values = values_in[:, (per_group + 1) * HD:].astype(jnp.bfloat16)
+    pages = [ref[...] for ref in page_refs]
+    keys = jnp.concatenate([page[:, :HD] for page in pages] + [fresh_keys], 0)
+    values = jnp.concatenate([page[:, HD:] for page in pages] + [fresh_values], 0)
+    prefix_len = len(pages) * pages[0].shape[0]
+    key_count = keys.shape[0]
+    rows = queries.shape[0]
+
+    scores = lax.dot_general(queries, keys, (((1,), (1,)), ((), ())),
+                             preferred_element_type=jnp.float32)
+    page_column = lax.broadcasted_iota(jnp.int32, (1, key_count), 1) // pages[0].shape[0]
+    page_flag = jnp.zeros((1, key_count), jnp.int32)
+    for index in range(len(pages)):
+        page_flag = page_flag + jnp.where(page_column == index, valid_ref[index], 0)
+    page_flag = page_flag.astype(jnp.float32)
+    column = lax.broadcasted_iota(jnp.int32, (rows, key_count), 1)
+    slot = lax.broadcasted_iota(jnp.int32, (rows, key_count), 0) % slots
+    suffix_pos = column - prefix_len
+    suffix_ok = (suffix_pos >= 0) & (suffix_pos <= slot) & (suffix_pos < length_ref[request])
+    exps = capped_exp(scores)
+    raw = jnp.where(suffix_ok, exps, jnp.where(column < prefix_len, exps * page_flag, 0.0))
+    totals = jnp.sum(raw, -1, keepdims=True)
+    weights = (raw / totals).astype(jnp.bfloat16)
+    attended = jnp.dot(weights, values, preferred_element_type=jnp.float32).astype(jnp.bfloat16)
+    out_ref[0] = jnp.concatenate(
+        [attended[q * slots:(q + 1) * slots] for q in range(per_group)], 1)
+
+
+def attend(qkv, cosine, sine, blocks, lengths, valid):
+    requests, slots, width = qkv.shape
+    per_group = width // HD - 2
+    page_len, page_width = blocks[0].shape
+    full = lambda shape: pl.BlockSpec(shape, lambda r, *_: (0,) * len(shape))
+    grid_spec = pltpu.PrefetchScalarGridSpec(
+        num_scalar_prefetch=2,
+        grid=(requests,),
+        in_specs=[pl.BlockSpec((1, slots, width), lambda r, *_: (r, 0, 0)),
+                  full(cosine.shape), full(sine.shape)]
+                 + [full((page_len, page_width)) for _ in blocks],
+        out_specs=pl.BlockSpec((1, slots, per_group * HD), lambda r, *_: (r, 0, 0)),
+    )
+    return pl.pallas_call(
+        attention_kernel,
+        grid_spec=grid_spec,
+        out_shape=jax.ShapeDtypeStruct((requests, slots, per_group * HD), jnp.bfloat16),
+    )(lengths, valid, qkv, cosine, sine, *blocks)
+
+
 def on_device(
     hidden, qkv, page_store, page_owner, page_slot, lengths, request_perm, w_out, post_gain,
     *, n_req, n_tp
@@ -77,40 +141,11 @@
     position = jnp.arange(slots, dtype=jnp.int32)
     live_mask = (position[None, :] < my_lengths[:, None]).astype(jnp.float32)
 
-    projections = qkv[:, :, 0].astype(jnp.float32).reshape(requests, slots, per_group + 2, HD)
     prefix_len = page_store.shape[1] * page_owner.shape[0]
-    cosine, sine = tables(prefix_len + position, HD)
-    queries = (
-        rotate(projections[:, :, :per_group], cosine[None, :, None, :], sine[None, :, None, :])
-        * HD ** (-0.5)
-    ).astype(jnp.bfloat16)
-    fresh_keys = rotate(projections[:, :, per_group], cosine[None], sine[None]).astype(jnp.bfloat16)
-    fresh_values = projections[:, :, per_group + 1].astype(jnp.bfloat16)
-
-    allowed = (position[None, None, :] <= position[None, :, None]) & (
-        position[None, None, :] < my_lengths[:, None, None]
-    )
-    suffix_raw = capped_exp(
-        jnp.einsum("rsqh,rth->rsqt", queries, fresh_keys, preferred_element_type=jnp.float32)
-    )
-    suffix_weights = jnp.where(allowed[:, :, None, :], suffix_raw, 0.0)
-    totals = jnp.sum(suffix_weights, -1)
-    attended = jnp.einsum(
-        "rsqt,rth->rsqh", suffix_weights.astype(jnp.bfloat16), fresh_values,
-        preferred_element_type=jnp.float32,
-    )
-    for index, block in enumerate(blocks):
-        raw = capped_exp(
-            jnp.einsum("rsqh,th->rsqt", queries, block[:, :HD], preferred_element_type=jnp.float32)
-        )
-        weights = jnp.where(valid[index], raw, 0.0)
-        totals = totals + jnp.sum(weights, -1)
-        attended = attended + jnp.einsum(
-            "rsqt,th->rsqh", weights.astype(jnp.bfloat16), block[:, HD:],
-            preferred_element_type=jnp.float32,
-        )
-    attended = attended / totals[..., None]
-    own = attended.astype(jnp.bfloat16).reshape(token_rows, per_group * HD)
+    cosine, sine = static_tables(prefix_len + np.arange(slots), HD)
+    attended = attend(qkv[:, :, 0], jnp.asarray(cosine), jnp.asarray(sine), blocks,
+                      my_lengths, valid.astype(jnp.int32))
+    own = attended.reshape(token_rows, per_group * HD)
 
     group_width = per_group * HD
     if n_tp == 4:

time: 75.1 us -> 62.1 us (0.83)
  the two profiles are of different devices: /device:TPU:0 before, /device:TPU:13 now
where the time goes in v3:
time: 62.1 us; the launch traced here: 61.8 us
  waiting for transfers between devices  28.5 us (46%)
  starting transfers between devices  14 us (23%)
  Pallas kernels  6.88 us (11%)
  other arithmetic  5.45 us (9%)
  local copies, waits for them, and re-layouts  2.9 us (5%)
  matrix products  2.03 us (3%)
  between operations  2.02 us (3%)
    ppermute x10, waiting for transfers between devices, shifted(): lax.ppermute(value, axis, [(i, (i + shift) % size) for i in range(size)])  17.3 us
    ppermute x3, waiting for transfers between devices, swapped(): return lax.ppermute(value, axis, [(i, i ^ mask) for i in range(size)])  11.2 us
    ppermute x10, starting transfers between devices, shifted(): lax.ppermute(value, axis, [(i, (i + shift) % size) for i in range(size)])  10.7 us
    pallas_call x1, Pallas kernels, attend(): pl.pallas_call(attention_kernel, grid_spec=grid_spec, out_shape=jax.Shape...  6.88 us
    ppermute x3, starting transfers between devices, swapped(): return lax.ppermute(value, axis, [(i, i ^ mask) for i in range(size)])  3.33 us
    dot_general x4, matrix products, on_device(): term = jnp.dot(block, rows, preferred_element_type=jnp.float32)  2.03 us
    reduce_sum x1, other arithmetic, gather_prefix(): slot = jnp.sum(jnp.where(mine, page_slot, 0))  1.52 us
    reduce_sum x1, other arithmetic, on_device(): my_lengths = jnp.sum(jnp.where(matches, lengths[None, :], 0), 1)  1.38 us
  transfers between devices with their start and end apart: 13, of which 7 were waited for; matrix products, arithmetic and copies ran while one was open for 8% of the time, Pallas kernels for 0%

profile of v3, /device:TPU:13, one launch (start us, length us, event | category | flops | bytes accessed | tf_op | source)
XLA Modules:
  0.0 61.8 jit_solution(15384029575484073779)
XLA Ops:
  0.0 1.5 %fusion.16 = s32[]{:T(128)} fusion(s32[8]{0:T(128)} %param.15, s32[8]{0:T(128)} %param.14, s32[]{:T(128)} %axis_index.27), kind=kLoop, calls=%fused_computation.27 | loop fusion | flops 23 | bytes 72 | tf_op jit(solution)/shard_map/reduce_sum | solution.py:34
  3.4 0.9 %dynamic-slice_bitcast_fusion.rest_0_ = bf16[128,512]{1,0:T(8,128)(2,1)S(1)} fusion(bf16[2,128,1,512]{3,1,2,0:T(8,128)(2,1)} %param.13, s32[]{:T(128)S(6)} %select_n.68), kind=kLoop, calls=%fused_computation.15 | loop fusion | bytes 262148 | tf_op jit(solution)/shard_map/squeeze | solution.py:35
  4.3 1.3 %collective-permute-start = (bf16[128,512]{1,0:T(8,128)(2,1)S(1)}, bf16[128,512]{1,0:T(8,128)(2,1)S(1)}, u32[]{:S(2)}, u32[]{:S(2)}) collective-permute-start(bf16[128,512]{1,0:T(8,128)(2,1)S(1)} %dynamic-slice_bitcast_fusion.rest_0_), channel_id=1, source_target_pairs={{0,4},{4,8},{8,12},{12,16},{16,20},{20,24},{24,28},{28,0},{1,5},{5... | collective-permute-start | bytes 393224 | tf_op jit(solution)/shard_map/ppermute | solution.py:22
  5.6 1.3 %collective-permute-start.1 = (bf16[128,512]{1,0:T(8,128)(2,1)S(1)}, bf16[128,512]{1,0:T(8,128)(2,1)S(1)}, u32[]{:S(2)}, u32[]{:S(2)}) collective-permute-start(bf16[128,512]{1,0:T(8,128)(2,1)S(1)} %dynamic-slice_bitcast_fusion.rest_0_), channel_id=1, source_target_pairs={{0,8},{4,12},{8,16},{12,20},{16,24},{20,28},{24,0},{28,4},{1,9},{5... | collective-permute-start | bytes 393224 | tf_op jit(solution)/shard_map/ppermute | solution.py:22
  6.9 1.0 %collective-permute-start.2 = (bf16[128,512]{1,0:T(8,128)(2,1)S(1)}, bf16[128,512]{1,0:T(8,128)(2,1)S(1)}, u32[]{:S(2)}, u32[]{:S(2)}) collective-permute-start(bf16[128,512]{1,0:T(8,128)(2,1)S(1)} %dynamic-slice_bitcast_fusion.rest_0_), channel_id=1, source_target_pairs={{0,12},{4,16},{8,20},{12,24},{16,28},{20,0},{24,4},{28,8},{1,13},{... | collective-permute-start | bytes 393224 | tf_op jit(solution)/shard_map/ppermute | solution.py:22
  7.9 1.3 %collective-permute-start.3 = (bf16[128,512]{1,0:T(8,128)(2,1)S(1)}, bf16[128,512]{1,0:T(8,128)(2,1)S(1)}, u32[]{:S(2)}, u32[]{:S(2)}) collective-permute-start(bf16[128,512]{1,0:T(8,128)(2,1)S(1)} %dynamic-slice_bitcast_fusion.rest_0_), channel_id=1, source_target_pairs={{0,16},{4,20},{8,24},{12,28},{16,0},{20,4},{24,8},{28,12},{1,17},{... | collective-permute-start | bytes 393224 | tf_op jit(solution)/shard_map/ppermute | solution.py:22
  9.2 1.0 %collective-permute-start.4 = (bf16[128,512]{1,0:T(8,128)(2,1)S(1)}, bf16[128,512]{1,0:T(8,128)(2,1)S(1)}, u32[]{:S(2)}, u32[]{:S(2)}) collective-permute-start(bf16[128,512]{1,0:T(8,128)(2,1)S(1)} %dynamic-slice_bitcast_fusion.rest_0_), channel_id=1, source_target_pairs={{0,20},{4,24},{8,28},{12,0},{16,4},{20,8},{24,12},{28,16},{1,21},{... | collective-permute-start | bytes 393224 | tf_op jit(solution)/shard_map/ppermute | solution.py:22
  10.3 1.3 %collective-permute-start.5 = (bf16[128,512]{1,0:T(8,128)(2,1)S(1)}, bf16[128,512]{1,0:T(8,128)(2,1)S(1)}, u32[]{:S(2)}, u32[]{:S(2)}) collective-permute-start(bf16[128,512]{1,0:T(8,128)(2,1)S(1)} %dynamic-slice_bitcast_fusion.rest_0_), channel_id=1, source_target_pairs={{0,24},{4,28},{8,0},{12,4},{16,8},{20,12},{24,16},{28,20},{1,25},{... | collective-permute-start | bytes 393224 | tf_op jit(solution)/shard_map/ppermute | solution.py:22
  11.6 1.4 %collective-permute-start.6 = (bf16[128,512]{1,0:T(8,128)(2,1)S(1)}, bf16[128,512]{1,0:T(8,128)(2,1)S(1)}, u32[]{:S(2)}, u32[]{:S(2)}) collective-permute-start(bf16[128,512]{1,0:T(8,128)(2,1)S(1)} %dynamic-slice_bitcast_fusion.rest_0_), channel_id=1, source_target_pairs={{0,28},{4,0},{8,4},{12,8},{16,12},{20,16},{24,20},{28,24},{1,29},{... | collective-permute-start | bytes 393224 | tf_op jit(solution)/shard_map/ppermute | solution.py:22
  13.0 0.8 %compare_reduce_fusion = pred[8]{0:T(512)(128)(4,1)S(1)} fusion(s32[8]{0:T(128)} %param.14, s32[8]{0:T(128)S(1)} %stack.35), kind=kLoop, calls=%fused_computation.16 | loop fusion | flops 120 | bytes 72 | tf_op jit(solution)/shard_map/reduce_or | solution.py:42
  14.4 0.7 %dynamic_slice.19 = s32[4]{0:T(128)S(1)} dynamic-slice(s32[32]{0:T(128)} %param.17, s32[]{:T(128)S(6)} %select_n.58), dynamic_slice_sizes={4} | dynamic-slice | bytes 36 | tf_op jit(solution)/shard_map/dynamic_slice | solution.py:138
  15.1 1.4 %select_reduce_fusion.length_ref = s32[4]{0:T(128)} fusion(s32[32]{0:T(128)} %param.16, s32[4]{0:T(128)S(1)} %dynamic_slice.19), kind=kLoop, calls=%fused_computation.19 | loop fusion | flops 380 | bytes 160 | tf_op jit(solution)/shard_map/reduce_sum | solution.py:140
  16.5 8.1 %collective-permute-done.2.rest_3_ = bf16[128,512]{1,0:T(8,128)(2,1)S(1)} collective-permute-done((bf16[128,512]{1,0:T(8,128)(2,1)S(1)}, bf16[128,512]{1,0:T(8,128)(2,1)S(1)}, u32[]{:S(2)}, u32[]{:S(2)}) %collective-permute-start.2) | collective-permute-done | bytes 131104 | tf_op jit(solution)/shard_map/ppermute | solution.py:22
  24.6 2.8 %collective-permute-done.3.rest_4_ = bf16[128,512]{1,0:T(8,128)(2,1)S(1)} collective-permute-done((bf16[128,512]{1,0:T(8,128)(2,1)S(1)}, bf16[128,512]{1,0:T(8,128)(2,1)S(1)}, u32[]{:S(2)}, u32[]{:S(2)}) %collective-permute-start.3) | collective-permute-done | bytes 131104 | tf_op jit(solution)/shard_map/ppermute | solution.py:22
  27.5 2.8 %collective-permute-done.5.rest_6_ = bf16[128,512]{1,0:T(8,128)(2,1)S(1)} collective-permute-done((bf16[128,512]{1,0:T(8,128)(2,1)S(1)}, bf16[128,512]{1,0:T(8,128)(2,1)S(1)}, u32[]{:S(2)}, u32[]{:S(2)}) %collective-permute-start.5) | collective-permute-done | bytes 131104 | tf_op jit(solution)/shard_map/ppermute | solution.py:22
  30.3 1.2 %collective-permute-done.6.rest_7_ = bf16[128,512]{1,0:T(8,128)(2,1)S(1)} collective-permute-done((bf16[128,512]{1,0:T(8,128)(2,1)S(1)}, bf16[128,512]{1,0:T(8,128)(2,1)S(1)}, u32[]{:S(2)}, u32[]{:S(2)}) %collective-permute-start.6) | collective-permute-done | bytes 131104 | tf_op jit(solution)/shard_map/ppermute | solution.py:22
  32.2 6.9 %shard_map.109 = bf16[4,128,512]{2,1,0:T(8,128)(2,1)} custom-call(s32[4]{0:T(128)} %select_reduce_fusion.length_ref, s32[8]{0:T(128)} %convert_element_type.17.valid_ref, bf16[4,128,1024]{2,1,0:T(8,128)(2,1)} %bitcast.34, f32[128,128]{1,0:T(8,128)} %constant.95.clone.cos_ref, f32[128,128]{1,0:T(8,128)} %constant.96.clone.sin_ref, ...), custom_call_target="tpu_custom_call" | custom-call | tf_op jit(solution)/shard_map/pallas_call | solution.py:119
  39.1 1.2 %collective-permute-start.8 = (bf16[512,512]{1,0:T(8,128)(2,1)}, bf16[512,512]{1,0:T(8,128)(2,1)S(1)}, u32[]{:S(2)}, u32[]{:S(2)}) collective-permute-start(bf16[512,512]{1,0:T(8,128)(2,1)} %bitcast.31), channel_id=1, source_target_pairs={{0,2},{1,3},{2,0},{3,1},{4,6},{5,7},{6,4},{7,5},{8,10},{9,11},{10,... | collective-permute-start | bytes 1572872 | tf_op jit(solution)/shard_map/ppermute | solution.py:26
  40.3 0.8 %collective-permute-start.7 = (bf16[512,512]{1,0:T(8,128)(2,1)}, bf16[512,512]{1,0:T(8,128)(2,1)S(1)}, u32[]{:S(2)}, u32[]{:S(2)}) collective-permute-start(bf16[512,512]{1,0:T(8,128)(2,1)} %bitcast.32), channel_id=1, source_target_pairs={{0,1},{1,0},{2,3},{3,2},{4,5},{5,4},{6,7},{7,6},{8,9},{9,8},{10,11... | collective-permute-start | bytes 1572872 | tf_op jit(solution)/shard_map/ppermute | solution.py:26
  41.0 11.2 %collective-permute-done.8 = bf16[512,512]{1,0:T(8,128)(2,1)S(1)} collective-permute-done((bf16[512,512]{1,0:T(8,128)(2,1)}, bf16[512,512]{1,0:T(8,128)(2,1)S(1)}, u32[]{:S(2)}, u32[]{:S(2)}) %collective-permute-start.8) | collective-permute-done | bytes 524320 | tf_op jit(solution)/shard_map/ppermute | solution.py:26
  52.3 1.3 %collective-permute-start.9 = (bf16[512,512]{1,0:T(8,128)(2,1)S(1)}, bf16[512,512]{1,0:T(8,128)(2,1)S(1)}, u32[]{:S(2)}, u32[]{:S(2)}) collective-permute-start(bf16[512,512]{1,0:T(8,128)(2,1)S(1)} %collective-permute-done.8), channel_id=1, source_target_pairs={{0,1},{1,0},{2,3},{3,2},{4,5},{5,4},{6,7},{7,6},{8,9},{9,8},{10,11... | collective-permute-start | bytes 1572872 | tf_op jit(solution)/shard_map/ppermute | solution.py:26
  56.2 1.1 %collective-permute-start.10 = (f32[4,128]{1,0:T(4,128)S(1)}, f32[4,128]{1,0:T(4,128)S(1)}, u32[]{:S(2)}, u32[]{:S(2)}) collective-permute-start(f32[4,128]{1,0:T(4,128)S(1)} %bitcast.35), channel_id=1, source_target_pairs={{0,1},{1,2},{2,3},{3,0},{4,5},{5,6},{6,7},{7,4},{8,9},{9,10},{10,1... | collective-permute-start | bytes 6152 | tf_op jit(solution)/shard_map/ppermute | solution.py:22
  58.4 1.6 %collective-permute-done.11 = f32[4,128]{1,0:T(4,128)S(1)} collective-permute-done((f32[4,128]{1,0:T(4,128)S(1)}, f32[4,128]{1,0:T(4,128)S(1)}, u32[]{:S(2)}, u32[]{:S(2)}) %collective-permute-start.11) | collective-permute-done | bytes 2080 | tf_op jit(solution)/shard_map/ppermute | solution.py:22
  60.7 1.1 %fusion.4 = bf16[4,128,576]{1,2,0:T(8,128)(2,1)} fusion(bf16[4,128,576]{1,2,0:T(8,128)(2,1)S(1)} %copy-done.2, f32[4,128]{1,0:T(4,128)S(1)} %fusion.11, f32[576]{0:T(1024)S(1)} %copy-done.11, f32[4,128]{1,0:T(4,128)S(1)} %add_rsqrt_fusion, f32[512,576]{0,1:T(8,128)S(1)} %get-tuple-element.6), kind=kLoop, calls=%fused_computation.7 | loop fusion | flops 1769472 | bytes 2365696 | tf_op jit(solution)/shard_map/convert_element_type | solution.py:173
  (43 shorter events, 5.5 us)
Async XLA Ops:
  0.0 53.6 %copy-start = (bf16[2048,576]{0,1:T(8,128)(2,1)S(1)}, bf16[2048,576]{0,1:T(8,128)(2,1)}, u32[]{:S(2)}) copy-start(bf16[2048,576]{0,1:T(8,128)(2,1)} %param.18) | copy-start | bytes 7077892
  4.3 27.2 %copy-start.3 = (bf16[128,512]{1,0:T(8,128)(2,1)}, bf16[128,512]{1,0:T(8,128)(2,1)S(1)}, u32[]{:S(2)}) copy-start(bf16[128,512]{1,0:T(8,128)(2,1)S(1)} %dynamic-slice_bitcast_fusion.rest_0_) | copy-start | bytes 393220
  4.3 6.0 %collective-permute-start = (bf16[128,512]{1,0:T(8,128)(2,1)S(1)}, bf16[128,512]{1,0:T(8,128)(2,1)S(1)}, u32[]{:S(2)}, u32[]{:S(2)}) collective-permute-start(bf16[128,512]{1,0:T(8,128)(2,1)S(1)} %dynamic-slice_bitcast_fusion.rest_0_), channel_id=1, source_target_pairs={{0,4},{4,8},{8,12},{12,16},{16,20},{20,24},{24,28},{28,0},{1,5},{5... | collective-permute-start | bytes 393224 | tf_op jit(solution)/shard_map/ppermute | solution.py:22
  5.6 6.0 %collective-permute-start.1 = (bf16[128,512]{1,0:T(8,128)(2,1)S(1)}, bf16[128,512]{1,0:T(8,128)(2,1)S(1)}, u32[]{:S(2)}, u32[]{:S(2)}) collective-permute-start(bf16[128,512]{1,0:T(8,128)(2,1)S(1)} %dynamic-slice_bitcast_fusion.rest_0_), channel_id=1, source_target_pairs={{0,8},{4,12},{8,16},{12,20},{16,24},{20,28},{24,0},{28,4},{1,9},{5... | collective-permute-start | bytes 393224 | tf_op jit(solution)/shard_map/ppermute | solution.py:22
  6.9 17.7 %collective-permute-start.2 = (bf16[128,512]{1,0:T(8,128)(2,1)S(1)}, bf16[128,512]{1,0:T(8,128)(2,1)S(1)}, u32[]{:S(2)}, u32[]{:S(2)}) collective-permute-start(bf16[128,512]{1,0:T(8,128)(2,1)S(1)} %dynamic-slice_bitcast_fusion.rest_0_), channel_id=1, source_target_pairs={{0,12},{4,16},{8,20},{12,24},{16,28},{20,0},{24,4},{28,8},{1,13},{... | collective-permute-start | bytes 393224 | tf_op jit(solution)/shard_map/ppermute | solution.py:22
  7.9 19.6 %collective-permute-start.3 = (bf16[128,512]{1,0:T(8,128)(2,1)S(1)}, bf16[128,512]{1,0:T(8,128)(2,1)S(1)}, u32[]{:S(2)}, u32[]{:S(2)}) collective-permute-start(bf16[128,512]{1,0:T(8,128)(2,1)S(1)} %dynamic-slice_bitcast_fusion.rest_0_), channel_id=1, source_target_pairs={{0,16},{4,20},{8,24},{12,28},{16,0},{20,4},{24,8},{28,12},{1,17},{... | collective-permute-start | bytes 393224 | tf_op jit(solution)/shard_map/ppermute | solution.py:22
  9.2 18.2 %collective-permute-start.4 = (bf16[128,512]{1,0:T(8,128)(2,1)S(1)}, bf16[128,512]{1,0:T(8,128)(2,1)S(1)}, u32[]{:S(2)}, u32[]{:S(2)}) collective-permute-start(bf16[128,512]{1,0:T(8,128)(2,1)S(1)} %dynamic-slice_bitcast_fusion.rest_0_), channel_id=1, source_target_pairs={{0,20},{4,24},{8,28},{12,0},{16,4},{20,8},{24,12},{28,16},{1,21},{... | collective-permute-start | bytes 393224 | tf_op jit(solution)/shard_map/ppermute | solution.py:22
  10.3 21.2 %copy-start.4 = (bf16[128,512]{1,0:T(8,128)(2,1)}, bf16[128,512]{1,0:T(8,128)(2,1)S(1)}, u32[]{:S(2)}) copy-start(bf16[128,512]{1,0:T(8,128)(2,1)S(1)} %collective-permute-done.rest_1_) | copy-start | bytes 393220
  10.3 20.0 %collective-permute-start.5 = (bf16[128,512]{1,0:T(8,128)(2,1)S(1)}, bf16[128,512]{1,0:T(8,128)(2,1)S(1)}, u32[]{:S(2)}, u32[]{:S(2)}) collective-permute-start(bf16[128,512]{1,0:T(8,128)(2,1)S(1)} %dynamic-slice_bitcast_fusion.rest_0_), channel_id=1, source_target_pairs={{0,24},{4,28},{8,0},{12,4},{16,8},{20,12},{24,16},{28,20},{1,25},{... | collective-permute-start | bytes 393224 | tf_op jit(solution)/shard_map/ppermute | solution.py:22
  11.6 19.9 %copy-start.5 = (bf16[128,512]{1,0:T(8,128)(2,1)}, bf16[128,512]{1,0:T(8,128)(2,1)S(1)}, u32[]{:S(2)}) copy-start(bf16[128,512]{1,0:T(8,128)(2,1)S(1)} %collective-permute-done.1.rest_2_) | copy-start | bytes 393220
  11.6 19.9 %collective-permute-start.6 = (bf16[128,512]{1,0:T(8,128)(2,1)S(1)}, bf16[128,512]{1,0:T(8,128)(2,1)S(1)}, u32[]{:S(2)}, u32[]{:S(2)}) collective-permute-start(bf16[128,512]{1,0:T(8,128)(2,1)S(1)} %dynamic-slice_bitcast_fusion.rest_0_), channel_id=1, source_target_pairs={{0,28},{4,0},{8,4},{12,8},{16,12},{20,16},{24,20},{28,24},{1,29},{... | collective-permute-start | bytes 393224 | tf_op jit(solution)/shard_map/ppermute | solution.py:22
  24.6 6.9 %copy-start.6 = (bf16[128,512]{1,0:T(8,128)(2,1)}, bf16[128,512]{1,0:T(8,128)(2,1)S(1)}, u32[]{:S(2)}) copy-start(bf16[128,512]{1,0:T(8,128)(2,1)S(1)} %collective-permute-done.2.rest_3_) | copy-start | bytes 393220
  27.5 4.1 %copy-start.7 = (bf16[128,512]{1,0:T(8,128)(2,1)}, bf16[128,512]{1,0:T(8,128)(2,1)S(1)}, u32[]{:S(2)}) copy-start(bf16[128,512]{1,0:T(8,128)(2,1)S(1)} %collective-permute-done.3.rest_4_) | copy-start | bytes 393220
  27.5 4.1 %copy-start.8 = (bf16[128,512]{1,0:T(8,128)(2,1)}, bf16[128,512]{1,0:T(8,128)(2,1)S(1)}, u32[]{:S(2)}) copy-start(bf16[128,512]{1,0:T(8,128)(2,1)S(1)} %collective-permute-done.4.rest_5_) | copy-start | bytes 393220
  30.3 1.3 %copy-start.9 = (bf16[128,512]{1,0:T(8,128)(2,1)}, bf16[128,512]{1,0:T(8,128)(2,1)S(1)}, u32[]{:S(2)}) copy-start(bf16[128,512]{1,0:T(8,128)(2,1)S(1)} %collective-permute-done.5.rest_6_) | copy-start | bytes 393220
  39.1 13.2 %collective-permute-start.8 = (bf16[512,512]{1,0:T(8,128)(2,1)}, bf16[512,512]{1,0:T(8,128)(2,1)S(1)}, u32[]{:S(2)}, u32[]{:S(2)}) collective-permute-start(bf16[512,512]{1,0:T(8,128)(2,1)} %bitcast.31), channel_id=1, source_target_pairs={{0,2},{1,3},{2,0},{3,1},{4,6},{5,7},{6,4},{7,5},{8,10},{9,11},{10,... | collective-permute-start | bytes 1572872 | tf_op jit(solution)/shard_map/ppermute | solution.py:26
  40.3 13.9 %collective-permute-start.7 = (bf16[512,512]{1,0:T(8,128)(2,1)}, bf16[512,512]{1,0:T(8,128)(2,1)S(1)}, u32[]{:S(2)}, u32[]{:S(2)}) collective-permute-start(bf16[512,512]{1,0:T(8,128)(2,1)} %bitcast.32), channel_id=1, source_target_pairs={{0,1},{1,0},{2,3},{3,2},{4,5},{5,4},{6,7},{7,6},{8,9},{9,8},{10,11... | collective-permute-start | bytes 1572872 | tf_op jit(solution)/shard_map/ppermute | solution.py:26
  52.3 3.4 %collective-permute-start.9 = (bf16[512,512]{1,0:T(8,128)(2,1)S(1)}, bf16[512,512]{1,0:T(8,128)(2,1)S(1)}, u32[]{:S(2)}, u32[]{:S(2)}) collective-permute-start(bf16[512,512]{1,0:T(8,128)(2,1)S(1)} %collective-permute-done.8), channel_id=1, source_target_pairs={{0,1},{1,0},{2,3},{3,2},{4,5},{5,4},{6,7},{7,6},{8,9},{9,8},{10,11... | collective-permute-start | bytes 1572872 | tf_op jit(solution)/shard_map/ppermute | solution.py:26
  55.7 2.6 %copy-start.12 = (s32[4]{0:T(128)S(1)}, s32[4]{0:T(128)}, u32[]{:S(2)}) copy-start(s32[4]{0:T(128)} %select_reduce_fusion.length_ref) | copy-start | bytes 52
  55.7 5.0 %copy-start.2 = (bf16[4,128,576]{1,2,0:T(8,128)(2,1)S(1)}, bf16[4,128,576]{1,2,0:T(8,128)(2,1)}, u32[]{:S(2)}) copy-start(bf16[4,128,576]{1,2,0:T(8,128)(2,1)} %param.11) | copy-start | bytes 1769476
  55.7 5.0 %copy-start.11 = (f32[576]{0:T(1024)S(1)}, f32[576]{0:T(1024)}, u32[]{:S(2)}) copy-start(f32[576]{0:T(1024)} %param.19) | copy-start | bytes 6916
  56.2 2.1 %collective-permute-start.10 = (f32[4,128]{1,0:T(4,128)S(1)}, f32[4,128]{1,0:T(4,128)S(1)}, u32[]{:S(2)}, u32[]{:S(2)}) collective-permute-start(f32[4,128]{1,0:T(4,128)S(1)} %bitcast.35), channel_id=1, source_target_pairs={{0,1},{1,2},{2,3},{3,0},{4,5},{5,6},{6,7},{7,4},{8,9},{9,10},{10,1... | collective-permute-start | bytes 6152 | tf_op jit(solution)/shard_map/ppermute | solution.py:22
  57.4 2.6 %collective-permute-start.11 = (f32[4,128]{1,0:T(4,128)S(1)}, f32[4,128]{1,0:T(4,128)S(1)}, u32[]{:S(2)}, u32[]{:S(2)}) collective-permute-start(f32[4,128]{1,0:T(4,128)S(1)} %bitcast.36), channel_id=1, source_target_pairs={{0,2},{1,3},{2,0},{3,1},{4,6},{5,7},{6,4},{7,5},{8,10},{9,11},{10,... | collective-permute-start | bytes 6152 | tf_op jit(solution)/shard_map/ppermute | solution.py:22
  57.6 3.0 %collective-permute-start.12 = (f32[4,128]{1,0:T(4,128)S(1)}, f32[4,128]{1,0:T(4,128)S(1)}, u32[]{:S(2)}, u32[]{:S(2)}) collective-permute-start(f32[4,128]{1,0:T(4,128)S(1)} %bitcast.37), channel_id=1, source_target_pairs={{0,3},{1,0},{2,1},{3,2},{4,7},{5,4},{6,5},{7,6},{8,11},{9,8},{10,9... | collective-permute-start | bytes 6152 | tf_op jit(solution)/shard_map/ppermute | solution.py:22
  (2 other events, 1.7 us)

commit v4 on v3

--- a/solution.py
+++ b/solution.py
@@ -123,6 +123,24 @@
     )(lengths, valid, qkv, cosine, sine, *blocks)
 
 
+def project(own, w_out, tp_index, n_tp, group_width):
+    if n_tp == 4:
+        near = swapped(own, "tp", n_tp, 1)
+        far = swapped(own, "tp", n_tp, 2)
+        farther = swapped(far, "tp", n_tp, 1)
+        parts = [(own, tp_index), (near, tp_index ^ 1), (far, tp_index ^ 2), (farther, tp_index ^ 3)]
+    else:
+        parts = [(own, tp_index)]
+        for shift in range(1, n_tp):
+            parts.append((shifted(own, "tp", n_tp, shift), (tp_index - shift) % n_tp))
+    projected = None
+    for block, group in parts:
+        rows = lax.dynamic_slice_in_dim(w_out, group * group_width, group_width, 0)
+        term = jnp.dot(block, rows, preferred_element_type=jnp.float32)
+        projected = term if projected is None else projected + term
+    return projected
+
+
 def on_device(
     hidden, qkv, page_store, page_owner, page_slot, lengths, request_perm, w_out, post_gain,
     *, n_req, n_tp
@@ -143,26 +161,15 @@
 
     prefix_len = page_store.shape[1] * page_owner.shape[0]
     cosine, sine = static_tables(prefix_len + np.arange(slots), HD)
-    attended = attend(qkv[:, :, 0], jnp.asarray(cosine), jnp.asarray(sine), blocks,
-                      my_lengths, valid.astype(jnp.int32))
-    own = attended.reshape(token_rows, per_group * HD)
-
     group_width = per_group * HD
-    if n_tp == 4:
-        near = swapped(own, "tp", n_tp, 1)
-        far = swapped(own, "tp", n_tp, 2)
-        farther = swapped(far, "tp", n_tp, 1)
-        parts = [(own, tp_index), (near, tp_index ^ 1), (far, tp_index ^ 2), (farther, tp_index ^ 3)]
-    else:
-        parts = [(own, tp_index)]
-        for shift in range(1, n_tp):
-            parts.append((shifted(own, "tp", n_tp, shift), (tp_index - shift) % n_tp))
-    projected = None
-    for block, group in parts:
-        rows = lax.dynamic_slice_in_dim(w_out, group * group_width, group_width, 0)
-        term = jnp.dot(block, rows, preferred_element_type=jnp.float32)
-        projected = term if projected is None else projected + term
-    projected = projected.reshape(requests, slots, local_width)
+    chunk = max(1, requests // 2)
+    projected_parts = []
+    for start in range(0, requests, chunk):
+        attended = attend(qkv[start:start + chunk, :, 0], jnp.asarray(cosine), jnp.asarray(sine),
+                          blocks, my_lengths[start:start + chunk], valid.astype(jnp.int32))
+        own = attended.reshape(chunk * slots, per_group * HD)
+        projected_parts.append(project(own, w_out, tp_index, n_tp, group_width))
+    projected = jnp.concatenate(projected_parts, 0).reshape(requests, slots, local_width)
 
     squares = jnp.sum(projected * projected, -1)
     branch_total = squares

time: 62.1 us -> 62.8 us (1.011)
  the two profiles are of different devices: /device:TPU:13 before, /device:TPU:0 now
where the time goes in v4:
time: 62.8 us; the launch traced here: 62.5 us
  waiting for transfers between devices  22.2 us (35%)
  starting transfers between devices  17 us (27%)
  Pallas kernels  9.55 us (15%)
  local copies, waits for them, and re-layouts  4.93 us (8%)
  other arithmetic  3.85 us (6%)
  matrix products  2.77 us (4%)
  between operations  2.19 us (3%)
    ppermute x10, waiting for transfers between devices, shifted(): lax.ppermute(value, axis, [(i, (i + shift) % size) for i in range(size)])  16.3 us
    ppermute x10, starting transfers between devices, shifted(): lax.ppermute(value, axis, [(i, (i + shift) % size) for i in range(size)])  14.5 us
    pallas_call x2, Pallas kernels, attend(): pl.pallas_call(attention_kernel, grid_spec=grid_spec, out_shape=jax.Shape...  9.55 us
    ppermute x6, waiting for transfers between devices, swapped(): return lax.ppermute(value, axis, [(i, i ^ mask) for i in range(size)])  5.83 us
    dot_general x8, matrix products, project(): term = jnp.dot(block, rows, preferred_element_type=jnp.float32)  2.77 us
    ppermute x6, starting transfers between devices, swapped(): return lax.ppermute(value, axis, [(i, i ^ mask) for i in range(size)])  2.54 us
    squeeze x1, local copies, waits for them, and re-layouts, on_device(): qkv[start:start + chunk, :, 0]  2.24 us
    reduce_sum x1, other arithmetic, gather_prefix(): slot = jnp.sum(jnp.where(mine, page_slot, 0))  1.46 us
  transfers between devices with their start and end apart: 16, of which 5 were waited for; matrix products, arithmetic and copies ran while one was open for 10% of the time, Pallas kernels for 8%

profile of v4, /device:TPU:0, one launch (start us, length us, event | category | flops | bytes accessed | tf_op | source)
XLA Modules:
  0.0 62.5 jit_solution(5453597282651574239)
XLA Ops:
  0.0 1.5 %fusion.28 = s32[]{:T(128)} fusion(s32[8]{0:T(128)} %param.15, s32[8]{0:T(128)} %param.14, s32[]{:T(128)} %axis_index.27), kind=kLoop, calls=%fused_computation.44 | loop fusion | flops 23 | bytes 72 | tf_op jit(solution)/shard_map/reduce_sum | solution.py:34
  3.4 0.9 %dynamic-slice_bitcast_fusion.rest_0_ = bf16[128,512]{1,0:T(8,128)(2,1)S(1)} fusion(bf16[2,128,1,512]{3,1,2,0:T(8,128)(2,1)} %param.13, s32[]{:T(128)S(6)} %select_n.72), kind=kLoop, calls=%fused_computation.28 | loop fusion | bytes 262148 | tf_op jit(solution)/shard_map/squeeze | solution.py:35
  4.4 6.1 %collective-permute-start.6 = (bf16[128,512]{1,0:T(8,128)(2,1)S(1)}, bf16[128,512]{1,0:T(8,128)(2,1)S(1)}, u32[]{:S(2)}, u32[]{:S(2)}) collective-permute-start(bf16[128,512]{1,0:T(8,128)(2,1)S(1)} %dynamic-slice_bitcast_fusion.rest_0_), channel_id=1, source_target_pairs={{0,28},{4,0},{8,4},{12,8},{16,12},{20,16},{24,20},{28,24},{1,29},{... | collective-permute-start | bytes 393224 | tf_op jit(solution)/shard_map/ppermute | solution.py:22
  10.4 0.4 collective-permute-start.5
  10.9 3.0 %collective-permute-start.3 = (bf16[128,512]{1,0:T(8,128)(2,1)S(1)}, bf16[128,512]{1,0:T(8,128)(2,1)S(1)}, u32[]{:S(2)}, u32[]{:S(2)}) collective-permute-start(bf16[128,512]{1,0:T(8,128)(2,1)S(1)} %dynamic-slice_bitcast_fusion.rest_0_), channel_id=1, source_target_pairs={{0,16},{4,20},{8,24},{12,28},{16,0},{20,4},{24,8},{28,12},{1,17},{... | collective-permute-start | bytes 393224 | tf_op jit(solution)/shard_map/ppermute | solution.py:22
  13.9 2.2 %slice_bitcast_fusion.1 = (bf16[2,128,1024]{2,1,0:T(8,128)(2,1)}, bf16[2,128,1024]{2,1,0:T(8,128)(2,1)}) fusion(bf16[4,128,1,1024]{3,1,0,2:T(8,128)(2,1)} %bitcast.40), kind=kLoop, calls=%fused_computation.15 | loop fusion | bytes 2097152 | tf_op jit(solution)/shard_map/squeeze | solution.py:168
  16.4 0.6 convert_element_type.18.valid_ref
  17.3 1.9 %collective-permute-start.1 = (bf16[128,512]{1,0:T(8,128)(2,1)S(1)}, bf16[128,512]{1,0:T(8,128)(2,1)S(1)}, u32[]{:S(2)}, u32[]{:S(2)}) collective-permute-start(bf16[128,512]{1,0:T(8,128)(2,1)S(1)} %dynamic-slice_bitcast_fusion.rest_0_), channel_id=1, source_target_pairs={{0,8},{4,12},{8,16},{12,20},{16,24},{20,28},{24,0},{28,4},{1,9},{5... | collective-permute-start | bytes 393224 | tf_op jit(solution)/shard_map/ppermute | solution.py:22
  19.2 1.1 %collective-permute-start = (bf16[128,512]{1,0:T(8,128)(2,1)S(1)}, bf16[128,512]{1,0:T(8,128)(2,1)S(1)}, u32[]{:S(2)}, u32[]{:S(2)}) collective-permute-start(bf16[128,512]{1,0:T(8,128)(2,1)S(1)} %dynamic-slice_bitcast_fusion.rest_0_), channel_id=1, source_target_pairs={{0,4},{4,8},{8,12},{12,16},{16,20},{20,24},{24,28},{28,0},{1,5},{5... | collective-permute-start | bytes 393224 | tf_op jit(solution)/shard_map/ppermute | solution.py:22
  20.3 0.6 %fusion.29 = (s32[2]{0:T(128)}, s32[2]{0:T(128)}) fusion(s32[4]{0:T(128)S(1)} %select_reduce_fusion), kind=kLoop, calls=%fused_computation.45 | loop fusion | bytes 32 | tf_op jit(solution)/shard_map/slice | solution.py:169
  21.0 11.8 %collective-permute-done.3.rest_4_ = bf16[128,512]{1,0:T(8,128)(2,1)S(1)} collective-permute-done((bf16[128,512]{1,0:T(8,128)(2,1)S(1)}, bf16[128,512]{1,0:T(8,128)(2,1)S(1)}, u32[]{:S(2)}, u32[]{:S(2)}) %collective-permute-start.3) | collective-permute-done | bytes 131104 | tf_op jit(solution)/shard_map/ppermute | solution.py:22
  32.8 1.6 %collective-permute-done.2.rest_3_ = bf16[128,512]{1,0:T(8,128)(2,1)S(1)} collective-permute-done((bf16[128,512]{1,0:T(8,128)(2,1)S(1)}, bf16[128,512]{1,0:T(8,128)(2,1)S(1)}, u32[]{:S(2)}, u32[]{:S(2)}) %collective-permute-start.2) | collective-permute-done | bytes 131104 | tf_op jit(solution)/shard_map/ppermute | solution.py:22
  34.4 0.6 copy-done.9
  35.1 4.8 %shard_map.109 = bf16[2,128,512]{2,1,0:T(8,128)(2,1)} custom-call(s32[2]{0:T(128)} %get-tuple-element.9.length_ref, s32[8]{0:T(128)} %convert_element_type.18.valid_ref, bf16[2,128,1024]{2,1,0:T(8,128)(2,1)} %get-tuple-element.7.qkv_ref, f32[128,128]{1,0:T(8,128)} %constant.95.clone.cos_ref, f32[128,128]{1,0:T(8,128)} %constant.96.clone.sin_ref, ...), custom_call_target="tpu_custom_call" | custom-call | tf_op jit(solution)/shard_map/pallas_call | solution.py:119
  39.9 1.5 %collective-permute-start.8 = (bf16[256,512]{1,0:T(8,128)(2,1)}, bf16[256,512]{1,0:T(8,128)(2,1)S(1)}, u32[]{:S(2)}, u32[]{:S(2)}) collective-permute-start(bf16[256,512]{1,0:T(8,128)(2,1)} %bitcast.41), channel_id=1, source_target_pairs={{0,2},{1,3},{2,0},{3,1},{4,6},{5,7},{6,4},{7,5},{8,10},{9,11},{10,... | collective-permute-start | bytes 786440 | tf_op jit(solution)/shard_map/ppermute | solution.py:26
  41.4 4.8 %shard_map.110 = bf16[2,128,512]{2,1,0:T(8,128)(2,1)} custom-call(s32[2]{0:T(128)} %get-tuple-element.10.length_ref, s32[8]{0:T(128)} %convert_element_type.18.valid_ref, bf16[2,128,1024]{2,1,0:T(8,128)(2,1)} %get-tuple-element.8.qkv_ref, f32[128,128]{1,0:T(8,128)} %constant.95.clone.cos_ref, f32[128,128]{1,0:T(8,128)} %constant.96.clone.sin_ref, ...), custom_call_target="tpu_custom_call" | custom-call | tf_op jit(solution)/shard_map/pallas_call | solution.py:119
  46.1 0.5 collective-permute-start.11
  46.7 0.5 collective-permute-start.10
  47.2 5.8 %collective-permute-done.11 = bf16[256,512]{1,0:T(8,128)(2,1)S(1)} collective-permute-done((bf16[256,512]{1,0:T(8,128)(2,1)}, bf16[256,512]{1,0:T(8,128)(2,1)S(1)}, u32[]{:S(2)}, u32[]{:S(2)}) %collective-permute-start.11) | collective-permute-done | bytes 262176 | tf_op jit(solution)/shard_map/ppermute | solution.py:26
  56.4 1.2 %collective-permute-start.14 = (f32[4,128]{1,0:T(4,128)S(1)}, f32[4,128]{1,0:T(4,128)S(1)}, u32[]{:S(2)}, u32[]{:S(2)}) collective-permute-start(f32[4,128]{1,0:T(4,128)S(1)} %bitcast.47), channel_id=1, source_target_pairs={{0,2},{1,3},{2,0},{3,1},{4,6},{5,7},{6,4},{7,5},{8,10},{9,11},{10,... | collective-permute-start | bytes 6152 | tf_op jit(solution)/shard_map/ppermute | solution.py:22
  57.6 0.7 %collective-permute-start.15 = (f32[4,128]{1,0:T(4,128)S(1)}, f32[4,128]{1,0:T(4,128)S(1)}, u32[]{:S(2)}, u32[]{:S(2)}) collective-permute-start(f32[4,128]{1,0:T(4,128)S(1)} %bitcast.48), channel_id=1, source_target_pairs={{0,3},{1,0},{2,1},{3,2},{4,7},{5,4},{6,5},{7,6},{8,11},{9,8},{10,9... | collective-permute-start | bytes 6152 | tf_op jit(solution)/shard_map/ppermute | solution.py:22
  58.4 1.7 %collective-permute-done.14 = f32[4,128]{1,0:T(4,128)S(1)} collective-permute-done((f32[4,128]{1,0:T(4,128)S(1)}, f32[4,128]{1,0:T(4,128)S(1)}, u32[]{:S(2)}, u32[]{:S(2)}) %collective-permute-start.14) | collective-permute-done | bytes 2080 | tf_op jit(solution)/shard_map/ppermute | solution.py:22
  60.1 1.3 %collective-permute-done.13 = f32[4,128]{1,0:T(4,128)S(1)} collective-permute-done((f32[4,128]{1,0:T(4,128)S(1)}, f32[4,128]{1,0:T(4,128)S(1)}, u32[]{:S(2)}, u32[]{:S(2)}) %collective-permute-start.13) | collective-permute-done | bytes 2080 | tf_op jit(solution)/shard_map/ppermute | solution.py:22
  61.4 1.1 %fusion.5 = bf16[4,128,576]{1,2,0:T(8,128)(2,1)} fusion(f32[72,4,8,128]{3,2,1,0:T(8,128)S(1)} %get-tuple-element.6, bf16[4,128,576]{1,2,0:T(8,128)(2,1)S(1)} %copy-done.4, f32[4,128]{1,0:T(4,128)S(1)} %fusion.19, f32[576]{0:T(1024)S(1)} %copy-done.12, f32[4,128]{1,0:T(4,128)S(1)} %add_rsqrt_fusion), kind=kLoop, calls=%fused_computation.10 | loop fusion | flops 1769472 | bytes 2365696 | tf_op jit(solution)/shard_map/convert_element_type | solution.py:180
  (63 shorter events, 4.1 us)
Async XLA Ops:
  0.0 53.0 %copy-start = (bf16[2048,576]{0,1:T(8,128)(2,1)S(1)}, bf16[2048,576]{0,1:T(8,128)(2,1)}, u32[]{:S(2)}) copy-start(bf16[2048,576]{0,1:T(8,128)(2,1)} %param.18) | copy-start | bytes 7077892
  0.0 16.2 %copy-start.13 = (s32[8]{0:T(128)S(1)}, s32[8]{0:T(128)}, u32[]{:S(2)}) copy-start(s32[8]{0:T(128)} %param.14) | copy-start | bytes 100
  0.0 17.0 %copy-start.14 = (s32[32]{0:T(128)S(1)}, s32[32]{0:T(128)}, u32[]{:S(2)}) copy-start(s32[32]{0:T(128)} %param.17) | copy-start | bytes 388
  0.0 17.1 %copy-start.15 = (s32[32]{0:T(128)S(1)}, s32[32]{0:T(128)}, u32[]{:S(2)}) copy-start(s32[32]{0:T(128)} %param.16) | copy-start | bytes 388
  4.3 30.0 %copy-start.1 = (bf16[128,512]{1,0:T(8,128)(2,1)}, bf16[128,512]{1,0:T(8,128)(2,1)S(1)}, u32[]{:S(2)}) copy-start(bf16[128,512]{1,0:T(8,128)(2,1)S(1)} %dynamic-slice_bitcast_fusion.rest_0_) | copy-start | bytes 393220
  4.4 12.9 %collective-permute-start.6 = (bf16[128,512]{1,0:T(8,128)(2,1)S(1)}, bf16[128,512]{1,0:T(8,128)(2,1)S(1)}, u32[]{:S(2)}, u32[]{:S(2)}) collective-permute-start(bf16[128,512]{1,0:T(8,128)(2,1)S(1)} %dynamic-slice_bitcast_fusion.rest_0_), channel_id=1, source_target_pairs={{0,28},{4,0},{8,4},{12,8},{16,12},{20,16},{24,20},{28,24},{1,29},{... | collective-permute-start | bytes 393224 | tf_op jit(solution)/shard_map/ppermute | solution.py:22
  10.4 8.7 %collective-permute-start.5 = (bf16[128,512]{1,0:T(8,128)(2,1)S(1)}, bf16[128,512]{1,0:T(8,128)(2,1)S(1)}, u32[]{:S(2)}, u32[]{:S(2)}) collective-permute-start(bf16[128,512]{1,0:T(8,128)(2,1)S(1)} %dynamic-slice_bitcast_fusion.rest_0_), channel_id=1, source_target_pairs={{0,24},{4,28},{8,0},{12,4},{16,8},{20,12},{24,16},{28,20},{1,25},{... | collective-permute-start | bytes 393224 | tf_op jit(solution)/shard_map/ppermute | solution.py:22
  10.9 10.1 %collective-permute-start.4 = (bf16[128,512]{1,0:T(8,128)(2,1)S(1)}, bf16[128,512]{1,0:T(8,128)(2,1)S(1)}, u32[]{:S(2)}, u32[]{:S(2)}) collective-permute-start(bf16[128,512]{1,0:T(8,128)(2,1)S(1)} %dynamic-slice_bitcast_fusion.rest_0_), channel_id=1, source_target_pairs={{0,20},{4,24},{8,28},{12,0},{16,4},{20,8},{24,12},{28,16},{1,21},{... | collective-permute-start | bytes 393224 | tf_op jit(solution)/shard_map/ppermute | solution.py:22
  10.9 21.9 %collective-permute-start.3 = (bf16[128,512]{1,0:T(8,128)(2,1)S(1)}, bf16[128,512]{1,0:T(8,128)(2,1)S(1)}, u32[]{:S(2)}, u32[]{:S(2)}) collective-permute-start(bf16[128,512]{1,0:T(8,128)(2,1)S(1)} %dynamic-slice_bitcast_fusion.rest_0_), channel_id=1, source_target_pairs={{0,16},{4,20},{8,24},{12,28},{16,0},{20,4},{24,8},{28,12},{1,17},{... | collective-permute-start | bytes 393224 | tf_op jit(solution)/shard_map/ppermute | solution.py:22
  13.9 20.5 %collective-permute-start.2 = (bf16[128,512]{1,0:T(8,128)(2,1)S(1)}, bf16[128,512]{1,0:T(8,128)(2,1)S(1)}, u32[]{:S(2)}, u32[]{:S(2)}) collective-permute-start(bf16[128,512]{1,0:T(8,128)(2,1)S(1)} %dynamic-slice_bitcast_fusion.rest_0_), channel_id=1, source_target_pairs={{0,12},{4,16},{8,20},{12,24},{16,28},{20,0},{24,4},{28,8},{1,13},{... | collective-permute-start | bytes 393224 | tf_op jit(solution)/shard_map/ppermute | solution.py:22
  17.3 17.1 %copy-start.5 = (bf16[128,512]{1,0:T(8,128)(2,1)}, bf16[128,512]{1,0:T(8,128)(2,1)S(1)}, u32[]{:S(2)}) copy-start(bf16[128,512]{1,0:T(8,128)(2,1)S(1)} %collective-permute-done.6.rest_7_) | copy-start | bytes 393220
  17.3 17.1 %collective-permute-start.1 = (bf16[128,512]{1,0:T(8,128)(2,1)S(1)}, bf16[128,512]{1,0:T(8,128)(2,1)S(1)}, u32[]{:S(2)}, u32[]{:S(2)}) collective-permute-start(bf16[128,512]{1,0:T(8,128)(2,1)S(1)} %dynamic-slice_bitcast_fusion.rest_0_), channel_id=1, source_target_pairs={{0,8},{4,12},{8,16},{12,20},{16,24},{20,28},{24,0},{28,4},{1,9},{5... | collective-permute-start | bytes 393224 | tf_op jit(solution)/shard_map/ppermute | solution.py:22
  19.2 15.2 %copy-start.6 = (bf16[128,512]{1,0:T(8,128)(2,1)}, bf16[128,512]{1,0:T(8,128)(2,1)S(1)}, u32[]{:S(2)}) copy-start(bf16[128,512]{1,0:T(8,128)(2,1)S(1)} %collective-permute-done.5.rest_6_) | copy-start | bytes 393220
  19.2 15.2 %collective-permute-start = (bf16[128,512]{1,0:T(8,128)(2,1)S(1)}, bf16[128,512]{1,0:T(8,128)(2,1)S(1)}, u32[]{:S(2)}, u32[]{:S(2)}) collective-permute-start(bf16[128,512]{1,0:T(8,128)(2,1)S(1)} %dynamic-slice_bitcast_fusion.rest_0_), channel_id=1, source_target_pairs={{0,4},{4,8},{8,12},{12,16},{16,20},{20,24},{24,28},{28,0},{1,5},{5... | collective-permute-start | bytes 393224 | tf_op jit(solution)/shard_map/ppermute | solution.py:22
  21.0 13.4 %copy-start.7 = (bf16[128,512]{1,0:T(8,128)(2,1)}, bf16[128,512]{1,0:T(8,128)(2,1)S(1)}, u32[]{:S(2)}) copy-start(bf16[128,512]{1,0:T(8,128)(2,1)S(1)} %collective-permute-done.4.rest_5_) | copy-start | bytes 393220
  39.9 7.3 %collective-permute-start.8 = (bf16[256,512]{1,0:T(8,128)(2,1)}, bf16[256,512]{1,0:T(8,128)(2,1)S(1)}, u32[]{:S(2)}, u32[]{:S(2)}) collective-permute-start(bf16[256,512]{1,0:T(8,128)(2,1)} %bitcast.41), channel_id=1, source_target_pairs={{0,2},{1,3},{2,0},{3,1},{4,6},{5,7},{6,4},{7,5},{8,10},{9,11},{10,... | collective-permute-start | bytes 786440 | tf_op jit(solution)/shard_map/ppermute | solution.py:26
  46.1 6.9 %collective-permute-start.11 = (bf16[256,512]{1,0:T(8,128)(2,1)}, bf16[256,512]{1,0:T(8,128)(2,1)S(1)}, u32[]{:S(2)}, u32[]{:S(2)}) collective-permute-start(bf16[256,512]{1,0:T(8,128)(2,1)} %bitcast.44), channel_id=1, source_target_pairs={{0,2},{1,3},{2,0},{3,1},{4,6},{5,7},{6,4},{7,5},{8,10},{9,11},{10,... | collective-permute-start | bytes 786440 | tf_op jit(solution)/shard_map/ppermute | solution.py:26
  46.7 7.8 %collective-permute-start.7 = (bf16[256,512]{1,0:T(8,128)(2,1)}, bf16[256,512]{1,0:T(8,128)(2,1)S(1)}, u32[]{:S(2)}, u32[]{:S(2)}) collective-permute-start(bf16[256,512]{1,0:T(8,128)(2,1)} %bitcast.42), channel_id=1, source_target_pairs={{0,1},{1,0},{2,3},{3,2},{4,5},{5,4},{6,7},{7,6},{8,9},{9,8},{10,11... | collective-permute-start | bytes 786440 | tf_op jit(solution)/shard_map/ppermute | solution.py:26
  46.7 7.0 %collective-permute-start.10 = (bf16[256,512]{1,0:T(8,128)(2,1)}, bf16[256,512]{1,0:T(8,128)(2,1)S(1)}, u32[]{:S(2)}, u32[]{:S(2)}) collective-permute-start(bf16[256,512]{1,0:T(8,128)(2,1)} %bitcast.45), channel_id=1, source_target_pairs={{0,1},{1,0},{2,3},{3,2},{4,5},{5,4},{6,7},{7,6},{8,9},{9,8},{10,11... | collective-permute-start | bytes 786440 | tf_op jit(solution)/shard_map/ppermute | solution.py:26
  47.2 8.6 %collective-permute-start.9 = (bf16[256,512]{1,0:T(8,128)(2,1)S(1)}, bf16[256,512]{1,0:T(8,128)(2,1)S(1)}, u32[]{:S(2)}, u32[]{:S(2)}) collective-permute-start(bf16[256,512]{1,0:T(8,128)(2,1)S(1)} %collective-permute-done.8), channel_id=1, source_target_pairs={{0,1},{1,0},{2,3},{3,2},{4,5},{5,4},{6,7},{7,6},{8,9},{9,8},{10,11... | collective-permute-start | bytes 786440 | tf_op jit(solution)/shard_map/ppermute | solution.py:26
  53.0 2.4 %collective-permute-start.12 = (bf16[256,512]{1,0:T(8,128)(2,1)S(1)}, bf16[256,512]{1,0:T(8,128)(2,1)S(1)}, u32[]{:S(2)}, u32[]{:S(2)}) collective-permute-start(bf16[256,512]{1,0:T(8,128)(2,1)S(1)} %collective-permute-done.11), channel_id=1, source_target_pairs={{0,1},{1,0},{2,3},{3,2},{4,5},{5,4},{6,7},{7,6},{8,9},{9,8},{10,11... | collective-permute-start | bytes 786440 | tf_op jit(solution)/shard_map/ppermute | solution.py:26
  56.4 3.6 %collective-permute-start.14 = (f32[4,128]{1,0:T(4,128)S(1)}, f32[4,128]{1,0:T(4,128)S(1)}, u32[]{:S(2)}, u32[]{:S(2)}) collective-permute-start(f32[4,128]{1,0:T(4,128)S(1)} %bitcast.47), channel_id=1, source_target_pairs={{0,2},{1,3},{2,0},{3,1},{4,6},{5,7},{6,4},{7,5},{8,10},{9,11},{10,... | collective-permute-start | bytes 6152 | tf_op jit(solution)/shard_map/ppermute | solution.py:22
  57.6 2.5 %collective-permute-start.15 = (f32[4,128]{1,0:T(4,128)S(1)}, f32[4,128]{1,0:T(4,128)S(1)}, u32[]{:S(2)}, u32[]{:S(2)}) collective-permute-start(f32[4,128]{1,0:T(4,128)S(1)} %bitcast.48), channel_id=1, source_target_pairs={{0,3},{1,0},{2,1},{3,2},{4,7},{5,4},{6,5},{7,6},{8,11},{9,8},{10,9... | collective-permute-start | bytes 6152 | tf_op jit(solution)/shard_map/ppermute | solution.py:22
  58.3 3.0 %collective-permute-start.13 = (f32[4,128]{1,0:T(4,128)S(1)}, f32[4,128]{1,0:T(4,128)S(1)}, u32[]{:S(2)}, u32[]{:S(2)}) collective-permute-start(f32[4,128]{1,0:T(4,128)S(1)} %bitcast.49), channel_id=1, source_target_pairs={{0,1},{1,2},{2,3},{3,0},{4,5},{5,6},{6,7},{7,4},{8,9},{9,10},{10,1... | collective-permute-start | bytes 6152 | tf_op jit(solution)/shard_map/ppermute | solution.py:22
  (8 other events, 23.8 us)

commit v5 on v4

--- a/solution.py
+++ b/solution.py
@@ -35,9 +35,18 @@
         own = lax.dynamic_index_in_dim(page_store, slot, 0, keepdims=False)[:, 0]
         blocks = [own]
         sources = [device_row]
-        for shift in range(1, n_req):
-            blocks.append(shifted(own, "req", n_req, shift))
-            sources.append((device_row - shift) % n_req)
+        if n_req == 8:
+            for mask in (1, 2, 3, 6):
+                blocks.append(swapped(own, "req", n_req, mask))
+                sources.append(device_row ^ mask)
+            mirror = blocks[-1]
+            for mask in (1, 2, 3):
+                blocks.append(swapped(mirror, "req", n_req, mask))
+                sources.append(device_row ^ 6 ^ mask)
+        else:
+            for shift in range(1, n_req):
+                blocks.append(shifted(own, "req", n_req, shift))
+                sources.append((device_row - shift) % n_req)
         sources = jnp.stack(sources)
         valid = jnp.any(page_owner[None, :] == sources[:, None], 1)
         return blocks, valid

time: 62.8 us -> 54.2 us (0.86)
  waiting for transfers between devices: 22.2 us -> 14.1 us
    ppermute x10 -> x3, waiting for transfers between devices: 16.3 us -> 2.94 us  [shifted(): lax.ppermute(value, axis, [(i, (i + shift) % size) for i in range(size)])]
    ppermute x10 -> x3, starting transfers between devices: 14.5 us -> 1.92 us  [shifted(): lax.ppermute(value, axis, [(i, (i + shift) % size) for i in range(size)])]
    ppermute x6 -> x13, starting transfers between devices: 2.54 us -> 14.7 us  [swapped(): return lax.ppermute(value, axis, [(i, i ^ mask) for i in range(size)])]
    ppermute x6 -> x13, waiting for transfers between devices: 5.83 us -> 11.1 us  [swapped(): return lax.ppermute(value, axis, [(i, i ^ mask) for i in range(size)])]
  transfers between devices with their start and end apart: 16 -> 16, of which waited for: 5 -> 7; matrix products, arithmetic and copies ran while one was open for 10% -> 12% of each run, Pallas kernels for 8% -> 9%
where the time goes in v5:
time: 54.2 us; the launch traced here: 53.9 us
  starting transfers between devices  16.7 us (31%)
  waiting for transfers between devices  14.1 us (26%)
  Pallas kernels  9.55 us (18%)
  local copies, waits for them, and re-layouts  4.84 us (9%)
  other arithmetic  3.85 us (7%)
  matrix products  2.77 us (5%)
  between operations  2.18 us (4%)
    ppermute x13, starting transfers between devices, swapped(): return lax.ppermute(value, axis, [(i, i ^ mask) for i in range(size)])  14.7 us
    ppermute x13, waiting for transfers between devices, swapped(): return lax.ppermute(value, axis, [(i, i ^ mask) for i in range(size)])  11.1 us
    pallas_call x2, Pallas kernels, attend(): pl.pallas_call(attention_kernel, grid_spec=grid_spec, out_shape=jax.Shape...  9.55 us
    ppermute x3, waiting for transfers between devices, shifted(): lax.ppermute(value, axis, [(i, (i + shift) % size) for i in range(size)])  2.94 us
    dot_general x8, matrix products, project(): term = jnp.dot(block, rows, preferred_element_type=jnp.float32)  2.77 us
    squeeze x1, local copies, waits for them, and re-layouts, on_device(): qkv[start:start + chunk, :, 0]  2.24 us
    ppermute x3, starting transfers between devices, shifted(): lax.ppermute(value, axis, [(i, (i + shift) % size) for i in range(size)])  1.92 us
    reduce_sum x1, other arithmetic, gather_prefix(): slot = jnp.sum(jnp.where(mine, page_slot, 0))  1.46 us
  transfers between devices with their start and end apart: 16, of which 7 were waited for; matrix products, arithmetic and copies ran while one was open for 12% of the time, Pallas kernels for 9%

profile of v5, /device:TPU:0, one launch (start us, length us, event | category | flops | bytes accessed | tf_op | source)
XLA Modules:
  0.0 53.9 jit_solution(7460307527278546761)
XLA Ops:
  0.0 1.5 %fusion.28 = s32[]{:T(128)} fusion(s32[8]{0:T(128)} %param.15, s32[8]{0:T(128)} %param.14, s32[]{:T(128)} %axis_index.27), kind=kLoop, calls=%fused_computation.44 | loop fusion | flops 23 | bytes 72 | tf_op jit(solution)/shard_map/reduce_sum | solution.py:34
  3.4 0.9 %dynamic-slice_bitcast_fusion.rest_0_ = bf16[128,512]{1,0:T(8,128)(2,1)S(1)} fusion(bf16[2,128,1,512]{3,1,2,0:T(8,128)(2,1)} %param.13, s32[]{:T(128)S(6)} %select_n.34), kind=kLoop, calls=%fused_computation.28 | loop fusion | bytes 262148 | tf_op jit(solution)/shard_map/squeeze | solution.py:35
  4.4 5.2 %collective-permute-start.3 = (bf16[128,512]{1,0:T(8,128)(2,1)S(1)}, bf16[128,512]{1,0:T(8,128)(2,1)S(1)}, u32[]{:S(2)}, u32[]{:S(2)}) collective-permute-start(bf16[128,512]{1,0:T(8,128)(2,1)S(1)} %dynamic-slice_bitcast_fusion.rest_0_), channel_id=1, source_target_pairs={{0,24},{4,28},{8,16},{12,20},{16,8},{20,12},{24,0},{28,4},{1,25},{... | collective-permute-start | bytes 393224 | tf_op jit(solution)/shard_map/ppermute | solution.py:26
  10.0 2.5 %collective-permute-start.1 = (bf16[128,512]{1,0:T(8,128)(2,1)S(1)}, bf16[128,512]{1,0:T(8,128)(2,1)S(1)}, u32[]{:S(2)}, u32[]{:S(2)}) collective-permute-start(bf16[128,512]{1,0:T(8,128)(2,1)S(1)} %dynamic-slice_bitcast_fusion.rest_0_), channel_id=1, source_target_pairs={{0,8},{4,12},{8,0},{12,4},{16,24},{20,28},{24,16},{28,20},{1,9},{5... | collective-permute-start | bytes 393224 | tf_op jit(solution)/shard_map/ppermute | solution.py:26
  13.0 2.2 %slice_bitcast_fusion.1 = (bf16[2,128,1024]{2,1,0:T(8,128)(2,1)}, bf16[2,128,1024]{2,1,0:T(8,128)(2,1)}) fusion(bf16[4,128,1,1024]{3,1,0,2:T(8,128)(2,1)} %bitcast.40), kind=kLoop, calls=%fused_computation.15 | loop fusion | bytes 2097152 | tf_op jit(solution)/shard_map/squeeze | solution.py:177
  15.5 0.6 %convert_element_type.18.valid_ref = s32[8]{0:T(128)} convert(pred[8]{0:T(512)(128)(4,1)S(1)} %compare_reduce_fusion) | non-fusion elementwise | flops 8 | bytes 40 | tf_op jit(solution)/shard_map/convert_element_type | solution.py:178
  16.4 1.0 %collective-permute-start.6 = (bf16[128,512]{1,0:T(8,128)(2,1)S(1)}, bf16[128,512]{1,0:T(8,128)(2,1)S(1)}, u32[]{:S(2)}, u32[]{:S(2)}) collective-permute-start(bf16[128,512]{1,0:T(8,128)(2,1)S(1)} %collective-permute-done.3.rest_4_), channel_id=1, source_target_pairs={{0,12},{4,8},{8,4},{12,0},{16,28},{20,24},{24,20},{28,16},{1,13},{... | collective-permute-start | bytes 393224 | tf_op jit(solution)/shard_map/ppermute | solution.py:26
  17.4 2.0 %collective-permute-start.5 = (bf16[128,512]{1,0:T(8,128)(2,1)S(1)}, bf16[128,512]{1,0:T(8,128)(2,1)S(1)}, u32[]{:S(2)}, u32[]{:S(2)}) collective-permute-start(bf16[128,512]{1,0:T(8,128)(2,1)S(1)} %collective-permute-done.3.rest_4_), channel_id=1, source_target_pairs={{0,8},{4,12},{8,0},{12,4},{16,24},{20,28},{24,16},{28,20},{1,9},{5... | collective-permute-start | bytes 393224 | tf_op jit(solution)/shard_map/ppermute | solution.py:26
  19.4 0.5 collective-permute-start.4
  19.9 0.6 %fusion.29 = (s32[2]{0:T(128)}, s32[2]{0:T(128)}) fusion(s32[4]{0:T(128)S(1)} %select_reduce_fusion), kind=kLoop, calls=%fused_computation.45 | loop fusion | bytes 32 | tf_op jit(solution)/shard_map/slice | solution.py:178
  20.6 3.1 %collective-permute-done.6.rest_7_ = bf16[128,512]{1,0:T(8,128)(2,1)S(1)} collective-permute-done((bf16[128,512]{1,0:T(8,128)(2,1)S(1)}, bf16[128,512]{1,0:T(8,128)(2,1)S(1)}, u32[]{:S(2)}, u32[]{:S(2)}) %collective-permute-start.6) | collective-permute-done | bytes 131104 | tf_op jit(solution)/shard_map/ppermute | solution.py:26
  23.7 0.8 %collective-permute-done.5.rest_6_ = bf16[128,512]{1,0:T(8,128)(2,1)S(1)} collective-permute-done((bf16[128,512]{1,0:T(8,128)(2,1)S(1)}, bf16[128,512]{1,0:T(8,128)(2,1)S(1)}, u32[]{:S(2)}, u32[]{:S(2)}) %collective-permute-start.5) | collective-permute-done | bytes 131104 | tf_op jit(solution)/shard_map/ppermute | solution.py:26
  24.5 0.8 %collective-permute-done.4.rest_5_ = bf16[128,512]{1,0:T(8,128)(2,1)S(1)} collective-permute-done((bf16[128,512]{1,0:T(8,128)(2,1)S(1)}, bf16[128,512]{1,0:T(8,128)(2,1)S(1)}, u32[]{:S(2)}, u32[]{:S(2)}) %collective-permute-start.4) | collective-permute-done | bytes 131104 | tf_op jit(solution)/shard_map/ppermute | solution.py:26
  25.4 0.6 %copy-done.11 = bf16[128,512]{1,0:T(8,128)(2,1)} copy-done((bf16[128,512]{1,0:T(8,128)(2,1)}, bf16[128,512]{1,0:T(8,128)(2,1)S(1)}, u32[]{:S(2)}) %copy-start.11) | copy-done | bytes 131096
  26.0 4.8 %shard_map.109 = bf16[2,128,512]{2,1,0:T(8,128)(2,1)} custom-call(s32[2]{0:T(128)} %get-tuple-element.9.length_ref, s32[8]{0:T(128)} %convert_element_type.18.valid_ref, bf16[2,128,1024]{2,1,0:T(8,128)(2,1)} %get-tuple-element.7.qkv_ref, f32[128,128]{1,0:T(8,128)} %constant.44.clone.cos_ref, f32[128,128]{1,0:T(8,128)} %constant.45.clone.sin_ref, ...), custom_call_target="tpu_custom_call" | custom-call | tf_op jit(solution)/shard_map/pallas_call | solution.py:128
  30.7 1.5 %collective-permute-start.8 = (bf16[256,512]{1,0:T(8,128)(2,1)}, bf16[256,512]{1,0:T(8,128)(2,1)S(1)}, u32[]{:S(2)}, u32[]{:S(2)}) collective-permute-start(bf16[256,512]{1,0:T(8,128)(2,1)} %bitcast.41), channel_id=1, source_target_pairs={{0,2},{1,3},{2,0},{3,1},{4,6},{5,7},{6,4},{7,5},{8,10},{9,11},{10,... | collective-permute-start | bytes 786440 | tf_op jit(solution)/shard_map/ppermute | solution.py:26
  32.2 4.8 %shard_map.110 = bf16[2,128,512]{2,1,0:T(8,128)(2,1)} custom-call(s32[2]{0:T(128)} %get-tuple-element.10.length_ref, s32[8]{0:T(128)} %convert_element_type.18.valid_ref, bf16[2,128,1024]{2,1,0:T(8,128)(2,1)} %get-tuple-element.8.qkv_ref, f32[128,128]{1,0:T(8,128)} %constant.44.clone.cos_ref, f32[128,128]{1,0:T(8,128)} %constant.45.clone.sin_ref, ...), custom_call_target="tpu_custom_call" | custom-call | tf_op jit(solution)/shard_map/pallas_call | solution.py:128
  37.0 0.5 collective-permute-start.11
  38.5 6.0 %collective-permute-done.11 = bf16[256,512]{1,0:T(8,128)(2,1)S(1)} collective-permute-done((bf16[256,512]{1,0:T(8,128)(2,1)}, bf16[256,512]{1,0:T(8,128)(2,1)S(1)}, u32[]{:S(2)}, u32[]{:S(2)}) %collective-permute-start.11) | collective-permute-done | bytes 262176 | tf_op jit(solution)/shard_map/ppermute | solution.py:26
  47.9 1.2 %collective-permute-start.14 = (f32[4,128]{1,0:T(4,128)S(1)}, f32[4,128]{1,0:T(4,128)S(1)}, u32[]{:S(2)}, u32[]{:S(2)}) collective-permute-start(f32[4,128]{1,0:T(4,128)S(1)} %bitcast.47), channel_id=1, source_target_pairs={{0,2},{1,3},{2,0},{3,1},{4,6},{5,7},{6,4},{7,5},{8,10},{9,11},{10,... | collective-permute-start | bytes 6152 | tf_op jit(solution)/shard_map/ppermute | solution.py:22
  49.0 0.7 %collective-permute-start.15 = (f32[4,128]{1,0:T(4,128)S(1)}, f32[4,128]{1,0:T(4,128)S(1)}, u32[]{:S(2)}, u32[]{:S(2)}) collective-permute-start(f32[4,128]{1,0:T(4,128)S(1)} %bitcast.48), channel_id=1, source_target_pairs={{0,3},{1,0},{2,1},{3,2},{4,7},{5,4},{6,5},{7,6},{8,11},{9,8},{10,9... | collective-permute-start | bytes 6152 | tf_op jit(solution)/shard_map/ppermute | solution.py:22
  49.9 1.7 %collective-permute-done.14 = f32[4,128]{1,0:T(4,128)S(1)} collective-permute-done((f32[4,128]{1,0:T(4,128)S(1)}, f32[4,128]{1,0:T(4,128)S(1)}, u32[]{:S(2)}, u32[]{:S(2)}) %collective-permute-start.14) | collective-permute-done | bytes 2080 | tf_op jit(solution)/shard_map/ppermute | solution.py:22
  51.5 1.3 %collective-permute-done.13 = f32[4,128]{1,0:T(4,128)S(1)} collective-permute-done((f32[4,128]{1,0:T(4,128)S(1)}, f32[4,128]{1,0:T(4,128)S(1)}, u32[]{:S(2)}, u32[]{:S(2)}) %collective-permute-start.13) | collective-permute-done | bytes 2080 | tf_op jit(solution)/shard_map/ppermute | solution.py:22
  52.8 1.1 %fusion.5 = bf16[4,128,576]{1,2,0:T(8,128)(2,1)} fusion(f32[72,4,8,128]{3,2,1,0:T(8,128)S(1)} %get-tuple-element.6, bf16[4,128,576]{1,2,0:T(8,128)(2,1)S(1)} %copy-done.4, f32[4,128]{1,0:T(4,128)S(1)} %fusion.19, f32[576]{0:T(1024)S(1)} %copy-done.12, f32[4,128]{1,0:T(4,128)S(1)} %add_rsqrt_fusion), kind=kLoop, calls=%fused_computation.10 | loop fusion | flops 1769472 | bytes 2365696 | tf_op jit(solution)/shard_map/convert_element_type | solution.py:189
  (63 shorter events, 5.9 us)
Async XLA Ops:
  0.0 44.5 %copy-start = (bf16[2048,576]{0,1:T(8,128)(2,1)S(1)}, bf16[2048,576]{0,1:T(8,128)(2,1)}, u32[]{:S(2)}) copy-start(bf16[2048,576]{0,1:T(8,128)(2,1)} %param.18) | copy-start | bytes 7077892
  0.0 15.3 %copy-start.13 = (s32[8]{0:T(128)S(1)}, s32[8]{0:T(128)}, u32[]{:S(2)}) copy-start(s32[8]{0:T(128)} %param.14) | copy-start | bytes 100
  0.0 16.1 %copy-start.14 = (s32[32]{0:T(128)S(1)}, s32[32]{0:T(128)}, u32[]{:S(2)}) copy-start(s32[32]{0:T(128)} %param.17) | copy-start | bytes 388
  0.0 16.2 %copy-start.15 = (s32[32]{0:T(128)S(1)}, s32[32]{0:T(128)}, u32[]{:S(2)}) copy-start(s32[32]{0:T(128)} %param.16) | copy-start | bytes 388
  4.3 21.0 %copy-start.1 = (bf16[128,512]{1,0:T(8,128)(2,1)}, bf16[128,512]{1,0:T(8,128)(2,1)S(1)}, u32[]{:S(2)}) copy-start(bf16[128,512]{1,0:T(8,128)(2,1)S(1)} %dynamic-slice_bitcast_fusion.rest_0_) | copy-start | bytes 393220
  4.4 12.0 %collective-permute-start.3 = (bf16[128,512]{1,0:T(8,128)(2,1)S(1)}, bf16[128,512]{1,0:T(8,128)(2,1)S(1)}, u32[]{:S(2)}, u32[]{:S(2)}) collective-permute-start(bf16[128,512]{1,0:T(8,128)(2,1)S(1)} %dynamic-slice_bitcast_fusion.rest_0_), channel_id=1, source_target_pairs={{0,24},{4,28},{8,16},{12,20},{16,8},{20,12},{24,0},{28,4},{1,25},{... | collective-permute-start | bytes 393224 | tf_op jit(solution)/shard_map/ppermute | solution.py:26
  9.5 9.9 %collective-permute-start.2 = (bf16[128,512]{1,0:T(8,128)(2,1)S(1)}, bf16[128,512]{1,0:T(8,128)(2,1)S(1)}, u32[]{:S(2)}, u32[]{:S(2)}) collective-permute-start(bf16[128,512]{1,0:T(8,128)(2,1)S(1)} %dynamic-slice_bitcast_fusion.rest_0_), channel_id=1, source_target_pairs={{0,12},{4,8},{8,4},{12,0},{16,28},{20,24},{24,20},{28,16},{1,13},{... | collective-permute-start | bytes 393224 | tf_op jit(solution)/shard_map/ppermute | solution.py:26
  10.0 10.6 %collective-permute-start.1 = (bf16[128,512]{1,0:T(8,128)(2,1)S(1)}, bf16[128,512]{1,0:T(8,128)(2,1)S(1)}, u32[]{:S(2)}, u32[]{:S(2)}) collective-permute-start(bf16[128,512]{1,0:T(8,128)(2,1)S(1)} %dynamic-slice_bitcast_fusion.rest_0_), channel_id=1, source_target_pairs={{0,8},{4,12},{8,0},{12,4},{16,24},{20,28},{24,16},{28,20},{1,9},{5... | collective-permute-start | bytes 393224 | tf_op jit(solution)/shard_map/ppermute | solution.py:26
  12.5 8.1 %collective-permute-start = (bf16[128,512]{1,0:T(8,128)(2,1)S(1)}, bf16[128,512]{1,0:T(8,128)(2,1)S(1)}, u32[]{:S(2)}, u32[]{:S(2)}) collective-permute-start(bf16[128,512]{1,0:T(8,128)(2,1)S(1)} %dynamic-slice_bitcast_fusion.rest_0_), channel_id=1, source_target_pairs={{0,4},{4,0},{8,12},{12,8},{16,20},{20,16},{24,28},{28,24},{1,5},{5... | collective-permute-start | bytes 393224 | tf_op jit(solution)/shard_map/ppermute | solution.py:26
  16.4 9.0 %copy-start.5 = (bf16[128,512]{1,0:T(8,128)(2,1)}, bf16[128,512]{1,0:T(8,128)(2,1)S(1)}, u32[]{:S(2)}) copy-start(bf16[128,512]{1,0:T(8,128)(2,1)S(1)} %collective-permute-done.3.rest_4_) | copy-start | bytes 393220
  16.4 7.3 %collective-permute-start.6 = (bf16[128,512]{1,0:T(8,128)(2,1)S(1)}, bf16[128,512]{1,0:T(8,128)(2,1)S(1)}, u32[]{:S(2)}, u32[]{:S(2)}) collective-permute-start(bf16[128,512]{1,0:T(8,128)(2,1)S(1)} %collective-permute-done.3.rest_4_), channel_id=1, source_target_pairs={{0,12},{4,8},{8,4},{12,0},{16,28},{20,24},{24,20},{28,16},{1,13},{... | collective-permute-start | bytes 393224 | tf_op jit(solution)/shard_map/ppermute | solution.py:26
  17.4 7.1 %collective-permute-start.5 = (bf16[128,512]{1,0:T(8,128)(2,1)S(1)}, bf16[128,512]{1,0:T(8,128)(2,1)S(1)}, u32[]{:S(2)}, u32[]{:S(2)}) collective-permute-start(bf16[128,512]{1,0:T(8,128)(2,1)S(1)} %collective-permute-done.3.rest_4_), channel_id=1, source_target_pairs={{0,8},{4,12},{8,0},{12,4},{16,24},{20,28},{24,16},{28,20},{1,9},{5... | collective-permute-start | bytes 393224 | tf_op jit(solution)/shard_map/ppermute | solution.py:26
  19.4 5.9 %copy-start.6 = (bf16[128,512]{1,0:T(8,128)(2,1)}, bf16[128,512]{1,0:T(8,128)(2,1)S(1)}, u32[]{:S(2)}) copy-start(bf16[128,512]{1,0:T(8,128)(2,1)S(1)} %collective-permute-done.2.rest_3_) | copy-start | bytes 393220
  19.4 5.9 %collective-permute-start.4 = (bf16[128,512]{1,0:T(8,128)(2,1)S(1)}, bf16[128,512]{1,0:T(8,128)(2,1)S(1)}, u32[]{:S(2)}, u32[]{:S(2)}) collective-permute-start(bf16[128,512]{1,0:T(8,128)(2,1)S(1)} %collective-permute-done.3.rest_4_), channel_id=1, source_target_pairs={{0,4},{4,0},{8,12},{12,8},{16,20},{20,16},{24,28},{28,24},{1,5},{5... | collective-permute-start | bytes 393224 | tf_op jit(solution)/shard_map/ppermute | solution.py:26
  30.7 7.7 %collective-permute-start.8 = (bf16[256,512]{1,0:T(8,128)(2,1)}, bf16[256,512]{1,0:T(8,128)(2,1)S(1)}, u32[]{:S(2)}, u32[]{:S(2)}) collective-permute-start(bf16[256,512]{1,0:T(8,128)(2,1)} %bitcast.41), channel_id=1, source_target_pairs={{0,2},{1,3},{2,0},{3,1},{4,6},{5,7},{6,4},{7,5},{8,10},{9,11},{10,... | collective-permute-start | bytes 786440 | tf_op jit(solution)/shard_map/ppermute | solution.py:26
  37.0 8.5 %copy-start.3 = (bf16[2,128,512]{2,1,0:T(8,128)(2,1)S(1)}, bf16[2,128,512]{2,1,0:T(8,128)(2,1)}, u32[]{:S(2)}) copy-start(bf16[2,128,512]{2,1,0:T(8,128)(2,1)} %shard_map.110) | copy-start | bytes 786436
  37.0 7.4 %collective-permute-start.11 = (bf16[256,512]{1,0:T(8,128)(2,1)}, bf16[256,512]{1,0:T(8,128)(2,1)S(1)}, u32[]{:S(2)}, u32[]{:S(2)}) collective-permute-start(bf16[256,512]{1,0:T(8,128)(2,1)} %bitcast.44), channel_id=1, source_target_pairs={{0,2},{1,3},{2,0},{3,1},{4,6},{5,7},{6,4},{7,5},{8,10},{9,11},{10,... | collective-permute-start | bytes 786440 | tf_op jit(solution)/shard_map/ppermute | solution.py:26
  37.6 8.3 %collective-permute-start.7 = (bf16[256,512]{1,0:T(8,128)(2,1)}, bf16[256,512]{1,0:T(8,128)(2,1)S(1)}, u32[]{:S(2)}, u32[]{:S(2)}) collective-permute-start(bf16[256,512]{1,0:T(8,128)(2,1)} %bitcast.42), channel_id=1, source_target_pairs={{0,1},{1,0},{2,3},{3,2},{4,5},{5,4},{6,7},{7,6},{8,9},{9,8},{10,11... | collective-permute-start | bytes 786440 | tf_op jit(solution)/shard_map/ppermute | solution.py:26
  37.6 7.6 %collective-permute-start.10 = (bf16[256,512]{1,0:T(8,128)(2,1)}, bf16[256,512]{1,0:T(8,128)(2,1)S(1)}, u32[]{:S(2)}, u32[]{:S(2)}) collective-permute-start(bf16[256,512]{1,0:T(8,128)(2,1)} %bitcast.45), channel_id=1, source_target_pairs={{0,1},{1,0},{2,3},{3,2},{4,5},{5,4},{6,7},{7,6},{8,9},{9,8},{10,11... | collective-permute-start | bytes 786440 | tf_op jit(solution)/shard_map/ppermute | solution.py:26
  38.5 8.8 %collective-permute-start.9 = (bf16[256,512]{1,0:T(8,128)(2,1)S(1)}, bf16[256,512]{1,0:T(8,128)(2,1)S(1)}, u32[]{:S(2)}, u32[]{:S(2)}) collective-permute-start(bf16[256,512]{1,0:T(8,128)(2,1)S(1)} %collective-permute-done.8), channel_id=1, source_target_pairs={{0,1},{1,0},{2,3},{3,2},{4,5},{5,4},{6,7},{7,6},{8,9},{9,8},{10,11... | collective-permute-start | bytes 786440 | tf_op jit(solution)/shard_map/ppermute | solution.py:26
  44.5 2.4 %collective-permute-start.12 = (bf16[256,512]{1,0:T(8,128)(2,1)S(1)}, bf16[256,512]{1,0:T(8,128)(2,1)S(1)}, u32[]{:S(2)}, u32[]{:S(2)}) collective-permute-start(bf16[256,512]{1,0:T(8,128)(2,1)S(1)} %collective-permute-done.11), channel_id=1, source_target_pairs={{0,1},{1,0},{2,3},{3,2},{4,5},{5,4},{6,7},{7,6},{8,9},{9,8},{10,11... | collective-permute-start | bytes 786440 | tf_op jit(solution)/shard_map/ppermute | solution.py:26
  47.9 3.6 %collective-permute-start.14 = (f32[4,128]{1,0:T(4,128)S(1)}, f32[4,128]{1,0:T(4,128)S(1)}, u32[]{:S(2)}, u32[]{:S(2)}) collective-permute-start(f32[4,128]{1,0:T(4,128)S(1)} %bitcast.47), channel_id=1, source_target_pairs={{0,2},{1,3},{2,0},{3,1},{4,6},{5,7},{6,4},{7,5},{8,10},{9,11},{10,... | collective-permute-start | bytes 6152 | tf_op jit(solution)/shard_map/ppermute | solution.py:22
  49.0 2.5 %collective-permute-start.15 = (f32[4,128]{1,0:T(4,128)S(1)}, f32[4,128]{1,0:T(4,128)S(1)}, u32[]{:S(2)}, u32[]{:S(2)}) collective-permute-start(f32[4,128]{1,0:T(4,128)S(1)} %bitcast.48), channel_id=1, source_target_pairs={{0,3},{1,0},{2,1},{3,2},{4,7},{5,4},{6,5},{7,6},{8,11},{9,8},{10,9... | collective-permute-start | bytes 6152 | tf_op jit(solution)/shard_map/ppermute | solution.py:22
  49.8 3.0 %collective-permute-start.13 = (f32[4,128]{1,0:T(4,128)S(1)}, f32[4,128]{1,0:T(4,128)S(1)}, u32[]{:S(2)}, u32[]{:S(2)}) collective-permute-start(f32[4,128]{1,0:T(4,128)S(1)} %bitcast.49), channel_id=1, source_target_pairs={{0,1},{1,2},{2,3},{3,0},{4,5},{5,6},{6,7},{7,4},{8,9},{9,10},{10,1... | collective-permute-start | bytes 6152 | tf_op jit(solution)/shard_map/ppermute | solution.py:22
  (8 other events, 24.8 us)

commit v6 on v5

--- a/solution.py
+++ b/solution.py
@@ -1,3 +1,5 @@
+import functools
+
 import numpy as np
 import jax
 import jax.numpy as jnp
@@ -32,7 +34,9 @@
     if n_req <= page_count:
         mine = page_owner == device_row
         slot = jnp.sum(jnp.where(mine, page_slot, 0))
-        own = lax.dynamic_index_in_dim(page_store, slot, 0, keepdims=False)[:, 0]
+        own = page_store[0, :, 0]
+        for index in range(1, page_store.shape[0]):
+            own = jnp.where(slot == index, page_store[index, :, 0], own)
         blocks = [own]
         sources = [device_row]
         if n_req == 8:
@@ -65,9 +69,9 @@
     return np.cos(angles).astype(np.float32), np.sin(angles).astype(np.float32)
 
 
-def attention_kernel(length_ref, valid_ref, qkv_ref, cos_ref, sin_ref, *rest):
+def attention_kernel(length_ref, valid_ref, qkv_ref, cos_ref, sin_ref, *rest, offset):
     page_refs, out_ref = rest[:-1], rest[-1]
-    request = pl.program_id(0)
+    request = pl.program_id(0) + offset
     slots = qkv_ref.shape[1]
     per_group = qkv_ref.shape[2] // HD - 2
     half = HD // 2
@@ -112,25 +116,24 @@
         [attended[q * slots:(q + 1) * slots] for q in range(per_group)], 1)
 
 
-def attend(qkv, cosine, sine, blocks, lengths, valid):
-    requests, slots, width = qkv.shape
+def attend(qkv, cosine, sine, blocks, lengths, valid, offset, count):
+    _, slots, width = qkv.shape
     per_group = width // HD - 2
     page_len, page_width = blocks[0].shape
     full = lambda shape: pl.BlockSpec(shape, lambda r, *_: (0,) * len(shape))
     grid_spec = pltpu.PrefetchScalarGridSpec(
         num_scalar_prefetch=2,
-        grid=(requests,),
-        in_specs=[pl.BlockSpec((1, slots, width), lambda r, *_: (r, 0, 0)),
+        grid=(count,),
+        in_specs=[pl.BlockSpec((1, slots, width), lambda r, *_: (r + offset, 0, 0)),
                   full(cosine.shape), full(sine.shape)]
                  + [full((page_len, page_width)) for _ in blocks],
         out_specs=pl.BlockSpec((1, slots, per_group * HD), lambda r, *_: (r, 0, 0)),
     )
     return pl.pallas_call(
-        attention_kernel,
+        functools.partial(attention_kernel, offset=offset),
         grid_spec=grid_spec,
-        out_shape=jax.ShapeDtypeStruct((requests, slots, per_group * HD), jnp.bfloat16),
+        out_shape=jax.ShapeDtypeStruct((count, slots, per_group * HD), jnp.bfloat16),
     )(lengths, valid, qkv, cosine, sine, *blocks)
-
 
 def project(own, w_out, tp_index, n_tp, group_width):
     if n_tp == 4:
@@ -174,8 +177,8 @@
     chunk = max(1, requests // 2)
     projected_parts = []
     for start in range(0, requests, chunk):
-        attended = attend(qkv[start:start + chunk, :, 0], jnp.asarray(cosine), jnp.asarray(sine),
-                          blocks, my_lengths[start:start + chunk], valid.astype(jnp.int32))
+        attended = attend(qkv[:, :, 0], jnp.asarray(cosine), jnp.asarray(sine), blocks,
+                          my_lengths, valid.astype(jnp.int32), start, chunk)
         own = attended.reshape(chunk * slots, per_group * HD)
         projected_parts.append(project(own, w_out, tp_index, n_tp, group_width))
     projected = jnp.concatenate(projected_parts, 0).reshape(requests, slots, local_width)

time: 54.2 us -> 52.7 us (0.972)
  local copies, waits for them, and re-layouts: 4.84 us -> 1.67 us
  other arithmetic: 3.85 us -> 6.71 us
  between operations: 2.18 us -> 0.92 us
  waiting for transfers between devices: 14.1 us -> 13.2 us
  starting transfers between devices: 16.7 us -> 17.3 us
    squeeze x2 -> x0, local copies, waits for them, and re-layouts: 3.16 us -> none  [the longest x1 2.24 us: on_device(): qkv[start:start + chunk, :, 0]]
    ppermute x3, waiting for transfers between devices: 2.94 us -> 1.48 us  [shifted(): lax.ppermute(value, axis, [(i, (i + shift) % size) for i in range(size)])]
    reduce_sum x1, other arithmetic: 0.18 us -> 1.32 us  [on_device(): my_lengths = jnp.sum(jnp.where(matches, lengths[None, :], 0), 1)]
    select_n x0 -> x1, other arithmetic: none -> 0.99 us  [gather_prefix(): own = jnp.where(slot == index, page_store[index, :, 0], own)]
    ppermute x3, starting transfers between devices: 1.92 us -> 2.6 us  [shifted(): lax.ppermute(value, axis, [(i, (i + shift) % size) for i in range(size)])]
    dynamic_slice x1, local copies, waits for them, and re-layouts: 0.07 us -> 0.73 us  [on_device(): lax.dynamic_slice_in_dim(request_perm, device_row * requests, requests)]
    reduce_or x1, other arithmetic: 0.18 us -> 0.84 us  [gather_prefix(): valid = jnp.any(page_owner[None, :] == sources[:, None], 1)]
    slice x1 -> x0, local copies, waits for them, and re-layouts: 0.65 us -> none  [on_device(): my_lengths[start:start + chunk]]
  transfers between devices with their start and end apart: 16 -> 16, of which waited for: 7 -> 8; matrix products, arithmetic and copies ran while one was open for 12% -> 12% of each run, Pallas kernels for 9% -> 9%
where the time goes in v6:
time: 52.7 us; the launch traced here: 52.1 us
  starting transfers between devices  17.3 us (33%)
  waiting for transfers between devices  13.2 us (25%)
  Pallas kernels  9.58 us (18%)
  other arithmetic  6.71 us (13%)
  matrix products  2.8 us (5%)
  local copies, waits for them, and re-layouts  1.67 us (3%)
  between operations  0.92 us (2%)
    ppermute x13, starting transfers between devices, swapped(): return lax.ppermute(value, axis, [(i, i ^ mask) for i in range(size)])  14.7 us
    ppermute x13, waiting for transfers between devices, swapped(): return lax.ppermute(value, axis, [(i, i ^ mask) for i in range(size)])  11.7 us
    pallas_call x2, Pallas kernels, attend(): pl.pallas_call(functools.partial(attention_kernel, offset=offset), grid_s...  9.58 us
    dot_general x8, matrix products, project(): term = jnp.dot(block, rows, preferred_element_type=jnp.float32)  2.8 us
    ppermute x3, starting transfers between devices, shifted(): lax.ppermute(value, axis, [(i, (i + shift) % size) for i in range(size)])  2.6 us
    reduce_sum x1, other arithmetic, gather_prefix(): slot = jnp.sum(jnp.where(mine, page_slot, 0))  1.54 us
    ppermute x3, waiting for transfers between devices, shifted(): lax.ppermute(value, axis, [(i, (i + shift) % size) for i in range(size)])  1.48 us
    reduce_sum x1, other arithmetic, on_device(): my_lengths = jnp.sum(jnp.where(matches, lengths[None, :], 0), 1)  1.32 us
  transfers between devices with their start and end apart: 16, of which 8 were waited for; matrix products, arithmetic and copies ran while one was open for 12% of the time, Pallas kernels for 9%

profile of v6, /device:TPU:0, one launch (start us, length us, event | category | flops | bytes accessed | tf_op | source)
XLA Modules:
  0.0 52.1 jit_solution(14801607665913646079)
XLA Ops:
  0.0 1.5 %fusion.28 = s32[]{:T(128)} fusion(s32[8]{0:T(128)} %param.15, s32[8]{0:T(128)} %param.14, s32[]{:T(128)} %axis_index.27), kind=kLoop, calls=%fused_computation.42 | loop fusion | flops 23 | bytes 72 | tf_op jit(solution)/shard_map/reduce_sum | solution.py:36
  2.2 1.0 %select_bitcast_fusion.rest_0_ = bf16[128,512]{1,0:T(8,128)(2,1)S(1)} fusion(bf16[2,128,1,512]{3,1,2,0:T(8,128)(2,1)} %param.13, pred[]{:T(512)S(6)} %eq.43), kind=kLoop, calls=%fused_computation.26 | loop fusion | flops 65536 | bytes 393217 | tf_op jit(solution)/shard_map/jit(_where)/select_n | solution.py:39
  3.2 5.1 %collective-permute-start.3 = (bf16[128,512]{1,0:T(8,128)(2,1)S(1)}, bf16[128,512]{1,0:T(8,128)(2,1)S(1)}, u32[]{:S(2)}, u32[]{:S(2)}) collective-permute-start(bf16[128,512]{1,0:T(8,128)(2,1)S(1)} %select_bitcast_fusion.rest_0_), channel_id=1, source_target_pairs={{0,24},{4,28},{8,16},{12,20},{16,8},{20,12},{24,0},{28,4},{1,25},{... | collective-permute-start | bytes 393224 | tf_op jit(solution)/shard_map/ppermute | solution.py:28
  8.4 1.5 %collective-permute-start = (bf16[128,512]{1,0:T(8,128)(2,1)S(1)}, bf16[128,512]{1,0:T(8,128)(2,1)S(1)}, u32[]{:S(2)}, u32[]{:S(2)}) collective-permute-start(bf16[128,512]{1,0:T(8,128)(2,1)S(1)} %select_bitcast_fusion.rest_0_), channel_id=1, source_target_pairs={{0,4},{4,0},{8,12},{12,8},{16,20},{20,16},{24,28},{28,24},{1,5},{5... | collective-permute-start | bytes 393224 | tf_op jit(solution)/shard_map/ppermute | solution.py:28
  9.9 2.0 %collective-permute-start.2 = (bf16[128,512]{1,0:T(8,128)(2,1)S(1)}, bf16[128,512]{1,0:T(8,128)(2,1)S(1)}, u32[]{:S(2)}, u32[]{:S(2)}) collective-permute-start(bf16[128,512]{1,0:T(8,128)(2,1)S(1)} %select_bitcast_fusion.rest_0_), channel_id=1, source_target_pairs={{0,12},{4,8},{8,4},{12,0},{16,28},{20,24},{24,20},{28,16},{1,13},{... | collective-permute-start | bytes 393224 | tf_op jit(solution)/shard_map/ppermute | solution.py:28
  12.0 0.8 %collective-permute-done.3.rest_4_ = bf16[128,512]{1,0:T(8,128)(2,1)S(1)} collective-permute-done((bf16[128,512]{1,0:T(8,128)(2,1)S(1)}, bf16[128,512]{1,0:T(8,128)(2,1)S(1)}, u32[]{:S(2)}, u32[]{:S(2)}) %collective-permute-start.3) | collective-permute-done | bytes 131104 | tf_op jit(solution)/shard_map/ppermute | solution.py:28
  12.8 1.7 %collective-permute-start.4 = (bf16[128,512]{1,0:T(8,128)(2,1)S(1)}, bf16[128,512]{1,0:T(8,128)(2,1)S(1)}, u32[]{:S(2)}, u32[]{:S(2)}) collective-permute-start(bf16[128,512]{1,0:T(8,128)(2,1)S(1)} %collective-permute-done.3.rest_4_), channel_id=1, source_target_pairs={{0,4},{4,0},{8,12},{12,8},{16,20},{20,16},{24,28},{28,24},{1,5},{5... | collective-permute-start | bytes 393224 | tf_op jit(solution)/shard_map/ppermute | solution.py:28
  14.5 1.5 %collective-permute-start.5 = (bf16[128,512]{1,0:T(8,128)(2,1)S(1)}, bf16[128,512]{1,0:T(8,128)(2,1)S(1)}, u32[]{:S(2)}, u32[]{:S(2)}) collective-permute-start(bf16[128,512]{1,0:T(8,128)(2,1)S(1)} %collective-permute-done.3.rest_4_), channel_id=1, source_target_pairs={{0,8},{4,12},{8,0},{12,4},{16,24},{20,28},{24,16},{28,20},{1,9},{5... | collective-permute-start | bytes 393224 | tf_op jit(solution)/shard_map/ppermute | solution.py:28
  16.3 0.8 %compare_reduce_fusion = pred[8]{0:T(512)(128)(4,1)S(1)} fusion(s32[8]{0:T(128)} %param.14, s32[8]{0:T(128)S(1)} %stack.35), kind=kLoop, calls=%fused_computation.27 | loop fusion | flops 120 | bytes 72 | tf_op jit(solution)/shard_map/reduce_or | solution.py:55
  17.1 0.6 %convert_element_type.18.valid_ref = s32[8]{0:T(128)} convert(pred[8]{0:T(512)(128)(4,1)S(1)} %compare_reduce_fusion) | non-fusion elementwise | flops 8 | bytes 40 | tf_op jit(solution)/shard_map/convert_element_type | solution.py:181
  17.7 0.7 %dynamic_slice.19 = s32[4]{0:T(128)S(1)} dynamic-slice(s32[32]{0:T(128)} %param.17, s32[]{:T(128)S(6)} %select_n.37), dynamic_slice_sizes={4} | dynamic-slice | bytes 36 | tf_op jit(solution)/shard_map/dynamic_slice | solution.py:168
  18.4 1.3 %select_reduce_fusion.length_ref = s32[4]{0:T(128)} fusion(s32[32]{0:T(128)} %param.16, s32[4]{0:T(128)S(1)} %dynamic_slice.19), kind=kLoop, calls=%fused_computation.30 | loop fusion | flops 380 | bytes 160 | tf_op jit(solution)/shard_map/reduce_sum | solution.py:170
  19.9 2.0 %collective-permute-done.5.rest_6_ = bf16[128,512]{1,0:T(8,128)(2,1)S(1)} collective-permute-done((bf16[128,512]{1,0:T(8,128)(2,1)S(1)}, bf16[128,512]{1,0:T(8,128)(2,1)S(1)}, u32[]{:S(2)}, u32[]{:S(2)}) %collective-permute-start.5) | collective-permute-done | bytes 131104 | tf_op jit(solution)/shard_map/ppermute | solution.py:28
  21.9 2.3 %collective-permute-done.6.rest_7_ = bf16[128,512]{1,0:T(8,128)(2,1)S(1)} collective-permute-done((bf16[128,512]{1,0:T(8,128)(2,1)S(1)}, bf16[128,512]{1,0:T(8,128)(2,1)S(1)}, u32[]{:S(2)}, u32[]{:S(2)}) %collective-permute-start.6) | collective-permute-done | bytes 131104 | tf_op jit(solution)/shard_map/ppermute | solution.py:28
  24.3 0.6 %copy-done.11 = bf16[128,512]{1,0:T(8,128)(2,1)} copy-done((bf16[128,512]{1,0:T(8,128)(2,1)}, bf16[128,512]{1,0:T(8,128)(2,1)S(1)}, u32[]{:S(2)}) %copy-start.11) | copy-done | bytes 131096
  24.9 4.8 %shard_map.109 = bf16[2,128,512]{2,1,0:T(8,128)(2,1)} custom-call(s32[4]{0:T(128)} %select_reduce_fusion.length_ref, s32[8]{0:T(128)} %convert_element_type.18.valid_ref, bf16[4,128,1024]{2,1,0:T(8,128)(2,1)} %bitcast.35, f32[128,128]{1,0:T(8,128)} %constant.40.clone.cos_ref, f32[128,128]{1,0:T(8,128)} %constant.41.clone.sin_ref, ...), custom_call_target="tpu_custom_call" | custom-call | tf_op jit(solution)/shard_map/pallas_call | solution.py:132
  29.6 1.4 %collective-permute-start.8 = (bf16[256,512]{1,0:T(8,128)(2,1)}, bf16[256,512]{1,0:T(8,128)(2,1)S(1)}, u32[]{:S(2)}, u32[]{:S(2)}) collective-permute-start(bf16[256,512]{1,0:T(8,128)(2,1)} %bitcast.40), channel_id=1, source_target_pairs={{0,2},{1,3},{2,0},{3,1},{4,6},{5,7},{6,4},{7,5},{8,10},{9,11},{10,... | collective-permute-start | bytes 786440 | tf_op jit(solution)/shard_map/ppermute | solution.py:28
  31.1 4.8 %shard_map.110 = bf16[2,128,512]{2,1,0:T(8,128)(2,1)} custom-call(s32[4]{0:T(128)} %select_reduce_fusion.length_ref, s32[8]{0:T(128)} %convert_element_type.18.valid_ref, bf16[4,128,1024]{2,1,0:T(8,128)(2,1)} %bitcast.36, f32[128,128]{1,0:T(8,128)} %constant.40.clone.cos_ref, f32[128,128]{1,0:T(8,128)} %constant.41.clone.sin_ref, ...), custom_call_target="tpu_custom_call" | custom-call | tf_op jit(solution)/shard_map/pallas_call | solution.py:132
  35.9 0.6 %collective-permute-start.11 = (bf16[256,512]{1,0:T(8,128)(2,1)}, bf16[256,512]{1,0:T(8,128)(2,1)S(1)}, u32[]{:S(2)}, u32[]{:S(2)}) collective-permute-start(bf16[256,512]{1,0:T(8,128)(2,1)} %bitcast.37), channel_id=1, source_target_pairs={{0,2},{1,3},{2,0},{3,1},{4,6},{5,7},{6,4},{7,5},{8,10},{9,11},{10,... | collective-permute-start | bytes 786440 | tf_op jit(solution)/shard_map/ppermute | solution.py:28
  37.5 6.0 %collective-permute-done.11 = bf16[256,512]{1,0:T(8,128)(2,1)S(1)} collective-permute-done((bf16[256,512]{1,0:T(8,128)(2,1)}, bf16[256,512]{1,0:T(8,128)(2,1)S(1)}, u32[]{:S(2)}, u32[]{:S(2)}) %collective-permute-start.11) | collective-permute-done | bytes 262176 | tf_op jit(solution)/shard_map/ppermute | solution.py:28
  47.4 1.1 %collective-permute-start.14 = (f32[4,128]{1,0:T(4,128)S(1)}, f32[4,128]{1,0:T(4,128)S(1)}, u32[]{:S(2)}, u32[]{:S(2)}) collective-permute-start(f32[4,128]{1,0:T(4,128)S(1)} %bitcast.44), channel_id=1, source_target_pairs={{0,2},{1,3},{2,0},{3,1},{4,6},{5,7},{6,4},{7,5},{8,10},{9,11},{10,... | collective-permute-start | bytes 6152 | tf_op jit(solution)/shard_map/ppermute | solution.py:24
  48.5 1.0 %collective-permute-start.15 = (f32[4,128]{1,0:T(4,128)S(1)}, f32[4,128]{1,0:T(4,128)S(1)}, u32[]{:S(2)}, u32[]{:S(2)}) collective-permute-start(f32[4,128]{1,0:T(4,128)S(1)} %bitcast.45), channel_id=1, source_target_pairs={{0,3},{1,0},{2,1},{3,2},{4,7},{5,4},{6,5},{7,6},{8,11},{9,8},{10,9... | collective-permute-start | bytes 6152 | tf_op jit(solution)/shard_map/ppermute | solution.py:24
  49.9 1.1 %collective-permute-done.14 = f32[4,128]{1,0:T(4,128)S(1)} collective-permute-done((f32[4,128]{1,0:T(4,128)S(1)}, f32[4,128]{1,0:T(4,128)S(1)}, u32[]{:S(2)}, u32[]{:S(2)}) %collective-permute-start.14) | collective-permute-done | bytes 2080 | tf_op jit(solution)/shard_map/ppermute | solution.py:24
  51.0 1.1 %fusion.5 = bf16[4,128,576]{1,2,0:T(8,128)(2,1)} fusion(f32[72,4,8,128]{3,2,1,0:T(8,128)S(1)} %get-tuple-element.6, bf16[4,128,576]{1,2,0:T(8,128)(2,1)S(1)} %copy-done.4, f32[4,128]{1,0:T(4,128)S(1)} %fusion.19, f32[576]{0:T(1024)S(1)} %copy-done.13, f32[4,128]{1,0:T(4,128)S(1)} %add_rsqrt_fusion), kind=kLoop, calls=%fused_computation.10 | loop fusion | flops 1769472 | bytes 2365696 | tf_op jit(solution)/shard_map/convert_element_type | solution.py:192
  (57 shorter events, 5.9 us)
Async XLA Ops:
  0.0 43.4 %copy-start = (bf16[2048,576]{0,1:T(8,128)(2,1)S(1)}, bf16[2048,576]{0,1:T(8,128)(2,1)}, u32[]{:S(2)}) copy-start(bf16[2048,576]{0,1:T(8,128)(2,1)} %param.18) | copy-start | bytes 7077892
  3.2 21.0 %copy-start.1 = (bf16[128,512]{1,0:T(8,128)(2,1)}, bf16[128,512]{1,0:T(8,128)(2,1)S(1)}, u32[]{:S(2)}) copy-start(bf16[128,512]{1,0:T(8,128)(2,1)S(1)} %select_bitcast_fusion.rest_0_) | copy-start | bytes 393220
  3.2 9.5 %collective-permute-start.3 = (bf16[128,512]{1,0:T(8,128)(2,1)S(1)}, bf16[128,512]{1,0:T(8,128)(2,1)S(1)}, u32[]{:S(2)}, u32[]{:S(2)}) collective-permute-start(bf16[128,512]{1,0:T(8,128)(2,1)S(1)} %select_bitcast_fusion.rest_0_), channel_id=1, source_target_pairs={{0,24},{4,28},{8,16},{12,20},{16,8},{20,12},{24,0},{28,4},{1,25},{... | collective-permute-start | bytes 393224 | tf_op jit(solution)/shard_map/ppermute | solution.py:28
  8.4 7.5 %collective-permute-start = (bf16[128,512]{1,0:T(8,128)(2,1)S(1)}, bf16[128,512]{1,0:T(8,128)(2,1)S(1)}, u32[]{:S(2)}, u32[]{:S(2)}) collective-permute-start(bf16[128,512]{1,0:T(8,128)(2,1)S(1)} %select_bitcast_fusion.rest_0_), channel_id=1, source_target_pairs={{0,4},{4,0},{8,12},{12,8},{16,20},{20,16},{24,28},{28,24},{1,5},{5... | collective-permute-start | bytes 393224 | tf_op jit(solution)/shard_map/ppermute | solution.py:28
  9.9 9.9 %collective-permute-start.1 = (bf16[128,512]{1,0:T(8,128)(2,1)S(1)}, bf16[128,512]{1,0:T(8,128)(2,1)S(1)}, u32[]{:S(2)}, u32[]{:S(2)}) collective-permute-start(bf16[128,512]{1,0:T(8,128)(2,1)S(1)} %select_bitcast_fusion.rest_0_), channel_id=1, source_target_pairs={{0,8},{4,12},{8,0},{12,4},{16,24},{20,28},{24,16},{28,20},{1,9},{5... | collective-permute-start | bytes 393224 | tf_op jit(solution)/shard_map/ppermute | solution.py:28
  9.9 9.9 %collective-permute-start.2 = (bf16[128,512]{1,0:T(8,128)(2,1)S(1)}, bf16[128,512]{1,0:T(8,128)(2,1)S(1)}, u32[]{:S(2)}, u32[]{:S(2)}) collective-permute-start(bf16[128,512]{1,0:T(8,128)(2,1)S(1)} %select_bitcast_fusion.rest_0_), channel_id=1, source_target_pairs={{0,12},{4,8},{8,4},{12,0},{16,28},{20,24},{24,20},{28,16},{1,13},{... | collective-permute-start | bytes 393224 | tf_op jit(solution)/shard_map/ppermute | solution.py:28
  12.8 11.4 %copy-start.5 = (bf16[128,512]{1,0:T(8,128)(2,1)}, bf16[128,512]{1,0:T(8,128)(2,1)S(1)}, u32[]{:S(2)}) copy-start(bf16[128,512]{1,0:T(8,128)(2,1)S(1)} %collective-permute-done.3.rest_4_) | copy-start | bytes 393220
  12.8 7.1 %collective-permute-start.4 = (bf16[128,512]{1,0:T(8,128)(2,1)S(1)}, bf16[128,512]{1,0:T(8,128)(2,1)S(1)}, u32[]{:S(2)}, u32[]{:S(2)}) collective-permute-start(bf16[128,512]{1,0:T(8,128)(2,1)S(1)} %collective-permute-done.3.rest_4_), channel_id=1, source_target_pairs={{0,4},{4,0},{8,12},{12,8},{16,20},{20,16},{24,28},{28,24},{1,5},{5... | collective-permute-start | bytes 393224 | tf_op jit(solution)/shard_map/ppermute | solution.py:28
  14.5 7.4 %collective-permute-start.5 = (bf16[128,512]{1,0:T(8,128)(2,1)S(1)}, bf16[128,512]{1,0:T(8,128)(2,1)S(1)}, u32[]{:S(2)}, u32[]{:S(2)}) collective-permute-start(bf16[128,512]{1,0:T(8,128)(2,1)S(1)} %collective-permute-done.3.rest_4_), channel_id=1, source_target_pairs={{0,8},{4,12},{8,0},{12,4},{16,24},{20,28},{24,16},{28,20},{1,9},{5... | collective-permute-start | bytes 393224 | tf_op jit(solution)/shard_map/ppermute | solution.py:28
  15.9 8.3 %copy-start.6 = (bf16[128,512]{1,0:T(8,128)(2,1)}, bf16[128,512]{1,0:T(8,128)(2,1)S(1)}, u32[]{:S(2)}) copy-start(bf16[128,512]{1,0:T(8,128)(2,1)S(1)} %collective-permute-done.rest_1_) | copy-start | bytes 393220
  15.9 8.3 %collective-permute-start.6 = (bf16[128,512]{1,0:T(8,128)(2,1)S(1)}, bf16[128,512]{1,0:T(8,128)(2,1)S(1)}, u32[]{:S(2)}, u32[]{:S(2)}) collective-permute-start(bf16[128,512]{1,0:T(8,128)(2,1)S(1)} %collective-permute-done.3.rest_4_), channel_id=1, source_target_pairs={{0,12},{4,8},{8,4},{12,0},{16,28},{20,24},{24,20},{28,16},{1,13},{... | collective-permute-start | bytes 393224 | tf_op jit(solution)/shard_map/ppermute | solution.py:28
  19.8 4.5 %copy-start.8 = (bf16[128,512]{1,0:T(8,128)(2,1)}, bf16[128,512]{1,0:T(8,128)(2,1)S(1)}, u32[]{:S(2)}) copy-start(bf16[128,512]{1,0:T(8,128)(2,1)S(1)} %collective-permute-done.2.rest_3_) | copy-start | bytes 393220
  29.6 6.8 %copy-start.3 = (bf16[2,128,512]{2,1,0:T(8,128)(2,1)S(1)}, bf16[2,128,512]{2,1,0:T(8,128)(2,1)}, u32[]{:S(2)}) copy-start(bf16[2,128,512]{2,1,0:T(8,128)(2,1)} %shard_map.109) | copy-start | bytes 786436
  29.6 7.8 %collective-permute-start.8 = (bf16[256,512]{1,0:T(8,128)(2,1)}, bf16[256,512]{1,0:T(8,128)(2,1)S(1)}, u32[]{:S(2)}, u32[]{:S(2)}) collective-permute-start(bf16[256,512]{1,0:T(8,128)(2,1)} %bitcast.40), channel_id=1, source_target_pairs={{0,2},{1,3},{2,0},{3,1},{4,6},{5,7},{6,4},{7,5},{8,10},{9,11},{10,... | collective-permute-start | bytes 786440 | tf_op jit(solution)/shard_map/ppermute | solution.py:28
  35.9 7.5 %collective-permute-start.11 = (bf16[256,512]{1,0:T(8,128)(2,1)}, bf16[256,512]{1,0:T(8,128)(2,1)S(1)}, u32[]{:S(2)}, u32[]{:S(2)}) collective-permute-start(bf16[256,512]{1,0:T(8,128)(2,1)} %bitcast.37), channel_id=1, source_target_pairs={{0,2},{1,3},{2,0},{3,1},{4,6},{5,7},{6,4},{7,5},{8,10},{9,11},{10,... | collective-permute-start | bytes 786440 | tf_op jit(solution)/shard_map/ppermute | solution.py:28
  36.5 7.7 %collective-permute-start.7 = (bf16[256,512]{1,0:T(8,128)(2,1)S(1)}, bf16[256,512]{1,0:T(8,128)(2,1)S(1)}, u32[]{:S(2)}, u32[]{:S(2)}) collective-permute-start(bf16[256,512]{1,0:T(8,128)(2,1)S(1)} %bitcast.41), channel_id=1, source_target_pairs={{0,1},{1,0},{2,3},{3,2},{4,5},{5,4},{6,7},{7,6},{8,9},{9,8},{10,11... | collective-permute-start | bytes 786440 | tf_op jit(solution)/shard_map/ppermute | solution.py:28
  36.5 8.4 %collective-permute-start.10 = (bf16[256,512]{1,0:T(8,128)(2,1)}, bf16[256,512]{1,0:T(8,128)(2,1)S(1)}, u32[]{:S(2)}, u32[]{:S(2)}) collective-permute-start(bf16[256,512]{1,0:T(8,128)(2,1)} %bitcast.38), channel_id=1, source_target_pairs={{0,1},{1,0},{2,3},{3,2},{4,5},{5,4},{6,7},{7,6},{8,9},{9,8},{10,11... | collective-permute-start | bytes 786440 | tf_op jit(solution)/shard_map/ppermute | solution.py:28
  37.5 8.4 %collective-permute-start.9 = (bf16[256,512]{1,0:T(8,128)(2,1)S(1)}, bf16[256,512]{1,0:T(8,128)(2,1)S(1)}, u32[]{:S(2)}, u32[]{:S(2)}) collective-permute-start(bf16[256,512]{1,0:T(8,128)(2,1)S(1)} %collective-permute-done.8), channel_id=1, source_target_pairs={{0,1},{1,0},{2,3},{3,2},{4,5},{5,4},{6,7},{7,6},{8,9},{9,8},{10,11... | collective-permute-start | bytes 786440 | tf_op jit(solution)/shard_map/ppermute | solution.py:28
  43.4 2.8 %collective-permute-start.12 = (bf16[256,512]{1,0:T(8,128)(2,1)S(1)}, bf16[256,512]{1,0:T(8,128)(2,1)S(1)}, u32[]{:S(2)}, u32[]{:S(2)}) collective-permute-start(bf16[256,512]{1,0:T(8,128)(2,1)S(1)} %collective-permute-done.11), channel_id=1, source_target_pairs={{0,1},{1,0},{2,3},{3,2},{4,5},{5,4},{6,7},{7,6},{8,9},{9,8},{10,11... | collective-permute-start | bytes 786440 | tf_op jit(solution)/shard_map/ppermute | solution.py:28
  46.2 4.8 %copy-start.4 = (bf16[4,128,576]{1,2,0:T(8,128)(2,1)S(1)}, bf16[4,128,576]{1,2,0:T(8,128)(2,1)}, u32[]{:S(2)}) copy-start(bf16[4,128,576]{1,2,0:T(8,128)(2,1)} %param.11) | copy-start | bytes 1769476
  46.2 4.8 %copy-start.13 = (f32[576]{0:T(1024)S(1)}, f32[576]{0:T(1024)}, u32[]{:S(2)}) copy-start(f32[576]{0:T(1024)} %param.19) | copy-start | bytes 6916
  46.8 3.1 %collective-permute-start.13 = (f32[4,128]{1,0:T(4,128)S(1)}, f32[4,128]{1,0:T(4,128)S(1)}, u32[]{:S(2)}, u32[]{:S(2)}) collective-permute-start(f32[4,128]{1,0:T(4,128)S(1)} %bitcast.43), channel_id=1, source_target_pairs={{0,1},{1,2},{2,3},{3,0},{4,5},{5,6},{6,7},{7,4},{8,9},{9,10},{10,1... | collective-permute-start | bytes 6152 | tf_op jit(solution)/shard_map/ppermute | solution.py:24
  47.4 3.6 %collective-permute-start.14 = (f32[4,128]{1,0:T(4,128)S(1)}, f32[4,128]{1,0:T(4,128)S(1)}, u32[]{:S(2)}, u32[]{:S(2)}) collective-permute-start(f32[4,128]{1,0:T(4,128)S(1)} %bitcast.44), channel_id=1, source_target_pairs={{0,2},{1,3},{2,0},{3,1},{4,6},{5,7},{6,4},{7,5},{8,10},{9,11},{10,... | collective-permute-start | bytes 6152 | tf_op jit(solution)/shard_map/ppermute | solution.py:24
  48.5 2.5 %collective-permute-start.15 = (f32[4,128]{1,0:T(4,128)S(1)}, f32[4,128]{1,0:T(4,128)S(1)}, u32[]{:S(2)}, u32[]{:S(2)}) collective-permute-start(f32[4,128]{1,0:T(4,128)S(1)} %bitcast.45), channel_id=1, source_target_pairs={{0,3},{1,0},{2,1},{3,2},{4,7},{5,4},{6,5},{7,6},{8,11},{9,8},{10,9... | collective-permute-start | bytes 6152 | tf_op jit(solution)/shard_map/ppermute | solution.py:24
  (6 other events, 16.1 us)

commit v7 on v6

--- a/solution.py
+++ b/solution.py
@@ -175,21 +175,22 @@
     cosine, sine = static_tables(prefix_len + np.arange(slots), HD)
     group_width = per_group * HD
     chunk = max(1, requests // 2)
-    projected_parts = []
+    results = []
     for start in range(0, requests, chunk):
         attended = attend(qkv[:, :, 0], jnp.asarray(cosine), jnp.asarray(sine), blocks,
                           my_lengths, valid.astype(jnp.int32), start, chunk)
         own = attended.reshape(chunk * slots, per_group * HD)
-        projected_parts.append(project(own, w_out, tp_index, n_tp, group_width))
-    projected = jnp.concatenate(projected_parts, 0).reshape(requests, slots, local_width)
-
-    squares = jnp.sum(projected * projected, -1)
-    branch_total = squares
-    for shift in range(1, n_tp):
-        branch_total = branch_total + shifted(squares, "tp", n_tp, shift)
-    branch = projected * lax.rsqrt(branch_total / D + EPSILON)[..., None] * post_gain
-    source = hidden.astype(jnp.float32)
-    return ((source + branch) * live_mask[..., None]).astype(jnp.bfloat16)
+        projected = project(own, w_out, tp_index, n_tp, group_width)
+        projected = projected.reshape(chunk, slots, local_width)
+        squares = jnp.sum(projected * projected, -1)
+        branch_total = squares
+        for shift in range(1, n_tp):
+            branch_total = branch_total + shifted(squares, "tp", n_tp, shift)
+        branch = projected * lax.rsqrt(branch_total / D + EPSILON)[..., None] * post_gain
+        source = hidden[start:start + chunk].astype(jnp.float32)
+        live = live_mask[start:start + chunk, :, None]
+        results.append(((source + branch) * live).astype(jnp.bfloat16))
+    return jnp.concatenate(results, 0)
 
 
 def solution(mesh):

time: 52.7 us -> 55.2 us (1.047)
  starting transfers between devices: 17.3 us -> 19.8 us
  other arithmetic: 6.71 us -> 5.77 us
  local copies, waits for them, and re-layouts: 1.67 us -> 2.52 us
    ppermute x3 -> x6, starting transfers between devices: 2.6 us -> 5.05 us  [shifted(): lax.ppermute(value, axis, [(i, (i + shift) % size) for i in range(size)])]
    unnamed x28 -> x32, local copies, waits for them, and re-layouts: 0.86 us -> 1.71 us
    convert_element_type x1 -> x2, other arithmetic: 1.1 us -> 0.39 us  [on_device(): results.append(((source + branch) * live).astype(jnp.bfloat16))]
    ppermute x3 -> x6, waiting for transfers between devices: 1.48 us -> 1.29 us  [shifted(): lax.ppermute(value, axis, [(i, (i + shift) % size) for i in range(size)])]
  transfers between devices with their start and end apart: 16 -> 19, of which waited for: 8 -> 7; matrix products, arithmetic and copies ran while one was open for 12% -> 12% of each run, Pallas kernels for 9% -> 9%
where the time goes in v7:
time: 55.2 us; the launch traced here: 54.2 us
  starting transfers between devices  19.8 us (36%)
  waiting for transfers between devices  12.8 us (23%)
  Pallas kernels  9.72 us (18%)
  other arithmetic  5.77 us (10%)
  matrix products  2.8 us (5%)
  local copies, waits for them, and re-layouts  2.52 us (5%)
  between operations  0.89 us (2%)
    ppermute x13, starting transfers between devices, swapped(): return lax.ppermute(value, axis, [(i, i ^ mask) for i in range(size)])  14.7 us
    ppermute x13, waiting for transfers between devices, swapped(): return lax.ppermute(value, axis, [(i, i ^ mask) for i in range(size)])  11.5 us
    pallas_call x2, Pallas kernels, attend(): pl.pallas_call(functools.partial(attention_kernel, offset=offset), grid_s...  9.72 us
    ppermute x6, starting transfers between devices, shifted(): lax.ppermute(value, axis, [(i, (i + shift) % size) for i in range(size)])  5.05 us
    dot_general x8, matrix products, project(): term = jnp.dot(block, rows, preferred_element_type=jnp.float32)  2.8 us
    unnamed x32, local copies, waits for them, and re-layouts  1.71 us
    reduce_sum x1, other arithmetic, gather_prefix(): slot = jnp.sum(jnp.where(mine, page_slot, 0))  1.46 us
    reduce_sum x1, other arithmetic, on_device(): my_lengths = jnp.sum(jnp.where(matches, lengths[None, :], 0), 1)  1.42 us
  transfers between devices with their start and end apart: 19, of which 7 were waited for; matrix products, arithmetic and copies ran while one was open for 12% of the time, Pallas kernels for 9%

profile of v7, /device:TPU:0, one launch (start us, length us, event | category | flops | bytes accessed | tf_op | source)
XLA Modules:
  0.0 54.2 jit_solution(15839745886074005913)
XLA Ops:
  0.0 1.5 %fusion.31 = s32[]{:T(128)} fusion(s32[8]{0:T(128)} %param.15, s32[8]{0:T(128)} %param.14, s32[]{:T(128)} %axis_index.27), kind=kLoop, calls=%fused_computation.48 | loop fusion | flops 23 | bytes 72 | tf_op jit(solution)/shard_map/reduce_sum | solution.py:36
  2.1 1.0 %select_bitcast_fusion.rest_0_ = bf16[128,512]{1,0:T(8,128)(2,1)S(1)} fusion(bf16[2,128,1,512]{3,1,2,0:T(8,128)(2,1)} %param.13, pred[]{:T(512)S(6)} %eq.43), kind=kLoop, calls=%fused_computation.31 | loop fusion | flops 65536 | bytes 393217 | tf_op jit(solution)/shard_map/jit(_where)/select_n | solution.py:39
  3.1 5.1 %collective-permute-start.3 = (bf16[128,512]{1,0:T(8,128)(2,1)S(1)}, bf16[128,512]{1,0:T(8,128)(2,1)S(1)}, u32[]{:S(2)}, u32[]{:S(2)}) collective-permute-start(bf16[128,512]{1,0:T(8,128)(2,1)S(1)} %select_bitcast_fusion.rest_0_), channel_id=1, source_target_pairs={{0,24},{4,28},{8,16},{12,20},{16,8},{20,12},{24,0},{28,4},{1,25},{... | collective-permute-start | bytes 393224 | tf_op jit(solution)/shard_map/ppermute | solution.py:28
  8.3 1.5 %collective-permute-start = (bf16[128,512]{1,0:T(8,128)(2,1)S(1)}, bf16[128,512]{1,0:T(8,128)(2,1)S(1)}, u32[]{:S(2)}, u32[]{:S(2)}) collective-permute-start(bf16[128,512]{1,0:T(8,128)(2,1)S(1)} %select_bitcast_fusion.rest_0_), channel_id=1, source_target_pairs={{0,4},{4,0},{8,12},{12,8},{16,20},{20,16},{24,28},{28,24},{1,5},{5... | collective-permute-start | bytes 393224 | tf_op jit(solution)/shard_map/ppermute | solution.py:28
  9.8 2.0 %collective-permute-start.2 = (bf16[128,512]{1,0:T(8,128)(2,1)S(1)}, bf16[128,512]{1,0:T(8,128)(2,1)S(1)}, u32[]{:S(2)}, u32[]{:S(2)}) collective-permute-start(bf16[128,512]{1,0:T(8,128)(2,1)S(1)} %select_bitcast_fusion.rest_0_), channel_id=1, source_target_pairs={{0,12},{4,8},{8,4},{12,0},{16,28},{20,24},{24,20},{28,16},{1,13},{... | collective-permute-start | bytes 393224 | tf_op jit(solution)/shard_map/ppermute | solution.py:28
  11.8 0.8 %collective-permute-done.3.rest_4_ = bf16[128,512]{1,0:T(8,128)(2,1)S(1)} collective-permute-done((bf16[128,512]{1,0:T(8,128)(2,1)S(1)}, bf16[128,512]{1,0:T(8,128)(2,1)S(1)}, u32[]{:S(2)}, u32[]{:S(2)}) %collective-permute-start.3) | collective-permute-done | bytes 131104 | tf_op jit(solution)/shard_map/ppermute | solution.py:28
  12.7 1.7 %collective-permute-start.4 = (bf16[128,512]{1,0:T(8,128)(2,1)S(1)}, bf16[128,512]{1,0:T(8,128)(2,1)S(1)}, u32[]{:S(2)}, u32[]{:S(2)}) collective-permute-start(bf16[128,512]{1,0:T(8,128)(2,1)S(1)} %collective-permute-done.3.rest_4_), channel_id=1, source_target_pairs={{0,4},{4,0},{8,12},{12,8},{16,20},{20,16},{24,28},{28,24},{1,5},{5... | collective-permute-start | bytes 393224 | tf_op jit(solution)/shard_map/ppermute | solution.py:28
  14.3 1.5 %collective-permute-start.5 = (bf16[128,512]{1,0:T(8,128)(2,1)S(1)}, bf16[128,512]{1,0:T(8,128)(2,1)S(1)}, u32[]{:S(2)}, u32[]{:S(2)}) collective-permute-start(bf16[128,512]{1,0:T(8,128)(2,1)S(1)} %collective-permute-done.3.rest_4_), channel_id=1, source_target_pairs={{0,8},{4,12},{8,0},{12,4},{16,24},{20,28},{24,16},{28,20},{1,9},{5... | collective-permute-start | bytes 393224 | tf_op jit(solution)/shard_map/ppermute | solution.py:28
  16.1 0.8 %compare_reduce_fusion = pred[8]{0:T(512)(128)(4,1)S(1)} fusion(s32[8]{0:T(128)} %param.14, s32[8]{0:T(128)S(1)} %stack.35), kind=kLoop, calls=%fused_computation.32 | loop fusion | flops 120 | bytes 72 | tf_op jit(solution)/shard_map/reduce_or | solution.py:55
  17.6 0.7 %dynamic_slice.19 = s32[4]{0:T(128)S(1)} dynamic-slice(s32[32]{0:T(128)} %param.17, s32[]{:T(128)S(6)} %select_n.37), dynamic_slice_sizes={4} | dynamic-slice | bytes 36 | tf_op jit(solution)/shard_map/dynamic_slice | solution.py:168
  18.3 1.4 %select_reduce_fusion.length_ref = s32[4]{0:T(128)} fusion(s32[32]{0:T(128)} %param.16, s32[4]{0:T(128)S(1)} %dynamic_slice.19), kind=kLoop, calls=%fused_computation.34 | loop fusion | flops 380 | bytes 160 | tf_op jit(solution)/shard_map/reduce_sum | solution.py:170
  19.8 2.0 %collective-permute-done.5.rest_6_ = bf16[128,512]{1,0:T(8,128)(2,1)S(1)} collective-permute-done((bf16[128,512]{1,0:T(8,128)(2,1)S(1)}, bf16[128,512]{1,0:T(8,128)(2,1)S(1)}, u32[]{:S(2)}, u32[]{:S(2)}) %collective-permute-start.5) | collective-permute-done | bytes 131104 | tf_op jit(solution)/shard_map/ppermute | solution.py:28
  21.8 2.3 %collective-permute-done.6.rest_7_ = bf16[128,512]{1,0:T(8,128)(2,1)S(1)} collective-permute-done((bf16[128,512]{1,0:T(8,128)(2,1)S(1)}, bf16[128,512]{1,0:T(8,128)(2,1)S(1)}, u32[]{:S(2)}, u32[]{:S(2)}) %collective-permute-start.6) | collective-permute-done | bytes 131104 | tf_op jit(solution)/shard_map/ppermute | solution.py:28
  24.8 4.9 %shard_map.110 = bf16[2,128,512]{2,1,0:T(8,128)(2,1)} custom-call(s32[4]{0:T(128)} %select_reduce_fusion.length_ref, s32[8]{0:T(128)} %convert_element_type.20.valid_ref, bf16[4,128,1024]{2,1,0:T(8,128)(2,1)} %bitcast.51, f32[128,128]{1,0:T(8,128)} %constant.41.clone.cos_ref, f32[128,128]{1,0:T(8,128)} %constant.42.clone.sin_ref, ...), custom_call_target="tpu_custom_call" | custom-call | tf_op jit(solution)/shard_map/pallas_call | solution.py:132
  29.7 1.4 %collective-permute-start.14 = (bf16[256,512]{1,0:T(8,128)(2,1)}, bf16[256,512]{1,0:T(8,128)(2,1)S(1)}, u32[]{:S(2)}, u32[]{:S(2)}) collective-permute-start(bf16[256,512]{1,0:T(8,128)(2,1)} %bitcast.56), channel_id=1, source_target_pairs={{0,2},{1,3},{2,0},{3,1},{4,6},{5,7},{6,4},{7,5},{8,10},{9,11},{10,... | collective-permute-start | bytes 786440 | tf_op jit(solution)/shard_map/ppermute | solution.py:28
  31.1 4.8 %shard_map.109 = bf16[2,128,512]{2,1,0:T(8,128)(2,1)} custom-call(s32[4]{0:T(128)} %select_reduce_fusion.length_ref, s32[8]{0:T(128)} %convert_element_type.20.valid_ref, bf16[4,128,1024]{2,1,0:T(8,128)(2,1)} %bitcast.52, f32[128,128]{1,0:T(8,128)} %constant.41.clone.cos_ref, f32[128,128]{1,0:T(8,128)} %constant.42.clone.sin_ref, ...), custom_call_target="tpu_custom_call" | custom-call | tf_op jit(solution)/shard_map/pallas_call | solution.py:132
  37.5 5.9 %collective-permute-done.8 = bf16[256,512]{1,0:T(8,128)(2,1)S(1)} collective-permute-done((bf16[256,512]{1,0:T(8,128)(2,1)}, bf16[256,512]{1,0:T(8,128)(2,1)S(1)}, u32[]{:S(2)}, u32[]{:S(2)}) %collective-permute-start.8) | collective-permute-done | bytes 262176 | tf_op jit(solution)/shard_map/ppermute | solution.py:28
  46.8 1.1 %collective-permute-start.17 = (f32[2,128]{1,0:T(2,128)S(1)}, f32[2,128]{1,0:T(2,128)S(1)}, u32[]{:S(2)}, u32[]{:S(2)}) collective-permute-start(f32[2,128]{1,0:T(2,128)S(1)} %bitcast.60), channel_id=1, source_target_pairs={{0,2},{1,3},{2,0},{3,1},{4,6},{5,7},{6,4},{7,5},{8,10},{9,11},{10,... | collective-permute-start | bytes 3080 | tf_op jit(solution)/shard_map/ppermute | solution.py:24
  47.9 1.0 %collective-permute-start.18 = (f32[2,128]{1,0:T(2,128)S(1)}, f32[2,128]{1,0:T(2,128)S(1)}, u32[]{:S(2)}, u32[]{:S(2)}) collective-permute-start(f32[2,128]{1,0:T(2,128)S(1)} %bitcast.61), channel_id=1, source_target_pairs={{0,3},{1,0},{2,1},{3,2},{4,7},{5,4},{6,5},{7,6},{8,11},{9,8},{10,9... | collective-permute-start | bytes 3080 | tf_op jit(solution)/shard_map/ppermute | solution.py:24
  49.3 1.0 %collective-permute-start.11 = (f32[2,128]{1,0:T(2,128)S(1)}, f32[2,128]{1,0:T(2,128)S(1)}, u32[]{:S(2)}, u32[]{:S(2)}) collective-permute-start(f32[2,128]{1,0:T(2,128)S(1)} %bitcast.63), channel_id=1, source_target_pairs={{0,2},{1,3},{2,0},{3,1},{4,6},{5,7},{6,4},{7,5},{8,10},{9,11},{10,... | collective-permute-start | bytes 3080 | tf_op jit(solution)/shard_map/ppermute | solution.py:24
  50.3 1.4 %collective-permute-start.12 = (f32[2,128]{1,0:T(2,128)S(1)}, f32[2,128]{1,0:T(2,128)S(1)}, u32[]{:S(2)}, u32[]{:S(2)}) collective-permute-start(f32[2,128]{1,0:T(2,128)S(1)} %bitcast.64), channel_id=1, source_target_pairs={{0,3},{1,0},{2,1},{3,2},{4,7},{5,4},{6,5},{7,6},{8,11},{9,8},{10,9... | collective-permute-start | bytes 3080 | tf_op jit(solution)/shard_map/ppermute | solution.py:24
  51.7 0.6 %collective-permute-done.10 = f32[2,128]{1,0:T(2,128)S(1)} collective-permute-done((f32[2,128]{1,0:T(2,128)S(1)}, f32[2,128]{1,0:T(2,128)S(1)}, u32[]{:S(2)}, u32[]{:S(2)}) %collective-permute-start.10) | collective-permute-done | bytes 1056 | tf_op jit(solution)/shard_map/ppermute | solution.py:24
  52.3 0.7 %collective-permute-done.11 = f32[2,128]{1,0:T(2,128)S(1)} collective-permute-done((f32[2,128]{1,0:T(2,128)S(1)}, f32[2,128]{1,0:T(2,128)S(1)}, u32[]{:S(2)}, u32[]{:S(2)}) %collective-permute-start.11) | collective-permute-done | bytes 1056 | tf_op jit(solution)/shard_map/ppermute | solution.py:24
  53.4 0.8 %copy-done.15 = bf16[4,128,576]{1,2,0:T(8,128)(2,1)} copy-done((bf16[4,128,576]{1,2,0:T(8,128)(2,1)}, bf16[4,128,576]{1,2,0:T(8,128)(2,1)S(1)}, u32[]{:S(2)}) %copy-start.15) | copy-done | bytes 589848
  (69 shorter events, 7.4 us)
Async XLA Ops:
  0.0 43.5 %copy-start = (bf16[2048,576]{0,1:T(8,128)(2,1)S(1)}, bf16[2048,576]{0,1:T(8,128)(2,1)}, u32[]{:S(2)}) copy-start(bf16[2048,576]{0,1:T(8,128)(2,1)} %param.18) | copy-start | bytes 7077892
  3.1 21.0 %copy-start.1 = (bf16[128,512]{1,0:T(8,128)(2,1)}, bf16[128,512]{1,0:T(8,128)(2,1)S(1)}, u32[]{:S(2)}) copy-start(bf16[128,512]{1,0:T(8,128)(2,1)S(1)} %select_bitcast_fusion.rest_0_) | copy-start | bytes 393220
  3.1 9.5 %collective-permute-start.3 = (bf16[128,512]{1,0:T(8,128)(2,1)S(1)}, bf16[128,512]{1,0:T(8,128)(2,1)S(1)}, u32[]{:S(2)}, u32[]{:S(2)}) collective-permute-start(bf16[128,512]{1,0:T(8,128)(2,1)S(1)} %select_bitcast_fusion.rest_0_), channel_id=1, source_target_pairs={{0,24},{4,28},{8,16},{12,20},{16,8},{20,12},{24,0},{28,4},{1,25},{... | collective-permute-start | bytes 393224 | tf_op jit(solution)/shard_map/ppermute | solution.py:28
  8.3 7.5 %collective-permute-start = (bf16[128,512]{1,0:T(8,128)(2,1)S(1)}, bf16[128,512]{1,0:T(8,128)(2,1)S(1)}, u32[]{:S(2)}, u32[]{:S(2)}) collective-permute-start(bf16[128,512]{1,0:T(8,128)(2,1)S(1)} %select_bitcast_fusion.rest_0_), channel_id=1, source_target_pairs={{0,4},{4,0},{8,12},{12,8},{16,20},{20,16},{24,28},{28,24},{1,5},{5... | collective-permute-start | bytes 393224 | tf_op jit(solution)/shard_map/ppermute | solution.py:28
  9.8 10.0 %collective-permute-start.1 = (bf16[128,512]{1,0:T(8,128)(2,1)S(1)}, bf16[128,512]{1,0:T(8,128)(2,1)S(1)}, u32[]{:S(2)}, u32[]{:S(2)}) collective-permute-start(bf16[128,512]{1,0:T(8,128)(2,1)S(1)} %select_bitcast_fusion.rest_0_), channel_id=1, source_target_pairs={{0,8},{4,12},{8,0},{12,4},{16,24},{20,28},{24,16},{28,20},{1,9},{5... | collective-permute-start | bytes 393224 | tf_op jit(solution)/shard_map/ppermute | solution.py:28
  9.8 10.0 %collective-permute-start.2 = (bf16[128,512]{1,0:T(8,128)(2,1)S(1)}, bf16[128,512]{1,0:T(8,128)(2,1)S(1)}, u32[]{:S(2)}, u32[]{:S(2)}) collective-permute-start(bf16[128,512]{1,0:T(8,128)(2,1)S(1)} %select_bitcast_fusion.rest_0_), channel_id=1, source_target_pairs={{0,12},{4,8},{8,4},{12,0},{16,28},{20,24},{24,20},{28,16},{1,13},{... | collective-permute-start | bytes 393224 | tf_op jit(solution)/shard_map/ppermute | solution.py:28
  12.7 11.4 %copy-start.5 = (bf16[128,512]{1,0:T(8,128)(2,1)}, bf16[128,512]{1,0:T(8,128)(2,1)S(1)}, u32[]{:S(2)}) copy-start(bf16[128,512]{1,0:T(8,128)(2,1)S(1)} %collective-permute-done.3.rest_4_) | copy-start | bytes 393220
  12.7 7.1 %collective-permute-start.4 = (bf16[128,512]{1,0:T(8,128)(2,1)S(1)}, bf16[128,512]{1,0:T(8,128)(2,1)S(1)}, u32[]{:S(2)}, u32[]{:S(2)}) collective-permute-start(bf16[128,512]{1,0:T(8,128)(2,1)S(1)} %collective-permute-done.3.rest_4_), channel_id=1, source_target_pairs={{0,4},{4,0},{8,12},{12,8},{16,20},{20,16},{24,28},{28,24},{1,5},{5... | collective-permute-start | bytes 393224 | tf_op jit(solution)/shard_map/ppermute | solution.py:28
  14.3 7.4 %collective-permute-start.5 = (bf16[128,512]{1,0:T(8,128)(2,1)S(1)}, bf16[128,512]{1,0:T(8,128)(2,1)S(1)}, u32[]{:S(2)}, u32[]{:S(2)}) collective-permute-start(bf16[128,512]{1,0:T(8,128)(2,1)S(1)} %collective-permute-done.3.rest_4_), channel_id=1, source_target_pairs={{0,8},{4,12},{8,0},{12,4},{16,24},{20,28},{24,16},{28,20},{1,9},{5... | collective-permute-start | bytes 393224 | tf_op jit(solution)/shard_map/ppermute | solution.py:28
  15.8 8.3 %copy-start.6 = (bf16[128,512]{1,0:T(8,128)(2,1)}, bf16[128,512]{1,0:T(8,128)(2,1)S(1)}, u32[]{:S(2)}) copy-start(bf16[128,512]{1,0:T(8,128)(2,1)S(1)} %collective-permute-done.rest_1_) | copy-start | bytes 393220
  15.8 8.3 %collective-permute-start.6 = (bf16[128,512]{1,0:T(8,128)(2,1)S(1)}, bf16[128,512]{1,0:T(8,128)(2,1)S(1)}, u32[]{:S(2)}, u32[]{:S(2)}) collective-permute-start(bf16[128,512]{1,0:T(8,128)(2,1)S(1)} %collective-permute-done.3.rest_4_), channel_id=1, source_target_pairs={{0,12},{4,8},{8,4},{12,0},{16,28},{20,24},{24,20},{28,16},{1,13},{... | collective-permute-start | bytes 393224 | tf_op jit(solution)/shard_map/ppermute | solution.py:28
  24.8 11.8 %copy-start.12 = (s32[4]{0:T(128)S(1)}, s32[4]{0:T(128)}, u32[]{:S(2)}) copy-start(s32[4]{0:T(128)} %select_reduce_fusion.length_ref) | copy-start | bytes 52
  29.7 7.8 %collective-permute-start.14 = (bf16[256,512]{1,0:T(8,128)(2,1)}, bf16[256,512]{1,0:T(8,128)(2,1)S(1)}, u32[]{:S(2)}, u32[]{:S(2)}) collective-permute-start(bf16[256,512]{1,0:T(8,128)(2,1)} %bitcast.56), channel_id=1, source_target_pairs={{0,2},{1,3},{2,0},{3,1},{4,6},{5,7},{6,4},{7,5},{8,10},{9,11},{10,... | collective-permute-start | bytes 786440 | tf_op jit(solution)/shard_map/ppermute | solution.py:28
  35.9 7.5 %collective-permute-start.8 = (bf16[256,512]{1,0:T(8,128)(2,1)}, bf16[256,512]{1,0:T(8,128)(2,1)S(1)}, u32[]{:S(2)}, u32[]{:S(2)}) collective-permute-start(bf16[256,512]{1,0:T(8,128)(2,1)} %bitcast.53), channel_id=1, source_target_pairs={{0,2},{1,3},{2,0},{3,1},{4,6},{5,7},{6,4},{7,5},{8,10},{9,11},{10,... | collective-permute-start | bytes 786440 | tf_op jit(solution)/shard_map/ppermute | solution.py:28
  36.6 7.6 %collective-permute-start.13 = (bf16[256,512]{1,0:T(8,128)(2,1)S(1)}, bf16[256,512]{1,0:T(8,128)(2,1)S(1)}, u32[]{:S(2)}, u32[]{:S(2)}) collective-permute-start(bf16[256,512]{1,0:T(8,128)(2,1)S(1)} %bitcast.57), channel_id=1, source_target_pairs={{0,1},{1,0},{2,3},{3,2},{4,5},{5,4},{6,7},{7,6},{8,9},{9,8},{10,11... | collective-permute-start | bytes 786440 | tf_op jit(solution)/shard_map/ppermute | solution.py:28
  36.7 8.2 %collective-permute-start.7 = (bf16[256,512]{1,0:T(8,128)(2,1)}, bf16[256,512]{1,0:T(8,128)(2,1)S(1)}, u32[]{:S(2)}, u32[]{:S(2)}) collective-permute-start(bf16[256,512]{1,0:T(8,128)(2,1)} %bitcast.54), channel_id=1, source_target_pairs={{0,1},{1,0},{2,3},{3,2},{4,5},{5,4},{6,7},{7,6},{8,9},{9,8},{10,11... | collective-permute-start | bytes 786440 | tf_op jit(solution)/shard_map/ppermute | solution.py:28
  37.5 8.3 %collective-permute-start.15 = (bf16[256,512]{1,0:T(8,128)(2,1)S(1)}, bf16[256,512]{1,0:T(8,128)(2,1)S(1)}, u32[]{:S(2)}, u32[]{:S(2)}) collective-permute-start(bf16[256,512]{1,0:T(8,128)(2,1)S(1)} %collective-permute-done.14), channel_id=1, source_target_pairs={{0,1},{1,0},{2,3},{3,2},{4,5},{5,4},{6,7},{7,6},{8,9},{9,8},{10,11... | collective-permute-start | bytes 786440 | tf_op jit(solution)/shard_map/ppermute | solution.py:28
  43.5 5.4 %collective-permute-start.9 = (bf16[256,512]{1,0:T(8,128)(2,1)S(1)}, bf16[256,512]{1,0:T(8,128)(2,1)S(1)}, u32[]{:S(2)}, u32[]{:S(2)}) collective-permute-start(bf16[256,512]{1,0:T(8,128)(2,1)S(1)} %collective-permute-done.8), channel_id=1, source_target_pairs={{0,1},{1,0},{2,3},{3,2},{4,5},{5,4},{6,7},{7,6},{8,9},{9,8},{10,11... | collective-permute-start | bytes 786440 | tf_op jit(solution)/shard_map/ppermute | solution.py:28
  46.3 4.0 %collective-permute-start.16 = (f32[2,128]{1,0:T(2,128)S(1)}, f32[2,128]{1,0:T(2,128)S(1)}, u32[]{:S(2)}, u32[]{:S(2)}) collective-permute-start(f32[2,128]{1,0:T(2,128)S(1)} %bitcast.59), channel_id=1, source_target_pairs={{0,1},{1,2},{2,3},{3,0},{4,5},{5,6},{6,7},{7,4},{8,9},{9,10},{10,1... | collective-permute-start | bytes 3080 | tf_op jit(solution)/shard_map/ppermute | solution.py:24
  46.8 4.9 %collective-permute-start.17 = (f32[2,128]{1,0:T(2,128)S(1)}, f32[2,128]{1,0:T(2,128)S(1)}, u32[]{:S(2)}, u32[]{:S(2)}) collective-permute-start(f32[2,128]{1,0:T(2,128)S(1)} %bitcast.60), channel_id=1, source_target_pairs={{0,2},{1,3},{2,0},{3,1},{4,6},{5,7},{6,4},{7,5},{8,10},{9,11},{10,... | collective-permute-start | bytes 3080 | tf_op jit(solution)/shard_map/ppermute | solution.py:24
  47.9 3.8 %collective-permute-start.18 = (f32[2,128]{1,0:T(2,128)S(1)}, f32[2,128]{1,0:T(2,128)S(1)}, u32[]{:S(2)}, u32[]{:S(2)}) collective-permute-start(f32[2,128]{1,0:T(2,128)S(1)} %bitcast.61), channel_id=1, source_target_pairs={{0,3},{1,0},{2,1},{3,2},{4,7},{5,4},{6,5},{7,6},{8,11},{9,8},{10,9... | collective-permute-start | bytes 3080 | tf_op jit(solution)/shard_map/ppermute | solution.py:24
  49.3 3.1 %collective-permute-start.10 = (f32[2,128]{1,0:T(2,128)S(1)}, f32[2,128]{1,0:T(2,128)S(1)}, u32[]{:S(2)}, u32[]{:S(2)}) collective-permute-start(f32[2,128]{1,0:T(2,128)S(1)} %bitcast.62), channel_id=1, source_target_pairs={{0,1},{1,2},{2,3},{3,0},{4,5},{5,6},{6,7},{7,4},{8,9},{9,10},{10,1... | collective-permute-start | bytes 3080 | tf_op jit(solution)/shard_map/ppermute | solution.py:24
  49.3 3.6 %collective-permute-start.11 = (f32[2,128]{1,0:T(2,128)S(1)}, f32[2,128]{1,0:T(2,128)S(1)}, u32[]{:S(2)}, u32[]{:S(2)}) collective-permute-start(f32[2,128]{1,0:T(2,128)S(1)} %bitcast.63), channel_id=1, source_target_pairs={{0,2},{1,3},{2,0},{3,1},{4,6},{5,7},{6,4},{7,5},{8,10},{9,11},{10,... | collective-permute-start | bytes 3080 | tf_op jit(solution)/shard_map/ppermute | solution.py:24
  50.3 2.7 %collective-permute-start.12 = (f32[2,128]{1,0:T(2,128)S(1)}, f32[2,128]{1,0:T(2,128)S(1)}, u32[]{:S(2)}, u32[]{:S(2)}) collective-permute-start(f32[2,128]{1,0:T(2,128)S(1)} %bitcast.64), channel_id=1, source_target_pairs={{0,3},{1,0},{2,1},{3,2},{4,7},{5,4},{6,5},{7,6},{8,11},{9,8},{10,9... | collective-permute-start | bytes 3080 | tf_op jit(solution)/shard_map/ppermute | solution.py:24
  (11 other events, 46.3 us)

commit v8 on v6

--- a/solution.py
+++ b/solution.py
@@ -89,29 +89,30 @@
          for q in range(per_group)], 0)
     fresh_keys = rope(values_in[:, per_group * HD:(per_group + 1) * HD]).astype(jnp.bfloat16)
     fresh_values = values_in[:, (per_group + 1) * HD:].astype(jnp.bfloat16)
-    pages = [ref[...] for ref in page_refs]
-    keys = jnp.concatenate([page[:, :HD] for page in pages] + [fresh_keys], 0)
-    values = jnp.concatenate([page[:, HD:] for page in pages] + [fresh_values], 0)
-    prefix_len = len(pages) * pages[0].shape[0]
-    key_count = keys.shape[0]
     rows = queries.shape[0]
-
-    scores = lax.dot_general(queries, keys, (((1,), (1,)), ((), ())),
-                             preferred_element_type=jnp.float32)
-    page_column = lax.broadcasted_iota(jnp.int32, (1, key_count), 1) // pages[0].shape[0]
-    page_flag = jnp.zeros((1, key_count), jnp.int32)
-    for index in range(len(pages)):
-        page_flag = page_flag + jnp.where(page_column == index, valid_ref[index], 0)
-    page_flag = page_flag.astype(jnp.float32)
-    column = lax.broadcasted_iota(jnp.int32, (rows, key_count), 1)
-    slot = lax.broadcasted_iota(jnp.int32, (rows, key_count), 0) % slots
-    suffix_pos = column - prefix_len
-    suffix_ok = (suffix_pos >= 0) & (suffix_pos <= slot) & (suffix_pos < length_ref[request])
-    exps = capped_exp(scores)
-    raw = jnp.where(suffix_ok, exps, jnp.where(column < prefix_len, exps * page_flag, 0.0))
-    totals = jnp.sum(raw, -1, keepdims=True)
-    weights = (raw / totals).astype(jnp.bfloat16)
-    attended = jnp.dot(weights, values, preferred_element_type=jnp.float32).astype(jnp.bfloat16)
+    contract = (((1,), (1,)), ((), ()))
+
+    page_weights = []
+    totals = jnp.zeros((rows, 1), jnp.float32)
+    for index, ref in enumerate(page_refs):
+        scores = lax.dot_general(queries, ref[:, :HD], contract, preferred_element_type=jnp.float32)
+        flag = jnp.where(valid_ref[index] != 0, 1.0, 0.0).astype(jnp.float32)
+        raw = capped_exp(scores) * flag
+        totals = totals + jnp.sum(raw, -1, keepdims=True)
+        page_weights.append(raw)
+    scores = lax.dot_general(queries, fresh_keys, contract, preferred_element_type=jnp.float32)
+    column = lax.broadcasted_iota(jnp.int32, scores.shape, 1)
+    slot = lax.broadcasted_iota(jnp.int32, scores.shape, 0) % slots
+    allowed = (column <= slot) & (column < length_ref[request])
+    fresh_raw = jnp.where(allowed, capped_exp(scores), 0.0)
+    totals = totals + jnp.sum(fresh_raw, -1, keepdims=True)
+    inverse = 1.0 / totals
+    attended = jnp.dot((fresh_raw * inverse).astype(jnp.bfloat16), fresh_values,
+                       preferred_element_type=jnp.float32)
+    for raw, ref in zip(page_weights, page_refs):
+        attended = attended + jnp.dot((raw * inverse).astype(jnp.bfloat16), ref[:, HD:],
+                                      preferred_element_type=jnp.float32)
+    attended = attended.astype(jnp.bfloat16)
     out_ref[0] = jnp.concatenate(
         [attended[q * slots:(q + 1) * slots] for q in range(per_group)], 1)
 

time: 52.7 us -> 54.7 us (1.038)
  Pallas kernels: 9.58 us -> 11.6 us
  starting transfers between devices: 17.3 us -> 16.7 us
    pallas_call x2, Pallas kernels: 9.58 us -> 11.6 us  [attend(): pl.pallas_call(functools.partial(attention_kernel, offset=offset), grid_s...]
  transfers between devices with their start and end apart: 16 -> 16, of which waited for: 8 -> 7; matrix products, arithmetic and copies ran while one was open for 12% -> 11% of each run, Pallas kernels for 9% -> 11%
where the time goes in v8:
time: 54.7 us; the launch traced here: 54.1 us
  starting transfers between devices  16.7 us (31%)
  waiting for transfers between devices  13.7 us (25%)
  Pallas kernels  11.6 us (21%)
  other arithmetic  6.71 us (12%)
  matrix products  2.78 us (5%)
  local copies, waits for them, and re-layouts  1.69 us (3%)
  between operations  0.92 us (2%)
    ppermute x13, starting transfers between devices, swapped(): return lax.ppermute(value, axis, [(i, i ^ mask) for i in range(size)])  14.7 us
    ppermute x13, waiting for transfers between devices, swapped(): return lax.ppermute(value, axis, [(i, i ^ mask) for i in range(size)])  11.7 us
    pallas_call x2, Pallas kernels, attend(): pl.pallas_call(functools.partial(attention_kernel, offset=offset), grid_s...  11.6 us
    dot_general x8, matrix products, project(): term = jnp.dot(block, rows, preferred_element_type=jnp.float32)  2.78 us
    ppermute x3, starting transfers between devices, shifted(): lax.ppermute(value, axis, [(i, (i + shift) % size) for i in range(size)])  2.08 us
    ppermute x3, waiting for transfers between devices, shifted(): lax.ppermute(value, axis, [(i, (i + shift) % size) for i in range(size)])  1.96 us
    reduce_sum x1, other arithmetic, gather_prefix(): slot = jnp.sum(jnp.where(mine, page_slot, 0))  1.54 us
    reduce_sum x1, other arithmetic, on_device(): my_lengths = jnp.sum(jnp.where(matches, lengths[None, :], 0), 1)  1.32 us
  transfers between devices with their start and end apart: 16, of which 7 were waited for; matrix products, arithmetic and copies ran while one was open for 11% of the time, Pallas kernels for 11%

profile of v8, /device:TPU:0, one launch (start us, length us, event | category | flops | bytes accessed | tf_op | source)
XLA Modules:
  0.0 54.1 jit_solution(10956478250286303837)
XLA Ops:
  0.0 1.5 %fusion.28 = s32[]{:T(128)} fusion(s32[8]{0:T(128)} %param.15, s32[8]{0:T(128)} %param.14, s32[]{:T(128)} %axis_index.27), kind=kLoop, calls=%fused_computation.42 | loop fusion | flops 23 | bytes 72 | tf_op jit(solution)/shard_map/reduce_sum | solution.py:36
  2.2 1.0 %select_bitcast_fusion.rest_0_ = bf16[128,512]{1,0:T(8,128)(2,1)S(1)} fusion(bf16[2,128,1,512]{3,1,2,0:T(8,128)(2,1)} %param.13, pred[]{:T(512)S(6)} %eq.43), kind=kLoop, calls=%fused_computation.26 | loop fusion | flops 65536 | bytes 393217 | tf_op jit(solution)/shard_map/jit(_where)/select_n | solution.py:39
  3.2 5.1 %collective-permute-start.3 = (bf16[128,512]{1,0:T(8,128)(2,1)S(1)}, bf16[128,512]{1,0:T(8,128)(2,1)S(1)}, u32[]{:S(2)}, u32[]{:S(2)}) collective-permute-start(bf16[128,512]{1,0:T(8,128)(2,1)S(1)} %select_bitcast_fusion.rest_0_), channel_id=1, source_target_pairs={{0,24},{4,28},{8,16},{12,20},{16,8},{20,12},{24,0},{28,4},{1,25},{... | collective-permute-start | bytes 393224 | tf_op jit(solution)/shard_map/ppermute | solution.py:28
  8.4 1.5 %collective-permute-start = (bf16[128,512]{1,0:T(8,128)(2,1)S(1)}, bf16[128,512]{1,0:T(8,128)(2,1)S(1)}, u32[]{:S(2)}, u32[]{:S(2)}) collective-permute-start(bf16[128,512]{1,0:T(8,128)(2,1)S(1)} %select_bitcast_fusion.rest_0_), channel_id=1, source_target_pairs={{0,4},{4,0},{8,12},{12,8},{16,20},{20,16},{24,28},{28,24},{1,5},{5... | collective-permute-start | bytes 393224 | tf_op jit(solution)/shard_map/ppermute | solution.py:28
  9.9 2.0 %collective-permute-start.2 = (bf16[128,512]{1,0:T(8,128)(2,1)S(1)}, bf16[128,512]{1,0:T(8,128)(2,1)S(1)}, u32[]{:S(2)}, u32[]{:S(2)}) collective-permute-start(bf16[128,512]{1,0:T(8,128)(2,1)S(1)} %select_bitcast_fusion.rest_0_), channel_id=1, source_target_pairs={{0,12},{4,8},{8,4},{12,0},{16,28},{20,24},{24,20},{28,16},{1,13},{... | collective-permute-start | bytes 393224 | tf_op jit(solution)/shard_map/ppermute | solution.py:28
  12.0 0.8 %collective-permute-done.3.rest_4_ = bf16[128,512]{1,0:T(8,128)(2,1)S(1)} collective-permute-done((bf16[128,512]{1,0:T(8,128)(2,1)S(1)}, bf16[128,512]{1,0:T(8,128)(2,1)S(1)}, u32[]{:S(2)}, u32[]{:S(2)}) %collective-permute-start.3) | collective-permute-done | bytes 131104 | tf_op jit(solution)/shard_map/ppermute | solution.py:28
  12.8 1.7 %collective-permute-start.4 = (bf16[128,512]{1,0:T(8,128)(2,1)S(1)}, bf16[128,512]{1,0:T(8,128)(2,1)S(1)}, u32[]{:S(2)}, u32[]{:S(2)}) collective-permute-start(bf16[128,512]{1,0:T(8,128)(2,1)S(1)} %collective-permute-done.3.rest_4_), channel_id=1, source_target_pairs={{0,4},{4,0},{8,12},{12,8},{16,20},{20,16},{24,28},{28,24},{1,5},{5... | collective-permute-start | bytes 393224 | tf_op jit(solution)/shard_map/ppermute | solution.py:28
  14.5 1.5 %collective-permute-start.5 = (bf16[128,512]{1,0:T(8,128)(2,1)S(1)}, bf16[128,512]{1,0:T(8,128)(2,1)S(1)}, u32[]{:S(2)}, u32[]{:S(2)}) collective-permute-start(bf16[128,512]{1,0:T(8,128)(2,1)S(1)} %collective-permute-done.3.rest_4_), channel_id=1, source_target_pairs={{0,8},{4,12},{8,0},{12,4},{16,24},{20,28},{24,16},{28,20},{1,9},{5... | collective-permute-start | bytes 393224 | tf_op jit(solution)/shard_map/ppermute | solution.py:28
  16.3 0.8 %compare_reduce_fusion = pred[8]{0:T(512)(128)(4,1)S(1)} fusion(s32[8]{0:T(128)} %param.14, s32[8]{0:T(128)S(1)} %stack.35), kind=kLoop, calls=%fused_computation.27 | loop fusion | flops 120 | bytes 72 | tf_op jit(solution)/shard_map/reduce_or | solution.py:55
  17.1 0.6 %convert_element_type.18.valid_ref = s32[8]{0:T(128)} convert(pred[8]{0:T(512)(128)(4,1)S(1)} %compare_reduce_fusion) | non-fusion elementwise | flops 8 | bytes 40 | tf_op jit(solution)/shard_map/convert_element_type | solution.py:182
  17.7 0.7 %dynamic_slice.19 = s32[4]{0:T(128)S(1)} dynamic-slice(s32[32]{0:T(128)} %param.17, s32[]{:T(128)S(6)} %select_n.37), dynamic_slice_sizes={4} | dynamic-slice | bytes 36 | tf_op jit(solution)/shard_map/dynamic_slice | solution.py:169
  18.4 1.3 %select_reduce_fusion.length_ref = s32[4]{0:T(128)} fusion(s32[32]{0:T(128)} %param.16, s32[4]{0:T(128)S(1)} %dynamic_slice.19), kind=kLoop, calls=%fused_computation.30 | loop fusion | flops 380 | bytes 160 | tf_op jit(solution)/shard_map/reduce_sum | solution.py:171
  19.9 2.0 %collective-permute-done.5.rest_6_ = bf16[128,512]{1,0:T(8,128)(2,1)S(1)} collective-permute-done((bf16[128,512]{1,0:T(8,128)(2,1)S(1)}, bf16[128,512]{1,0:T(8,128)(2,1)S(1)}, u32[]{:S(2)}, u32[]{:S(2)}) %collective-permute-start.5) | collective-permute-done | bytes 131104 | tf_op jit(solution)/shard_map/ppermute | solution.py:28
  21.9 2.3 %collective-permute-done.6.rest_7_ = bf16[128,512]{1,0:T(8,128)(2,1)S(1)} collective-permute-done((bf16[128,512]{1,0:T(8,128)(2,1)S(1)}, bf16[128,512]{1,0:T(8,128)(2,1)S(1)}, u32[]{:S(2)}, u32[]{:S(2)}) %collective-permute-start.6) | collective-permute-done | bytes 131104 | tf_op jit(solution)/shard_map/ppermute | solution.py:28
  24.3 0.6 %copy-done.11 = bf16[128,512]{1,0:T(8,128)(2,1)} copy-done((bf16[128,512]{1,0:T(8,128)(2,1)}, bf16[128,512]{1,0:T(8,128)(2,1)S(1)}, u32[]{:S(2)}) %copy-start.11) | copy-done | bytes 131096
  24.9 5.8 %shard_map.109 = bf16[2,128,512]{2,1,0:T(8,128)(2,1)} custom-call(s32[4]{0:T(128)} %select_reduce_fusion.length_ref, s32[8]{0:T(128)} %convert_element_type.18.valid_ref, bf16[4,128,1024]{2,1,0:T(8,128)(2,1)} %bitcast.35, f32[128,128]{1,0:T(8,128)} %constant.40.clone.cos_ref, f32[128,128]{1,0:T(8,128)} %constant.41.clone.sin_ref, ...), custom_call_target="tpu_custom_call" | custom-call | tf_op jit(solution)/shard_map/pallas_call | solution.py:133
  30.7 1.4 %collective-permute-start.8 = (bf16[256,512]{1,0:T(8,128)(2,1)}, bf16[256,512]{1,0:T(8,128)(2,1)S(1)}, u32[]{:S(2)}, u32[]{:S(2)}) collective-permute-start(bf16[256,512]{1,0:T(8,128)(2,1)} %bitcast.40), channel_id=1, source_target_pairs={{0,2},{1,3},{2,0},{3,1},{4,6},{5,7},{6,4},{7,5},{8,10},{9,11},{10,... | collective-permute-start | bytes 786440 | tf_op jit(solution)/shard_map/ppermute | solution.py:28
  32.1 5.8 %shard_map.110 = bf16[2,128,512]{2,1,0:T(8,128)(2,1)} custom-call(s32[4]{0:T(128)} %select_reduce_fusion.length_ref, s32[8]{0:T(128)} %convert_element_type.18.valid_ref, bf16[4,128,1024]{2,1,0:T(8,128)(2,1)} %bitcast.36, f32[128,128]{1,0:T(8,128)} %constant.40.clone.cos_ref, f32[128,128]{1,0:T(8,128)} %constant.41.clone.sin_ref, ...), custom_call_target="tpu_custom_call" | custom-call | tf_op jit(solution)/shard_map/pallas_call | solution.py:133
  39.0 6.4 %collective-permute-done.11 = bf16[256,512]{1,0:T(8,128)(2,1)S(1)} collective-permute-done((bf16[256,512]{1,0:T(8,128)(2,1)}, bf16[256,512]{1,0:T(8,128)(2,1)S(1)}, u32[]{:S(2)}, u32[]{:S(2)}) %collective-permute-start.11) | collective-permute-done | bytes 262176 | tf_op jit(solution)/shard_map/ppermute | solution.py:28
  49.4 0.6 %collective-permute-start.14 = (f32[4,128]{1,0:T(4,128)S(1)}, f32[4,128]{1,0:T(4,128)S(1)}, u32[]{:S(2)}, u32[]{:S(2)}) collective-permute-start(f32[4,128]{1,0:T(4,128)S(1)} %bitcast.44), channel_id=1, source_target_pairs={{0,2},{1,3},{2,0},{3,1},{4,6},{5,7},{6,4},{7,5},{8,10},{9,11},{10,... | collective-permute-start | bytes 6152 | tf_op jit(solution)/shard_map/ppermute | solution.py:24
  50.0 1.0 %collective-permute-start.15 = (f32[4,128]{1,0:T(4,128)S(1)}, f32[4,128]{1,0:T(4,128)S(1)}, u32[]{:S(2)}, u32[]{:S(2)}) collective-permute-start(f32[4,128]{1,0:T(4,128)S(1)} %bitcast.45), channel_id=1, source_target_pairs={{0,3},{1,0},{2,1},{3,2},{4,7},{5,4},{6,5},{7,6},{8,11},{9,8},{10,9... | collective-permute-start | bytes 6152 | tf_op jit(solution)/shard_map/ppermute | solution.py:24
  51.0 0.9 %collective-permute-done.13 = f32[4,128]{1,0:T(4,128)S(1)} collective-permute-done((f32[4,128]{1,0:T(4,128)S(1)}, f32[4,128]{1,0:T(4,128)S(1)}, u32[]{:S(2)}, u32[]{:S(2)}) %collective-permute-start.13) | collective-permute-done | bytes 2080 | tf_op jit(solution)/shard_map/ppermute | solution.py:24
  52.0 1.1 %collective-permute-done.14 = f32[4,128]{1,0:T(4,128)S(1)} collective-permute-done((f32[4,128]{1,0:T(4,128)S(1)}, f32[4,128]{1,0:T(4,128)S(1)}, u32[]{:S(2)}, u32[]{:S(2)}) %collective-permute-start.14) | collective-permute-done | bytes 2080 | tf_op jit(solution)/shard_map/ppermute | solution.py:24
  53.0 1.1 %fusion.5 = bf16[4,128,576]{1,2,0:T(8,128)(2,1)} fusion(f32[72,4,8,128]{3,2,1,0:T(8,128)S(1)} %get-tuple-element.6, bf16[4,128,576]{1,2,0:T(8,128)(2,1)S(1)} %copy-done.4, f32[4,128]{1,0:T(4,128)S(1)} %fusion.19, f32[576]{0:T(1024)S(1)} %copy-done.13, f32[4,128]{1,0:T(4,128)S(1)} %add_rsqrt_fusion), kind=kLoop, calls=%fused_computation.10 | loop fusion | flops 1769472 | bytes 2365696 | tf_op jit(solution)/shard_map/convert_element_type | solution.py:193
  (57 shorter events, 5.6 us)
Async XLA Ops:
  0.0 45.5 %copy-start = (bf16[2048,576]{0,1:T(8,128)(2,1)S(1)}, bf16[2048,576]{0,1:T(8,128)(2,1)}, u32[]{:S(2)}) copy-start(bf16[2048,576]{0,1:T(8,128)(2,1)} %param.18) | copy-start | bytes 7077892
  3.2 21.0 %copy-start.1 = (bf16[128,512]{1,0:T(8,128)(2,1)}, bf16[128,512]{1,0:T(8,128)(2,1)S(1)}, u32[]{:S(2)}) copy-start(bf16[128,512]{1,0:T(8,128)(2,1)S(1)} %select_bitcast_fusion.rest_0_) | copy-start | bytes 393220
  3.2 9.5 %collective-permute-start.3 = (bf16[128,512]{1,0:T(8,128)(2,1)S(1)}, bf16[128,512]{1,0:T(8,128)(2,1)S(1)}, u32[]{:S(2)}, u32[]{:S(2)}) collective-permute-start(bf16[128,512]{1,0:T(8,128)(2,1)S(1)} %select_bitcast_fusion.rest_0_), channel_id=1, source_target_pairs={{0,24},{4,28},{8,16},{12,20},{16,8},{20,12},{24,0},{28,4},{1,25},{... | collective-permute-start | bytes 393224 | tf_op jit(solution)/shard_map/ppermute | solution.py:28
  8.4 7.5 %collective-permute-start = (bf16[128,512]{1,0:T(8,128)(2,1)S(1)}, bf16[128,512]{1,0:T(8,128)(2,1)S(1)}, u32[]{:S(2)}, u32[]{:S(2)}) collective-permute-start(bf16[128,512]{1,0:T(8,128)(2,1)S(1)} %select_bitcast_fusion.rest_0_), channel_id=1, source_target_pairs={{0,4},{4,0},{8,12},{12,8},{16,20},{20,16},{24,28},{28,24},{1,5},{5... | collective-permute-start | bytes 393224 | tf_op jit(solution)/shard_map/ppermute | solution.py:28
  9.9 9.9 %collective-permute-start.1 = (bf16[128,512]{1,0:T(8,128)(2,1)S(1)}, bf16[128,512]{1,0:T(8,128)(2,1)S(1)}, u32[]{:S(2)}, u32[]{:S(2)}) collective-permute-start(bf16[128,512]{1,0:T(8,128)(2,1)S(1)} %select_bitcast_fusion.rest_0_), channel_id=1, source_target_pairs={{0,8},{4,12},{8,0},{12,4},{16,24},{20,28},{24,16},{28,20},{1,9},{5... | collective-permute-start | bytes 393224 | tf_op jit(solution)/shard_map/ppermute | solution.py:28
  9.9 9.9 %collective-permute-start.2 = (bf16[128,512]{1,0:T(8,128)(2,1)S(1)}, bf16[128,512]{1,0:T(8,128)(2,1)S(1)}, u32[]{:S(2)}, u32[]{:S(2)}) collective-permute-start(bf16[128,512]{1,0:T(8,128)(2,1)S(1)} %select_bitcast_fusion.rest_0_), channel_id=1, source_target_pairs={{0,12},{4,8},{8,4},{12,0},{16,28},{20,24},{24,20},{28,16},{1,13},{... | collective-permute-start | bytes 393224 | tf_op jit(solution)/shard_map/ppermute | solution.py:28
  12.8 11.4 %copy-start.5 = (bf16[128,512]{1,0:T(8,128)(2,1)}, bf16[128,512]{1,0:T(8,128)(2,1)S(1)}, u32[]{:S(2)}) copy-start(bf16[128,512]{1,0:T(8,128)(2,1)S(1)} %collective-permute-done.3.rest_4_) | copy-start | bytes 393220
  12.8 7.1 %collective-permute-start.4 = (bf16[128,512]{1,0:T(8,128)(2,1)S(1)}, bf16[128,512]{1,0:T(8,128)(2,1)S(1)}, u32[]{:S(2)}, u32[]{:S(2)}) collective-permute-start(bf16[128,512]{1,0:T(8,128)(2,1)S(1)} %collective-permute-done.3.rest_4_), channel_id=1, source_target_pairs={{0,4},{4,0},{8,12},{12,8},{16,20},{20,16},{24,28},{28,24},{1,5},{5... | collective-permute-start | bytes 393224 | tf_op jit(solution)/shard_map/ppermute | solution.py:28
  14.5 7.4 %collective-permute-start.5 = (bf16[128,512]{1,0:T(8,128)(2,1)S(1)}, bf16[128,512]{1,0:T(8,128)(2,1)S(1)}, u32[]{:S(2)}, u32[]{:S(2)}) collective-permute-start(bf16[128,512]{1,0:T(8,128)(2,1)S(1)} %collective-permute-done.3.rest_4_), channel_id=1, source_target_pairs={{0,8},{4,12},{8,0},{12,4},{16,24},{20,28},{24,16},{28,20},{1,9},{5... | collective-permute-start | bytes 393224 | tf_op jit(solution)/shard_map/ppermute | solution.py:28
  15.9 8.3 %copy-start.6 = (bf16[128,512]{1,0:T(8,128)(2,1)}, bf16[128,512]{1,0:T(8,128)(2,1)S(1)}, u32[]{:S(2)}) copy-start(bf16[128,512]{1,0:T(8,128)(2,1)S(1)} %collective-permute-done.rest_1_) | copy-start | bytes 393220
  15.9 8.3 %collective-permute-start.6 = (bf16[128,512]{1,0:T(8,128)(2,1)S(1)}, bf16[128,512]{1,0:T(8,128)(2,1)S(1)}, u32[]{:S(2)}, u32[]{:S(2)}) collective-permute-start(bf16[128,512]{1,0:T(8,128)(2,1)S(1)} %collective-permute-done.3.rest_4_), channel_id=1, source_target_pairs={{0,12},{4,8},{8,4},{12,0},{16,28},{20,24},{24,20},{28,16},{1,13},{... | collective-permute-start | bytes 393224 | tf_op jit(solution)/shard_map/ppermute | solution.py:28
  19.8 4.5 %copy-start.8 = (bf16[128,512]{1,0:T(8,128)(2,1)}, bf16[128,512]{1,0:T(8,128)(2,1)S(1)}, u32[]{:S(2)}) copy-start(bf16[128,512]{1,0:T(8,128)(2,1)S(1)} %collective-permute-done.2.rest_3_) | copy-start | bytes 393220
  30.7 7.9 %copy-start.3 = (bf16[2,128,512]{2,1,0:T(8,128)(2,1)S(1)}, bf16[2,128,512]{2,1,0:T(8,128)(2,1)}, u32[]{:S(2)}) copy-start(bf16[2,128,512]{2,1,0:T(8,128)(2,1)} %shard_map.109) | copy-start | bytes 786436
  30.7 8.4 %collective-permute-start.8 = (bf16[256,512]{1,0:T(8,128)(2,1)}, bf16[256,512]{1,0:T(8,128)(2,1)S(1)}, u32[]{:S(2)}, u32[]{:S(2)}) collective-permute-start(bf16[256,512]{1,0:T(8,128)(2,1)} %bitcast.40), channel_id=1, source_target_pairs={{0,2},{1,3},{2,0},{3,1},{4,6},{5,7},{6,4},{7,5},{8,10},{9,11},{10,... | collective-permute-start | bytes 786440 | tf_op jit(solution)/shard_map/ppermute | solution.py:28
  37.9 7.5 %collective-permute-start.11 = (bf16[256,512]{1,0:T(8,128)(2,1)}, bf16[256,512]{1,0:T(8,128)(2,1)S(1)}, u32[]{:S(2)}, u32[]{:S(2)}) collective-permute-start(bf16[256,512]{1,0:T(8,128)(2,1)} %bitcast.37), channel_id=1, source_target_pairs={{0,2},{1,3},{2,0},{3,1},{4,6},{5,7},{6,4},{7,5},{8,10},{9,11},{10,... | collective-permute-start | bytes 786440 | tf_op jit(solution)/shard_map/ppermute | solution.py:28
  38.5 7.7 %collective-permute-start.7 = (bf16[256,512]{1,0:T(8,128)(2,1)S(1)}, bf16[256,512]{1,0:T(8,128)(2,1)S(1)}, u32[]{:S(2)}, u32[]{:S(2)}) collective-permute-start(bf16[256,512]{1,0:T(8,128)(2,1)S(1)} %bitcast.41), channel_id=1, source_target_pairs={{0,1},{1,0},{2,3},{3,2},{4,5},{5,4},{6,7},{7,6},{8,9},{9,8},{10,11... | collective-permute-start | bytes 786440 | tf_op jit(solution)/shard_map/ppermute | solution.py:28
  38.5 8.4 %collective-permute-start.10 = (bf16[256,512]{1,0:T(8,128)(2,1)}, bf16[256,512]{1,0:T(8,128)(2,1)S(1)}, u32[]{:S(2)}, u32[]{:S(2)}) collective-permute-start(bf16[256,512]{1,0:T(8,128)(2,1)} %bitcast.38), channel_id=1, source_target_pairs={{0,1},{1,0},{2,3},{3,2},{4,5},{5,4},{6,7},{7,6},{8,9},{9,8},{10,11... | collective-permute-start | bytes 786440 | tf_op jit(solution)/shard_map/ppermute | solution.py:28
  39.0 8.8 %collective-permute-start.9 = (bf16[256,512]{1,0:T(8,128)(2,1)S(1)}, bf16[256,512]{1,0:T(8,128)(2,1)S(1)}, u32[]{:S(2)}, u32[]{:S(2)}) collective-permute-start(bf16[256,512]{1,0:T(8,128)(2,1)S(1)} %collective-permute-done.8), channel_id=1, source_target_pairs={{0,1},{1,0},{2,3},{3,2},{4,5},{5,4},{6,7},{7,6},{8,9},{9,8},{10,11... | collective-permute-start | bytes 786440 | tf_op jit(solution)/shard_map/ppermute | solution.py:28
  45.5 2.8 %collective-permute-start.12 = (bf16[256,512]{1,0:T(8,128)(2,1)S(1)}, bf16[256,512]{1,0:T(8,128)(2,1)S(1)}, u32[]{:S(2)}, u32[]{:S(2)}) collective-permute-start(bf16[256,512]{1,0:T(8,128)(2,1)S(1)} %collective-permute-done.11), channel_id=1, source_target_pairs={{0,1},{1,0},{2,3},{3,2},{4,5},{5,4},{6,7},{7,6},{8,9},{9,8},{10,11... | collective-permute-start | bytes 786440 | tf_op jit(solution)/shard_map/ppermute | solution.py:28
  48.2 4.8 %copy-start.4 = (bf16[4,128,576]{1,2,0:T(8,128)(2,1)S(1)}, bf16[4,128,576]{1,2,0:T(8,128)(2,1)}, u32[]{:S(2)}) copy-start(bf16[4,128,576]{1,2,0:T(8,128)(2,1)} %param.11) | copy-start | bytes 1769476
  48.2 4.8 %copy-start.13 = (f32[576]{0:T(1024)S(1)}, f32[576]{0:T(1024)}, u32[]{:S(2)}) copy-start(f32[576]{0:T(1024)} %param.19) | copy-start | bytes 6916
  48.9 3.1 %collective-permute-start.13 = (f32[4,128]{1,0:T(4,128)S(1)}, f32[4,128]{1,0:T(4,128)S(1)}, u32[]{:S(2)}, u32[]{:S(2)}) collective-permute-start(f32[4,128]{1,0:T(4,128)S(1)} %bitcast.43), channel_id=1, source_target_pairs={{0,1},{1,2},{2,3},{3,0},{4,5},{5,6},{6,7},{7,4},{8,9},{9,10},{10,1... | collective-permute-start | bytes 6152 | tf_op jit(solution)/shard_map/ppermute | solution.py:24
  49.4 3.6 %collective-permute-start.14 = (f32[4,128]{1,0:T(4,128)S(1)}, f32[4,128]{1,0:T(4,128)S(1)}, u32[]{:S(2)}, u32[]{:S(2)}) collective-permute-start(f32[4,128]{1,0:T(4,128)S(1)} %bitcast.44), channel_id=1, source_target_pairs={{0,2},{1,3},{2,0},{3,1},{4,6},{5,7},{6,4},{7,5},{8,10},{9,11},{10,... | collective-permute-start | bytes 6152 | tf_op jit(solution)/shard_map/ppermute | solution.py:24
  50.0 3.0 %collective-permute-start.15 = (f32[4,128]{1,0:T(4,128)S(1)}, f32[4,128]{1,0:T(4,128)S(1)}, u32[]{:S(2)}, u32[]{:S(2)}) collective-permute-start(f32[4,128]{1,0:T(4,128)S(1)} %bitcast.45), channel_id=1, source_target_pairs={{0,3},{1,0},{2,1},{3,2},{4,7},{5,4},{6,5},{7,6},{8,11},{9,8},{10,9... | collective-permute-start | bytes 6152 | tf_op jit(solution)/shard_map/ppermute | solution.py:24
  (6 other events, 15.6 us)

commit v9 on v6

--- a/solution.py
+++ b/solution.py
@@ -138,7 +138,9 @@
 def project(own, w_out, tp_index, n_tp, group_width):
     if n_tp == 4:
         near = swapped(own, "tp", n_tp, 1)
-        far = swapped(own, "tp", n_tp, 2)
+        half_rows = own.shape[0] // 2
+        far = jnp.concatenate([swapped(own[:half_rows], "tp", n_tp, 2),
+                               swapped(own[half_rows:], "tp", n_tp, 2)], 0)
         farther = swapped(far, "tp", n_tp, 1)
         parts = [(own, tp_index), (near, tp_index ^ 1), (far, tp_index ^ 2), (farther, tp_index ^ 3)]
     else:

time: 52.7 us -> 56.6 us (1.074)
  starting transfers between devices: 17.3 us -> 19.9 us
  local copies, waits for them, and re-layouts: 1.67 us -> 3.69 us
  waiting for transfers between devices: 13.2 us -> 12.5 us
    ppermute x13 -> x15, starting transfers between devices: 14.7 us -> 16.9 us  [swapped(): return lax.ppermute(value, axis, [(i, i ^ mask) for i in range(size)])]
    slice x0 -> x2, local copies, waits for them, and re-layouts: none -> 1.97 us  [project(): own[half_rows:]]
    ppermute x13 -> x15, waiting for transfers between devices: 11.7 us -> 11.3 us  [swapped(): return lax.ppermute(value, axis, [(i, i ^ mask) for i in range(size)])]
  transfers between devices with their start and end apart: 16 -> 18, of which waited for: 8 -> 8; matrix products, arithmetic and copies ran while one was open for 12% -> 12% of each run, Pallas kernels for 9% -> 9%
where the time goes in v9:
time: 56.6 us; the launch traced here: 56.1 us
  starting transfers between devices  19.9 us (35%)
  waiting for transfers between devices  12.5 us (22%)
  Pallas kernels  9.58 us (17%)
  other arithmetic  6.74 us (12%)
  local copies, waits for them, and re-layouts  3.69 us (7%)
  matrix products  2.76 us (5%)
  between operations  0.89 us (2%)
    ppermute x15, starting transfers between devices, swapped(): return lax.ppermute(value, axis, [(i, i ^ mask) for i in range(size)])  16.9 us
    ppermute x15, waiting for transfers between devices, swapped(): return lax.ppermute(value, axis, [(i, i ^ mask) for i in range(size)])  11.3 us
    pallas_call x2, Pallas kernels, attend(): pl.pallas_call(functools.partial(attention_kernel, offset=offset), grid_s...  9.58 us
    ppermute x3, starting transfers between devices, shifted(): lax.ppermute(value, axis, [(i, (i + shift) % size) for i in range(size)])  2.96 us
    dot_general x8, matrix products, project(): term = jnp.dot(block, rows, preferred_element_type=jnp.float32)  2.76 us
    slice x2, local copies, waits for them, and re-layouts, project(): own[half_rows:]  1.97 us
    reduce_sum x1, other arithmetic, gather_prefix(): slot = jnp.sum(jnp.where(mine, page_slot, 0))  1.52 us
    reduce_sum x1, other arithmetic, on_device(): my_lengths = jnp.sum(jnp.where(matches, lengths[None, :], 0), 1)  1.37 us
  transfers between devices with their start and end apart: 18, of which 8 were waited for; matrix products, arithmetic and copies ran while one was open for 12% of the time, Pallas kernels for 9%

profile of v9, /device:TPU:0, one launch (start us, length us, event | category | flops | bytes accessed | tf_op | source)
XLA Modules:
  0.0 56.1 jit_solution(7558505790558268944)
XLA Ops:
  0.0 1.5 %fusion.32 = s32[]{:T(128)} fusion(s32[8]{0:T(128)} %param.15, s32[8]{0:T(128)} %param.14, s32[]{:T(128)} %axis_index.27), kind=kLoop, calls=%fused_computation.52 | loop fusion | flops 23 | bytes 72 | tf_op jit(solution)/shard_map/reduce_sum | solution.py:36
  2.2 1.0 %select_bitcast_fusion.rest_0_ = bf16[128,512]{1,0:T(8,128)(2,1)S(1)} fusion(bf16[2,128,1,512]{3,1,2,0:T(8,128)(2,1)} %param.13, pred[]{:T(512)S(6)} %eq.43), kind=kLoop, calls=%fused_computation.32 | loop fusion | flops 65536 | bytes 393217 | tf_op jit(solution)/shard_map/jit(_where)/select_n | solution.py:39
  3.2 5.1 %collective-permute-start.3 = (bf16[128,512]{1,0:T(8,128)(2,1)S(1)}, bf16[128,512]{1,0:T(8,128)(2,1)S(1)}, u32[]{:S(2)}, u32[]{:S(2)}) collective-permute-start(bf16[128,512]{1,0:T(8,128)(2,1)S(1)} %select_bitcast_fusion.rest_0_), channel_id=1, source_target_pairs={{0,24},{4,28},{8,16},{12,20},{16,8},{20,12},{24,0},{28,4},{1,25},{... | collective-permute-start | bytes 393224 | tf_op jit(solution)/shard_map/ppermute | solution.py:28
  8.3 1.5 %collective-permute-start = (bf16[128,512]{1,0:T(8,128)(2,1)S(1)}, bf16[128,512]{1,0:T(8,128)(2,1)S(1)}, u32[]{:S(2)}, u32[]{:S(2)}) collective-permute-start(bf16[128,512]{1,0:T(8,128)(2,1)S(1)} %select_bitcast_fusion.rest_0_), channel_id=1, source_target_pairs={{0,4},{4,0},{8,12},{12,8},{16,20},{20,16},{24,28},{28,24},{1,5},{5... | collective-permute-start | bytes 393224 | tf_op jit(solution)/shard_map/ppermute | solution.py:28
  9.8 2.0 %collective-permute-start.2 = (bf16[128,512]{1,0:T(8,128)(2,1)S(1)}, bf16[128,512]{1,0:T(8,128)(2,1)S(1)}, u32[]{:S(2)}, u32[]{:S(2)}) collective-permute-start(bf16[128,512]{1,0:T(8,128)(2,1)S(1)} %select_bitcast_fusion.rest_0_), channel_id=1, source_target_pairs={{0,12},{4,8},{8,4},{12,0},{16,28},{20,24},{24,20},{28,16},{1,13},{... | collective-permute-start | bytes 393224 | tf_op jit(solution)/shard_map/ppermute | solution.py:28
  11.9 0.8 %collective-permute-done.3.rest_4_ = bf16[128,512]{1,0:T(8,128)(2,1)S(1)} collective-permute-done((bf16[128,512]{1,0:T(8,128)(2,1)S(1)}, bf16[128,512]{1,0:T(8,128)(2,1)S(1)}, u32[]{:S(2)}, u32[]{:S(2)}) %collective-permute-start.3) | collective-permute-done | bytes 131104 | tf_op jit(solution)/shard_map/ppermute | solution.py:28
  12.7 1.7 %collective-permute-start.4 = (bf16[128,512]{1,0:T(8,128)(2,1)S(1)}, bf16[128,512]{1,0:T(8,128)(2,1)S(1)}, u32[]{:S(2)}, u32[]{:S(2)}) collective-permute-start(bf16[128,512]{1,0:T(8,128)(2,1)S(1)} %collective-permute-done.3.rest_4_), channel_id=1, source_target_pairs={{0,4},{4,0},{8,12},{12,8},{16,20},{20,16},{24,28},{28,24},{1,5},{5... | collective-permute-start | bytes 393224 | tf_op jit(solution)/shard_map/ppermute | solution.py:28
  14.4 1.5 %collective-permute-start.5 = (bf16[128,512]{1,0:T(8,128)(2,1)S(1)}, bf16[128,512]{1,0:T(8,128)(2,1)S(1)}, u32[]{:S(2)}, u32[]{:S(2)}) collective-permute-start(bf16[128,512]{1,0:T(8,128)(2,1)S(1)} %collective-permute-done.3.rest_4_), channel_id=1, source_target_pairs={{0,8},{4,12},{8,0},{12,4},{16,24},{20,28},{24,16},{28,20},{1,9},{5... | collective-permute-start | bytes 393224 | tf_op jit(solution)/shard_map/ppermute | solution.py:28
  16.2 0.8 %compare_reduce_fusion = pred[8]{0:T(512)(128)(4,1)S(1)} fusion(s32[8]{0:T(128)} %param.14, s32[8]{0:T(128)S(1)} %stack.35), kind=kLoop, calls=%fused_computation.37 | loop fusion | flops 120 | bytes 72 | tf_op jit(solution)/shard_map/reduce_or | solution.py:55
  18.3 1.4 %select_reduce_fusion.length_ref = s32[4]{0:T(128)} fusion(s32[32]{0:T(128)} %param.16, s32[4]{0:T(128)S(1)} %dynamic_slice.19), kind=kLoop, calls=%fused_computation.40 | loop fusion | flops 380 | bytes 160 | tf_op jit(solution)/shard_map/reduce_sum | solution.py:172
  19.8 2.0 %collective-permute-done.5.rest_6_ = bf16[128,512]{1,0:T(8,128)(2,1)S(1)} collective-permute-done((bf16[128,512]{1,0:T(8,128)(2,1)S(1)}, bf16[128,512]{1,0:T(8,128)(2,1)S(1)}, u32[]{:S(2)}, u32[]{:S(2)}) %collective-permute-start.5) | collective-permute-done | bytes 131104 | tf_op jit(solution)/shard_map/ppermute | solution.py:28
  21.8 2.3 %collective-permute-done.6.rest_7_ = bf16[128,512]{1,0:T(8,128)(2,1)S(1)} collective-permute-done((bf16[128,512]{1,0:T(8,128)(2,1)S(1)}, bf16[128,512]{1,0:T(8,128)(2,1)S(1)}, u32[]{:S(2)}, u32[]{:S(2)}) %collective-permute-start.6) | collective-permute-done | bytes 131104 | tf_op jit(solution)/shard_map/ppermute | solution.py:28
  24.8 4.8 %shard_map.109 = bf16[2,128,512]{2,1,0:T(8,128)(2,1)} custom-call(s32[4]{0:T(128)} %select_reduce_fusion.length_ref, s32[8]{0:T(128)} %convert_element_type.18.valid_ref, bf16[4,128,1024]{2,1,0:T(8,128)(2,1)} %bitcast.43, f32[128,128]{1,0:T(8,128)} %constant.40.clone.cos_ref, f32[128,128]{1,0:T(8,128)} %constant.41.clone.sin_ref, ...), custom_call_target="tpu_custom_call" | custom-call | tf_op jit(solution)/shard_map/pallas_call | solution.py:132
  29.6 1.0 %slice_bitcast_fusion.2 = (bf16[128,512]{1,0:T(8,128)(2,1)S(1)}, bf16[128,512]{1,0:T(8,128)(2,1)S(1)}) fusion(bf16[2,128,512]{2,1,0:T(8,128)(2,1)} %shard_map.109), kind=kLoop, calls=%fused_computation.30 | loop fusion | bytes 524288 | tf_op jit(solution)/shard_map/slice | solution.py:143
  30.5 1.5 %collective-permute-start.8 = (bf16[128,512]{1,0:T(8,128)(2,1)S(1)}, bf16[128,512]{1,0:T(8,128)(2,1)S(1)}, u32[]{:S(2)}, u32[]{:S(2)}) collective-permute-start(bf16[128,512]{1,0:T(8,128)(2,1)S(1)} %get-tuple-element.8), channel_id=1, source_target_pairs={{0,2},{1,3},{2,0},{3,1},{4,6},{5,7},{6,4},{7,5},{8,10},{9,11},{10,... | collective-permute-start | bytes 393224 | tf_op jit(solution)/shard_map/ppermute | solution.py:28
  32.6 4.8 %shard_map.110 = bf16[2,128,512]{2,1,0:T(8,128)(2,1)} custom-call(s32[4]{0:T(128)} %select_reduce_fusion.length_ref, s32[8]{0:T(128)} %convert_element_type.18.valid_ref, bf16[4,128,1024]{2,1,0:T(8,128)(2,1)} %bitcast.44, f32[128,128]{1,0:T(8,128)} %constant.40.clone.cos_ref, f32[128,128]{1,0:T(8,128)} %constant.41.clone.sin_ref, ...), custom_call_target="tpu_custom_call" | custom-call | tf_op jit(solution)/shard_map/pallas_call | solution.py:132
  37.4 1.0 %slice_bitcast_fusion = (bf16[128,512]{1,0:T(8,128)(2,1)S(1)}, bf16[128,512]{1,0:T(8,128)(2,1)S(1)}) fusion(bf16[2,128,512]{2,1,0:T(8,128)(2,1)} %shard_map.110), kind=kLoop, calls=%fused_computation.28 | loop fusion | bytes 524288 | tf_op jit(solution)/shard_map/slice | solution.py:143
  38.4 1.5 %collective-permute-start.12 = (bf16[128,512]{1,0:T(8,128)(2,1)S(1)}, bf16[128,512]{1,0:T(8,128)(2,1)S(1)}, u32[]{:S(2)}, u32[]{:S(2)}) collective-permute-start(bf16[128,512]{1,0:T(8,128)(2,1)S(1)} %get-tuple-element.10), channel_id=1, source_target_pairs={{0,2},{1,3},{2,0},{3,1},{4,6},{5,7},{6,4},{7,5},{8,10},{9,11},{10,... | collective-permute-start | bytes 393224 | tf_op jit(solution)/shard_map/ppermute | solution.py:28
  41.1 3.7 %collective-permute-done.12 = bf16[128,512]{1,0:T(8,128)(2,1)S(1)} collective-permute-done((bf16[128,512]{1,0:T(8,128)(2,1)S(1)}, bf16[128,512]{1,0:T(8,128)(2,1)S(1)}, u32[]{:S(2)}, u32[]{:S(2)}) %collective-permute-start.12) | collective-permute-done | bytes 131104 | tf_op jit(solution)/shard_map/ppermute | solution.py:28
  44.9 2.3 %collective-permute-done.13 = bf16[128,512]{1,0:T(8,128)(2,1)S(1)} collective-permute-done((bf16[128,512]{1,0:T(8,128)(2,1)S(1)}, bf16[128,512]{1,0:T(8,128)(2,1)S(1)}, u32[]{:S(2)}, u32[]{:S(2)}) %collective-permute-start.13) | collective-permute-done | bytes 131104 | tf_op jit(solution)/shard_map/ppermute | solution.py:28
  51.2 1.4 %collective-permute-start.16 = (f32[4,128]{1,0:T(4,128)S(1)}, f32[4,128]{1,0:T(4,128)S(1)}, u32[]{:S(2)}, u32[]{:S(2)}) collective-permute-start(f32[4,128]{1,0:T(4,128)S(1)} %bitcast.50), channel_id=1, source_target_pairs={{0,2},{1,3},{2,0},{3,1},{4,6},{5,7},{6,4},{7,5},{8,10},{9,11},{10,... | collective-permute-start | bytes 6152 | tf_op jit(solution)/shard_map/ppermute | solution.py:24
  52.7 1.0 %collective-permute-start.17 = (f32[4,128]{1,0:T(4,128)S(1)}, f32[4,128]{1,0:T(4,128)S(1)}, u32[]{:S(2)}, u32[]{:S(2)}) collective-permute-start(f32[4,128]{1,0:T(4,128)S(1)} %bitcast.51), channel_id=1, source_target_pairs={{0,3},{1,0},{2,1},{3,2},{4,7},{5,4},{6,5},{7,6},{8,11},{9,8},{10,9... | collective-permute-start | bytes 6152 | tf_op jit(solution)/shard_map/ppermute | solution.py:24
  53.8 1.1 %collective-permute-done.16 = f32[4,128]{1,0:T(4,128)S(1)} collective-permute-done((f32[4,128]{1,0:T(4,128)S(1)}, f32[4,128]{1,0:T(4,128)S(1)}, u32[]{:S(2)}, u32[]{:S(2)}) %collective-permute-start.16) | collective-permute-done | bytes 2080 | tf_op jit(solution)/shard_map/ppermute | solution.py:24
  55.0 1.1 %fusion.7 = bf16[4,128,576]{1,2,0:T(8,128)(2,1)} fusion(f32[72,4,8,128]{3,2,1,0:T(8,128)S(1)} %get-tuple-element.6, bf16[4,128,576]{1,2,0:T(8,128)(2,1)S(1)} %copy-done.4, f32[4,128]{1,0:T(4,128)S(1)} %fusion.23, f32[576]{0:T(1024)S(1)} %copy-done.13, f32[4,128]{1,0:T(4,128)S(1)} %add_rsqrt_fusion), kind=kLoop, calls=%fused_computation.10 | loop fusion | flops 1769472 | bytes 2365696 | tf_op jit(solution)/shard_map/convert_element_type | solution.py:194
  (67 shorter events, 8.4 us)
Async XLA Ops:
  0.0 47.3 %copy-start = (bf16[2048,576]{0,1:T(8,128)(2,1)S(1)}, bf16[2048,576]{0,1:T(8,128)(2,1)}, u32[]{:S(2)}) copy-start(bf16[2048,576]{0,1:T(8,128)(2,1)} %param.18) | copy-start | bytes 7077892
  3.1 21.0 %copy-start.3 = (bf16[128,512]{1,0:T(8,128)(2,1)}, bf16[128,512]{1,0:T(8,128)(2,1)S(1)}, u32[]{:S(2)}) copy-start(bf16[128,512]{1,0:T(8,128)(2,1)S(1)} %select_bitcast_fusion.rest_0_) | copy-start | bytes 393220
  3.2 9.5 %collective-permute-start.3 = (bf16[128,512]{1,0:T(8,128)(2,1)S(1)}, bf16[128,512]{1,0:T(8,128)(2,1)S(1)}, u32[]{:S(2)}, u32[]{:S(2)}) collective-permute-start(bf16[128,512]{1,0:T(8,128)(2,1)S(1)} %select_bitcast_fusion.rest_0_), channel_id=1, source_target_pairs={{0,24},{4,28},{8,16},{12,20},{16,8},{20,12},{24,0},{28,4},{1,25},{... | collective-permute-start | bytes 393224 | tf_op jit(solution)/shard_map/ppermute | solution.py:28
  8.3 7.5 %collective-permute-start = (bf16[128,512]{1,0:T(8,128)(2,1)S(1)}, bf16[128,512]{1,0:T(8,128)(2,1)S(1)}, u32[]{:S(2)}, u32[]{:S(2)}) collective-permute-start(bf16[128,512]{1,0:T(8,128)(2,1)S(1)} %select_bitcast_fusion.rest_0_), channel_id=1, source_target_pairs={{0,4},{4,0},{8,12},{12,8},{16,20},{20,16},{24,28},{28,24},{1,5},{5... | collective-permute-start | bytes 393224 | tf_op jit(solution)/shard_map/ppermute | solution.py:28
  9.8 9.9 %collective-permute-start.1 = (bf16[128,512]{1,0:T(8,128)(2,1)S(1)}, bf16[128,512]{1,0:T(8,128)(2,1)S(1)}, u32[]{:S(2)}, u32[]{:S(2)}) collective-permute-start(bf16[128,512]{1,0:T(8,128)(2,1)S(1)} %select_bitcast_fusion.rest_0_), channel_id=1, source_target_pairs={{0,8},{4,12},{8,0},{12,4},{16,24},{20,28},{24,16},{28,20},{1,9},{5... | collective-permute-start | bytes 393224 | tf_op jit(solution)/shard_map/ppermute | solution.py:28
  9.8 9.9 %collective-permute-start.2 = (bf16[128,512]{1,0:T(8,128)(2,1)S(1)}, bf16[128,512]{1,0:T(8,128)(2,1)S(1)}, u32[]{:S(2)}, u32[]{:S(2)}) collective-permute-start(bf16[128,512]{1,0:T(8,128)(2,1)S(1)} %select_bitcast_fusion.rest_0_), channel_id=1, source_target_pairs={{0,12},{4,8},{8,4},{12,0},{16,28},{20,24},{24,20},{28,16},{1,13},{... | collective-permute-start | bytes 393224 | tf_op jit(solution)/shard_map/ppermute | solution.py:28
  12.7 11.4 %copy-start.5 = (bf16[128,512]{1,0:T(8,128)(2,1)}, bf16[128,512]{1,0:T(8,128)(2,1)S(1)}, u32[]{:S(2)}) copy-start(bf16[128,512]{1,0:T(8,128)(2,1)S(1)} %collective-permute-done.3.rest_4_) | copy-start | bytes 393220
  12.7 7.1 %collective-permute-start.4 = (bf16[128,512]{1,0:T(8,128)(2,1)S(1)}, bf16[128,512]{1,0:T(8,128)(2,1)S(1)}, u32[]{:S(2)}, u32[]{:S(2)}) collective-permute-start(bf16[128,512]{1,0:T(8,128)(2,1)S(1)} %collective-permute-done.3.rest_4_), channel_id=1, source_target_pairs={{0,4},{4,0},{8,12},{12,8},{16,20},{20,16},{24,28},{28,24},{1,5},{5... | collective-permute-start | bytes 393224 | tf_op jit(solution)/shard_map/ppermute | solution.py:28
  14.4 7.4 %collective-permute-start.5 = (bf16[128,512]{1,0:T(8,128)(2,1)S(1)}, bf16[128,512]{1,0:T(8,128)(2,1)S(1)}, u32[]{:S(2)}, u32[]{:S(2)}) collective-permute-start(bf16[128,512]{1,0:T(8,128)(2,1)S(1)} %collective-permute-done.3.rest_4_), channel_id=1, source_target_pairs={{0,8},{4,12},{8,0},{12,4},{16,24},{20,28},{24,16},{28,20},{1,9},{5... | collective-permute-start | bytes 393224 | tf_op jit(solution)/shard_map/ppermute | solution.py:28
  15.8 8.3 %copy-start.6 = (bf16[128,512]{1,0:T(8,128)(2,1)}, bf16[128,512]{1,0:T(8,128)(2,1)S(1)}, u32[]{:S(2)}) copy-start(bf16[128,512]{1,0:T(8,128)(2,1)S(1)} %collective-permute-done.rest_1_) | copy-start | bytes 393220
  15.8 8.3 %collective-permute-start.6 = (bf16[128,512]{1,0:T(8,128)(2,1)S(1)}, bf16[128,512]{1,0:T(8,128)(2,1)S(1)}, u32[]{:S(2)}, u32[]{:S(2)}) collective-permute-start(bf16[128,512]{1,0:T(8,128)(2,1)S(1)} %collective-permute-done.3.rest_4_), channel_id=1, source_target_pairs={{0,12},{4,8},{8,4},{12,0},{16,28},{20,24},{24,20},{28,16},{1,13},{... | collective-permute-start | bytes 393224 | tf_op jit(solution)/shard_map/ppermute | solution.py:28
  30.5 10.0 %collective-permute-start.8 = (bf16[128,512]{1,0:T(8,128)(2,1)S(1)}, bf16[128,512]{1,0:T(8,128)(2,1)S(1)}, u32[]{:S(2)}, u32[]{:S(2)}) collective-permute-start(bf16[128,512]{1,0:T(8,128)(2,1)S(1)} %get-tuple-element.8), channel_id=1, source_target_pairs={{0,2},{1,3},{2,0},{3,1},{4,6},{5,7},{6,4},{7,5},{8,10},{9,11},{10,... | collective-permute-start | bytes 393224 | tf_op jit(solution)/shard_map/ppermute | solution.py:28
  32.1 8.5 %collective-permute-start.9 = (bf16[128,512]{1,0:T(8,128)(2,1)S(1)}, bf16[128,512]{1,0:T(8,128)(2,1)S(1)}, u32[]{:S(2)}, u32[]{:S(2)}) collective-permute-start(bf16[128,512]{1,0:T(8,128)(2,1)S(1)} %get-tuple-element.7), channel_id=1, source_target_pairs={{0,2},{1,3},{2,0},{3,1},{4,6},{5,7},{6,4},{7,5},{8,10},{9,11},{10,... | collective-permute-start | bytes 393224 | tf_op jit(solution)/shard_map/ppermute | solution.py:28
  32.6 15.4 %collective-permute-start.7 = (bf16[256,512]{1,0:T(8,128)(2,1)}, bf16[256,512]{1,0:T(8,128)(2,1)S(1)}, u32[]{:S(2)}, u32[]{:S(2)}) collective-permute-start(bf16[256,512]{1,0:T(8,128)(2,1)} %bitcast.45), channel_id=1, source_target_pairs={{0,1},{1,0},{2,3},{3,2},{4,5},{5,4},{6,7},{7,6},{8,9},{9,8},{10,11... | collective-permute-start | bytes 786440 | tf_op jit(solution)/shard_map/ppermute | solution.py:28
  38.4 6.4 %collective-permute-start.12 = (bf16[128,512]{1,0:T(8,128)(2,1)S(1)}, bf16[128,512]{1,0:T(8,128)(2,1)S(1)}, u32[]{:S(2)}, u32[]{:S(2)}) collective-permute-start(bf16[128,512]{1,0:T(8,128)(2,1)S(1)} %get-tuple-element.10), channel_id=1, source_target_pairs={{0,2},{1,3},{2,0},{3,1},{4,6},{5,7},{6,4},{7,5},{8,10},{9,11},{10,... | collective-permute-start | bytes 393224 | tf_op jit(solution)/shard_map/ppermute | solution.py:28
  39.9 7.3 %collective-permute-start.13 = (bf16[128,512]{1,0:T(8,128)(2,1)S(1)}, bf16[128,512]{1,0:T(8,128)(2,1)S(1)}, u32[]{:S(2)}, u32[]{:S(2)}) collective-permute-start(bf16[128,512]{1,0:T(8,128)(2,1)S(1)} %get-tuple-element.9), channel_id=1, source_target_pairs={{0,2},{1,3},{2,0},{3,1},{4,6},{5,7},{6,4},{7,5},{8,10},{9,11},{10,... | collective-permute-start | bytes 393224 | tf_op jit(solution)/shard_map/ppermute | solution.py:28
  40.5 7.9 %collective-permute-start.11 = (bf16[256,512]{1,0:T(8,128)(2,1)}, bf16[256,512]{1,0:T(8,128)(2,1)S(1)}, u32[]{:S(2)}, u32[]{:S(2)}) collective-permute-start(bf16[256,512]{1,0:T(8,128)(2,1)} %bitcast.47), channel_id=1, source_target_pairs={{0,1},{1,0},{2,3},{3,2},{4,5},{5,4},{6,7},{7,6},{8,9},{9,8},{10,11... | collective-permute-start | bytes 786440 | tf_op jit(solution)/shard_map/ppermute | solution.py:28
  40.6 8.2 %collective-permute-start.10 = (bf16[256,512]{1,0:T(8,128)(2,1)S(1)}, bf16[256,512]{1,0:T(8,128)(2,1)S(1)}, u32[]{:S(2)}, u32[]{:S(2)}) collective-permute-start(bf16[256,512]{1,0:T(8,128)(2,1)S(1)} %constant_dynamic-update-slice_fusion), channel_id=1, source_target_pairs={{0,1},{1,0},{2,3},{3,2},{4,5},{5,4},{6,7},{7,6},{8,9},{9,8},{10,11... | collective-permute-start | bytes 786440 | tf_op jit(solution)/shard_map/ppermute | solution.py:28
  47.2 2.3 %collective-permute-start.14 = (bf16[256,512]{1,0:T(8,128)(2,1)S(1)}, bf16[256,512]{1,0:T(8,128)(2,1)S(1)}, u32[]{:S(2)}, u32[]{:S(2)}) collective-permute-start(bf16[256,512]{1,0:T(8,128)(2,1)S(1)} %constant_dynamic-update-slice_fusion.2), channel_id=1, source_target_pairs={{0,1},{1,0},{2,3},{3,2},{4,5},{5,4},{6,7},{7,6},{8,9},{9,8},{10,11... | collective-permute-start | bytes 786440 | tf_op jit(solution)/shard_map/ppermute | solution.py:28
  50.1 4.9 %copy-start.4 = (bf16[4,128,576]{1,2,0:T(8,128)(2,1)S(1)}, bf16[4,128,576]{1,2,0:T(8,128)(2,1)}, u32[]{:S(2)}) copy-start(bf16[4,128,576]{1,2,0:T(8,128)(2,1)} %param.11) | copy-start | bytes 1769476
  50.1 4.9 %copy-start.13 = (f32[576]{0:T(1024)S(1)}, f32[576]{0:T(1024)}, u32[]{:S(2)}) copy-start(f32[576]{0:T(1024)} %param.19) | copy-start | bytes 6916
  50.7 3.1 %collective-permute-start.15 = (f32[4,128]{1,0:T(4,128)S(1)}, f32[4,128]{1,0:T(4,128)S(1)}, u32[]{:S(2)}, u32[]{:S(2)}) collective-permute-start(f32[4,128]{1,0:T(4,128)S(1)} %bitcast.49), channel_id=1, source_target_pairs={{0,1},{1,2},{2,3},{3,0},{4,5},{5,6},{6,7},{7,4},{8,9},{9,10},{10,1... | collective-permute-start | bytes 6152 | tf_op jit(solution)/shard_map/ppermute | solution.py:24
  51.2 3.6 %collective-permute-start.16 = (f32[4,128]{1,0:T(4,128)S(1)}, f32[4,128]{1,0:T(4,128)S(1)}, u32[]{:S(2)}, u32[]{:S(2)}) collective-permute-start(f32[4,128]{1,0:T(4,128)S(1)} %bitcast.50), channel_id=1, source_target_pairs={{0,2},{1,3},{2,0},{3,1},{4,6},{5,7},{6,4},{7,5},{8,10},{9,11},{10,... | collective-permute-start | bytes 6152 | tf_op jit(solution)/shard_map/ppermute | solution.py:24
  52.7 2.3 %collective-permute-start.17 = (f32[4,128]{1,0:T(4,128)S(1)}, f32[4,128]{1,0:T(4,128)S(1)}, u32[]{:S(2)}, u32[]{:S(2)}) collective-permute-start(f32[4,128]{1,0:T(4,128)S(1)} %bitcast.51), channel_id=1, source_target_pairs={{0,3},{1,0},{2,1},{3,2},{4,7},{5,4},{6,5},{7,6},{8,11},{9,8},{10,9... | collective-permute-start | bytes 6152 | tf_op jit(solution)/shard_map/ppermute | solution.py:24
  (8 other events, 21.9 us)

commit v10 on v8

--- a/solution.py
+++ b/solution.py
@@ -69,8 +69,14 @@
     return np.cos(angles).astype(np.float32), np.sin(angles).astype(np.float32)
 
 
-def attention_kernel(length_ref, valid_ref, qkv_ref, cos_ref, sin_ref, *rest, offset):
-    page_refs, out_ref = rest[:-1], rest[-1]
+def attention_kernel(length_ref, valid_ref, qkv_ref, cos_ref, sin_ref, *rest,
+                     offset, first_block, page_count, first, last):
+    index = 0
+    if not first:
+        sum_in_ref, total_in_ref = rest[0], rest[1]
+        index = 2
+    page_refs = rest[index:index + page_count]
+    outs = rest[index + page_count:]
     request = pl.program_id(0) + offset
     slots = qkv_ref.shape[1]
     per_group = qkv_ref.shape[2] // HD - 2
@@ -80,61 +86,95 @@
     values_in = qkv_ref[0].astype(jnp.float32)
 
     def rope(part):
-        first = part[:, :half]
-        second = part[:, half:]
-        return jnp.concatenate([first * cosine - second * sine, second * cosine + first * sine], -1)
+        first_half = part[:, :half]
+        second_half = part[:, half:]
+        return jnp.concatenate(
+            [first_half * cosine - second_half * sine, second_half * cosine + first_half * sine], -1)
 
     queries = jnp.concatenate(
         [(rope(values_in[:, q * HD:(q + 1) * HD]) * HD ** (-0.5)).astype(jnp.bfloat16)
          for q in range(per_group)], 0)
-    fresh_keys = rope(values_in[:, per_group * HD:(per_group + 1) * HD]).astype(jnp.bfloat16)
-    fresh_values = values_in[:, (per_group + 1) * HD:].astype(jnp.bfloat16)
     rows = queries.shape[0]
-    contract = (((1,), (1,)), ((), ()))
-
-    page_weights = []
-    totals = jnp.zeros((rows, 1), jnp.float32)
-    for index, ref in enumerate(page_refs):
-        scores = lax.dot_general(queries, ref[:, :HD], contract, preferred_element_type=jnp.float32)
-        flag = jnp.where(valid_ref[index] != 0, 1.0, 0.0).astype(jnp.float32)
-        raw = capped_exp(scores) * flag
+    pages = [ref[...] for ref in page_refs]
+    key_parts = [page[:, :HD] for page in pages]
+    value_parts = [page[:, HD:] for page in pages]
+    if first:
+        key_parts.append(rope(values_in[:, per_group * HD:(per_group + 1) * HD]).astype(jnp.bfloat16))
+        value_parts.append(values_in[:, (per_group + 1) * HD:].astype(jnp.bfloat16))
+    if first:
+        sums = jnp.zeros((rows, HD), jnp.float32)
+        totals = jnp.zeros((rows, 1), jnp.float32)
+    else:
+        sums = sum_in_ref[0]
+        totals = total_in_ref[0]
+    if key_parts:
+        keys = jnp.concatenate(key_parts, 0)
+        values = jnp.concatenate(value_parts, 0)
+        key_count = keys.shape[0]
+        prefix_len = sum(page.shape[0] for page in pages)
+        scores = lax.dot_general(queries, keys, (((1,), (1,)), ((), ())),
+                                 preferred_element_type=jnp.float32)
+        exps = capped_exp(scores)
+        column = lax.broadcasted_iota(jnp.int32, (rows, key_count), 1)
+        if pages:
+            page_len = pages[0].shape[0]
+            page_column = lax.broadcasted_iota(jnp.int32, (1, key_count), 1) // page_len
+            page_flag = jnp.zeros((1, key_count), jnp.int32)
+            for number in range(len(pages)):
+                page_flag = page_flag + jnp.where(
+                    page_column == number, valid_ref[first_block + number], 0)
+            page_flag = page_flag.astype(jnp.float32)
+        else:
+            page_flag = jnp.zeros((1, key_count), jnp.float32)
+        if first:
+            slot = lax.broadcasted_iota(jnp.int32, (rows, key_count), 0) % slots
+            suffix_pos = column - prefix_len
+            suffix_ok = (suffix_pos >= 0) & (suffix_pos <= slot) & (suffix_pos < length_ref[request])
+            raw = jnp.where(suffix_ok, exps, jnp.where(column < prefix_len, exps * page_flag, 0.0))
+        else:
+            raw = exps * page_flag
         totals = totals + jnp.sum(raw, -1, keepdims=True)
-        page_weights.append(raw)
-    scores = lax.dot_general(queries, fresh_keys, contract, preferred_element_type=jnp.float32)
-    column = lax.broadcasted_iota(jnp.int32, scores.shape, 1)
-    slot = lax.broadcasted_iota(jnp.int32, scores.shape, 0) % slots
-    allowed = (column <= slot) & (column < length_ref[request])
-    fresh_raw = jnp.where(allowed, capped_exp(scores), 0.0)
-    totals = totals + jnp.sum(fresh_raw, -1, keepdims=True)
-    inverse = 1.0 / totals
-    attended = jnp.dot((fresh_raw * inverse).astype(jnp.bfloat16), fresh_values,
-                       preferred_element_type=jnp.float32)
-    for raw, ref in zip(page_weights, page_refs):
-        attended = attended + jnp.dot((raw * inverse).astype(jnp.bfloat16), ref[:, HD:],
-                                      preferred_element_type=jnp.float32)
-    attended = attended.astype(jnp.bfloat16)
-    out_ref[0] = jnp.concatenate(
-        [attended[q * slots:(q + 1) * slots] for q in range(per_group)], 1)
-
-
-def attend(qkv, cosine, sine, blocks, lengths, valid, offset, count):
+        sums = sums + jnp.dot(raw.astype(jnp.bfloat16), values, preferred_element_type=jnp.float32)
+    if last:
+        attended = (sums / totals).astype(jnp.bfloat16)
+        outs[0][0] = jnp.concatenate(
+            [attended[q * slots:(q + 1) * slots] for q in range(per_group)], 1)
+    else:
+        outs[0][0] = sums
+        outs[1][0] = totals
+
+
+def attend(qkv, cosine, sine, blocks, lengths, valid, offset, count, first_block,
+           partial=None, last=True):
     _, slots, width = qkv.shape
     per_group = width // HD - 2
-    page_len, page_width = blocks[0].shape
+    rows = per_group * slots
+    first = partial is None
     full = lambda shape: pl.BlockSpec(shape, lambda r, *_: (0,) * len(shape))
+    per_request = lambda shape: pl.BlockSpec((1,) + shape, lambda r, *_: (r + offset, 0, 0))
+    in_specs = [per_request((slots, width)), full(cosine.shape), full(sine.shape)]
+    operands = [qkv, cosine, sine]
+    if not first:
+        in_specs += [per_request((rows, HD)), per_request((rows, 1))]
+        operands += list(partial)
+    in_specs += [full(block.shape) for block in blocks]
+    operands += list(blocks)
+    own_block = lambda shape: pl.BlockSpec((1,) + shape, lambda r, *_: (r, 0, 0))
+    if last:
+        out_specs = [own_block((slots, per_group * HD))]
+        out_shape = [jax.ShapeDtypeStruct((count, slots, per_group * HD), jnp.bfloat16)]
+    else:
+        out_specs = [own_block((rows, HD)), own_block((rows, 1))]
+        out_shape = [jax.ShapeDtypeStruct((count, rows, HD), jnp.float32),
+                     jax.ShapeDtypeStruct((count, rows, 1), jnp.float32)]
     grid_spec = pltpu.PrefetchScalarGridSpec(
-        num_scalar_prefetch=2,
-        grid=(count,),
-        in_specs=[pl.BlockSpec((1, slots, width), lambda r, *_: (r + offset, 0, 0)),
-                  full(cosine.shape), full(sine.shape)]
-                 + [full((page_len, page_width)) for _ in blocks],
-        out_specs=pl.BlockSpec((1, slots, per_group * HD), lambda r, *_: (r, 0, 0)),
-    )
-    return pl.pallas_call(
-        functools.partial(attention_kernel, offset=offset),
-        grid_spec=grid_spec,
-        out_shape=jax.ShapeDtypeStruct((count, slots, per_group * HD), jnp.bfloat16),
-    )(lengths, valid, qkv, cosine, sine, *blocks)
+        num_scalar_prefetch=2, grid=(count,), in_specs=in_specs, out_specs=out_specs)
+    kernel = functools.partial(attention_kernel, offset=offset, first_block=first_block,
+                               page_count=len(blocks), first=first, last=last)
+    result = pl.pallas_call(kernel, grid_spec=grid_spec, out_shape=out_shape)(
+        lengths, valid, *operands)
+    return result[0] if last else result
+
 
 def project(own, w_out, tp_index, n_tp, group_width):
     if n_tp == 4:
@@ -176,10 +216,16 @@
     cosine, sine = static_tables(prefix_len + np.arange(slots), HD)
     group_width = per_group * HD
     chunk = max(1, requests // 2)
+    early = min(len(blocks), 5)
+    qkv_rows = qkv[:, :, 0]
+    cos_in, sin_in = jnp.asarray(cosine), jnp.asarray(sine)
+    valid_in = valid.astype(jnp.int32)
+    partial = attend(qkv_rows, cos_in, sin_in, blocks[:early], my_lengths, valid_in,
+                     0, requests, 0, last=False)
     projected_parts = []
     for start in range(0, requests, chunk):
-        attended = attend(qkv[:, :, 0], jnp.asarray(cosine), jnp.asarray(sine), blocks,
-                          my_lengths, valid.astype(jnp.int32), start, chunk)
+        attended = attend(qkv_rows, cos_in, sin_in, blocks[early:], my_lengths, valid_in,
+                          start, chunk, early, partial=partial)
         own = attended.reshape(chunk * slots, per_group * HD)
         projected_parts.append(project(own, w_out, tp_index, n_tp, group_width))
     projected = jnp.concatenate(projected_parts, 0).reshape(requests, slots, local_width)

time: 54.7 us -> 53.1 us (0.971)
  waiting for transfers between devices: 13.7 us -> 9.88 us
  Pallas kernels: 11.6 us -> 12.8 us
  starting transfers between devices: 16.7 us -> 17.5 us
  local copies, waits for them, and re-layouts: 1.69 us -> 2.45 us
    ppermute x13, waiting for transfers between devices: 11.7 us -> 7.23 us  [swapped(): return lax.ppermute(value, axis, [(i, i ^ mask) for i in range(size)])]
    pallas_call x2 -> x3, Pallas kernels: 11.6 us -> 12.8 us  [attend(): pl.pallas_call(kernel, grid_spec=grid_spec, out_shape=out_shape)]
    unnamed x28, local copies, waits for them, and re-layouts: 0.88 us -> 1.64 us
    ppermute x3, waiting for transfers between devices: 1.96 us -> 2.65 us  [shifted(): lax.ppermute(value, axis, [(i, (i + shift) % size) for i in range(size)])]
    ppermute x13, starting transfers between devices: 14.7 us -> 15.3 us  [swapped(): return lax.ppermute(value, axis, [(i, i ^ mask) for i in range(size)])]
  transfers between devices with their start and end apart: 16 -> 16, of which waited for: 7 -> 6; matrix products, arithmetic and copies ran while one was open for 11% -> 11% of each run, Pallas kernels for 11% -> 17%
where the time goes in v10:
time: 53.1 us; the launch traced here: 52.8 us
  starting transfers between devices  17.5 us (33%)
  Pallas kernels  12.8 us (24%)
  waiting for transfers between devices  9.88 us (19%)
  other arithmetic  6.58 us (12%)
  matrix products  2.77 us (5%)
  local copies, waits for them, and re-layouts  2.45 us (5%)
  between operations  0.81 us (2%)
    ppermute x13, starting transfers between devices, swapped(): return lax.ppermute(value, axis, [(i, i ^ mask) for i in range(size)])  15.3 us
    pallas_call x3, Pallas kernels, attend(): pl.pallas_call(kernel, grid_spec=grid_spec, out_shape=out_shape)  12.8 us
    ppermute x13, waiting for transfers between devices, swapped(): return lax.ppermute(value, axis, [(i, i ^ mask) for i in range(size)])  7.23 us
    dot_general x8, matrix products, project(): term = jnp.dot(block, rows, preferred_element_type=jnp.float32)  2.77 us
    ppermute x3, waiting for transfers between devices, shifted(): lax.ppermute(value, axis, [(i, (i + shift) % size) for i in range(size)])  2.65 us
    ppermute x3, starting transfers between devices, shifted(): lax.ppermute(value, axis, [(i, (i + shift) % size) for i in range(size)])  2.21 us
    unnamed x28, local copies, waits for them, and re-layouts  1.64 us
    reduce_sum x1, other arithmetic, gather_prefix(): slot = jnp.sum(jnp.where(mine, page_slot, 0))  1.46 us
  transfers between devices with their start and end apart: 16, of which 6 were waited for; matrix products, arithmetic and copies ran while one was open for 11% of the time, Pallas kernels for 17%

profile of v10, /device:TPU:0, one launch (start us, length us, event | category | flops | bytes accessed | tf_op | source)
XLA Modules:
  0.0 52.8 jit_solution(14587950466209662989)
XLA Ops:
  0.0 1.5 %fusion.28 = s32[]{:T(128)} fusion(s32[8]{0:T(128)} %param.15, s32[8]{0:T(128)} %param.14, s32[]{:T(128)} %axis_index.27), kind=kLoop, calls=%fused_computation.42 | loop fusion | flops 23 | bytes 72 | tf_op jit(solution)/shard_map/reduce_sum | solution.py:36
  2.0 1.0 %select_bitcast_fusion.rest_0_ = bf16[128,512]{1,0:T(8,128)(2,1)S(1)} fusion(bf16[2,128,1,512]{3,1,2,0:T(8,128)(2,1)} %param.13, pred[]{:T(512)S(6)} %eq.43), kind=kLoop, calls=%fused_computation.26 | loop fusion | flops 65536 | bytes 393217 | tf_op jit(solution)/shard_map/jit(_where)/select_n | solution.py:39
  3.0 5.1 %collective-permute-start.3 = (bf16[128,512]{1,0:T(8,128)(2,1)S(1)}, bf16[128,512]{1,0:T(8,128)(2,1)S(1)}, u32[]{:S(2)}, u32[]{:S(2)}) collective-permute-start(bf16[128,512]{1,0:T(8,128)(2,1)S(1)} %select_bitcast_fusion.rest_0_), channel_id=1, source_target_pairs={{0,24},{4,28},{8,16},{12,20},{16,8},{20,12},{24,0},{28,4},{1,25},{... | collective-permute-start | bytes 393224 | tf_op jit(solution)/shard_map/ppermute | solution.py:28
  8.7 2.5 %collective-permute-start.1 = (bf16[128,512]{1,0:T(8,128)(2,1)S(1)}, bf16[128,512]{1,0:T(8,128)(2,1)S(1)}, u32[]{:S(2)}, u32[]{:S(2)}) collective-permute-start(bf16[128,512]{1,0:T(8,128)(2,1)S(1)} %select_bitcast_fusion.rest_0_), channel_id=1, source_target_pairs={{0,8},{4,12},{8,0},{12,4},{16,24},{20,28},{24,16},{28,20},{1,9},{5... | collective-permute-start | bytes 393224 | tf_op jit(solution)/shard_map/ppermute | solution.py:28
  11.7 0.8 %collective-permute-done.3.rest_4_ = bf16[128,512]{1,0:T(8,128)(2,1)S(1)} collective-permute-done((bf16[128,512]{1,0:T(8,128)(2,1)S(1)}, bf16[128,512]{1,0:T(8,128)(2,1)S(1)}, u32[]{:S(2)}, u32[]{:S(2)}) %collective-permute-start.3) | collective-permute-done | bytes 131104 | tf_op jit(solution)/shard_map/ppermute | solution.py:28
  12.6 2.6 %collective-permute-start.6 = (bf16[128,512]{1,0:T(8,128)(2,1)S(1)}, bf16[128,512]{1,0:T(8,128)(2,1)S(1)}, u32[]{:S(2)}, u32[]{:S(2)}) collective-permute-start(bf16[128,512]{1,0:T(8,128)(2,1)S(1)} %collective-permute-done.3.rest_4_), channel_id=1, source_target_pairs={{0,12},{4,8},{8,4},{12,0},{16,28},{20,24},{24,20},{28,16},{1,13},{... | collective-permute-start | bytes 393224 | tf_op jit(solution)/shard_map/ppermute | solution.py:28
  15.1 0.6 %collective-permute-start.5 = (bf16[128,512]{1,0:T(8,128)(2,1)S(1)}, bf16[128,512]{1,0:T(8,128)(2,1)S(1)}, u32[]{:S(2)}, u32[]{:S(2)}) collective-permute-start(bf16[128,512]{1,0:T(8,128)(2,1)S(1)} %collective-permute-done.3.rest_4_), channel_id=1, source_target_pairs={{0,8},{4,12},{8,0},{12,4},{16,24},{20,28},{24,16},{28,20},{1,9},{5... | collective-permute-start | bytes 393224 | tf_op jit(solution)/shard_map/ppermute | solution.py:28
  16.0 1.0 %collective-permute-start.4 = (bf16[128,512]{1,0:T(8,128)(2,1)S(1)}, bf16[128,512]{1,0:T(8,128)(2,1)S(1)}, u32[]{:S(2)}, u32[]{:S(2)}) collective-permute-start(bf16[128,512]{1,0:T(8,128)(2,1)S(1)} %collective-permute-done.3.rest_4_), channel_id=1, source_target_pairs={{0,4},{4,0},{8,12},{12,8},{16,20},{20,16},{24,28},{28,24},{1,5},{5... | collective-permute-start | bytes 393224 | tf_op jit(solution)/shard_map/ppermute | solution.py:28
  17.0 0.8 %compare_reduce_fusion = pred[8]{0:T(512)(128)(4,1)S(1)} fusion(s32[8]{0:T(128)} %param.14, s32[8]{0:T(128)S(1)} %stack.35), kind=kLoop, calls=%fused_computation.27 | loop fusion | flops 120 | bytes 72 | tf_op jit(solution)/shard_map/reduce_or | solution.py:55
  17.8 0.5 %convert_element_type.17.valid_ref = s32[8]{0:T(128)} convert(pred[8]{0:T(512)(128)(4,1)S(1)} %compare_reduce_fusion) | non-fusion elementwise | flops 8 | bytes 40 | tf_op jit(solution)/shard_map/convert_element_type | solution.py:222
  18.4 0.7 %dynamic_slice.19 = s32[4]{0:T(128)S(1)} dynamic-slice(s32[32]{0:T(128)} %param.17, s32[]{:T(128)S(6)} %select_n.37), dynamic_slice_sizes={4} | dynamic-slice | bytes 36 | tf_op jit(solution)/shard_map/dynamic_slice | solution.py:209
  19.1 1.3 %select_reduce_fusion.length_ref = s32[4]{0:T(128)} fusion(s32[32]{0:T(128)} %param.16, s32[4]{0:T(128)S(1)} %dynamic_slice.19), kind=kLoop, calls=%fused_computation.30 | loop fusion | flops 380 | bytes 160 | tf_op jit(solution)/shard_map/reduce_sum | solution.py:211
  20.5 0.6 %copy-done.10 = bf16[128,512]{1,0:T(8,128)(2,1)} copy-done((bf16[128,512]{1,0:T(8,128)(2,1)}, bf16[128,512]{1,0:T(8,128)(2,1)S(1)}, u32[]{:S(2)}) %copy-start.10) | copy-done | bytes 131096
  21.1 5.4 %shard_map.109 = (f32[4,256,256]{2,1,0:T(8,128)}, f32[4,256,1]{2,1,0:T(8,128)}) custom-call(s32[4]{0:T(128)} %select_reduce_fusion.length_ref, s32[8]{0:T(128)} %convert_element_type.17.valid_ref, bf16[4,128,1024]{2,1,0:T(8,128)(2,1)} %bitcast.35, f32[128,128]{1,0:T(8,128)} %constant.40.clone.cos_ref, f32[128,128]{1,0:T(8,128)} %constant.41.clone.sin_ref, ...), custom_call_target="tpu_custom_call" | custom-call | tf_op jit(solution)/shard_map/pallas_call | solution.py:174
  26.6 0.6 %copy-done.4 = bf16[128,512]{1,0:T(8,128)(2,1)} copy-done((bf16[128,512]{1,0:T(8,128)(2,1)}, bf16[128,512]{1,0:T(8,128)(2,1)S(1)}, u32[]{:S(2)}) %copy-start.4) | copy-done | bytes 131096
  27.3 3.7 %shard_map.111 = bf16[2,128,512]{2,1,0:T(8,128)(2,1)} custom-call(s32[4]{0:T(128)} %select_reduce_fusion.length_ref, s32[8]{0:T(128)} %convert_element_type.17.valid_ref, bf16[4,128,1024]{2,1,0:T(8,128)(2,1)} %bitcast.36, f32[128,128]{1,0:T(8,128)} %constant.40.clone.cos_ref, f32[128,128]{1,0:T(8,128)} %constant.41.clone.sin_ref, ...), custom_call_target="tpu_custom_call" | custom-call | tf_op jit(solution)/shard_map/pallas_call | solution.py:174
  31.0 1.5 %collective-permute-start.11 = (bf16[256,512]{1,0:T(8,128)(2,1)}, bf16[256,512]{1,0:T(8,128)(2,1)S(1)}, u32[]{:S(2)}, u32[]{:S(2)}) collective-permute-start(bf16[256,512]{1,0:T(8,128)(2,1)} %bitcast.41), channel_id=1, source_target_pairs={{0,2},{1,3},{2,0},{3,1},{4,6},{5,7},{6,4},{7,5},{8,10},{9,11},{10,... | collective-permute-start | bytes 786440 | tf_op jit(solution)/shard_map/ppermute | solution.py:28
  32.5 3.7 %shard_map.110 = bf16[2,128,512]{2,1,0:T(8,128)(2,1)} custom-call(s32[4]{0:T(128)} %select_reduce_fusion.length_ref, s32[8]{0:T(128)} %convert_element_type.17.valid_ref, bf16[4,128,1024]{2,1,0:T(8,128)(2,1)} %bitcast.37, f32[128,128]{1,0:T(8,128)} %constant.40.clone.cos_ref, f32[128,128]{1,0:T(8,128)} %constant.41.clone.sin_ref, ...), custom_call_target="tpu_custom_call" | custom-call | tf_op jit(solution)/shard_map/pallas_call | solution.py:174
  37.2 1.5 %collective-permute-done.11 = bf16[256,512]{1,0:T(8,128)(2,1)S(1)} collective-permute-done((bf16[256,512]{1,0:T(8,128)(2,1)}, bf16[256,512]{1,0:T(8,128)(2,1)S(1)}, u32[]{:S(2)}, u32[]{:S(2)}) %collective-permute-start.11) | collective-permute-done | bytes 262176 | tf_op jit(solution)/shard_map/ppermute | solution.py:28
  38.7 4.6 %collective-permute-done.8 = bf16[256,512]{1,0:T(8,128)(2,1)S(1)} collective-permute-done((bf16[256,512]{1,0:T(8,128)(2,1)}, bf16[256,512]{1,0:T(8,128)(2,1)S(1)}, u32[]{:S(2)}, u32[]{:S(2)}) %collective-permute-start.8) | collective-permute-done | bytes 262176 | tf_op jit(solution)/shard_map/ppermute | solution.py:28
  46.7 1.7 %collective-permute-start.14 = (f32[4,128]{1,0:T(4,128)S(1)}, f32[4,128]{1,0:T(4,128)S(1)}, u32[]{:S(2)}, u32[]{:S(2)}) collective-permute-start(f32[4,128]{1,0:T(4,128)S(1)} %bitcast.44), channel_id=1, source_target_pairs={{0,2},{1,3},{2,0},{3,1},{4,6},{5,7},{6,4},{7,5},{8,10},{9,11},{10,... | collective-permute-start | bytes 6152 | tf_op jit(solution)/shard_map/ppermute | solution.py:24
  49.0 1.4 %collective-permute-done.14 = f32[4,128]{1,0:T(4,128)S(1)} collective-permute-done((f32[4,128]{1,0:T(4,128)S(1)}, f32[4,128]{1,0:T(4,128)S(1)}, u32[]{:S(2)}, u32[]{:S(2)}) %collective-permute-start.14) | collective-permute-done | bytes 2080 | tf_op jit(solution)/shard_map/ppermute | solution.py:24
  50.4 1.3 %collective-permute-done.13 = f32[4,128]{1,0:T(4,128)S(1)} collective-permute-done((f32[4,128]{1,0:T(4,128)S(1)}, f32[4,128]{1,0:T(4,128)S(1)}, u32[]{:S(2)}, u32[]{:S(2)}) %collective-permute-start.13) | collective-permute-done | bytes 2080 | tf_op jit(solution)/shard_map/ppermute | solution.py:24
  51.7 1.1 %fusion.5 = bf16[4,128,576]{1,2,0:T(8,128)(2,1)} fusion(f32[72,4,8,128]{3,2,1,0:T(8,128)S(1)} %get-tuple-element.10, bf16[4,128,576]{1,2,0:T(8,128)(2,1)S(1)} %copy-done.3, f32[4,128]{1,0:T(4,128)S(1)} %fusion.19, f32[576]{0:T(1024)S(1)} %copy-done.13, f32[4,128]{1,0:T(4,128)S(1)} %add_rsqrt_fusion), kind=kLoop, calls=%fused_computation.10 | loop fusion | flops 1769472 | bytes 2365696 | tf_op jit(solution)/shard_map/convert_element_type | solution.py:239
  (58 shorter events, 6.5 us)
Async XLA Ops:
  0.0 43.3 %copy-start = (bf16[2048,576]{0,1:T(8,128)(2,1)S(1)}, bf16[2048,576]{0,1:T(8,128)(2,1)}, u32[]{:S(2)}) copy-start(bf16[2048,576]{0,1:T(8,128)(2,1)} %param.18) | copy-start | bytes 7077892
  3.0 17.4 %copy-start.7 = (bf16[128,512]{1,0:T(8,128)(2,1)}, bf16[128,512]{1,0:T(8,128)(2,1)S(1)}, u32[]{:S(2)}) copy-start(bf16[128,512]{1,0:T(8,128)(2,1)S(1)} %select_bitcast_fusion.rest_0_) | copy-start | bytes 393220
  3.0 9.5 %collective-permute-start.3 = (bf16[128,512]{1,0:T(8,128)(2,1)S(1)}, bf16[128,512]{1,0:T(8,128)(2,1)S(1)}, u32[]{:S(2)}, u32[]{:S(2)}) collective-permute-start(bf16[128,512]{1,0:T(8,128)(2,1)S(1)} %select_bitcast_fusion.rest_0_), channel_id=1, source_target_pairs={{0,24},{4,28},{8,16},{12,20},{16,8},{20,12},{24,0},{28,4},{1,25},{... | collective-permute-start | bytes 393224 | tf_op jit(solution)/shard_map/ppermute | solution.py:28
  8.2 7.8 %collective-permute-start.2 = (bf16[128,512]{1,0:T(8,128)(2,1)S(1)}, bf16[128,512]{1,0:T(8,128)(2,1)S(1)}, u32[]{:S(2)}, u32[]{:S(2)}) collective-permute-start(bf16[128,512]{1,0:T(8,128)(2,1)S(1)} %select_bitcast_fusion.rest_0_), channel_id=1, source_target_pairs={{0,12},{4,8},{8,4},{12,0},{16,28},{20,24},{24,20},{28,16},{1,13},{... | collective-permute-start | bytes 393224 | tf_op jit(solution)/shard_map/ppermute | solution.py:28
  8.7 11.8 %collective-permute-start.1 = (bf16[128,512]{1,0:T(8,128)(2,1)S(1)}, bf16[128,512]{1,0:T(8,128)(2,1)S(1)}, u32[]{:S(2)}, u32[]{:S(2)}) collective-permute-start(bf16[128,512]{1,0:T(8,128)(2,1)S(1)} %select_bitcast_fusion.rest_0_), channel_id=1, source_target_pairs={{0,8},{4,12},{8,0},{12,4},{16,24},{20,28},{24,16},{28,20},{1,9},{5... | collective-permute-start | bytes 393224 | tf_op jit(solution)/shard_map/ppermute | solution.py:28
  11.2 9.3 %collective-permute-start = (bf16[128,512]{1,0:T(8,128)(2,1)S(1)}, bf16[128,512]{1,0:T(8,128)(2,1)S(1)}, u32[]{:S(2)}, u32[]{:S(2)}) collective-permute-start(bf16[128,512]{1,0:T(8,128)(2,1)S(1)} %select_bitcast_fusion.rest_0_), channel_id=1, source_target_pairs={{0,4},{4,0},{8,12},{12,8},{16,20},{20,16},{24,28},{28,24},{1,5},{5... | collective-permute-start | bytes 393224 | tf_op jit(solution)/shard_map/ppermute | solution.py:28
  12.6 7.9 %copy-start.8 = (bf16[128,512]{1,0:T(8,128)(2,1)}, bf16[128,512]{1,0:T(8,128)(2,1)S(1)}, u32[]{:S(2)}) copy-start(bf16[128,512]{1,0:T(8,128)(2,1)S(1)} %collective-permute-done.3.rest_4_) | copy-start | bytes 393220
  12.6 13.9 %collective-permute-start.6 = (bf16[128,512]{1,0:T(8,128)(2,1)S(1)}, bf16[128,512]{1,0:T(8,128)(2,1)S(1)}, u32[]{:S(2)}, u32[]{:S(2)}) collective-permute-start(bf16[128,512]{1,0:T(8,128)(2,1)S(1)} %collective-permute-done.3.rest_4_), channel_id=1, source_target_pairs={{0,12},{4,8},{8,4},{12,0},{16,28},{20,24},{24,20},{28,16},{1,13},{... | collective-permute-start | bytes 393224 | tf_op jit(solution)/shard_map/ppermute | solution.py:28
  15.1 11.4 %collective-permute-start.5 = (bf16[128,512]{1,0:T(8,128)(2,1)S(1)}, bf16[128,512]{1,0:T(8,128)(2,1)S(1)}, u32[]{:S(2)}, u32[]{:S(2)}) collective-permute-start(bf16[128,512]{1,0:T(8,128)(2,1)S(1)} %collective-permute-done.3.rest_4_), channel_id=1, source_target_pairs={{0,8},{4,12},{8,0},{12,4},{16,24},{20,28},{24,16},{28,20},{1,9},{5... | collective-permute-start | bytes 393224 | tf_op jit(solution)/shard_map/ppermute | solution.py:28
  16.0 4.5 %copy-start.9 = (bf16[128,512]{1,0:T(8,128)(2,1)}, bf16[128,512]{1,0:T(8,128)(2,1)S(1)}, u32[]{:S(2)}) copy-start(bf16[128,512]{1,0:T(8,128)(2,1)S(1)} %collective-permute-done.2.rest_3_) | copy-start | bytes 393220
  16.0 10.5 %collective-permute-start.4 = (bf16[128,512]{1,0:T(8,128)(2,1)S(1)}, bf16[128,512]{1,0:T(8,128)(2,1)S(1)}, u32[]{:S(2)}, u32[]{:S(2)}) collective-permute-start(bf16[128,512]{1,0:T(8,128)(2,1)S(1)} %collective-permute-done.3.rest_4_), channel_id=1, source_target_pairs={{0,4},{4,0},{8,12},{12,8},{16,20},{20,16},{24,28},{28,24},{1,5},{5... | collective-permute-start | bytes 393224 | tf_op jit(solution)/shard_map/ppermute | solution.py:28
  31.0 5.7 %copy-start.2 = (bf16[2,128,512]{2,1,0:T(8,128)(2,1)S(1)}, bf16[2,128,512]{2,1,0:T(8,128)(2,1)}, u32[]{:S(2)}) copy-start(bf16[2,128,512]{2,1,0:T(8,128)(2,1)} %shard_map.111) | copy-start | bytes 786436
  31.0 7.8 %collective-permute-start.11 = (bf16[256,512]{1,0:T(8,128)(2,1)}, bf16[256,512]{1,0:T(8,128)(2,1)S(1)}, u32[]{:S(2)}, u32[]{:S(2)}) collective-permute-start(bf16[256,512]{1,0:T(8,128)(2,1)} %bitcast.41), channel_id=1, source_target_pairs={{0,2},{1,3},{2,0},{3,1},{4,6},{5,7},{6,4},{7,5},{8,10},{9,11},{10,... | collective-permute-start | bytes 786440 | tf_op jit(solution)/shard_map/ppermute | solution.py:28
  36.2 7.1 %collective-permute-start.8 = (bf16[256,512]{1,0:T(8,128)(2,1)}, bf16[256,512]{1,0:T(8,128)(2,1)S(1)}, u32[]{:S(2)}, u32[]{:S(2)}) collective-permute-start(bf16[256,512]{1,0:T(8,128)(2,1)} %bitcast.38), channel_id=1, source_target_pairs={{0,2},{1,3},{2,0},{3,1},{4,6},{5,7},{6,4},{7,5},{8,10},{9,11},{10,... | collective-permute-start | bytes 786440 | tf_op jit(solution)/shard_map/ppermute | solution.py:28
  36.7 7.3 %collective-permute-start.10 = (bf16[256,512]{1,0:T(8,128)(2,1)S(1)}, bf16[256,512]{1,0:T(8,128)(2,1)S(1)}, u32[]{:S(2)}, u32[]{:S(2)}) collective-permute-start(bf16[256,512]{1,0:T(8,128)(2,1)S(1)} %bitcast.42), channel_id=1, source_target_pairs={{0,1},{1,0},{2,3},{3,2},{4,5},{5,4},{6,7},{7,6},{8,9},{9,8},{10,11... | collective-permute-start | bytes 786440 | tf_op jit(solution)/shard_map/ppermute | solution.py:28
  36.7 8.1 %collective-permute-start.7 = (bf16[256,512]{1,0:T(8,128)(2,1)}, bf16[256,512]{1,0:T(8,128)(2,1)S(1)}, u32[]{:S(2)}, u32[]{:S(2)}) collective-permute-start(bf16[256,512]{1,0:T(8,128)(2,1)} %bitcast.39), channel_id=1, source_target_pairs={{0,1},{1,0},{2,3},{3,2},{4,5},{5,4},{6,7},{7,6},{8,9},{9,8},{10,11... | collective-permute-start | bytes 786440 | tf_op jit(solution)/shard_map/ppermute | solution.py:28
  38.7 6.9 %collective-permute-start.12 = (bf16[256,512]{1,0:T(8,128)(2,1)S(1)}, bf16[256,512]{1,0:T(8,128)(2,1)S(1)}, u32[]{:S(2)}, u32[]{:S(2)}) collective-permute-start(bf16[256,512]{1,0:T(8,128)(2,1)S(1)} %collective-permute-done.11), channel_id=1, source_target_pairs={{0,1},{1,0},{2,3},{3,2},{4,5},{5,4},{6,7},{7,6},{8,9},{9,8},{10,11... | collective-permute-start | bytes 786440 | tf_op jit(solution)/shard_map/ppermute | solution.py:28
  43.3 2.8 %collective-permute-start.9 = (bf16[256,512]{1,0:T(8,128)(2,1)S(1)}, bf16[256,512]{1,0:T(8,128)(2,1)S(1)}, u32[]{:S(2)}, u32[]{:S(2)}) collective-permute-start(bf16[256,512]{1,0:T(8,128)(2,1)S(1)} %collective-permute-done.8), channel_id=1, source_target_pairs={{0,1},{1,0},{2,3},{3,2},{4,5},{5,4},{6,7},{7,6},{8,9},{9,8},{10,11... | collective-permute-start | bytes 786440 | tf_op jit(solution)/shard_map/ppermute | solution.py:28
  46.1 2.9 %copy-start.12 = (s32[4]{0:T(128)S(1)}, s32[4]{0:T(128)}, u32[]{:S(2)}) copy-start(s32[4]{0:T(128)} %select_reduce_fusion.length_ref) | copy-start | bytes 52
  46.1 5.6 %copy-start.3 = (bf16[4,128,576]{1,2,0:T(8,128)(2,1)S(1)}, bf16[4,128,576]{1,2,0:T(8,128)(2,1)}, u32[]{:S(2)}) copy-start(bf16[4,128,576]{1,2,0:T(8,128)(2,1)} %param.11) | copy-start | bytes 1769476
  46.1 5.6 %copy-start.13 = (f32[576]{0:T(1024)S(1)}, f32[576]{0:T(1024)}, u32[]{:S(2)}) copy-start(f32[576]{0:T(1024)} %param.19) | copy-start | bytes 6916
  46.7 3.6 %collective-permute-start.14 = (f32[4,128]{1,0:T(4,128)S(1)}, f32[4,128]{1,0:T(4,128)S(1)}, u32[]{:S(2)}, u32[]{:S(2)}) collective-permute-start(f32[4,128]{1,0:T(4,128)S(1)} %bitcast.44), channel_id=1, source_target_pairs={{0,2},{1,3},{2,0},{3,1},{4,6},{5,7},{6,4},{7,5},{8,10},{9,11},{10,... | collective-permute-start | bytes 6152 | tf_op jit(solution)/shard_map/ppermute | solution.py:24
  48.4 2.0 %collective-permute-start.15 = (f32[4,128]{1,0:T(4,128)S(1)}, f32[4,128]{1,0:T(4,128)S(1)}, u32[]{:S(2)}, u32[]{:S(2)}) collective-permute-start(f32[4,128]{1,0:T(4,128)S(1)} %bitcast.45), channel_id=1, source_target_pairs={{0,3},{1,0},{2,1},{3,2},{4,7},{5,4},{6,5},{7,6},{8,11},{9,8},{10,9... | collective-permute-start | bytes 6152 | tf_op jit(solution)/shard_map/ppermute | solution.py:24
  48.6 3.0 %collective-permute-start.13 = (f32[4,128]{1,0:T(4,128)S(1)}, f32[4,128]{1,0:T(4,128)S(1)}, u32[]{:S(2)}, u32[]{:S(2)}) collective-permute-start(f32[4,128]{1,0:T(4,128)S(1)} %bitcast.46), channel_id=1, source_target_pairs={{0,1},{1,2},{2,3},{3,0},{4,5},{5,6},{6,7},{7,4},{8,9},{9,10},{10,1... | collective-permute-start | bytes 6152 | tf_op jit(solution)/shard_map/ppermute | solution.py:24
  (6 other events, 4.4 us)

commit v11 on v6

--- a/solution.py
+++ b/solution.py
@@ -98,19 +98,22 @@
 
     scores = lax.dot_general(queries, keys, (((1,), (1,)), ((), ())),
                              preferred_element_type=jnp.float32)
-    page_column = lax.broadcasted_iota(jnp.int32, (1, key_count), 1) // pages[0].shape[0]
-    page_flag = jnp.zeros((1, key_count), jnp.int32)
+    exps = capped_exp(scores)
+    page_len = pages[0].shape[0]
+    page_column = lax.broadcasted_iota(jnp.int32, (1, prefix_len), 1) // page_len
+    page_flag = jnp.zeros((1, prefix_len), jnp.int32)
     for index in range(len(pages)):
         page_flag = page_flag + jnp.where(page_column == index, valid_ref[index], 0)
-    page_flag = page_flag.astype(jnp.float32)
-    column = lax.broadcasted_iota(jnp.int32, (rows, key_count), 1)
-    slot = lax.broadcasted_iota(jnp.int32, (rows, key_count), 0) % slots
-    suffix_pos = column - prefix_len
-    suffix_ok = (suffix_pos >= 0) & (suffix_pos <= slot) & (suffix_pos < length_ref[request])
-    exps = capped_exp(scores)
-    raw = jnp.where(suffix_ok, exps, jnp.where(column < prefix_len, exps * page_flag, 0.0))
-    totals = jnp.sum(raw, -1, keepdims=True)
-    weights = (raw / totals).astype(jnp.bfloat16)
+    prefix_raw = exps[:, :prefix_len] * page_flag.astype(jnp.float32)
+    suffix_shape = (rows, key_count - prefix_len)
+    column = lax.broadcasted_iota(jnp.int32, suffix_shape, 1)
+    slot = lax.broadcasted_iota(jnp.int32, suffix_shape, 0) % slots
+    allowed = (column <= slot) & (column < length_ref[request])
+    suffix_raw = jnp.where(allowed, exps[:, prefix_len:], 0.0)
+    totals = jnp.sum(prefix_raw, -1, keepdims=True) + jnp.sum(suffix_raw, -1, keepdims=True)
+    inverse = 1.0 / totals
+    weights = jnp.concatenate([(prefix_raw * inverse).astype(jnp.bfloat16),
+                               (suffix_raw * inverse).astype(jnp.bfloat16)], 1)
     attended = jnp.dot(weights, values, preferred_element_type=jnp.float32).astype(jnp.bfloat16)
     out_ref[0] = jnp.concatenate(
         [attended[q * slots:(q + 1) * slots] for q in range(per_group)], 1)

time: 52.7 us -> 52.7 us (level)
  no operation moved by 1% of the time
where the time goes in v11:
time: 52.7 us; the launch traced here: 52.1 us
  starting transfers between devices  17.3 us (33%)
  waiting for transfers between devices  13.1 us (25%)
  Pallas kernels  9.58 us (18%)
  other arithmetic  6.71 us (13%)
  matrix products  2.8 us (5%)
  local copies, waits for them, and re-layouts  1.67 us (3%)
  between operations  0.92 us (2%)
    ppermute x13, starting transfers between devices, swapped(): return lax.ppermute(value, axis, [(i, i ^ mask) for i in range(size)])  14.7 us
    ppermute x13, waiting for transfers between devices, swapped(): return lax.ppermute(value, axis, [(i, i ^ mask) for i in range(size)])  11.7 us
    pallas_call x2, Pallas kernels, attend(): pl.pallas_call(functools.partial(attention_kernel, offset=offset), grid_s...  9.58 us
    dot_general x8, matrix products, project(): term = jnp.dot(block, rows, preferred_element_type=jnp.float32)  2.8 us
    ppermute x3, starting transfers between devices, shifted(): lax.ppermute(value, axis, [(i, (i + shift) % size) for i in range(size)])  2.61 us
    reduce_sum x1, other arithmetic, gather_prefix(): slot = jnp.sum(jnp.where(mine, page_slot, 0))  1.54 us
    ppermute x3, waiting for transfers between devices, shifted(): lax.ppermute(value, axis, [(i, (i + shift) % size) for i in range(size)])  1.43 us
    reduce_sum x1, other arithmetic, on_device(): my_lengths = jnp.sum(jnp.where(matches, lengths[None, :], 0), 1)  1.32 us
  transfers between devices with their start and end apart: 16, of which 8 were waited for; matrix products, arithmetic and copies ran while one was open for 12% of the time, Pallas kernels for 9%

profile of v11, /device:TPU:0, one launch (start us, length us, event | category | flops | bytes accessed | tf_op | source)
XLA Modules:
  0.0 52.1 jit_solution(12457545779793215730)
XLA Ops:
  0.0 1.5 %fusion.28 = s32[]{:T(128)} fusion(s32[8]{0:T(128)} %param.15, s32[8]{0:T(128)} %param.14, s32[]{:T(128)} %axis_index.27), kind=kLoop, calls=%fused_computation.42 | loop fusion | flops 23 | bytes 72 | tf_op jit(solution)/shard_map/reduce_sum | solution.py:36
  2.2 1.0 %select_bitcast_fusion.rest_0_ = bf16[128,512]{1,0:T(8,128)(2,1)S(1)} fusion(bf16[2,128,1,512]{3,1,2,0:T(8,128)(2,1)} %param.13, pred[]{:T(512)S(6)} %eq.43), kind=kLoop, calls=%fused_computation.26 | loop fusion | flops 65536 | bytes 393217 | tf_op jit(solution)/shard_map/jit(_where)/select_n | solution.py:39
  3.2 5.1 %collective-permute-start.3 = (bf16[128,512]{1,0:T(8,128)(2,1)S(1)}, bf16[128,512]{1,0:T(8,128)(2,1)S(1)}, u32[]{:S(2)}, u32[]{:S(2)}) collective-permute-start(bf16[128,512]{1,0:T(8,128)(2,1)S(1)} %select_bitcast_fusion.rest_0_), channel_id=1, source_target_pairs={{0,24},{4,28},{8,16},{12,20},{16,8},{20,12},{24,0},{28,4},{1,25},{... | collective-permute-start | bytes 393224 | tf_op jit(solution)/shard_map/ppermute | solution.py:28
  8.4 1.5 %collective-permute-start = (bf16[128,512]{1,0:T(8,128)(2,1)S(1)}, bf16[128,512]{1,0:T(8,128)(2,1)S(1)}, u32[]{:S(2)}, u32[]{:S(2)}) collective-permute-start(bf16[128,512]{1,0:T(8,128)(2,1)S(1)} %select_bitcast_fusion.rest_0_), channel_id=1, source_target_pairs={{0,4},{4,0},{8,12},{12,8},{16,20},{20,16},{24,28},{28,24},{1,5},{5... | collective-permute-start | bytes 393224 | tf_op jit(solution)/shard_map/ppermute | solution.py:28
  9.9 2.0 %collective-permute-start.2 = (bf16[128,512]{1,0:T(8,128)(2,1)S(1)}, bf16[128,512]{1,0:T(8,128)(2,1)S(1)}, u32[]{:S(2)}, u32[]{:S(2)}) collective-permute-start(bf16[128,512]{1,0:T(8,128)(2,1)S(1)} %select_bitcast_fusion.rest_0_), channel_id=1, source_target_pairs={{0,12},{4,8},{8,4},{12,0},{16,28},{20,24},{24,20},{28,16},{1,13},{... | collective-permute-start | bytes 393224 | tf_op jit(solution)/shard_map/ppermute | solution.py:28
  12.0 0.8 %collective-permute-done.3.rest_4_ = bf16[128,512]{1,0:T(8,128)(2,1)S(1)} collective-permute-done((bf16[128,512]{1,0:T(8,128)(2,1)S(1)}, bf16[128,512]{1,0:T(8,128)(2,1)S(1)}, u32[]{:S(2)}, u32[]{:S(2)}) %collective-permute-start.3) | collective-permute-done | bytes 131104 | tf_op jit(solution)/shard_map/ppermute | solution.py:28
  12.8 1.7 %collective-permute-start.4 = (bf16[128,512]{1,0:T(8,128)(2,1)S(1)}, bf16[128,512]{1,0:T(8,128)(2,1)S(1)}, u32[]{:S(2)}, u32[]{:S(2)}) collective-permute-start(bf16[128,512]{1,0:T(8,128)(2,1)S(1)} %collective-permute-done.3.rest_4_), channel_id=1, source_target_pairs={{0,4},{4,0},{8,12},{12,8},{16,20},{20,16},{24,28},{28,24},{1,5},{5... | collective-permute-start | bytes 393224 | tf_op jit(solution)/shard_map/ppermute | solution.py:28
  14.5 1.5 %collective-permute-start.5 = (bf16[128,512]{1,0:T(8,128)(2,1)S(1)}, bf16[128,512]{1,0:T(8,128)(2,1)S(1)}, u32[]{:S(2)}, u32[]{:S(2)}) collective-permute-start(bf16[128,512]{1,0:T(8,128)(2,1)S(1)} %collective-permute-done.3.rest_4_), channel_id=1, source_target_pairs={{0,8},{4,12},{8,0},{12,4},{16,24},{20,28},{24,16},{28,20},{1,9},{5... | collective-permute-start | bytes 393224 | tf_op jit(solution)/shard_map/ppermute | solution.py:28
  16.3 0.8 %compare_reduce_fusion = pred[8]{0:T(512)(128)(4,1)S(1)} fusion(s32[8]{0:T(128)} %param.14, s32[8]{0:T(128)S(1)} %stack.35), kind=kLoop, calls=%fused_computation.27 | loop fusion | flops 120 | bytes 72 | tf_op jit(solution)/shard_map/reduce_or | solution.py:55
  17.1 0.6 %convert_element_type.18.valid_ref = s32[8]{0:T(128)} convert(pred[8]{0:T(512)(128)(4,1)S(1)} %compare_reduce_fusion) | non-fusion elementwise | flops 8 | bytes 40 | tf_op jit(solution)/shard_map/convert_element_type | solution.py:184
  17.7 0.7 %dynamic_slice.19 = s32[4]{0:T(128)S(1)} dynamic-slice(s32[32]{0:T(128)} %param.17, s32[]{:T(128)S(6)} %select_n.37), dynamic_slice_sizes={4} | dynamic-slice | bytes 36 | tf_op jit(solution)/shard_map/dynamic_slice | solution.py:171
  18.4 1.3 %select_reduce_fusion.length_ref = s32[4]{0:T(128)} fusion(s32[32]{0:T(128)} %param.16, s32[4]{0:T(128)S(1)} %dynamic_slice.19), kind=kLoop, calls=%fused_computation.30 | loop fusion | flops 380 | bytes 160 | tf_op jit(solution)/shard_map/reduce_sum | solution.py:173
  19.9 2.0 %collective-permute-done.5.rest_6_ = bf16[128,512]{1,0:T(8,128)(2,1)S(1)} collective-permute-done((bf16[128,512]{1,0:T(8,128)(2,1)S(1)}, bf16[128,512]{1,0:T(8,128)(2,1)S(1)}, u32[]{:S(2)}, u32[]{:S(2)}) %collective-permute-start.5) | collective-permute-done | bytes 131104 | tf_op jit(solution)/shard_map/ppermute | solution.py:28
  21.9 2.3 %collective-permute-done.6.rest_7_ = bf16[128,512]{1,0:T(8,128)(2,1)S(1)} collective-permute-done((bf16[128,512]{1,0:T(8,128)(2,1)S(1)}, bf16[128,512]{1,0:T(8,128)(2,1)S(1)}, u32[]{:S(2)}, u32[]{:S(2)}) %collective-permute-start.6) | collective-permute-done | bytes 131104 | tf_op jit(solution)/shard_map/ppermute | solution.py:28
  24.3 0.6 %copy-done.11 = bf16[128,512]{1,0:T(8,128)(2,1)} copy-done((bf16[128,512]{1,0:T(8,128)(2,1)}, bf16[128,512]{1,0:T(8,128)(2,1)S(1)}, u32[]{:S(2)}) %copy-start.11) | copy-done | bytes 131096
  24.9 4.8 %shard_map.109 = bf16[2,128,512]{2,1,0:T(8,128)(2,1)} custom-call(s32[4]{0:T(128)} %select_reduce_fusion.length_ref, s32[8]{0:T(128)} %convert_element_type.18.valid_ref, bf16[4,128,1024]{2,1,0:T(8,128)(2,1)} %bitcast.35, f32[128,128]{1,0:T(8,128)} %constant.40.clone.cos_ref, f32[128,128]{1,0:T(8,128)} %constant.41.clone.sin_ref, ...), custom_call_target="tpu_custom_call" | custom-call | tf_op jit(solution)/shard_map/pallas_call | solution.py:135
  29.6 1.4 %collective-permute-start.8 = (bf16[256,512]{1,0:T(8,128)(2,1)}, bf16[256,512]{1,0:T(8,128)(2,1)S(1)}, u32[]{:S(2)}, u32[]{:S(2)}) collective-permute-start(bf16[256,512]{1,0:T(8,128)(2,1)} %bitcast.40), channel_id=1, source_target_pairs={{0,2},{1,3},{2,0},{3,1},{4,6},{5,7},{6,4},{7,5},{8,10},{9,11},{10,... | collective-permute-start | bytes 786440 | tf_op jit(solution)/shard_map/ppermute | solution.py:28
  31.1 4.8 %shard_map.110 = bf16[2,128,512]{2,1,0:T(8,128)(2,1)} custom-call(s32[4]{0:T(128)} %select_reduce_fusion.length_ref, s32[8]{0:T(128)} %convert_element_type.18.valid_ref, bf16[4,128,1024]{2,1,0:T(8,128)(2,1)} %bitcast.36, f32[128,128]{1,0:T(8,128)} %constant.40.clone.cos_ref, f32[128,128]{1,0:T(8,128)} %constant.41.clone.sin_ref, ...), custom_call_target="tpu_custom_call" | custom-call | tf_op jit(solution)/shard_map/pallas_call | solution.py:135
  35.9 0.6 %collective-permute-start.11 = (bf16[256,512]{1,0:T(8,128)(2,1)}, bf16[256,512]{1,0:T(8,128)(2,1)S(1)}, u32[]{:S(2)}, u32[]{:S(2)}) collective-permute-start(bf16[256,512]{1,0:T(8,128)(2,1)} %bitcast.37), channel_id=1, source_target_pairs={{0,2},{1,3},{2,0},{3,1},{4,6},{5,7},{6,4},{7,5},{8,10},{9,11},{10,... | collective-permute-start | bytes 786440 | tf_op jit(solution)/shard_map/ppermute | solution.py:28
  37.5 6.0 %collective-permute-done.11 = bf16[256,512]{1,0:T(8,128)(2,1)S(1)} collective-permute-done((bf16[256,512]{1,0:T(8,128)(2,1)}, bf16[256,512]{1,0:T(8,128)(2,1)S(1)}, u32[]{:S(2)}, u32[]{:S(2)}) %collective-permute-start.11) | collective-permute-done | bytes 262176 | tf_op jit(solution)/shard_map/ppermute | solution.py:28
  47.4 1.1 %collective-permute-start.14 = (f32[4,128]{1,0:T(4,128)S(1)}, f32[4,128]{1,0:T(4,128)S(1)}, u32[]{:S(2)}, u32[]{:S(2)}) collective-permute-start(f32[4,128]{1,0:T(4,128)S(1)} %bitcast.44), channel_id=1, source_target_pairs={{0,2},{1,3},{2,0},{3,1},{4,6},{5,7},{6,4},{7,5},{8,10},{9,11},{10,... | collective-permute-start | bytes 6152 | tf_op jit(solution)/shard_map/ppermute | solution.py:24
  48.5 1.0 %collective-permute-start.15 = (f32[4,128]{1,0:T(4,128)S(1)}, f32[4,128]{1,0:T(4,128)S(1)}, u32[]{:S(2)}, u32[]{:S(2)}) collective-permute-start(f32[4,128]{1,0:T(4,128)S(1)} %bitcast.45), channel_id=1, source_target_pairs={{0,3},{1,0},{2,1},{3,2},{4,7},{5,4},{6,5},{7,6},{8,11},{9,8},{10,9... | collective-permute-start | bytes 6152 | tf_op jit(solution)/shard_map/ppermute | solution.py:24
  49.9 1.1 %collective-permute-done.14 = f32[4,128]{1,0:T(4,128)S(1)} collective-permute-done((f32[4,128]{1,0:T(4,128)S(1)}, f32[4,128]{1,0:T(4,128)S(1)}, u32[]{:S(2)}, u32[]{:S(2)}) %collective-permute-start.14) | collective-permute-done | bytes 2080 | tf_op jit(solution)/shard_map/ppermute | solution.py:24
  51.0 1.1 %fusion.5 = bf16[4,128,576]{1,2,0:T(8,128)(2,1)} fusion(f32[72,4,8,128]{3,2,1,0:T(8,128)S(1)} %get-tuple-element.6, bf16[4,128,576]{1,2,0:T(8,128)(2,1)S(1)} %copy-done.4, f32[4,128]{1,0:T(4,128)S(1)} %fusion.19, f32[576]{0:T(1024)S(1)} %copy-done.13, f32[4,128]{1,0:T(4,128)S(1)} %add_rsqrt_fusion), kind=kLoop, calls=%fused_computation.10 | loop fusion | flops 1769472 | bytes 2365696 | tf_op jit(solution)/shard_map/convert_element_type | solution.py:195
  (57 shorter events, 5.9 us)
Async XLA Ops:
  0.0 43.4 %copy-start = (bf16[2048,576]{0,1:T(8,128)(2,1)S(1)}, bf16[2048,576]{0,1:T(8,128)(2,1)}, u32[]{:S(2)}) copy-start(bf16[2048,576]{0,1:T(8,128)(2,1)} %param.18) | copy-start | bytes 7077892
  3.2 21.0 %copy-start.1 = (bf16[128,512]{1,0:T(8,128)(2,1)}, bf16[128,512]{1,0:T(8,128)(2,1)S(1)}, u32[]{:S(2)}) copy-start(bf16[128,512]{1,0:T(8,128)(2,1)S(1)} %select_bitcast_fusion.rest_0_) | copy-start | bytes 393220
  3.2 9.5 %collective-permute-start.3 = (bf16[128,512]{1,0:T(8,128)(2,1)S(1)}, bf16[128,512]{1,0:T(8,128)(2,1)S(1)}, u32[]{:S(2)}, u32[]{:S(2)}) collective-permute-start(bf16[128,512]{1,0:T(8,128)(2,1)S(1)} %select_bitcast_fusion.rest_0_), channel_id=1, source_target_pairs={{0,24},{4,28},{8,16},{12,20},{16,8},{20,12},{24,0},{28,4},{1,25},{... | collective-permute-start | bytes 393224 | tf_op jit(solution)/shard_map/ppermute | solution.py:28
  8.4 7.5 %collective-permute-start = (bf16[128,512]{1,0:T(8,128)(2,1)S(1)}, bf16[128,512]{1,0:T(8,128)(2,1)S(1)}, u32[]{:S(2)}, u32[]{:S(2)}) collective-permute-start(bf16[128,512]{1,0:T(8,128)(2,1)S(1)} %select_bitcast_fusion.rest_0_), channel_id=1, source_target_pairs={{0,4},{4,0},{8,12},{12,8},{16,20},{20,16},{24,28},{28,24},{1,5},{5... | collective-permute-start | bytes 393224 | tf_op jit(solution)/shard_map/ppermute | solution.py:28
  9.9 9.9 %collective-permute-start.1 = (bf16[128,512]{1,0:T(8,128)(2,1)S(1)}, bf16[128,512]{1,0:T(8,128)(2,1)S(1)}, u32[]{:S(2)}, u32[]{:S(2)}) collective-permute-start(bf16[128,512]{1,0:T(8,128)(2,1)S(1)} %select_bitcast_fusion.rest_0_), channel_id=1, source_target_pairs={{0,8},{4,12},{8,0},{12,4},{16,24},{20,28},{24,16},{28,20},{1,9},{5... | collective-permute-start | bytes 393224 | tf_op jit(solution)/shard_map/ppermute | solution.py:28
  9.9 9.9 %collective-permute-start.2 = (bf16[128,512]{1,0:T(8,128)(2,1)S(1)}, bf16[128,512]{1,0:T(8,128)(2,1)S(1)}, u32[]{:S(2)}, u32[]{:S(2)}) collective-permute-start(bf16[128,512]{1,0:T(8,128)(2,1)S(1)} %select_bitcast_fusion.rest_0_), channel_id=1, source_target_pairs={{0,12},{4,8},{8,4},{12,0},{16,28},{20,24},{24,20},{28,16},{1,13},{... | collective-permute-start | bytes 393224 | tf_op jit(solution)/shard_map/ppermute | solution.py:28
  12.8 11.4 %copy-start.5 = (bf16[128,512]{1,0:T(8,128)(2,1)}, bf16[128,512]{1,0:T(8,128)(2,1)S(1)}, u32[]{:S(2)}) copy-start(bf16[128,512]{1,0:T(8,128)(2,1)S(1)} %collective-permute-done.3.rest_4_) | copy-start | bytes 393220
  12.8 7.1 %collective-permute-start.4 = (bf16[128,512]{1,0:T(8,128)(2,1)S(1)}, bf16[128,512]{1,0:T(8,128)(2,1)S(1)}, u32[]{:S(2)}, u32[]{:S(2)}) collective-permute-start(bf16[128,512]{1,0:T(8,128)(2,1)S(1)} %collective-permute-done.3.rest_4_), channel_id=1, source_target_pairs={{0,4},{4,0},{8,12},{12,8},{16,20},{20,16},{24,28},{28,24},{1,5},{5... | collective-permute-start | bytes 393224 | tf_op jit(solution)/shard_map/ppermute | solution.py:28
  14.5 7.4 %collective-permute-start.5 = (bf16[128,512]{1,0:T(8,128)(2,1)S(1)}, bf16[128,512]{1,0:T(8,128)(2,1)S(1)}, u32[]{:S(2)}, u32[]{:S(2)}) collective-permute-start(bf16[128,512]{1,0:T(8,128)(2,1)S(1)} %collective-permute-done.3.rest_4_), channel_id=1, source_target_pairs={{0,8},{4,12},{8,0},{12,4},{16,24},{20,28},{24,16},{28,20},{1,9},{5... | collective-permute-start | bytes 393224 | tf_op jit(solution)/shard_map/ppermute | solution.py:28
  15.9 8.3 %copy-start.6 = (bf16[128,512]{1,0:T(8,128)(2,1)}, bf16[128,512]{1,0:T(8,128)(2,1)S(1)}, u32[]{:S(2)}) copy-start(bf16[128,512]{1,0:T(8,128)(2,1)S(1)} %collective-permute-done.rest_1_) | copy-start | bytes 393220
  15.9 8.3 %collective-permute-start.6 = (bf16[128,512]{1,0:T(8,128)(2,1)S(1)}, bf16[128,512]{1,0:T(8,128)(2,1)S(1)}, u32[]{:S(2)}, u32[]{:S(2)}) collective-permute-start(bf16[128,512]{1,0:T(8,128)(2,1)S(1)} %collective-permute-done.3.rest_4_), channel_id=1, source_target_pairs={{0,12},{4,8},{8,4},{12,0},{16,28},{20,24},{24,20},{28,16},{1,13},{... | collective-permute-start | bytes 393224 | tf_op jit(solution)/shard_map/ppermute | solution.py:28
  19.8 4.5 %copy-start.8 = (bf16[128,512]{1,0:T(8,128)(2,1)}, bf16[128,512]{1,0:T(8,128)(2,1)S(1)}, u32[]{:S(2)}) copy-start(bf16[128,512]{1,0:T(8,128)(2,1)S(1)} %collective-permute-done.2.rest_3_) | copy-start | bytes 393220
  29.6 6.8 %copy-start.3 = (bf16[2,128,512]{2,1,0:T(8,128)(2,1)S(1)}, bf16[2,128,512]{2,1,0:T(8,128)(2,1)}, u32[]{:S(2)}) copy-start(bf16[2,128,512]{2,1,0:T(8,128)(2,1)} %shard_map.109) | copy-start | bytes 786436
  29.6 7.8 %collective-permute-start.8 = (bf16[256,512]{1,0:T(8,128)(2,1)}, bf16[256,512]{1,0:T(8,128)(2,1)S(1)}, u32[]{:S(2)}, u32[]{:S(2)}) collective-permute-start(bf16[256,512]{1,0:T(8,128)(2,1)} %bitcast.40), channel_id=1, source_target_pairs={{0,2},{1,3},{2,0},{3,1},{4,6},{5,7},{6,4},{7,5},{8,10},{9,11},{10,... | collective-permute-start | bytes 786440 | tf_op jit(solution)/shard_map/ppermute | solution.py:28
  35.9 7.5 %collective-permute-start.11 = (bf16[256,512]{1,0:T(8,128)(2,1)}, bf16[256,512]{1,0:T(8,128)(2,1)S(1)}, u32[]{:S(2)}, u32[]{:S(2)}) collective-permute-start(bf16[256,512]{1,0:T(8,128)(2,1)} %bitcast.37), channel_id=1, source_target_pairs={{0,2},{1,3},{2,0},{3,1},{4,6},{5,7},{6,4},{7,5},{8,10},{9,11},{10,... | collective-permute-start | bytes 786440 | tf_op jit(solution)/shard_map/ppermute | solution.py:28
  36.5 7.7 %collective-permute-start.7 = (bf16[256,512]{1,0:T(8,128)(2,1)S(1)}, bf16[256,512]{1,0:T(8,128)(2,1)S(1)}, u32[]{:S(2)}, u32[]{:S(2)}) collective-permute-start(bf16[256,512]{1,0:T(8,128)(2,1)S(1)} %bitcast.41), channel_id=1, source_target_pairs={{0,1},{1,0},{2,3},{3,2},{4,5},{5,4},{6,7},{7,6},{8,9},{9,8},{10,11... | collective-permute-start | bytes 786440 | tf_op jit(solution)/shard_map/ppermute | solution.py:28
  36.5 8.4 %collective-permute-start.10 = (bf16[256,512]{1,0:T(8,128)(2,1)}, bf16[256,512]{1,0:T(8,128)(2,1)S(1)}, u32[]{:S(2)}, u32[]{:S(2)}) collective-permute-start(bf16[256,512]{1,0:T(8,128)(2,1)} %bitcast.38), channel_id=1, source_target_pairs={{0,1},{1,0},{2,3},{3,2},{4,5},{5,4},{6,7},{7,6},{8,9},{9,8},{10,11... | collective-permute-start | bytes 786440 | tf_op jit(solution)/shard_map/ppermute | solution.py:28
  37.5 8.4 %collective-permute-start.9 = (bf16[256,512]{1,0:T(8,128)(2,1)S(1)}, bf16[256,512]{1,0:T(8,128)(2,1)S(1)}, u32[]{:S(2)}, u32[]{:S(2)}) collective-permute-start(bf16[256,512]{1,0:T(8,128)(2,1)S(1)} %collective-permute-done.8), channel_id=1, source_target_pairs={{0,1},{1,0},{2,3},{3,2},{4,5},{5,4},{6,7},{7,6},{8,9},{9,8},{10,11... | collective-permute-start | bytes 786440 | tf_op jit(solution)/shard_map/ppermute | solution.py:28
  43.4 2.8 %collective-permute-start.12 = (bf16[256,512]{1,0:T(8,128)(2,1)S(1)}, bf16[256,512]{1,0:T(8,128)(2,1)S(1)}, u32[]{:S(2)}, u32[]{:S(2)}) collective-permute-start(bf16[256,512]{1,0:T(8,128)(2,1)S(1)} %collective-permute-done.11), channel_id=1, source_target_pairs={{0,1},{1,0},{2,3},{3,2},{4,5},{5,4},{6,7},{7,6},{8,9},{9,8},{10,11... | collective-permute-start | bytes 786440 | tf_op jit(solution)/shard_map/ppermute | solution.py:28
  46.2 4.8 %copy-start.4 = (bf16[4,128,576]{1,2,0:T(8,128)(2,1)S(1)}, bf16[4,128,576]{1,2,0:T(8,128)(2,1)}, u32[]{:S(2)}) copy-start(bf16[4,128,576]{1,2,0:T(8,128)(2,1)} %param.11) | copy-start | bytes 1769476
  46.2 4.8 %copy-start.13 = (f32[576]{0:T(1024)S(1)}, f32[576]{0:T(1024)}, u32[]{:S(2)}) copy-start(f32[576]{0:T(1024)} %param.19) | copy-start | bytes 6916
  46.8 3.1 %collective-permute-start.13 = (f32[4,128]{1,0:T(4,128)S(1)}, f32[4,128]{1,0:T(4,128)S(1)}, u32[]{:S(2)}, u32[]{:S(2)}) collective-permute-start(f32[4,128]{1,0:T(4,128)S(1)} %bitcast.43), channel_id=1, source_target_pairs={{0,1},{1,2},{2,3},{3,0},{4,5},{5,6},{6,7},{7,4},{8,9},{9,10},{10,1... | collective-permute-start | bytes 6152 | tf_op jit(solution)/shard_map/ppermute | solution.py:24
  47.4 3.6 %collective-permute-start.14 = (f32[4,128]{1,0:T(4,128)S(1)}, f32[4,128]{1,0:T(4,128)S(1)}, u32[]{:S(2)}, u32[]{:S(2)}) collective-permute-start(f32[4,128]{1,0:T(4,128)S(1)} %bitcast.44), channel_id=1, source_target_pairs={{0,2},{1,3},{2,0},{3,1},{4,6},{5,7},{6,4},{7,5},{8,10},{9,11},{10,... | collective-permute-start | bytes 6152 | tf_op jit(solution)/shard_map/ppermute | solution.py:24
  48.5 2.5 %collective-permute-start.15 = (f32[4,128]{1,0:T(4,128)S(1)}, f32[4,128]{1,0:T(4,128)S(1)}, u32[]{:S(2)}, u32[]{:S(2)}) collective-permute-start(f32[4,128]{1,0:T(4,128)S(1)} %bitcast.45), channel_id=1, source_target_pairs={{0,3},{1,0},{2,1},{3,2},{4,7},{5,4},{6,5},{7,6},{8,11},{9,8},{10,9... | collective-permute-start | bytes 6152 | tf_op jit(solution)/shard_map/ppermute | solution.py:24
  (6 other events, 16.1 us)

commit v12 on v11

--- a/solution.py
+++ b/solution.py
@@ -70,7 +70,7 @@
 
 
 def attention_kernel(length_ref, valid_ref, qkv_ref, cos_ref, sin_ref, *rest, offset):
-    page_refs, out_ref = rest[:-1], rest[-1]
+    page_refs, out_ref, key_scratch, value_scratch = rest[:-3], rest[-3], rest[-2], rest[-1]
     request = pl.program_id(0) + offset
     slots = qkv_ref.shape[1]
     per_group = qkv_ref.shape[2] // HD - 2
@@ -89,20 +89,28 @@
          for q in range(per_group)], 0)
     fresh_keys = rope(values_in[:, per_group * HD:(per_group + 1) * HD]).astype(jnp.bfloat16)
     fresh_values = values_in[:, (per_group + 1) * HD:].astype(jnp.bfloat16)
-    pages = [ref[...] for ref in page_refs]
-    keys = jnp.concatenate([page[:, :HD] for page in pages] + [fresh_keys], 0)
-    values = jnp.concatenate([page[:, HD:] for page in pages] + [fresh_values], 0)
-    prefix_len = len(pages) * pages[0].shape[0]
+    page_len = page_refs[0].shape[0]
+    prefix_len = len(page_refs) * page_len
+
+    @pl.when(pl.program_id(0) == 0)
+    def _():
+        for index, ref in enumerate(page_refs):
+            key_scratch[index * page_len:(index + 1) * page_len] = ref[:, :HD]
+            value_scratch[index * page_len:(index + 1) * page_len] = ref[:, HD:]
+
+    key_scratch[prefix_len:] = fresh_keys
+    value_scratch[prefix_len:] = fresh_values
+    keys = key_scratch[...]
+    values = value_scratch[...]
     key_count = keys.shape[0]
     rows = queries.shape[0]
 
     scores = lax.dot_general(queries, keys, (((1,), (1,)), ((), ())),
                              preferred_element_type=jnp.float32)
     exps = capped_exp(scores)
-    page_len = pages[0].shape[0]
     page_column = lax.broadcasted_iota(jnp.int32, (1, prefix_len), 1) // page_len
     page_flag = jnp.zeros((1, prefix_len), jnp.int32)
-    for index in range(len(pages)):
+    for index in range(len(page_refs)):
         page_flag = page_flag + jnp.where(page_column == index, valid_ref[index], 0)
     prefix_raw = exps[:, :prefix_len] * page_flag.astype(jnp.float32)
     suffix_shape = (rows, key_count - prefix_len)
@@ -131,6 +139,8 @@
                   full(cosine.shape), full(sine.shape)]
                  + [full((page_len, page_width)) for _ in blocks],
         out_specs=pl.BlockSpec((1, slots, per_group * HD), lambda r, *_: (r, 0, 0)),
+        scratch_shapes=[pltpu.VMEM((len(blocks) * page_len + slots, HD), jnp.bfloat16),
+                        pltpu.VMEM((len(blocks) * page_len + slots, HD), jnp.bfloat16)],
     )
     return pl.pallas_call(
         functools.partial(attention_kernel, offset=offset),

time: 52.7 us -> 53.2 us (level)
  transfers between devices with their start and end apart: 16 -> 16, of which waited for: 8 -> 8; matrix products, arithmetic and copies ran while one was open for 12% -> 12% of each run, Pallas kernels for 9% -> 10%
where the time goes in v12:
time: 53.2 us; the launch traced here: 52.6 us
  starting transfers between devices  17 us (32%)
  waiting for transfers between devices  13.4 us (25%)
  Pallas kernels  10.1 us (19%)
  other arithmetic  6.71 us (13%)
  matrix products  2.78 us (5%)
  local copies, waits for them, and re-layouts  1.67 us (3%)
  between operations  0.92 us (2%)
    ppermute x13, starting transfers between devices, swapped(): return lax.ppermute(value, axis, [(i, i ^ mask) for i in range(size)])  14.7 us
    ppermute x13, waiting for transfers between devices, swapped(): return lax.ppermute(value, axis, [(i, i ^ mask) for i in range(size)])  11.7 us
    pallas_call x2, Pallas kernels, attend(): pl.pallas_call(functools.partial(attention_kernel, offset=offset), grid_s...  10.1 us
    dot_general x8, matrix products, project(): term = jnp.dot(block, rows, preferred_element_type=jnp.float32)  2.78 us
    ppermute x3, starting transfers between devices, shifted(): lax.ppermute(value, axis, [(i, (i + shift) % size) for i in range(size)])  2.35 us
    ppermute x3, waiting for transfers between devices, shifted(): lax.ppermute(value, axis, [(i, (i + shift) % size) for i in range(size)])  1.71 us
    reduce_sum x1, other arithmetic, gather_prefix(): slot = jnp.sum(jnp.where(mine, page_slot, 0))  1.54 us
    reduce_sum x1, other arithmetic, on_device(): my_lengths = jnp.sum(jnp.where(matches, lengths[None, :], 0), 1)  1.32 us
  transfers between devices with their start and end apart: 16, of which 8 were waited for; matrix products, arithmetic and copies ran while one was open for 12% of the time, Pallas kernels for 10%

profile of v12, /device:TPU:0, one launch (start us, length us, event | category | flops | bytes accessed | tf_op | source)
XLA Modules:
  0.0 52.6 jit_solution(2545225114835427587)
XLA Ops:
  0.0 1.5 %fusion.28 = s32[]{:T(128)} fusion(s32[8]{0:T(128)} %param.15, s32[8]{0:T(128)} %param.14, s32[]{:T(128)} %axis_index.27), kind=kLoop, calls=%fused_computation.42 | loop fusion | flops 23 | bytes 72 | tf_op jit(solution)/shard_map/reduce_sum | solution.py:36
  2.2 1.0 %select_bitcast_fusion.rest_0_ = bf16[128,512]{1,0:T(8,128)(2,1)S(1)} fusion(bf16[2,128,1,512]{3,1,2,0:T(8,128)(2,1)} %param.13, pred[]{:T(512)S(6)} %eq.43), kind=kLoop, calls=%fused_computation.26 | loop fusion | flops 65536 | bytes 393217 | tf_op jit(solution)/shard_map/jit(_where)/select_n | solution.py:39
  3.2 5.1 %collective-permute-start.3 = (bf16[128,512]{1,0:T(8,128)(2,1)S(1)}, bf16[128,512]{1,0:T(8,128)(2,1)S(1)}, u32[]{:S(2)}, u32[]{:S(2)}) collective-permute-start(bf16[128,512]{1,0:T(8,128)(2,1)S(1)} %select_bitcast_fusion.rest_0_), channel_id=1, source_target_pairs={{0,24},{4,28},{8,16},{12,20},{16,8},{20,12},{24,0},{28,4},{1,25},{... | collective-permute-start | bytes 393224 | tf_op jit(solution)/shard_map/ppermute | solution.py:28
  8.4 1.5 %collective-permute-start = (bf16[128,512]{1,0:T(8,128)(2,1)S(1)}, bf16[128,512]{1,0:T(8,128)(2,1)S(1)}, u32[]{:S(2)}, u32[]{:S(2)}) collective-permute-start(bf16[128,512]{1,0:T(8,128)(2,1)S(1)} %select_bitcast_fusion.rest_0_), channel_id=1, source_target_pairs={{0,4},{4,0},{8,12},{12,8},{16,20},{20,16},{24,28},{28,24},{1,5},{5... | collective-permute-start | bytes 393224 | tf_op jit(solution)/shard_map/ppermute | solution.py:28
  9.9 2.0 %collective-permute-start.2 = (bf16[128,512]{1,0:T(8,128)(2,1)S(1)}, bf16[128,512]{1,0:T(8,128)(2,1)S(1)}, u32[]{:S(2)}, u32[]{:S(2)}) collective-permute-start(bf16[128,512]{1,0:T(8,128)(2,1)S(1)} %select_bitcast_fusion.rest_0_), channel_id=1, source_target_pairs={{0,12},{4,8},{8,4},{12,0},{16,28},{20,24},{24,20},{28,16},{1,13},{... | collective-permute-start | bytes 393224 | tf_op jit(solution)/shard_map/ppermute | solution.py:28
  12.0 0.8 %collective-permute-done.3.rest_4_ = bf16[128,512]{1,0:T(8,128)(2,1)S(1)} collective-permute-done((bf16[128,512]{1,0:T(8,128)(2,1)S(1)}, bf16[128,512]{1,0:T(8,128)(2,1)S(1)}, u32[]{:S(2)}, u32[]{:S(2)}) %collective-permute-start.3) | collective-permute-done | bytes 131104 | tf_op jit(solution)/shard_map/ppermute | solution.py:28
  12.8 1.7 %collective-permute-start.4 = (bf16[128,512]{1,0:T(8,128)(2,1)S(1)}, bf16[128,512]{1,0:T(8,128)(2,1)S(1)}, u32[]{:S(2)}, u32[]{:S(2)}) collective-permute-start(bf16[128,512]{1,0:T(8,128)(2,1)S(1)} %collective-permute-done.3.rest_4_), channel_id=1, source_target_pairs={{0,4},{4,0},{8,12},{12,8},{16,20},{20,16},{24,28},{28,24},{1,5},{5... | collective-permute-start | bytes 393224 | tf_op jit(solution)/shard_map/ppermute | solution.py:28
  14.5 1.5 %collective-permute-start.5 = (bf16[128,512]{1,0:T(8,128)(2,1)S(1)}, bf16[128,512]{1,0:T(8,128)(2,1)S(1)}, u32[]{:S(2)}, u32[]{:S(2)}) collective-permute-start(bf16[128,512]{1,0:T(8,128)(2,1)S(1)} %collective-permute-done.3.rest_4_), channel_id=1, source_target_pairs={{0,8},{4,12},{8,0},{12,4},{16,24},{20,28},{24,16},{28,20},{1,9},{5... | collective-permute-start | bytes 393224 | tf_op jit(solution)/shard_map/ppermute | solution.py:28
  16.3 0.8 %compare_reduce_fusion = pred[8]{0:T(512)(128)(4,1)S(1)} fusion(s32[8]{0:T(128)} %param.14, s32[8]{0:T(128)S(1)} %stack.35), kind=kLoop, calls=%fused_computation.27 | loop fusion | flops 120 | bytes 72 | tf_op jit(solution)/shard_map/reduce_or | solution.py:55
  17.1 0.6 %convert_element_type.18.valid_ref = s32[8]{0:T(128)} convert(pred[8]{0:T(512)(128)(4,1)S(1)} %compare_reduce_fusion) | non-fusion elementwise | flops 8 | bytes 40 | tf_op jit(solution)/shard_map/convert_element_type | solution.py:194
  17.7 0.7 %dynamic_slice.19 = s32[4]{0:T(128)S(1)} dynamic-slice(s32[32]{0:T(128)} %param.17, s32[]{:T(128)S(6)} %select_n.37), dynamic_slice_sizes={4} | dynamic-slice | bytes 36 | tf_op jit(solution)/shard_map/dynamic_slice | solution.py:181
  18.4 1.3 %select_reduce_fusion.length_ref = s32[4]{0:T(128)} fusion(s32[32]{0:T(128)} %param.16, s32[4]{0:T(128)S(1)} %dynamic_slice.19), kind=kLoop, calls=%fused_computation.30 | loop fusion | flops 380 | bytes 160 | tf_op jit(solution)/shard_map/reduce_sum | solution.py:183
  19.9 2.0 %collective-permute-done.5.rest_6_ = bf16[128,512]{1,0:T(8,128)(2,1)S(1)} collective-permute-done((bf16[128,512]{1,0:T(8,128)(2,1)S(1)}, bf16[128,512]{1,0:T(8,128)(2,1)S(1)}, u32[]{:S(2)}, u32[]{:S(2)}) %collective-permute-start.5) | collective-permute-done | bytes 131104 | tf_op jit(solution)/shard_map/ppermute | solution.py:28
  21.9 2.3 %collective-permute-done.6.rest_7_ = bf16[128,512]{1,0:T(8,128)(2,1)S(1)} collective-permute-done((bf16[128,512]{1,0:T(8,128)(2,1)S(1)}, bf16[128,512]{1,0:T(8,128)(2,1)S(1)}, u32[]{:S(2)}, u32[]{:S(2)}) %collective-permute-start.6) | collective-permute-done | bytes 131104 | tf_op jit(solution)/shard_map/ppermute | solution.py:28
  24.3 0.6 %copy-done.11 = bf16[128,512]{1,0:T(8,128)(2,1)} copy-done((bf16[128,512]{1,0:T(8,128)(2,1)}, bf16[128,512]{1,0:T(8,128)(2,1)S(1)}, u32[]{:S(2)}) %copy-start.11) | copy-done | bytes 131096
  24.9 5.0 %shard_map.109 = bf16[2,128,512]{2,1,0:T(8,128)(2,1)} custom-call(s32[4]{0:T(128)} %select_reduce_fusion.length_ref, s32[8]{0:T(128)} %convert_element_type.18.valid_ref, bf16[4,128,1024]{2,1,0:T(8,128)(2,1)} %bitcast.35, f32[128,128]{1,0:T(8,128)} %constant.40.clone.cos_ref, f32[128,128]{1,0:T(8,128)} %constant.41.clone.sin_ref, ...), custom_call_target="tpu_custom_call" | custom-call | tf_op jit(solution)/shard_map/pallas_call | solution.py:145
  29.9 1.4 %collective-permute-start.8 = (bf16[256,512]{1,0:T(8,128)(2,1)}, bf16[256,512]{1,0:T(8,128)(2,1)S(1)}, u32[]{:S(2)}, u32[]{:S(2)}) collective-permute-start(bf16[256,512]{1,0:T(8,128)(2,1)} %bitcast.40), channel_id=1, source_target_pairs={{0,2},{1,3},{2,0},{3,1},{4,6},{5,7},{6,4},{7,5},{8,10},{9,11},{10,... | collective-permute-start | bytes 786440 | tf_op jit(solution)/shard_map/ppermute | solution.py:28
  31.3 5.1 %shard_map.110 = bf16[2,128,512]{2,1,0:T(8,128)(2,1)} custom-call(s32[4]{0:T(128)} %select_reduce_fusion.length_ref, s32[8]{0:T(128)} %convert_element_type.18.valid_ref, bf16[4,128,1024]{2,1,0:T(8,128)(2,1)} %bitcast.36, f32[128,128]{1,0:T(8,128)} %constant.40.clone.cos_ref, f32[128,128]{1,0:T(8,128)} %constant.41.clone.sin_ref, ...), custom_call_target="tpu_custom_call" | custom-call | tf_op jit(solution)/shard_map/pallas_call | solution.py:145
  37.7 6.2 %collective-permute-done.11 = bf16[256,512]{1,0:T(8,128)(2,1)S(1)} collective-permute-done((bf16[256,512]{1,0:T(8,128)(2,1)}, bf16[256,512]{1,0:T(8,128)(2,1)S(1)}, u32[]{:S(2)}, u32[]{:S(2)}) %collective-permute-start.11) | collective-permute-done | bytes 262176 | tf_op jit(solution)/shard_map/ppermute | solution.py:28
  47.9 0.8 %collective-permute-start.14 = (f32[4,128]{1,0:T(4,128)S(1)}, f32[4,128]{1,0:T(4,128)S(1)}, u32[]{:S(2)}, u32[]{:S(2)}) collective-permute-start(f32[4,128]{1,0:T(4,128)S(1)} %bitcast.44), channel_id=1, source_target_pairs={{0,2},{1,3},{2,0},{3,1},{4,6},{5,7},{6,4},{7,5},{8,10},{9,11},{10,... | collective-permute-start | bytes 6152 | tf_op jit(solution)/shard_map/ppermute | solution.py:24
  48.7 1.0 %collective-permute-start.15 = (f32[4,128]{1,0:T(4,128)S(1)}, f32[4,128]{1,0:T(4,128)S(1)}, u32[]{:S(2)}, u32[]{:S(2)}) collective-permute-start(f32[4,128]{1,0:T(4,128)S(1)} %bitcast.45), channel_id=1, source_target_pairs={{0,3},{1,0},{2,1},{3,2},{4,7},{5,4},{6,5},{7,6},{8,11},{9,8},{10,9... | collective-permute-start | bytes 6152 | tf_op jit(solution)/shard_map/ppermute | solution.py:24
  49.8 0.6 %collective-permute-done.13 = f32[4,128]{1,0:T(4,128)S(1)} collective-permute-done((f32[4,128]{1,0:T(4,128)S(1)}, f32[4,128]{1,0:T(4,128)S(1)}, u32[]{:S(2)}, u32[]{:S(2)}) %collective-permute-start.13) | collective-permute-done | bytes 2080 | tf_op jit(solution)/shard_map/ppermute | solution.py:24
  50.4 1.1 %collective-permute-done.14 = f32[4,128]{1,0:T(4,128)S(1)} collective-permute-done((f32[4,128]{1,0:T(4,128)S(1)}, f32[4,128]{1,0:T(4,128)S(1)}, u32[]{:S(2)}, u32[]{:S(2)}) %collective-permute-start.14) | collective-permute-done | bytes 2080 | tf_op jit(solution)/shard_map/ppermute | solution.py:24
  51.5 1.1 %fusion.5 = bf16[4,128,576]{1,2,0:T(8,128)(2,1)} fusion(f32[72,4,8,128]{3,2,1,0:T(8,128)S(1)} %get-tuple-element.6, bf16[4,128,576]{1,2,0:T(8,128)(2,1)S(1)} %copy-done.4, f32[4,128]{1,0:T(4,128)S(1)} %fusion.19, f32[576]{0:T(1024)S(1)} %copy-done.13, f32[4,128]{1,0:T(4,128)S(1)} %add_rsqrt_fusion), kind=kLoop, calls=%fused_computation.10 | loop fusion | flops 1769472 | bytes 2365696 | tf_op jit(solution)/shard_map/convert_element_type | solution.py:205
  (57 shorter events, 5.8 us)
Async XLA Ops:
  0.0 43.9 %copy-start = (bf16[2048,576]{0,1:T(8,128)(2,1)S(1)}, bf16[2048,576]{0,1:T(8,128)(2,1)}, u32[]{:S(2)}) copy-start(bf16[2048,576]{0,1:T(8,128)(2,1)} %param.18) | copy-start | bytes 7077892
  3.2 21.0 %copy-start.1 = (bf16[128,512]{1,0:T(8,128)(2,1)}, bf16[128,512]{1,0:T(8,128)(2,1)S(1)}, u32[]{:S(2)}) copy-start(bf16[128,512]{1,0:T(8,128)(2,1)S(1)} %select_bitcast_fusion.rest_0_) | copy-start | bytes 393220
  3.2 9.5 %collective-permute-start.3 = (bf16[128,512]{1,0:T(8,128)(2,1)S(1)}, bf16[128,512]{1,0:T(8,128)(2,1)S(1)}, u32[]{:S(2)}, u32[]{:S(2)}) collective-permute-start(bf16[128,512]{1,0:T(8,128)(2,1)S(1)} %select_bitcast_fusion.rest_0_), channel_id=1, source_target_pairs={{0,24},{4,28},{8,16},{12,20},{16,8},{20,12},{24,0},{28,4},{1,25},{... | collective-permute-start | bytes 393224 | tf_op jit(solution)/shard_map/ppermute | solution.py:28
  8.4 7.5 %collective-permute-start = (bf16[128,512]{1,0:T(8,128)(2,1)S(1)}, bf16[128,512]{1,0:T(8,128)(2,1)S(1)}, u32[]{:S(2)}, u32[]{:S(2)}) collective-permute-start(bf16[128,512]{1,0:T(8,128)(2,1)S(1)} %select_bitcast_fusion.rest_0_), channel_id=1, source_target_pairs={{0,4},{4,0},{8,12},{12,8},{16,20},{20,16},{24,28},{28,24},{1,5},{5... | collective-permute-start | bytes 393224 | tf_op jit(solution)/shard_map/ppermute | solution.py:28
  9.9 9.9 %collective-permute-start.1 = (bf16[128,512]{1,0:T(8,128)(2,1)S(1)}, bf16[128,512]{1,0:T(8,128)(2,1)S(1)}, u32[]{:S(2)}, u32[]{:S(2)}) collective-permute-start(bf16[128,512]{1,0:T(8,128)(2,1)S(1)} %select_bitcast_fusion.rest_0_), channel_id=1, source_target_pairs={{0,8},{4,12},{8,0},{12,4},{16,24},{20,28},{24,16},{28,20},{1,9},{5... | collective-permute-start | bytes 393224 | tf_op jit(solution)/shard_map/ppermute | solution.py:28
  9.9 9.9 %collective-permute-start.2 = (bf16[128,512]{1,0:T(8,128)(2,1)S(1)}, bf16[128,512]{1,0:T(8,128)(2,1)S(1)}, u32[]{:S(2)}, u32[]{:S(2)}) collective-permute-start(bf16[128,512]{1,0:T(8,128)(2,1)S(1)} %select_bitcast_fusion.rest_0_), channel_id=1, source_target_pairs={{0,12},{4,8},{8,4},{12,0},{16,28},{20,24},{24,20},{28,16},{1,13},{... | collective-permute-start | bytes 393224 | tf_op jit(solution)/shard_map/ppermute | solution.py:28
  12.8 11.4 %copy-start.5 = (bf16[128,512]{1,0:T(8,128)(2,1)}, bf16[128,512]{1,0:T(8,128)(2,1)S(1)}, u32[]{:S(2)}) copy-start(bf16[128,512]{1,0:T(8,128)(2,1)S(1)} %collective-permute-done.3.rest_4_) | copy-start | bytes 393220
  12.8 7.1 %collective-permute-start.4 = (bf16[128,512]{1,0:T(8,128)(2,1)S(1)}, bf16[128,512]{1,0:T(8,128)(2,1)S(1)}, u32[]{:S(2)}, u32[]{:S(2)}) collective-permute-start(bf16[128,512]{1,0:T(8,128)(2,1)S(1)} %collective-permute-done.3.rest_4_), channel_id=1, source_target_pairs={{0,4},{4,0},{8,12},{12,8},{16,20},{20,16},{24,28},{28,24},{1,5},{5... | collective-permute-start | bytes 393224 | tf_op jit(solution)/shard_map/ppermute | solution.py:28
  14.5 7.4 %collective-permute-start.5 = (bf16[128,512]{1,0:T(8,128)(2,1)S(1)}, bf16[128,512]{1,0:T(8,128)(2,1)S(1)}, u32[]{:S(2)}, u32[]{:S(2)}) collective-permute-start(bf16[128,512]{1,0:T(8,128)(2,1)S(1)} %collective-permute-done.3.rest_4_), channel_id=1, source_target_pairs={{0,8},{4,12},{8,0},{12,4},{16,24},{20,28},{24,16},{28,20},{1,9},{5... | collective-permute-start | bytes 393224 | tf_op jit(solution)/shard_map/ppermute | solution.py:28
  15.9 8.3 %copy-start.6 = (bf16[128,512]{1,0:T(8,128)(2,1)}, bf16[128,512]{1,0:T(8,128)(2,1)S(1)}, u32[]{:S(2)}) copy-start(bf16[128,512]{1,0:T(8,128)(2,1)S(1)} %collective-permute-done.rest_1_) | copy-start | bytes 393220
  15.9 8.3 %collective-permute-start.6 = (bf16[128,512]{1,0:T(8,128)(2,1)S(1)}, bf16[128,512]{1,0:T(8,128)(2,1)S(1)}, u32[]{:S(2)}, u32[]{:S(2)}) collective-permute-start(bf16[128,512]{1,0:T(8,128)(2,1)S(1)} %collective-permute-done.3.rest_4_), channel_id=1, source_target_pairs={{0,12},{4,8},{8,4},{12,0},{16,28},{20,24},{24,20},{28,16},{1,13},{... | collective-permute-start | bytes 393224 | tf_op jit(solution)/shard_map/ppermute | solution.py:28
  19.8 4.5 %copy-start.8 = (bf16[128,512]{1,0:T(8,128)(2,1)}, bf16[128,512]{1,0:T(8,128)(2,1)S(1)}, u32[]{:S(2)}) copy-start(bf16[128,512]{1,0:T(8,128)(2,1)S(1)} %collective-permute-done.2.rest_3_) | copy-start | bytes 393220
  29.9 7.1 %copy-start.3 = (bf16[2,128,512]{2,1,0:T(8,128)(2,1)S(1)}, bf16[2,128,512]{2,1,0:T(8,128)(2,1)}, u32[]{:S(2)}) copy-start(bf16[2,128,512]{2,1,0:T(8,128)(2,1)} %shard_map.109) | copy-start | bytes 786436
  29.9 7.8 %collective-permute-start.8 = (bf16[256,512]{1,0:T(8,128)(2,1)}, bf16[256,512]{1,0:T(8,128)(2,1)S(1)}, u32[]{:S(2)}, u32[]{:S(2)}) collective-permute-start(bf16[256,512]{1,0:T(8,128)(2,1)} %bitcast.40), channel_id=1, source_target_pairs={{0,2},{1,3},{2,0},{3,1},{4,6},{5,7},{6,4},{7,5},{8,10},{9,11},{10,... | collective-permute-start | bytes 786440 | tf_op jit(solution)/shard_map/ppermute | solution.py:28
  36.4 7.5 %collective-permute-start.11 = (bf16[256,512]{1,0:T(8,128)(2,1)}, bf16[256,512]{1,0:T(8,128)(2,1)S(1)}, u32[]{:S(2)}, u32[]{:S(2)}) collective-permute-start(bf16[256,512]{1,0:T(8,128)(2,1)} %bitcast.37), channel_id=1, source_target_pairs={{0,2},{1,3},{2,0},{3,1},{4,6},{5,7},{6,4},{7,5},{8,10},{9,11},{10,... | collective-permute-start | bytes 786440 | tf_op jit(solution)/shard_map/ppermute | solution.py:28
  37.0 7.7 %collective-permute-start.7 = (bf16[256,512]{1,0:T(8,128)(2,1)S(1)}, bf16[256,512]{1,0:T(8,128)(2,1)S(1)}, u32[]{:S(2)}, u32[]{:S(2)}) collective-permute-start(bf16[256,512]{1,0:T(8,128)(2,1)S(1)} %bitcast.41), channel_id=1, source_target_pairs={{0,1},{1,0},{2,3},{3,2},{4,5},{5,4},{6,7},{7,6},{8,9},{9,8},{10,11... | collective-permute-start | bytes 786440 | tf_op jit(solution)/shard_map/ppermute | solution.py:28
  37.0 8.4 %collective-permute-start.10 = (bf16[256,512]{1,0:T(8,128)(2,1)}, bf16[256,512]{1,0:T(8,128)(2,1)S(1)}, u32[]{:S(2)}, u32[]{:S(2)}) collective-permute-start(bf16[256,512]{1,0:T(8,128)(2,1)} %bitcast.38), channel_id=1, source_target_pairs={{0,1},{1,0},{2,3},{3,2},{4,5},{5,4},{6,7},{7,6},{8,9},{9,8},{10,11... | collective-permute-start | bytes 786440 | tf_op jit(solution)/shard_map/ppermute | solution.py:28
  37.7 8.6 %collective-permute-start.9 = (bf16[256,512]{1,0:T(8,128)(2,1)S(1)}, bf16[256,512]{1,0:T(8,128)(2,1)S(1)}, u32[]{:S(2)}, u32[]{:S(2)}) collective-permute-start(bf16[256,512]{1,0:T(8,128)(2,1)S(1)} %collective-permute-done.8), channel_id=1, source_target_pairs={{0,1},{1,0},{2,3},{3,2},{4,5},{5,4},{6,7},{7,6},{8,9},{9,8},{10,11... | collective-permute-start | bytes 786440 | tf_op jit(solution)/shard_map/ppermute | solution.py:28
  43.9 2.8 %collective-permute-start.12 = (bf16[256,512]{1,0:T(8,128)(2,1)S(1)}, bf16[256,512]{1,0:T(8,128)(2,1)S(1)}, u32[]{:S(2)}, u32[]{:S(2)}) collective-permute-start(bf16[256,512]{1,0:T(8,128)(2,1)S(1)} %collective-permute-done.11), channel_id=1, source_target_pairs={{0,1},{1,0},{2,3},{3,2},{4,5},{5,4},{6,7},{7,6},{8,9},{9,8},{10,11... | collective-permute-start | bytes 786440 | tf_op jit(solution)/shard_map/ppermute | solution.py:28
  46.7 4.8 %copy-start.4 = (bf16[4,128,576]{1,2,0:T(8,128)(2,1)S(1)}, bf16[4,128,576]{1,2,0:T(8,128)(2,1)}, u32[]{:S(2)}) copy-start(bf16[4,128,576]{1,2,0:T(8,128)(2,1)} %param.11) | copy-start | bytes 1769476
  46.7 4.8 %copy-start.13 = (f32[576]{0:T(1024)S(1)}, f32[576]{0:T(1024)}, u32[]{:S(2)}) copy-start(f32[576]{0:T(1024)} %param.19) | copy-start | bytes 6916
  47.3 3.1 %collective-permute-start.13 = (f32[4,128]{1,0:T(4,128)S(1)}, f32[4,128]{1,0:T(4,128)S(1)}, u32[]{:S(2)}, u32[]{:S(2)}) collective-permute-start(f32[4,128]{1,0:T(4,128)S(1)} %bitcast.43), channel_id=1, source_target_pairs={{0,1},{1,2},{2,3},{3,0},{4,5},{5,6},{6,7},{7,4},{8,9},{9,10},{10,1... | collective-permute-start | bytes 6152 | tf_op jit(solution)/shard_map/ppermute | solution.py:24
  47.9 3.6 %collective-permute-start.14 = (f32[4,128]{1,0:T(4,128)S(1)}, f32[4,128]{1,0:T(4,128)S(1)}, u32[]{:S(2)}, u32[]{:S(2)}) collective-permute-start(f32[4,128]{1,0:T(4,128)S(1)} %bitcast.44), channel_id=1, source_target_pairs={{0,2},{1,3},{2,0},{3,1},{4,6},{5,7},{6,4},{7,5},{8,10},{9,11},{10,... | collective-permute-start | bytes 6152 | tf_op jit(solution)/shard_map/ppermute | solution.py:24
  48.7 2.7 %collective-permute-start.15 = (f32[4,128]{1,0:T(4,128)S(1)}, f32[4,128]{1,0:T(4,128)S(1)}, u32[]{:S(2)}, u32[]{:S(2)}) collective-permute-start(f32[4,128]{1,0:T(4,128)S(1)} %bitcast.45), channel_id=1, source_target_pairs={{0,3},{1,0},{2,1},{3,2},{4,7},{5,4},{6,5},{7,6},{8,11},{9,8},{10,9... | collective-permute-start | bytes 6152 | tf_op jit(solution)/shard_map/ppermute | solution.py:24
  (6 other events, 15.8 us)

commit v13 on v11

--- a/solution.py
+++ b/solution.py
@@ -187,9 +187,13 @@
     projected = jnp.concatenate(projected_parts, 0).reshape(requests, slots, local_width)
 
     squares = jnp.sum(projected * projected, -1)
-    branch_total = squares
-    for shift in range(1, n_tp):
-        branch_total = branch_total + shifted(squares, "tp", n_tp, shift)
+    if n_tp == 4:
+        branch_total = squares + swapped(squares, "tp", n_tp, 2)
+        branch_total = branch_total + swapped(branch_total, "tp", n_tp, 1)
+    else:
+        branch_total = squares
+        for shift in range(1, n_tp):
+            branch_total = branch_total + shifted(squares, "tp", n_tp, shift)
     branch = projected * lax.rsqrt(branch_total / D + EPSILON)[..., None] * post_gain
     source = hidden.astype(jnp.float32)
     return ((source + branch) * live_mask[..., None]).astype(jnp.bfloat16)

time: 52.7 us -> 53.1 us (level)
  waiting for transfers between devices: 13.1 us -> 15.3 us
  starting transfers between devices: 17.3 us -> 15.8 us
    ppermute x13 -> x15, waiting for transfers between devices: 11.7 us -> 15.3 us  [swapped(): return lax.ppermute(value, axis, [(i, i ^ mask) for i in range(size)])]
    ppermute x3 -> x0, starting transfers between devices: 2.61 us -> none  [shifted(): lax.ppermute(value, axis, [(i, (i + shift) % size) for i in range(size)])]
    ppermute x3 -> x0, waiting for transfers between devices: 1.43 us -> none  [shifted(): lax.ppermute(value, axis, [(i, (i + shift) % size) for i in range(size)])]
    ppermute x13 -> x15, starting transfers between devices: 14.7 us -> 15.8 us  [swapped(): return lax.ppermute(value, axis, [(i, i ^ mask) for i in range(size)])]
  transfers between devices with their start and end apart: 16 -> 15, of which waited for: 8 -> 8; matrix products, arithmetic and copies ran while one was open for 12% -> 11% of each run, Pallas kernels for 9% -> 9%
where the time goes in v13:
time: 53.1 us; the launch traced here: 52.8 us
  starting transfers between devices  15.8 us (30%)
  waiting for transfers between devices  15.3 us (29%)
  Pallas kernels  9.58 us (18%)
  other arithmetic  6.7 us (13%)
  matrix products  2.8 us (5%)
  local copies, waits for them, and re-layouts  1.66 us (3%)
  between operations  0.91 us (2%)
    ppermute x15, starting transfers between devices, swapped(): return lax.ppermute(value, axis, [(i, i ^ mask) for i in range(size)])  15.8 us
    ppermute x15, waiting for transfers between devices, swapped(): return lax.ppermute(value, axis, [(i, i ^ mask) for i in range(size)])  15.3 us
    pallas_call x2, Pallas kernels, attend(): pl.pallas_call(functools.partial(attention_kernel, offset=offset), grid_s...  9.58 us
    dot_general x8, matrix products, project(): term = jnp.dot(block, rows, preferred_element_type=jnp.float32)  2.8 us
    reduce_sum x1, other arithmetic, gather_prefix(): slot = jnp.sum(jnp.where(mine, page_slot, 0))  1.54 us
    reduce_sum x1, other arithmetic, on_device(): my_lengths = jnp.sum(jnp.where(matches, lengths[None, :], 0), 1)  1.41 us
    convert_element_type x1, other arithmetic, on_device(): return ((source + branch) * live_mask[..., None]).astype(jnp.bfloat16)  1.11 us
  transfers between devices with their start and end apart: 15, of which 8 were waited for; matrix products, arithmetic and copies ran while one was open for 11% of the time, Pallas kernels for 9%

profile of v13, /device:TPU:0, one launch (start us, length us, event | category | flops | bytes accessed | tf_op | source)
XLA Modules:
  0.0 52.8 jit_solution(15627536559634688467)
XLA Ops:
  0.0 1.5 %fusion.28 = s32[]{:T(128)} fusion(s32[8]{0:T(128)} %param.15, s32[8]{0:T(128)} %param.14, s32[]{:T(128)} %axis_index.27), kind=kLoop, calls=%fused_computation.42 | loop fusion | flops 23 | bytes 72 | tf_op jit(solution)/shard_map/reduce_sum | solution.py:36
  2.2 1.0 %select_bitcast_fusion.rest_0_ = bf16[128,512]{1,0:T(8,128)(2,1)S(1)} fusion(bf16[2,128,1,512]{3,1,2,0:T(8,128)(2,1)} %param.13, pred[]{:T(512)S(6)} %eq.43), kind=kLoop, calls=%fused_computation.26 | loop fusion | flops 65536 | bytes 393217 | tf_op jit(solution)/shard_map/jit(_where)/select_n | solution.py:39
  3.2 5.1 %collective-permute-start.3 = (bf16[128,512]{1,0:T(8,128)(2,1)S(1)}, bf16[128,512]{1,0:T(8,128)(2,1)S(1)}, u32[]{:S(2)}, u32[]{:S(2)}) collective-permute-start(bf16[128,512]{1,0:T(8,128)(2,1)S(1)} %select_bitcast_fusion.rest_0_), channel_id=1, source_target_pairs={{0,24},{4,28},{8,16},{12,20},{16,8},{20,12},{24,0},{28,4},{1,25},{... | collective-permute-start | bytes 393224 | tf_op jit(solution)/shard_map/ppermute | solution.py:28
  8.4 1.5 %collective-permute-start = (bf16[128,512]{1,0:T(8,128)(2,1)S(1)}, bf16[128,512]{1,0:T(8,128)(2,1)S(1)}, u32[]{:S(2)}, u32[]{:S(2)}) collective-permute-start(bf16[128,512]{1,0:T(8,128)(2,1)S(1)} %select_bitcast_fusion.rest_0_), channel_id=1, source_target_pairs={{0,4},{4,0},{8,12},{12,8},{16,20},{20,16},{24,28},{28,24},{1,5},{5... | collective-permute-start | bytes 393224 | tf_op jit(solution)/shard_map/ppermute | solution.py:28
  9.9 2.0 %collective-permute-start.2 = (bf16[128,512]{1,0:T(8,128)(2,1)S(1)}, bf16[128,512]{1,0:T(8,128)(2,1)S(1)}, u32[]{:S(2)}, u32[]{:S(2)}) collective-permute-start(bf16[128,512]{1,0:T(8,128)(2,1)S(1)} %select_bitcast_fusion.rest_0_), channel_id=1, source_target_pairs={{0,12},{4,8},{8,4},{12,0},{16,28},{20,24},{24,20},{28,16},{1,13},{... | collective-permute-start | bytes 393224 | tf_op jit(solution)/shard_map/ppermute | solution.py:28
  11.9 0.8 %collective-permute-done.3.rest_4_ = bf16[128,512]{1,0:T(8,128)(2,1)S(1)} collective-permute-done((bf16[128,512]{1,0:T(8,128)(2,1)S(1)}, bf16[128,512]{1,0:T(8,128)(2,1)S(1)}, u32[]{:S(2)}, u32[]{:S(2)}) %collective-permute-start.3) | collective-permute-done | bytes 131104 | tf_op jit(solution)/shard_map/ppermute | solution.py:28
  12.8 1.7 %collective-permute-start.4 = (bf16[128,512]{1,0:T(8,128)(2,1)S(1)}, bf16[128,512]{1,0:T(8,128)(2,1)S(1)}, u32[]{:S(2)}, u32[]{:S(2)}) collective-permute-start(bf16[128,512]{1,0:T(8,128)(2,1)S(1)} %collective-permute-done.3.rest_4_), channel_id=1, source_target_pairs={{0,4},{4,0},{8,12},{12,8},{16,20},{20,16},{24,28},{28,24},{1,5},{5... | collective-permute-start | bytes 393224 | tf_op jit(solution)/shard_map/ppermute | solution.py:28
  14.5 1.5 %collective-permute-start.5 = (bf16[128,512]{1,0:T(8,128)(2,1)S(1)}, bf16[128,512]{1,0:T(8,128)(2,1)S(1)}, u32[]{:S(2)}, u32[]{:S(2)}) collective-permute-start(bf16[128,512]{1,0:T(8,128)(2,1)S(1)} %collective-permute-done.3.rest_4_), channel_id=1, source_target_pairs={{0,8},{4,12},{8,0},{12,4},{16,24},{20,28},{24,16},{28,20},{1,9},{5... | collective-permute-start | bytes 393224 | tf_op jit(solution)/shard_map/ppermute | solution.py:28
  16.3 0.8 %compare_reduce_fusion = pred[8]{0:T(512)(128)(4,1)S(1)} fusion(s32[8]{0:T(128)} %param.14, s32[8]{0:T(128)S(1)} %stack.35), kind=kLoop, calls=%fused_computation.27 | loop fusion | flops 120 | bytes 72 | tf_op jit(solution)/shard_map/reduce_or | solution.py:55
  17.6 0.7 %dynamic_slice.19 = s32[4]{0:T(128)S(1)} dynamic-slice(s32[32]{0:T(128)} %param.17, s32[]{:T(128)S(6)} %select_n.37), dynamic_slice_sizes={4} | dynamic-slice | bytes 36 | tf_op jit(solution)/shard_map/dynamic_slice | solution.py:171
  18.3 1.4 %select_reduce_fusion.length_ref = s32[4]{0:T(128)} fusion(s32[32]{0:T(128)} %param.16, s32[4]{0:T(128)S(1)} %dynamic_slice.19), kind=kLoop, calls=%fused_computation.30 | loop fusion | flops 380 | bytes 160 | tf_op jit(solution)/shard_map/reduce_sum | solution.py:173
  19.9 2.0 %collective-permute-done.5.rest_6_ = bf16[128,512]{1,0:T(8,128)(2,1)S(1)} collective-permute-done((bf16[128,512]{1,0:T(8,128)(2,1)S(1)}, bf16[128,512]{1,0:T(8,128)(2,1)S(1)}, u32[]{:S(2)}, u32[]{:S(2)}) %collective-permute-start.5) | collective-permute-done | bytes 131104 | tf_op jit(solution)/shard_map/ppermute | solution.py:28
  21.9 2.3 %collective-permute-done.6.rest_7_ = bf16[128,512]{1,0:T(8,128)(2,1)S(1)} collective-permute-done((bf16[128,512]{1,0:T(8,128)(2,1)S(1)}, bf16[128,512]{1,0:T(8,128)(2,1)S(1)}, u32[]{:S(2)}, u32[]{:S(2)}) %collective-permute-start.6) | collective-permute-done | bytes 131104 | tf_op jit(solution)/shard_map/ppermute | solution.py:28
  24.3 0.6 %copy-done.11 = bf16[128,512]{1,0:T(8,128)(2,1)} copy-done((bf16[128,512]{1,0:T(8,128)(2,1)}, bf16[128,512]{1,0:T(8,128)(2,1)S(1)}, u32[]{:S(2)}) %copy-start.11) | copy-done | bytes 131096
  24.8 4.8 %shard_map.109 = bf16[2,128,512]{2,1,0:T(8,128)(2,1)} custom-call(s32[4]{0:T(128)} %select_reduce_fusion.length_ref, s32[8]{0:T(128)} %convert_element_type.18.valid_ref, bf16[4,128,1024]{2,1,0:T(8,128)(2,1)} %bitcast.37, f32[128,128]{1,0:T(8,128)} %constant.40.clone.cos_ref, f32[128,128]{1,0:T(8,128)} %constant.41.clone.sin_ref, ...), custom_call_target="tpu_custom_call" | custom-call | tf_op jit(solution)/shard_map/pallas_call | solution.py:135
  29.6 1.4 %collective-permute-start.8 = (bf16[256,512]{1,0:T(8,128)(2,1)}, bf16[256,512]{1,0:T(8,128)(2,1)S(1)}, u32[]{:S(2)}, u32[]{:S(2)}) collective-permute-start(bf16[256,512]{1,0:T(8,128)(2,1)} %bitcast.42), channel_id=1, source_target_pairs={{0,2},{1,3},{2,0},{3,1},{4,6},{5,7},{6,4},{7,5},{8,10},{9,11},{10,... | collective-permute-start | bytes 786440 | tf_op jit(solution)/shard_map/ppermute | solution.py:28
  31.1 4.8 %shard_map.110 = bf16[2,128,512]{2,1,0:T(8,128)(2,1)} custom-call(s32[4]{0:T(128)} %select_reduce_fusion.length_ref, s32[8]{0:T(128)} %convert_element_type.18.valid_ref, bf16[4,128,1024]{2,1,0:T(8,128)(2,1)} %bitcast.38, f32[128,128]{1,0:T(8,128)} %constant.40.clone.cos_ref, f32[128,128]{1,0:T(8,128)} %constant.41.clone.sin_ref, ...), custom_call_target="tpu_custom_call" | custom-call | tf_op jit(solution)/shard_map/pallas_call | solution.py:135
  35.9 0.6 %collective-permute-start.11 = (bf16[256,512]{1,0:T(8,128)(2,1)}, bf16[256,512]{1,0:T(8,128)(2,1)S(1)}, u32[]{:S(2)}, u32[]{:S(2)}) collective-permute-start(bf16[256,512]{1,0:T(8,128)(2,1)} %bitcast.39), channel_id=1, source_target_pairs={{0,2},{1,3},{2,0},{3,1},{4,6},{5,7},{6,4},{7,5},{8,10},{9,11},{10,... | collective-permute-start | bytes 786440 | tf_op jit(solution)/shard_map/ppermute | solution.py:28
  36.5 0.5 collective-permute-start.10
  37.4 6.0 %collective-permute-done.11 = bf16[256,512]{1,0:T(8,128)(2,1)S(1)} collective-permute-done((bf16[256,512]{1,0:T(8,128)(2,1)}, bf16[256,512]{1,0:T(8,128)(2,1)S(1)}, u32[]{:S(2)}, u32[]{:S(2)}) %collective-permute-start.11) | collective-permute-done | bytes 262176 | tf_op jit(solution)/shard_map/ppermute | solution.py:28
  46.8 1.1 %collective-permute-start.13 = (f32[4,128]{1,0:T(4,128)S(1)}, f32[4,128]{1,0:T(4,128)S(1)}, u32[]{:S(2)}, u32[]{:S(2)}) collective-permute-start(f32[4,128]{1,0:T(4,128)S(1)} %bitcast.45), channel_id=1, source_target_pairs={{0,2},{1,3},{2,0},{3,1},{4,6},{5,7},{6,4},{7,5},{8,10},{9,11},{10,... | collective-permute-start | bytes 6152 | tf_op jit(solution)/shard_map/ppermute | solution.py:28
  48.0 2.5 %collective-permute-done.13 = f32[4,128]{1,0:T(4,128)S(1)} collective-permute-done((f32[4,128]{1,0:T(4,128)S(1)}, f32[4,128]{1,0:T(4,128)S(1)}, u32[]{:S(2)}, u32[]{:S(2)}) %collective-permute-start.13) | collective-permute-done | bytes 2080 | tf_op jit(solution)/shard_map/ppermute | solution.py:28
  50.6 1.1 %collective-permute-done.14 = f32[4,128]{1,0:T(4,128)S(1)} collective-permute-done((f32[4,128]{1,0:T(4,128)S(1)}, f32[4,128]{1,0:T(4,128)S(1)}, u32[]{:S(2)}, u32[]{:S(2)}) %collective-permute-start.14) | collective-permute-done | bytes 2080 | tf_op jit(solution)/shard_map/ppermute | solution.py:28
  51.7 1.1 %fusion.5 = bf16[4,128,576]{1,2,0:T(8,128)(2,1)} fusion(f32[72,4,8,128]{3,2,1,0:T(8,128)S(1)} %get-tuple-element.6, bf16[4,128,576]{1,2,0:T(8,128)(2,1)S(1)} %copy-done.4, f32[4,128]{1,0:T(4,128)S(1)} %fusion.19, f32[576]{0:T(1024)S(1)} %copy-done.13, f32[4,128]{1,0:T(4,128)S(1)} %add_rsqrt_fusion), kind=kLoop, calls=%fused_computation.10 | loop fusion | flops 1769472 | bytes 2365696 | tf_op jit(solution)/shard_map/convert_element_type | solution.py:199
  (56 shorter events, 5.0 us)
Async XLA Ops:
  0.0 43.4 %copy-start = (bf16[2048,576]{0,1:T(8,128)(2,1)S(1)}, bf16[2048,576]{0,1:T(8,128)(2,1)}, u32[]{:S(2)}) copy-start(bf16[2048,576]{0,1:T(8,128)(2,1)} %param.18) | copy-start | bytes 7077892
  3.2 21.0 %copy-start.1 = (bf16[128,512]{1,0:T(8,128)(2,1)}, bf16[128,512]{1,0:T(8,128)(2,1)S(1)}, u32[]{:S(2)}) copy-start(bf16[128,512]{1,0:T(8,128)(2,1)S(1)} %select_bitcast_fusion.rest_0_) | copy-start | bytes 393220
  3.2 9.5 %collective-permute-start.3 = (bf16[128,512]{1,0:T(8,128)(2,1)S(1)}, bf16[128,512]{1,0:T(8,128)(2,1)S(1)}, u32[]{:S(2)}, u32[]{:S(2)}) collective-permute-start(bf16[128,512]{1,0:T(8,128)(2,1)S(1)} %select_bitcast_fusion.rest_0_), channel_id=1, source_target_pairs={{0,24},{4,28},{8,16},{12,20},{16,8},{20,12},{24,0},{28,4},{1,25},{... | collective-permute-start | bytes 393224 | tf_op jit(solution)/shard_map/ppermute | solution.py:28
  8.4 7.5 %collective-permute-start = (bf16[128,512]{1,0:T(8,128)(2,1)S(1)}, bf16[128,512]{1,0:T(8,128)(2,1)S(1)}, u32[]{:S(2)}, u32[]{:S(2)}) collective-permute-start(bf16[128,512]{1,0:T(8,128)(2,1)S(1)} %select_bitcast_fusion.rest_0_), channel_id=1, source_target_pairs={{0,4},{4,0},{8,12},{12,8},{16,20},{20,16},{24,28},{28,24},{1,5},{5... | collective-permute-start | bytes 393224 | tf_op jit(solution)/shard_map/ppermute | solution.py:28
  9.9 9.8 %collective-permute-start.1 = (bf16[128,512]{1,0:T(8,128)(2,1)S(1)}, bf16[128,512]{1,0:T(8,128)(2,1)S(1)}, u32[]{:S(2)}, u32[]{:S(2)}) collective-permute-start(bf16[128,512]{1,0:T(8,128)(2,1)S(1)} %select_bitcast_fusion.rest_0_), channel_id=1, source_target_pairs={{0,8},{4,12},{8,0},{12,4},{16,24},{20,28},{24,16},{28,20},{1,9},{5... | collective-permute-start | bytes 393224 | tf_op jit(solution)/shard_map/ppermute | solution.py:28
  9.9 9.8 %collective-permute-start.2 = (bf16[128,512]{1,0:T(8,128)(2,1)S(1)}, bf16[128,512]{1,0:T(8,128)(2,1)S(1)}, u32[]{:S(2)}, u32[]{:S(2)}) collective-permute-start(bf16[128,512]{1,0:T(8,128)(2,1)S(1)} %select_bitcast_fusion.rest_0_), channel_id=1, source_target_pairs={{0,12},{4,8},{8,4},{12,0},{16,28},{20,24},{24,20},{28,16},{1,13},{... | collective-permute-start | bytes 393224 | tf_op jit(solution)/shard_map/ppermute | solution.py:28
  12.8 11.4 %copy-start.5 = (bf16[128,512]{1,0:T(8,128)(2,1)}, bf16[128,512]{1,0:T(8,128)(2,1)S(1)}, u32[]{:S(2)}) copy-start(bf16[128,512]{1,0:T(8,128)(2,1)S(1)} %collective-permute-done.3.rest_4_) | copy-start | bytes 393220
  12.8 7.1 %collective-permute-start.4 = (bf16[128,512]{1,0:T(8,128)(2,1)S(1)}, bf16[128,512]{1,0:T(8,128)(2,1)S(1)}, u32[]{:S(2)}, u32[]{:S(2)}) collective-permute-start(bf16[128,512]{1,0:T(8,128)(2,1)S(1)} %collective-permute-done.3.rest_4_), channel_id=1, source_target_pairs={{0,4},{4,0},{8,12},{12,8},{16,20},{20,16},{24,28},{28,24},{1,5},{5... | collective-permute-start | bytes 393224 | tf_op jit(solution)/shard_map/ppermute | solution.py:28
  14.5 7.4 %collective-permute-start.5 = (bf16[128,512]{1,0:T(8,128)(2,1)S(1)}, bf16[128,512]{1,0:T(8,128)(2,1)S(1)}, u32[]{:S(2)}, u32[]{:S(2)}) collective-permute-start(bf16[128,512]{1,0:T(8,128)(2,1)S(1)} %collective-permute-done.3.rest_4_), channel_id=1, source_target_pairs={{0,8},{4,12},{8,0},{12,4},{16,24},{20,28},{24,16},{28,20},{1,9},{5... | collective-permute-start | bytes 393224 | tf_op jit(solution)/shard_map/ppermute | solution.py:28
  15.9 8.3 %copy-start.6 = (bf16[128,512]{1,0:T(8,128)(2,1)}, bf16[128,512]{1,0:T(8,128)(2,1)S(1)}, u32[]{:S(2)}) copy-start(bf16[128,512]{1,0:T(8,128)(2,1)S(1)} %collective-permute-done.rest_1_) | copy-start | bytes 393220
  15.9 8.3 %collective-permute-start.6 = (bf16[128,512]{1,0:T(8,128)(2,1)S(1)}, bf16[128,512]{1,0:T(8,128)(2,1)S(1)}, u32[]{:S(2)}, u32[]{:S(2)}) collective-permute-start(bf16[128,512]{1,0:T(8,128)(2,1)S(1)} %collective-permute-done.3.rest_4_), channel_id=1, source_target_pairs={{0,12},{4,8},{8,4},{12,0},{16,28},{20,24},{24,20},{28,16},{1,13},{... | collective-permute-start | bytes 393224 | tf_op jit(solution)/shard_map/ppermute | solution.py:28
  19.7 4.5 %copy-start.7 = (bf16[128,512]{1,0:T(8,128)(2,1)}, bf16[128,512]{1,0:T(8,128)(2,1)S(1)}, u32[]{:S(2)}) copy-start(bf16[128,512]{1,0:T(8,128)(2,1)S(1)} %collective-permute-done.1.rest_2_) | copy-start | bytes 393220
  19.7 4.5 %copy-start.8 = (bf16[128,512]{1,0:T(8,128)(2,1)}, bf16[128,512]{1,0:T(8,128)(2,1)S(1)}, u32[]{:S(2)}) copy-start(bf16[128,512]{1,0:T(8,128)(2,1)S(1)} %collective-permute-done.2.rest_3_) | copy-start | bytes 393220
  29.6 6.8 %copy-start.3 = (bf16[2,128,512]{2,1,0:T(8,128)(2,1)S(1)}, bf16[2,128,512]{2,1,0:T(8,128)(2,1)}, u32[]{:S(2)}) copy-start(bf16[2,128,512]{2,1,0:T(8,128)(2,1)} %shard_map.109) | copy-start | bytes 786436
  29.6 7.8 %collective-permute-start.8 = (bf16[256,512]{1,0:T(8,128)(2,1)}, bf16[256,512]{1,0:T(8,128)(2,1)S(1)}, u32[]{:S(2)}, u32[]{:S(2)}) collective-permute-start(bf16[256,512]{1,0:T(8,128)(2,1)} %bitcast.42), channel_id=1, source_target_pairs={{0,2},{1,3},{2,0},{3,1},{4,6},{5,7},{6,4},{7,5},{8,10},{9,11},{10,... | collective-permute-start | bytes 786440 | tf_op jit(solution)/shard_map/ppermute | solution.py:28
  35.9 7.5 %collective-permute-start.11 = (bf16[256,512]{1,0:T(8,128)(2,1)}, bf16[256,512]{1,0:T(8,128)(2,1)S(1)}, u32[]{:S(2)}, u32[]{:S(2)}) collective-permute-start(bf16[256,512]{1,0:T(8,128)(2,1)} %bitcast.39), channel_id=1, source_target_pairs={{0,2},{1,3},{2,0},{3,1},{4,6},{5,7},{6,4},{7,5},{8,10},{9,11},{10,... | collective-permute-start | bytes 786440 | tf_op jit(solution)/shard_map/ppermute | solution.py:28
  36.5 7.7 %collective-permute-start.7 = (bf16[256,512]{1,0:T(8,128)(2,1)S(1)}, bf16[256,512]{1,0:T(8,128)(2,1)S(1)}, u32[]{:S(2)}, u32[]{:S(2)}) collective-permute-start(bf16[256,512]{1,0:T(8,128)(2,1)S(1)} %bitcast.43), channel_id=1, source_target_pairs={{0,1},{1,0},{2,3},{3,2},{4,5},{5,4},{6,7},{7,6},{8,9},{9,8},{10,11... | collective-permute-start | bytes 786440 | tf_op jit(solution)/shard_map/ppermute | solution.py:28
  36.5 8.4 %collective-permute-start.10 = (bf16[256,512]{1,0:T(8,128)(2,1)}, bf16[256,512]{1,0:T(8,128)(2,1)S(1)}, u32[]{:S(2)}, u32[]{:S(2)}) collective-permute-start(bf16[256,512]{1,0:T(8,128)(2,1)} %bitcast.40), channel_id=1, source_target_pairs={{0,1},{1,0},{2,3},{3,2},{4,5},{5,4},{6,7},{7,6},{8,9},{9,8},{10,11... | collective-permute-start | bytes 786440 | tf_op jit(solution)/shard_map/ppermute | solution.py:28
  37.4 8.4 %collective-permute-start.9 = (bf16[256,512]{1,0:T(8,128)(2,1)S(1)}, bf16[256,512]{1,0:T(8,128)(2,1)S(1)}, u32[]{:S(2)}, u32[]{:S(2)}) collective-permute-start(bf16[256,512]{1,0:T(8,128)(2,1)S(1)} %collective-permute-done.8), channel_id=1, source_target_pairs={{0,1},{1,0},{2,3},{3,2},{4,5},{5,4},{6,7},{7,6},{8,9},{9,8},{10,11... | collective-permute-start | bytes 786440 | tf_op jit(solution)/shard_map/ppermute | solution.py:28
  43.4 2.8 %collective-permute-start.12 = (bf16[256,512]{1,0:T(8,128)(2,1)S(1)}, bf16[256,512]{1,0:T(8,128)(2,1)S(1)}, u32[]{:S(2)}, u32[]{:S(2)}) collective-permute-start(bf16[256,512]{1,0:T(8,128)(2,1)S(1)} %collective-permute-done.11), channel_id=1, source_target_pairs={{0,1},{1,0},{2,3},{3,2},{4,5},{5,4},{6,7},{7,6},{8,9},{9,8},{10,11... | collective-permute-start | bytes 786440 | tf_op jit(solution)/shard_map/ppermute | solution.py:28
  46.2 5.5 %copy-start.4 = (bf16[4,128,576]{1,2,0:T(8,128)(2,1)S(1)}, bf16[4,128,576]{1,2,0:T(8,128)(2,1)}, u32[]{:S(2)}) copy-start(bf16[4,128,576]{1,2,0:T(8,128)(2,1)} %param.11) | copy-start | bytes 1769476
  46.2 5.5 %copy-start.13 = (f32[576]{0:T(1024)S(1)}, f32[576]{0:T(1024)}, u32[]{:S(2)}) copy-start(f32[576]{0:T(1024)} %param.19) | copy-start | bytes 6916
  46.8 3.6 %collective-permute-start.13 = (f32[4,128]{1,0:T(4,128)S(1)}, f32[4,128]{1,0:T(4,128)S(1)}, u32[]{:S(2)}, u32[]{:S(2)}) collective-permute-start(f32[4,128]{1,0:T(4,128)S(1)} %bitcast.45), channel_id=1, source_target_pairs={{0,2},{1,3},{2,0},{3,1},{4,6},{5,7},{6,4},{7,5},{8,10},{9,11},{10,... | collective-permute-start | bytes 6152 | tf_op jit(solution)/shard_map/ppermute | solution.py:28
  50.5 1.2 %collective-permute-start.14 = (f32[4,128]{1,0:T(4,128)S(1)}, f32[4,128]{1,0:T(4,128)S(1)}, u32[]{:S(2)}, u32[]{:S(2)}) collective-permute-start(f32[4,128]{1,0:T(4,128)S(1)} %bitcast_add_fusion), channel_id=1, source_target_pairs={{0,1},{1,0},{2,3},{3,2},{4,5},{5,4},{6,7},{7,6},{8,9},{9,8},{10,11... | collective-permute-start | bytes 6152 | tf_op jit(solution)/shard_map/ppermute | solution.py:28
  (5 other events, 12.6 us)

commit v14 on v6

--- a/solution.py
+++ b/solution.py
@@ -135,23 +135,16 @@
         out_shape=jax.ShapeDtypeStruct((count, slots, per_group * HD), jnp.bfloat16),
     )(lengths, valid, qkv, cosine, sine, *blocks)
 
-def project(own, w_out, tp_index, n_tp, group_width):
+def exchange(own, tp_index, n_tp):
     if n_tp == 4:
         near = swapped(own, "tp", n_tp, 1)
         far = swapped(own, "tp", n_tp, 2)
         farther = swapped(far, "tp", n_tp, 1)
-        parts = [(own, tp_index), (near, tp_index ^ 1), (far, tp_index ^ 2), (farther, tp_index ^ 3)]
-    else:
-        parts = [(own, tp_index)]
-        for shift in range(1, n_tp):
-            parts.append((shifted(own, "tp", n_tp, shift), (tp_index - shift) % n_tp))
-    projected = None
-    for block, group in parts:
-        rows = lax.dynamic_slice_in_dim(w_out, group * group_width, group_width, 0)
-        term = jnp.dot(block, rows, preferred_element_type=jnp.float32)
-        projected = term if projected is None else projected + term
-    return projected
-
+        return [(own, tp_index), (near, tp_index ^ 1), (far, tp_index ^ 2), (farther, tp_index ^ 3)]
+    parts = [(own, tp_index)]
+    for shift in range(1, n_tp):
+        parts.append((shifted(own, "tp", n_tp, shift), (tp_index - shift) % n_tp))
+    return parts
 
 def on_device(
     hidden, qkv, page_store, page_owner, page_slot, lengths, request_perm, w_out, post_gain,
@@ -175,13 +168,19 @@
     cosine, sine = static_tables(prefix_len + np.arange(slots), HD)
     group_width = per_group * HD
     chunk = max(1, requests // 2)
-    projected_parts = []
+    chunk_parts = []
     for start in range(0, requests, chunk):
         attended = attend(qkv[:, :, 0], jnp.asarray(cosine), jnp.asarray(sine), blocks,
                           my_lengths, valid.astype(jnp.int32), start, chunk)
-        own = attended.reshape(chunk * slots, per_group * HD)
-        projected_parts.append(project(own, w_out, tp_index, n_tp, group_width))
-    projected = jnp.concatenate(projected_parts, 0).reshape(requests, slots, local_width)
+        chunk_parts.append(exchange(attended.reshape(chunk * slots, per_group * HD), tp_index, n_tp))
+    projected = None
+    for number in range(n_tp):
+        block = jnp.concatenate([parts[number][0] for parts in chunk_parts], 0)
+        group = chunk_parts[0][number][1]
+        rows = lax.dynamic_slice_in_dim(w_out, group * group_width, group_width, 0)
+        term = jnp.dot(block, rows, preferred_element_type=jnp.float32)
+        projected = term if projected is None else projected + term
+    projected = projected.reshape(requests, slots, local_width)
 
     squares = jnp.sum(projected * projected, -1)
     branch_total = squares

time: 52.7 us -> 52.9 us (level)
  waiting for transfers between devices: 13.2 us -> 13.9 us
  starting transfers between devices: 17.3 us -> 16.6 us
    ppermute x13, waiting for transfers between devices: 11.7 us -> 12.4 us  [swapped(): return lax.ppermute(value, axis, [(i, i ^ mask) for i in range(size)])]
    dot_general x8 -> x4, matrix products: 2.8 us -> 2.97 us  [on_device(): term = jnp.dot(block, rows, preferred_element_type=jnp.float32)]
  transfers between devices with their start and end apart: 16 -> 16, of which waited for: 8 -> 9; matrix products, arithmetic and copies ran while one was open for 12% -> 12% of each run, Pallas kernels for 9% -> 9%
where the time goes in v14:
time: 52.9 us; the launch traced here: 51.9 us
  starting transfers between devices  16.6 us (31%)
  waiting for transfers between devices  13.9 us (26%)
  Pallas kernels  9.58 us (18%)
  other arithmetic  6.46 us (12%)
  matrix products  2.97 us (6%)
  local copies, waits for them, and re-layouts  1.46 us (3%)
  between operations  0.88 us (2%)
    ppermute x13, starting transfers between devices, swapped(): return lax.ppermute(value, axis, [(i, i ^ mask) for i in range(size)])  14.4 us
    ppermute x13, waiting for transfers between devices, swapped(): return lax.ppermute(value, axis, [(i, i ^ mask) for i in range(size)])  12.4 us
    pallas_call x2, Pallas kernels, attend(): pl.pallas_call(functools.partial(attention_kernel, offset=offset), grid_s...  9.58 us
    dot_general x4, matrix products, on_device(): term = jnp.dot(block, rows, preferred_element_type=jnp.float32)  2.97 us
    ppermute x3, starting transfers between devices, shifted(): lax.ppermute(value, axis, [(i, (i + shift) % size) for i in range(size)])  2.2 us
    reduce_sum x1, other arithmetic, gather_prefix(): slot = jnp.sum(jnp.where(mine, page_slot, 0))  1.54 us
    ppermute x3, waiting for transfers between devices, shifted(): lax.ppermute(value, axis, [(i, (i + shift) % size) for i in range(size)])  1.51 us
    reduce_sum x1, other arithmetic, on_device(): my_lengths = jnp.sum(jnp.where(matches, lengths[None, :], 0), 1)  1.32 us
  transfers between devices with their start and end apart: 16, of which 9 were waited for; matrix products, arithmetic and copies ran while one was open for 12% of the time, Pallas kernels for 9%

profile of v14, /device:TPU:0, one launch (start us, length us, event | category | flops | bytes accessed | tf_op | source)
XLA Modules:
  0.0 51.9 jit_solution(9695694000536458733)
XLA Ops:
  0.0 1.5 %fusion.26 = s32[]{:T(128)} fusion(s32[8]{0:T(128)} %param.15, s32[8]{0:T(128)} %param.14, s32[]{:T(128)} %axis_index.27), kind=kLoop, calls=%fused_computation.38 | loop fusion | flops 23 | bytes 72 | tf_op jit(solution)/shard_map/reduce_sum | solution.py:36
  2.2 1.0 %select_bitcast_fusion.rest_0_ = bf16[128,512]{1,0:T(8,128)(2,1)S(1)} fusion(bf16[2,128,1,512]{3,1,2,0:T(8,128)(2,1)} %param.13, pred[]{:T(512)S(6)} %eq.43), kind=kLoop, calls=%fused_computation.26 | loop fusion | flops 65536 | bytes 393217 | tf_op jit(solution)/shard_map/jit(_where)/select_n | solution.py:39
  3.2 5.1 %collective-permute-start.3 = (bf16[128,512]{1,0:T(8,128)(2,1)S(1)}, bf16[128,512]{1,0:T(8,128)(2,1)S(1)}, u32[]{:S(2)}, u32[]{:S(2)}) collective-permute-start(bf16[128,512]{1,0:T(8,128)(2,1)S(1)} %select_bitcast_fusion.rest_0_), channel_id=1, source_target_pairs={{0,24},{4,28},{8,16},{12,20},{16,8},{20,12},{24,0},{28,4},{1,25},{... | collective-permute-start | bytes 393224 | tf_op jit(solution)/shard_map/ppermute | solution.py:28
  8.4 1.5 %collective-permute-start = (bf16[128,512]{1,0:T(8,128)(2,1)S(1)}, bf16[128,512]{1,0:T(8,128)(2,1)S(1)}, u32[]{:S(2)}, u32[]{:S(2)}) collective-permute-start(bf16[128,512]{1,0:T(8,128)(2,1)S(1)} %select_bitcast_fusion.rest_0_), channel_id=1, source_target_pairs={{0,4},{4,0},{8,12},{12,8},{16,20},{20,16},{24,28},{28,24},{1,5},{5... | collective-permute-start | bytes 393224 | tf_op jit(solution)/shard_map/ppermute | solution.py:28
  9.9 2.0 %collective-permute-start.2 = (bf16[128,512]{1,0:T(8,128)(2,1)S(1)}, bf16[128,512]{1,0:T(8,128)(2,1)S(1)}, u32[]{:S(2)}, u32[]{:S(2)}) collective-permute-start(bf16[128,512]{1,0:T(8,128)(2,1)S(1)} %select_bitcast_fusion.rest_0_), channel_id=1, source_target_pairs={{0,12},{4,8},{8,4},{12,0},{16,28},{20,24},{24,20},{28,16},{1,13},{... | collective-permute-start | bytes 393224 | tf_op jit(solution)/shard_map/ppermute | solution.py:28
  12.0 0.8 %collective-permute-done.3.rest_4_ = bf16[128,512]{1,0:T(8,128)(2,1)S(1)} collective-permute-done((bf16[128,512]{1,0:T(8,128)(2,1)S(1)}, bf16[128,512]{1,0:T(8,128)(2,1)S(1)}, u32[]{:S(2)}, u32[]{:S(2)}) %collective-permute-start.3) | collective-permute-done | bytes 131104 | tf_op jit(solution)/shard_map/ppermute | solution.py:28
  12.8 1.7 %collective-permute-start.4 = (bf16[128,512]{1,0:T(8,128)(2,1)S(1)}, bf16[128,512]{1,0:T(8,128)(2,1)S(1)}, u32[]{:S(2)}, u32[]{:S(2)}) collective-permute-start(bf16[128,512]{1,0:T(8,128)(2,1)S(1)} %collective-permute-done.3.rest_4_), channel_id=1, source_target_pairs={{0,4},{4,0},{8,12},{12,8},{16,20},{20,16},{24,28},{28,24},{1,5},{5... | collective-permute-start | bytes 393224 | tf_op jit(solution)/shard_map/ppermute | solution.py:28
  14.5 1.5 %collective-permute-start.5 = (bf16[128,512]{1,0:T(8,128)(2,1)S(1)}, bf16[128,512]{1,0:T(8,128)(2,1)S(1)}, u32[]{:S(2)}, u32[]{:S(2)}) collective-permute-start(bf16[128,512]{1,0:T(8,128)(2,1)S(1)} %collective-permute-done.3.rest_4_), channel_id=1, source_target_pairs={{0,8},{4,12},{8,0},{12,4},{16,24},{20,28},{24,16},{28,20},{1,9},{5... | collective-permute-start | bytes 393224 | tf_op jit(solution)/shard_map/ppermute | solution.py:28
  16.3 0.8 %compare_reduce_fusion = pred[8]{0:T(512)(128)(4,1)S(1)} fusion(s32[8]{0:T(128)} %param.14, s32[8]{0:T(128)S(1)} %stack.35), kind=kLoop, calls=%fused_computation.27 | loop fusion | flops 120 | bytes 72 | tf_op jit(solution)/shard_map/reduce_or | solution.py:55
  17.7 0.7 %dynamic_slice.15 = s32[4]{0:T(128)S(1)} dynamic-slice(s32[32]{0:T(128)} %param.17, s32[]{:T(128)S(6)} %select_n.33), dynamic_slice_sizes={4} | dynamic-slice | bytes 36 | tf_op jit(solution)/shard_map/dynamic_slice | solution.py:161
  18.4 1.3 %select_reduce_fusion.length_ref = s32[4]{0:T(128)} fusion(s32[32]{0:T(128)} %param.16, s32[4]{0:T(128)S(1)} %dynamic_slice.15), kind=kLoop, calls=%fused_computation.30 | loop fusion | flops 380 | bytes 160 | tf_op jit(solution)/shard_map/reduce_sum | solution.py:163
  19.9 2.0 %collective-permute-done.5.rest_6_ = bf16[128,512]{1,0:T(8,128)(2,1)S(1)} collective-permute-done((bf16[128,512]{1,0:T(8,128)(2,1)S(1)}, bf16[128,512]{1,0:T(8,128)(2,1)S(1)}, u32[]{:S(2)}, u32[]{:S(2)}) %collective-permute-start.5) | collective-permute-done | bytes 131104 | tf_op jit(solution)/shard_map/ppermute | solution.py:28
  21.9 2.3 %collective-permute-done.6.rest_7_ = bf16[128,512]{1,0:T(8,128)(2,1)S(1)} collective-permute-done((bf16[128,512]{1,0:T(8,128)(2,1)S(1)}, bf16[128,512]{1,0:T(8,128)(2,1)S(1)}, u32[]{:S(2)}, u32[]{:S(2)}) %collective-permute-start.6) | collective-permute-done | bytes 131104 | tf_op jit(solution)/shard_map/ppermute | solution.py:28
  24.9 4.8 %shard_map.109 = bf16[2,128,512]{2,1,0:T(8,128)(2,1)} custom-call(s32[4]{0:T(128)} %select_reduce_fusion.length_ref, s32[8]{0:T(128)} %convert_element_type.18.valid_ref, bf16[4,128,1024]{2,1,0:T(8,128)(2,1)} %bitcast.28, f32[128,128]{1,0:T(8,128)} %constant.40.clone.cos_ref, f32[128,128]{1,0:T(8,128)} %constant.41.clone.sin_ref, ...), custom_call_target="tpu_custom_call" | custom-call | tf_op jit(solution)/shard_map/pallas_call | solution.py:132
  29.6 1.5 %collective-permute-start.9 = (bf16[256,512]{1,0:T(8,128)(2,1)}, bf16[256,512]{1,0:T(8,128)(2,1)S(1)}, u32[]{:S(2)}, u32[]{:S(2)}) collective-permute-start(bf16[256,512]{1,0:T(8,128)(2,1)} %bitcast.31), channel_id=1, source_target_pairs={{0,2},{1,3},{2,0},{3,1},{4,6},{5,7},{6,4},{7,5},{8,10},{9,11},{10,... | collective-permute-start | bytes 786440 | tf_op jit(solution)/shard_map/ppermute | solution.py:28
  31.1 4.8 %shard_map.110 = bf16[2,128,512]{2,1,0:T(8,128)(2,1)} custom-call(s32[4]{0:T(128)} %select_reduce_fusion.length_ref, s32[8]{0:T(128)} %convert_element_type.18.valid_ref, bf16[4,128,1024]{2,1,0:T(8,128)(2,1)} %bitcast.29, f32[128,128]{1,0:T(8,128)} %constant.40.clone.cos_ref, f32[128,128]{1,0:T(8,128)} %constant.41.clone.sin_ref, ...), custom_call_target="tpu_custom_call" | custom-call | tf_op jit(solution)/shard_map/pallas_call | solution.py:132
  36.8 1.8 %collective-permute-done.9 = bf16[256,512]{1,0:T(8,128)(2,1)S(1)} collective-permute-done((bf16[256,512]{1,0:T(8,128)(2,1)}, bf16[256,512]{1,0:T(8,128)(2,1)S(1)}, u32[]{:S(2)}, u32[]{:S(2)}) %collective-permute-start.9) | collective-permute-done | bytes 262176 | tf_op jit(solution)/shard_map/ppermute | solution.py:28
  38.6 1.5 %fusion.6 = f32[512,576]{0,1:T(8,128)S(1)} fusion(bf16[2048,576]{0,1:T(8,128)(2,1)S(1)} %copy-done, s32[]{:T(128)S(6)} %select_n.40, bf16[256,512]{1,0:T(8,128)(2,1)} %collective-permute-done.8, bf16[256,512]{1,0:T(8,128)(2,1)S(1)} %collective-permute-done.7), kind=kOutput, calls=%fused_computation.11 | convolution fusion | flops 303038464 | bytes 2293764 | tf_op jit(solution)/shard_map/dot_general | solution.py:181
  40.6 4.4 %collective-permute-done.10 = bf16[256,512]{1,0:T(8,128)(2,1)S(1)} collective-permute-done((bf16[256,512]{1,0:T(8,128)(2,1)}, bf16[256,512]{1,0:T(8,128)(2,1)S(1)}, u32[]{:S(2)}, u32[]{:S(2)}) %collective-permute-start.10) | collective-permute-done | bytes 262176 | tf_op jit(solution)/shard_map/ppermute | solution.py:28
  45.5 1.0 %collective-permute-done.12 = bf16[256,512]{1,0:T(8,128)(2,1)S(1)} collective-permute-done((bf16[256,512]{1,0:T(8,128)(2,1)S(1)}, bf16[256,512]{1,0:T(8,128)(2,1)S(1)}, u32[]{:S(2)}, u32[]{:S(2)}) %collective-permute-start.12) | collective-permute-done | bytes 262176 | tf_op jit(solution)/shard_map/ppermute | solution.py:28
  47.9 1.3 %collective-permute-start.15 = (f32[4,128]{1,0:T(4,128)S(1)}, f32[4,128]{1,0:T(4,128)S(1)}, u32[]{:S(2)}, u32[]{:S(2)}) collective-permute-start(f32[4,128]{1,0:T(4,128)S(1)} %bitcast.38), channel_id=1, source_target_pairs={{0,3},{1,0},{2,1},{3,2},{4,7},{5,4},{6,5},{7,6},{8,11},{9,8},{10,9... | collective-permute-start | bytes 6152 | tf_op jit(solution)/shard_map/ppermute | solution.py:24
  49.3 0.8 %collective-permute-done.13 = f32[4,128]{1,0:T(4,128)S(1)} collective-permute-done((f32[4,128]{1,0:T(4,128)S(1)}, f32[4,128]{1,0:T(4,128)S(1)}, u32[]{:S(2)}, u32[]{:S(2)}) %collective-permute-start.13) | collective-permute-done | bytes 2080 | tf_op jit(solution)/shard_map/ppermute | solution.py:24
  50.1 0.7 %collective-permute-done.14 = f32[4,128]{1,0:T(4,128)S(1)} collective-permute-done((f32[4,128]{1,0:T(4,128)S(1)}, f32[4,128]{1,0:T(4,128)S(1)}, u32[]{:S(2)}, u32[]{:S(2)}) %collective-permute-start.14) | collective-permute-done | bytes 2080 | tf_op jit(solution)/shard_map/ppermute | solution.py:24
  50.8 1.1 %fusion.3 = bf16[4,128,576]{1,2,0:T(8,128)(2,1)} fusion(bf16[4,128,576]{1,2,0:T(8,128)(2,1)S(1)} %copy-done.4, f32[4,128]{1,0:T(4,128)S(1)} %fusion.21, f32[576]{0:T(1024)S(1)} %copy-done.13, f32[4,128]{1,0:T(4,128)S(1)} %add_rsqrt_fusion, f32[512,576]{0,1:T(8,128)S(1)} %get-tuple-element.6), kind=kLoop, calls=%fused_computation.7 | loop fusion | flops 1769472 | bytes 2365696 | tf_op jit(solution)/shard_map/convert_element_type | solution.py:191
  (52 shorter events, 5.1 us)
Async XLA Ops:
  0.0 38.6 %copy-start = (bf16[2048,576]{0,1:T(8,128)(2,1)S(1)}, bf16[2048,576]{0,1:T(8,128)(2,1)}, u32[]{:S(2)}) copy-start(bf16[2048,576]{0,1:T(8,128)(2,1)} %param.18) | copy-start | bytes 7077892
  3.2 21.0 %copy-start.1 = (bf16[128,512]{1,0:T(8,128)(2,1)}, bf16[128,512]{1,0:T(8,128)(2,1)S(1)}, u32[]{:S(2)}) copy-start(bf16[128,512]{1,0:T(8,128)(2,1)S(1)} %select_bitcast_fusion.rest_0_) | copy-start | bytes 393220
  3.2 9.5 %collective-permute-start.3 = (bf16[128,512]{1,0:T(8,128)(2,1)S(1)}, bf16[128,512]{1,0:T(8,128)(2,1)S(1)}, u32[]{:S(2)}, u32[]{:S(2)}) collective-permute-start(bf16[128,512]{1,0:T(8,128)(2,1)S(1)} %select_bitcast_fusion.rest_0_), channel_id=1, source_target_pairs={{0,24},{4,28},{8,16},{12,20},{16,8},{20,12},{24,0},{28,4},{1,25},{... | collective-permute-start | bytes 393224 | tf_op jit(solution)/shard_map/ppermute | solution.py:28
  8.4 7.5 %collective-permute-start = (bf16[128,512]{1,0:T(8,128)(2,1)S(1)}, bf16[128,512]{1,0:T(8,128)(2,1)S(1)}, u32[]{:S(2)}, u32[]{:S(2)}) collective-permute-start(bf16[128,512]{1,0:T(8,128)(2,1)S(1)} %select_bitcast_fusion.rest_0_), channel_id=1, source_target_pairs={{0,4},{4,0},{8,12},{12,8},{16,20},{20,16},{24,28},{28,24},{1,5},{5... | collective-permute-start | bytes 393224 | tf_op jit(solution)/shard_map/ppermute | solution.py:28
  9.9 9.9 %collective-permute-start.1 = (bf16[128,512]{1,0:T(8,128)(2,1)S(1)}, bf16[128,512]{1,0:T(8,128)(2,1)S(1)}, u32[]{:S(2)}, u32[]{:S(2)}) collective-permute-start(bf16[128,512]{1,0:T(8,128)(2,1)S(1)} %select_bitcast_fusion.rest_0_), channel_id=1, source_target_pairs={{0,8},{4,12},{8,0},{12,4},{16,24},{20,28},{24,16},{28,20},{1,9},{5... | collective-permute-start | bytes 393224 | tf_op jit(solution)/shard_map/ppermute | solution.py:28
  9.9 9.9 %collective-permute-start.2 = (bf16[128,512]{1,0:T(8,128)(2,1)S(1)}, bf16[128,512]{1,0:T(8,128)(2,1)S(1)}, u32[]{:S(2)}, u32[]{:S(2)}) collective-permute-start(bf16[128,512]{1,0:T(8,128)(2,1)S(1)} %select_bitcast_fusion.rest_0_), channel_id=1, source_target_pairs={{0,12},{4,8},{8,4},{12,0},{16,28},{20,24},{24,20},{28,16},{1,13},{... | collective-permute-start | bytes 393224 | tf_op jit(solution)/shard_map/ppermute | solution.py:28
  12.8 11.4 %copy-start.5 = (bf16[128,512]{1,0:T(8,128)(2,1)}, bf16[128,512]{1,0:T(8,128)(2,1)S(1)}, u32[]{:S(2)}) copy-start(bf16[128,512]{1,0:T(8,128)(2,1)S(1)} %collective-permute-done.3.rest_4_) | copy-start | bytes 393220
  12.8 7.1 %collective-permute-start.4 = (bf16[128,512]{1,0:T(8,128)(2,1)S(1)}, bf16[128,512]{1,0:T(8,128)(2,1)S(1)}, u32[]{:S(2)}, u32[]{:S(2)}) collective-permute-start(bf16[128,512]{1,0:T(8,128)(2,1)S(1)} %collective-permute-done.3.rest_4_), channel_id=1, source_target_pairs={{0,4},{4,0},{8,12},{12,8},{16,20},{20,16},{24,28},{28,24},{1,5},{5... | collective-permute-start | bytes 393224 | tf_op jit(solution)/shard_map/ppermute | solution.py:28
  14.5 7.4 %collective-permute-start.5 = (bf16[128,512]{1,0:T(8,128)(2,1)S(1)}, bf16[128,512]{1,0:T(8,128)(2,1)S(1)}, u32[]{:S(2)}, u32[]{:S(2)}) collective-permute-start(bf16[128,512]{1,0:T(8,128)(2,1)S(1)} %collective-permute-done.3.rest_4_), channel_id=1, source_target_pairs={{0,8},{4,12},{8,0},{12,4},{16,24},{20,28},{24,16},{28,20},{1,9},{5... | collective-permute-start | bytes 393224 | tf_op jit(solution)/shard_map/ppermute | solution.py:28
  15.9 8.3 %copy-start.6 = (bf16[128,512]{1,0:T(8,128)(2,1)}, bf16[128,512]{1,0:T(8,128)(2,1)S(1)}, u32[]{:S(2)}) copy-start(bf16[128,512]{1,0:T(8,128)(2,1)S(1)} %collective-permute-done.rest_1_) | copy-start | bytes 393220
  15.9 8.3 %collective-permute-start.6 = (bf16[128,512]{1,0:T(8,128)(2,1)S(1)}, bf16[128,512]{1,0:T(8,128)(2,1)S(1)}, u32[]{:S(2)}, u32[]{:S(2)}) collective-permute-start(bf16[128,512]{1,0:T(8,128)(2,1)S(1)} %collective-permute-done.3.rest_4_), channel_id=1, source_target_pairs={{0,12},{4,8},{8,4},{12,0},{16,28},{20,24},{24,20},{28,16},{1,13},{... | collective-permute-start | bytes 393224 | tf_op jit(solution)/shard_map/ppermute | solution.py:28
  19.8 4.5 %copy-start.7 = (bf16[128,512]{1,0:T(8,128)(2,1)}, bf16[128,512]{1,0:T(8,128)(2,1)S(1)}, u32[]{:S(2)}) copy-start(bf16[128,512]{1,0:T(8,128)(2,1)S(1)} %collective-permute-done.1.rest_2_) | copy-start | bytes 393220
  19.8 4.5 %copy-start.8 = (bf16[128,512]{1,0:T(8,128)(2,1)}, bf16[128,512]{1,0:T(8,128)(2,1)S(1)}, u32[]{:S(2)}) copy-start(bf16[128,512]{1,0:T(8,128)(2,1)S(1)} %collective-permute-done.2.rest_3_) | copy-start | bytes 393220
  29.6 8.9 %collective-permute-start.7 = (bf16[256,512]{1,0:T(8,128)(2,1)}, bf16[256,512]{1,0:T(8,128)(2,1)S(1)}, u32[]{:S(2)}, u32[]{:S(2)}) collective-permute-start(bf16[256,512]{1,0:T(8,128)(2,1)} %bitcast.30), channel_id=1, source_target_pairs={{0,1},{1,0},{2,3},{3,2},{4,5},{5,4},{6,7},{7,6},{8,9},{9,8},{10,11... | collective-permute-start | bytes 786440 | tf_op jit(solution)/shard_map/ppermute | solution.py:28
  29.6 8.9 %collective-permute-start.9 = (bf16[256,512]{1,0:T(8,128)(2,1)}, bf16[256,512]{1,0:T(8,128)(2,1)S(1)}, u32[]{:S(2)}, u32[]{:S(2)}) collective-permute-start(bf16[256,512]{1,0:T(8,128)(2,1)} %bitcast.31), channel_id=1, source_target_pairs={{0,2},{1,3},{2,0},{3,1},{4,6},{5,7},{6,4},{7,5},{8,10},{9,11},{10,... | collective-permute-start | bytes 786440 | tf_op jit(solution)/shard_map/ppermute | solution.py:28
  36.0 2.6 %collective-permute-start.8 = (bf16[256,512]{1,0:T(8,128)(2,1)}, bf16[256,512]{1,0:T(8,128)(2,1)}, u32[]{:S(2)}, u32[]{:S(2)}) collective-permute-start(bf16[256,512]{1,0:T(8,128)(2,1)} %bitcast.33), channel_id=1, source_target_pairs={{0,1},{1,0},{2,3},{3,2},{4,5},{5,4},{6,7},{7,6},{8,9},{9,8},{10,11... | collective-permute-start | bytes 786440 | tf_op jit(solution)/shard_map/ppermute | solution.py:28
  36.2 8.8 %collective-permute-start.10 = (bf16[256,512]{1,0:T(8,128)(2,1)}, bf16[256,512]{1,0:T(8,128)(2,1)S(1)}, u32[]{:S(2)}, u32[]{:S(2)}) collective-permute-start(bf16[256,512]{1,0:T(8,128)(2,1)} %bitcast.34), channel_id=1, source_target_pairs={{0,2},{1,3},{2,0},{3,1},{4,6},{5,7},{6,4},{7,5},{8,10},{9,11},{10,... | collective-permute-start | bytes 786440 | tf_op jit(solution)/shard_map/ppermute | solution.py:28
  38.6 6.9 %collective-permute-start.11 = (bf16[256,512]{1,0:T(8,128)(2,1)S(1)}, bf16[256,512]{1,0:T(8,128)(2,1)S(1)}, u32[]{:S(2)}, u32[]{:S(2)}) collective-permute-start(bf16[256,512]{1,0:T(8,128)(2,1)S(1)} %collective-permute-done.9), channel_id=1, source_target_pairs={{0,1},{1,0},{2,3},{3,2},{4,5},{5,4},{6,7},{7,6},{8,9},{9,8},{10,11... | collective-permute-start | bytes 786440 | tf_op jit(solution)/shard_map/ppermute | solution.py:28
  45.0 1.5 %collective-permute-start.12 = (bf16[256,512]{1,0:T(8,128)(2,1)S(1)}, bf16[256,512]{1,0:T(8,128)(2,1)S(1)}, u32[]{:S(2)}, u32[]{:S(2)}) collective-permute-start(bf16[256,512]{1,0:T(8,128)(2,1)S(1)} %collective-permute-done.10), channel_id=1, source_target_pairs={{0,1},{1,0},{2,3},{3,2},{4,5},{5,4},{6,7},{7,6},{8,9},{9,8},{10,11... | collective-permute-start | bytes 786440 | tf_op jit(solution)/shard_map/ppermute | solution.py:28
  45.5 5.3 %copy-start.4 = (bf16[4,128,576]{1,2,0:T(8,128)(2,1)S(1)}, bf16[4,128,576]{1,2,0:T(8,128)(2,1)}, u32[]{:S(2)}) copy-start(bf16[4,128,576]{1,2,0:T(8,128)(2,1)} %param.11) | copy-start | bytes 1769476
  45.5 5.3 %copy-start.13 = (f32[576]{0:T(1024)S(1)}, f32[576]{0:T(1024)}, u32[]{:S(2)}) copy-start(f32[576]{0:T(1024)} %param.19) | copy-start | bytes 6916
  47.0 3.1 %collective-permute-start.13 = (f32[4,128]{1,0:T(4,128)S(1)}, f32[4,128]{1,0:T(4,128)S(1)}, u32[]{:S(2)}, u32[]{:S(2)}) collective-permute-start(f32[4,128]{1,0:T(4,128)S(1)} %bitcast.36), channel_id=1, source_target_pairs={{0,1},{1,2},{2,3},{3,0},{4,5},{5,6},{6,7},{7,4},{8,9},{9,10},{10,1... | collective-permute-start | bytes 6152 | tf_op jit(solution)/shard_map/ppermute | solution.py:24
  47.2 3.6 %collective-permute-start.14 = (f32[4,128]{1,0:T(4,128)S(1)}, f32[4,128]{1,0:T(4,128)S(1)}, u32[]{:S(2)}, u32[]{:S(2)}) collective-permute-start(f32[4,128]{1,0:T(4,128)S(1)} %bitcast.37), channel_id=1, source_target_pairs={{0,2},{1,3},{2,0},{3,1},{4,6},{5,7},{6,4},{7,5},{8,10},{9,11},{10,... | collective-permute-start | bytes 6152 | tf_op jit(solution)/shard_map/ppermute | solution.py:24
  47.9 2.9 %collective-permute-start.15 = (f32[4,128]{1,0:T(4,128)S(1)}, f32[4,128]{1,0:T(4,128)S(1)}, u32[]{:S(2)}, u32[]{:S(2)}) collective-permute-start(f32[4,128]{1,0:T(4,128)S(1)} %bitcast.38), channel_id=1, source_target_pairs={{0,3},{1,0},{2,1},{3,2},{4,7},{5,4},{6,5},{7,6},{8,11},{9,8},{10,9... | collective-permute-start | bytes 6152 | tf_op jit(solution)/shard_map/ppermute | solution.py:24
  (6 other events, 19.3 us)

commit v15 on v6

--- a/solution.py
+++ b/solution.py
@@ -69,9 +69,8 @@
     return np.cos(angles).astype(np.float32), np.sin(angles).astype(np.float32)
 
 
-def attention_kernel(length_ref, valid_ref, qkv_ref, cos_ref, sin_ref, *rest, offset):
+def attention_kernel(limit_ref, flag_ref, qkv_ref, cos_ref, sin_ref, *rest):
     page_refs, out_ref = rest[:-1], rest[-1]
-    request = pl.program_id(0) + offset
     slots = qkv_ref.shape[1]
     per_group = qkv_ref.shape[2] // HD - 2
     half = HD // 2
@@ -98,17 +97,13 @@
 
     scores = lax.dot_general(queries, keys, (((1,), (1,)), ((), ())),
                              preferred_element_type=jnp.float32)
-    page_column = lax.broadcasted_iota(jnp.int32, (1, key_count), 1) // pages[0].shape[0]
-    page_flag = jnp.zeros((1, key_count), jnp.int32)
-    for index in range(len(pages)):
-        page_flag = page_flag + jnp.where(page_column == index, valid_ref[index], 0)
-    page_flag = page_flag.astype(jnp.float32)
     column = lax.broadcasted_iota(jnp.int32, (rows, key_count), 1)
     slot = lax.broadcasted_iota(jnp.int32, (rows, key_count), 0) % slots
     suffix_pos = column - prefix_len
-    suffix_ok = (suffix_pos >= 0) & (suffix_pos <= slot) & (suffix_pos < length_ref[request])
-    exps = capped_exp(scores)
-    raw = jnp.where(suffix_ok, exps, jnp.where(column < prefix_len, exps * page_flag, 0.0))
+    limit = limit_ref[0]
+    suffix_ok = (suffix_pos <= slot) & (suffix_pos < limit)
+    exps = capped_exp(scores) * flag_ref[...]
+    raw = jnp.where(suffix_ok, exps, 0.0)
     totals = jnp.sum(raw, -1, keepdims=True)
     weights = (raw / totals).astype(jnp.bfloat16)
     attended = jnp.dot(weights, values, preferred_element_type=jnp.float32).astype(jnp.bfloat16)
@@ -117,23 +112,30 @@
 
 
 def attend(qkv, cosine, sine, blocks, lengths, valid, offset, count):
-    _, slots, width = qkv.shape
+    requests, slots, width = qkv.shape
     per_group = width // HD - 2
     page_len, page_width = blocks[0].shape
-    full = lambda shape: pl.BlockSpec(shape, lambda r, *_: (0,) * len(shape))
-    grid_spec = pltpu.PrefetchScalarGridSpec(
-        num_scalar_prefetch=2,
+    prefix_len = page_len * len(blocks)
+    key_count = prefix_len + slots
+    flags = jnp.concatenate([jnp.repeat(valid.astype(jnp.float32), page_len),
+                             jnp.ones((slots,), jnp.float32)])
+    flags = flags[None, :]
+    limits = jnp.concatenate(
+        [jnp.broadcast_to(jnp.full((requests, 1), prefix_len + slots, jnp.int32), (requests, prefix_len)),
+         jnp.broadcast_to(lengths[:, None], (requests, slots))], 1)
+    limits = limits[:, None, :]
+    full = lambda shape: pl.BlockSpec(shape, lambda r: (0,) * len(shape))
+    return pl.pallas_call(
+        attention_kernel,
         grid=(count,),
-        in_specs=[pl.BlockSpec((1, slots, width), lambda r, *_: (r + offset, 0, 0)),
+        in_specs=[pl.BlockSpec((1, 1, key_count), lambda r: (r + offset, 0, 0)),
+                  full((1, key_count)),
+                  pl.BlockSpec((1, slots, width), lambda r: (r + offset, 0, 0)),
                   full(cosine.shape), full(sine.shape)]
                  + [full((page_len, page_width)) for _ in blocks],
-        out_specs=pl.BlockSpec((1, slots, per_group * HD), lambda r, *_: (r, 0, 0)),
-    )
-    return pl.pallas_call(
-        functools.partial(attention_kernel, offset=offset),
-        grid_spec=grid_spec,
+        out_specs=pl.BlockSpec((1, slots, per_group * HD), lambda r: (r, 0, 0)),
         out_shape=jax.ShapeDtypeStruct((count, slots, per_group * HD), jnp.bfloat16),
-    )(lengths, valid, qkv, cosine, sine, *blocks)
+    )(limits, flags, qkv, cosine, sine, *blocks)
 
 def project(own, w_out, tp_index, n_tp, group_width):
     if n_tp == 4:

time: 52.7 us -> 51.7 us (0.981)
  local copies, waits for them, and re-layouts: 1.67 us -> 3.02 us
  Pallas kernels: 9.58 us -> 8.27 us
  other arithmetic: 6.71 us -> 5.64 us
    pallas_call x2, Pallas kernels: 9.58 us -> 8.27 us  [attend(): pl.pallas_call(attention_kernel, grid=(count,), in_specs=[pl.BlockSpec((1...]
    broadcast_in_dim x0 -> x3, local copies, waits for them, and re-layouts: none -> 1.28 us  [the longest x1 0.61 us: attend(): limits = limits[:, None, :]]
    convert_element_type x1, other arithmetic: 0.6 us -> 0.01 us  [attend(): valid.astype(jnp.float32)]
  transfers between devices with their start and end apart: 16 -> 16, of which waited for: 8 -> 7; matrix products, arithmetic and copies ran while one was open for 12% -> 12% of each run, Pallas kernels for 9% -> 8%
where the time goes in v15:
time: 51.7 us; the launch traced here: 51.3 us
  starting transfers between devices  17.7 us (34%)
  waiting for transfers between devices  12.9 us (25%)
  Pallas kernels  8.27 us (16%)
  other arithmetic  5.64 us (11%)
  local copies, waits for them, and re-layouts  3.02 us (6%)
  matrix products  2.78 us (5%)
  between operations  0.92 us (2%)
    ppermute x13, starting transfers between devices, swapped(): return lax.ppermute(value, axis, [(i, i ^ mask) for i in range(size)])  14.8 us
    ppermute x13, waiting for transfers between devices, swapped(): return lax.ppermute(value, axis, [(i, i ^ mask) for i in range(size)])  11.6 us
    pallas_call x2, Pallas kernels, attend(): pl.pallas_call(attention_kernel, grid=(count,), in_specs=[pl.BlockSpec((1...  8.27 us
    ppermute x3, starting transfers between devices, shifted(): lax.ppermute(value, axis, [(i, (i + shift) % size) for i in range(size)])  2.96 us
    dot_general x8, matrix products, project(): term = jnp.dot(block, rows, preferred_element_type=jnp.float32)  2.78 us
    reduce_sum x1, other arithmetic, gather_prefix(): slot = jnp.sum(jnp.where(mine, page_slot, 0))  1.54 us
    ppermute x3, waiting for transfers between devices, shifted(): lax.ppermute(value, axis, [(i, (i + shift) % size) for i in range(size)])  1.24 us
    convert_element_type x1, other arithmetic, on_device(): return ((source + branch) * live_mask[..., None]).astype(jnp.bfloat16)  1.1 us
  transfers between devices with their start and end apart: 16, of which 7 were waited for; matrix products, arithmetic and copies ran while one was open for 12% of the time, Pallas kernels for 8%

profile of v15, /device:TPU:0, one launch (start us, length us, event | category | flops | bytes accessed | tf_op | source)
XLA Modules:
  0.0 51.3 jit_solution(16973909428662675952)
XLA Ops:
  0.0 1.5 %fusion.28 = s32[]{:T(128)} fusion(s32[8]{0:T(128)} %param.15, s32[8]{0:T(128)} %param.14, s32[]{:T(128)} %axis_index.27), kind=kLoop, calls=%fused_computation.43 | loop fusion | flops 23 | bytes 72 | tf_op jit(solution)/shard_map/reduce_sum | solution.py:36
  2.2 1.0 %select_bitcast_fusion.rest_0_ = bf16[128,512]{1,0:T(8,128)(2,1)S(1)} fusion(bf16[2,128,1,512]{3,1,2,0:T(8,128)(2,1)} %param.13, pred[]{:T(512)S(6)} %eq.43), kind=kLoop, calls=%fused_computation.26 | loop fusion | flops 65536 | bytes 393217 | tf_op jit(solution)/shard_map/jit(_where)/select_n | solution.py:39
  3.2 5.1 %collective-permute-start.3 = (bf16[128,512]{1,0:T(8,128)(2,1)S(1)}, bf16[128,512]{1,0:T(8,128)(2,1)S(1)}, u32[]{:S(2)}, u32[]{:S(2)}) collective-permute-start(bf16[128,512]{1,0:T(8,128)(2,1)S(1)} %select_bitcast_fusion.rest_0_), channel_id=1, source_target_pairs={{0,24},{4,28},{8,16},{12,20},{16,8},{20,12},{24,0},{28,4},{1,25},{... | collective-permute-start | bytes 393224 | tf_op jit(solution)/shard_map/ppermute | solution.py:28
  8.4 1.5 %collective-permute-start = (bf16[128,512]{1,0:T(8,128)(2,1)S(1)}, bf16[128,512]{1,0:T(8,128)(2,1)S(1)}, u32[]{:S(2)}, u32[]{:S(2)}) collective-permute-start(bf16[128,512]{1,0:T(8,128)(2,1)S(1)} %select_bitcast_fusion.rest_0_), channel_id=1, source_target_pairs={{0,4},{4,0},{8,12},{12,8},{16,20},{20,16},{24,28},{28,24},{1,5},{5... | collective-permute-start | bytes 393224 | tf_op jit(solution)/shard_map/ppermute | solution.py:28
  9.9 2.0 %collective-permute-start.2 = (bf16[128,512]{1,0:T(8,128)(2,1)S(1)}, bf16[128,512]{1,0:T(8,128)(2,1)S(1)}, u32[]{:S(2)}, u32[]{:S(2)}) collective-permute-start(bf16[128,512]{1,0:T(8,128)(2,1)S(1)} %select_bitcast_fusion.rest_0_), channel_id=1, source_target_pairs={{0,12},{4,8},{8,4},{12,0},{16,28},{20,24},{24,20},{28,16},{1,13},{... | collective-permute-start | bytes 393224 | tf_op jit(solution)/shard_map/ppermute | solution.py:28
  11.9 0.8 %compare_reduce_fusion = pred[8]{0:T(512)(128)(4,1)S(1)} fusion(s32[8]{0:T(128)} %param.14, s32[8]{0:T(128)S(1)} %stack.35), kind=kLoop, calls=%fused_computation.27 | loop fusion | flops 120 | bytes 72 | tf_op jit(solution)/shard_map/reduce_or | solution.py:55
  12.8 1.7 %collective-permute-start.4 = (bf16[128,512]{1,0:T(8,128)(2,1)S(1)}, bf16[128,512]{1,0:T(8,128)(2,1)S(1)}, u32[]{:S(2)}, u32[]{:S(2)}) collective-permute-start(bf16[128,512]{1,0:T(8,128)(2,1)S(1)} %collective-permute-done.3.rest_4_), channel_id=1, source_target_pairs={{0,4},{4,0},{8,12},{12,8},{16,20},{20,16},{24,28},{28,24},{1,5},{5... | collective-permute-start | bytes 393224 | tf_op jit(solution)/shard_map/ppermute | solution.py:28
  14.5 1.5 %collective-permute-start.5 = (bf16[128,512]{1,0:T(8,128)(2,1)S(1)}, bf16[128,512]{1,0:T(8,128)(2,1)S(1)}, u32[]{:S(2)}, u32[]{:S(2)}) collective-permute-start(bf16[128,512]{1,0:T(8,128)(2,1)S(1)} %collective-permute-done.3.rest_4_), channel_id=1, source_target_pairs={{0,8},{4,12},{8,0},{12,4},{16,24},{20,28},{24,16},{28,20},{1,9},{5... | collective-permute-start | bytes 393224 | tf_op jit(solution)/shard_map/ppermute | solution.py:28
  16.4 0.6 %broadcast_in_dim.29.flag_ref = f32[1,1152]{1,0:T(1,128)} reshape(f32[1152]{0:T(1024)S(1)} %concatenate.12) | data formatting | bytes 9216 | tf_op jit(solution)/shard_map/broadcast_in_dim | solution.py:122
  17.0 0.7 %dynamic_slice.19 = s32[4]{0:T(128)S(1)} dynamic-slice(s32[32]{0:T(128)} %param.17, s32[]{:T(128)S(6)} %select_n.37), dynamic_slice_sizes={4} | dynamic-slice | bytes 36 | tf_op jit(solution)/shard_map/dynamic_slice | solution.py:170
  17.8 0.8 %select_reduce_fusion = s32[4]{0:T(128)S(1)} fusion(s32[32]{0:T(128)} %param.16, s32[4]{0:T(128)S(1)} %dynamic_slice.19), kind=kLoop, calls=%fused_computation.31 | loop fusion | flops 380 | bytes 160 | tf_op jit(solution)/shard_map/reduce_sum | solution.py:172
  18.7 0.6 %broadcast_in_dim.27.limit_ref = s32[4,1,1152]{2,1,0:T(1,128)} reshape(s32[4,1152]{1,0:T(4,128)S(1)} %concatenate.11) | data formatting | bytes 36864 | tf_op jit(solution)/shard_map/broadcast_in_dim | solution.py:126
  19.3 0.6 %collective-permute-done.4.rest_5_ = bf16[128,512]{1,0:T(8,128)(2,1)S(1)} collective-permute-done((bf16[128,512]{1,0:T(8,128)(2,1)S(1)}, bf16[128,512]{1,0:T(8,128)(2,1)S(1)}, u32[]{:S(2)}, u32[]{:S(2)}) %collective-permute-start.4) | collective-permute-done | bytes 131104 | tf_op jit(solution)/shard_map/ppermute | solution.py:28
  19.9 1.9 %collective-permute-done.5.rest_6_ = bf16[128,512]{1,0:T(8,128)(2,1)S(1)} collective-permute-done((bf16[128,512]{1,0:T(8,128)(2,1)S(1)}, bf16[128,512]{1,0:T(8,128)(2,1)S(1)}, u32[]{:S(2)}, u32[]{:S(2)}) %collective-permute-start.5) | collective-permute-done | bytes 131104 | tf_op jit(solution)/shard_map/ppermute | solution.py:28
  21.9 2.3 %collective-permute-done.6.rest_7_ = bf16[128,512]{1,0:T(8,128)(2,1)S(1)} collective-permute-done((bf16[128,512]{1,0:T(8,128)(2,1)S(1)}, bf16[128,512]{1,0:T(8,128)(2,1)S(1)}, u32[]{:S(2)}, u32[]{:S(2)}) %collective-permute-start.6) | collective-permute-done | bytes 131104 | tf_op jit(solution)/shard_map/ppermute | solution.py:28
  24.8 4.1 %shard_map.109 = bf16[2,128,512]{2,1,0:T(8,128)(2,1)} custom-call(s32[4,1,1152]{2,1,0:T(1,128)} %broadcast_in_dim.27.limit_ref, f32[1,1152]{1,0:T(1,128)} %broadcast_in_dim.29.flag_ref, bf16[4,128,1024]{2,1,0:T(8,128)(2,1)} %bitcast.37, f32[128,128]{1,0:T(8,128)} %constant.44.clone.cos_ref, f32[128,128]{1,0:T(8,128)} %constant.45.clone.sin_ref, ...), custom_call_target="tpu_custom_call" | custom-call | tf_op jit(solution)/shard_map/pallas_call | solution.py:128
  29.0 1.5 %collective-permute-start.8 = (bf16[256,512]{1,0:T(8,128)(2,1)}, bf16[256,512]{1,0:T(8,128)(2,1)S(1)}, u32[]{:S(2)}, u32[]{:S(2)}) collective-permute-start(bf16[256,512]{1,0:T(8,128)(2,1)} %bitcast.42), channel_id=1, source_target_pairs={{0,2},{1,3},{2,0},{3,1},{4,6},{5,7},{6,4},{7,5},{8,10},{9,11},{10,... | collective-permute-start | bytes 786440 | tf_op jit(solution)/shard_map/ppermute | solution.py:28
  30.5 4.1 %shard_map.110 = bf16[2,128,512]{2,1,0:T(8,128)(2,1)} custom-call(s32[4,1,1152]{2,1,0:T(1,128)} %broadcast_in_dim.27.limit_ref, f32[1,1152]{1,0:T(1,128)} %broadcast_in_dim.29.flag_ref, bf16[4,128,1024]{2,1,0:T(8,128)(2,1)} %bitcast.38, f32[128,128]{1,0:T(8,128)} %constant.44.clone.cos_ref, f32[128,128]{1,0:T(8,128)} %constant.45.clone.sin_ref, ...), custom_call_target="tpu_custom_call" | custom-call | tf_op jit(solution)/shard_map/pallas_call | solution.py:128
  35.7 1.4 %collective-permute-done.8 = bf16[256,512]{1,0:T(8,128)(2,1)S(1)} collective-permute-done((bf16[256,512]{1,0:T(8,128)(2,1)}, bf16[256,512]{1,0:T(8,128)(2,1)S(1)}, u32[]{:S(2)}, u32[]{:S(2)}) %collective-permute-start.8) | collective-permute-done | bytes 262176 | tf_op jit(solution)/shard_map/ppermute | solution.py:28
  37.2 5.3 %collective-permute-done.11 = bf16[256,512]{1,0:T(8,128)(2,1)S(1)} collective-permute-done((bf16[256,512]{1,0:T(8,128)(2,1)}, bf16[256,512]{1,0:T(8,128)(2,1)S(1)}, u32[]{:S(2)}, u32[]{:S(2)}) %collective-permute-start.11) | collective-permute-done | bytes 262176 | tf_op jit(solution)/shard_map/ppermute | solution.py:28
  46.4 1.5 %collective-permute-start.14 = (f32[4,128]{1,0:T(4,128)S(1)}, f32[4,128]{1,0:T(4,128)S(1)}, u32[]{:S(2)}, u32[]{:S(2)}) collective-permute-start(f32[4,128]{1,0:T(4,128)S(1)} %bitcast.46), channel_id=1, source_target_pairs={{0,2},{1,3},{2,0},{3,1},{4,6},{5,7},{6,4},{7,5},{8,10},{9,11},{10,... | collective-permute-start | bytes 6152 | tf_op jit(solution)/shard_map/ppermute | solution.py:24
  47.9 0.9 %collective-permute-start.15 = (f32[4,128]{1,0:T(4,128)S(1)}, f32[4,128]{1,0:T(4,128)S(1)}, u32[]{:S(2)}, u32[]{:S(2)}) collective-permute-start(f32[4,128]{1,0:T(4,128)S(1)} %bitcast.47), channel_id=1, source_target_pairs={{0,3},{1,0},{2,1},{3,2},{4,7},{5,4},{6,5},{7,6},{8,11},{9,8},{10,9... | collective-permute-start | bytes 6152 | tf_op jit(solution)/shard_map/ppermute | solution.py:24
  48.9 1.1 %collective-permute-done.14 = f32[4,128]{1,0:T(4,128)S(1)} collective-permute-done((f32[4,128]{1,0:T(4,128)S(1)}, f32[4,128]{1,0:T(4,128)S(1)}, u32[]{:S(2)}, u32[]{:S(2)}) %collective-permute-start.14) | collective-permute-done | bytes 2080 | tf_op jit(solution)/shard_map/ppermute | solution.py:24
  50.2 1.1 %fusion.5 = bf16[4,128,576]{1,2,0:T(8,128)(2,1)} fusion(f32[72,4,8,128]{3,2,1,0:T(8,128)S(1)} %get-tuple-element.6, bf16[4,128,576]{1,2,0:T(8,128)(2,1)S(1)} %copy-done.4, f32[4,128]{1,0:T(4,128)S(1)} %fusion.19, f32[576]{0:T(1024)S(1)} %copy-done.12, f32[4,128]{1,0:T(4,128)S(1)} %add_rsqrt_fusion), kind=kLoop, calls=%fused_computation.10 | loop fusion | flops 1769472 | bytes 2365696 | tf_op jit(solution)/shard_map/convert_element_type | solution.py:194
  (61 shorter events, 6.5 us)
Async XLA Ops:
  0.0 42.5 %copy-start = (bf16[2048,576]{0,1:T(8,128)(2,1)S(1)}, bf16[2048,576]{0,1:T(8,128)(2,1)}, u32[]{:S(2)}) copy-start(bf16[2048,576]{0,1:T(8,128)(2,1)} %param.18) | copy-start | bytes 7077892
  3.2 21.0 %copy-start.1 = (bf16[128,512]{1,0:T(8,128)(2,1)}, bf16[128,512]{1,0:T(8,128)(2,1)S(1)}, u32[]{:S(2)}) copy-start(bf16[128,512]{1,0:T(8,128)(2,1)S(1)} %select_bitcast_fusion.rest_0_) | copy-start | bytes 393220
  3.2 9.6 %collective-permute-start.3 = (bf16[128,512]{1,0:T(8,128)(2,1)S(1)}, bf16[128,512]{1,0:T(8,128)(2,1)S(1)}, u32[]{:S(2)}, u32[]{:S(2)}) collective-permute-start(bf16[128,512]{1,0:T(8,128)(2,1)S(1)} %select_bitcast_fusion.rest_0_), channel_id=1, source_target_pairs={{0,24},{4,28},{8,16},{12,20},{16,8},{20,12},{24,0},{28,4},{1,25},{... | collective-permute-start | bytes 393224 | tf_op jit(solution)/shard_map/ppermute | solution.py:28
  8.4 7.5 %collective-permute-start = (bf16[128,512]{1,0:T(8,128)(2,1)S(1)}, bf16[128,512]{1,0:T(8,128)(2,1)S(1)}, u32[]{:S(2)}, u32[]{:S(2)}) collective-permute-start(bf16[128,512]{1,0:T(8,128)(2,1)S(1)} %select_bitcast_fusion.rest_0_), channel_id=1, source_target_pairs={{0,4},{4,0},{8,12},{12,8},{16,20},{20,16},{24,28},{28,24},{1,5},{5... | collective-permute-start | bytes 393224 | tf_op jit(solution)/shard_map/ppermute | solution.py:28
  9.9 9.4 %collective-permute-start.1 = (bf16[128,512]{1,0:T(8,128)(2,1)S(1)}, bf16[128,512]{1,0:T(8,128)(2,1)S(1)}, u32[]{:S(2)}, u32[]{:S(2)}) collective-permute-start(bf16[128,512]{1,0:T(8,128)(2,1)S(1)} %select_bitcast_fusion.rest_0_), channel_id=1, source_target_pairs={{0,8},{4,12},{8,0},{12,4},{16,24},{20,28},{24,16},{28,20},{1,9},{5... | collective-permute-start | bytes 393224 | tf_op jit(solution)/shard_map/ppermute | solution.py:28
  9.9 9.4 %collective-permute-start.2 = (bf16[128,512]{1,0:T(8,128)(2,1)S(1)}, bf16[128,512]{1,0:T(8,128)(2,1)S(1)}, u32[]{:S(2)}, u32[]{:S(2)}) collective-permute-start(bf16[128,512]{1,0:T(8,128)(2,1)S(1)} %select_bitcast_fusion.rest_0_), channel_id=1, source_target_pairs={{0,12},{4,8},{8,4},{12,0},{16,28},{20,24},{24,20},{28,16},{1,13},{... | collective-permute-start | bytes 393224 | tf_op jit(solution)/shard_map/ppermute | solution.py:28
  12.8 11.4 %copy-start.5 = (bf16[128,512]{1,0:T(8,128)(2,1)}, bf16[128,512]{1,0:T(8,128)(2,1)S(1)}, u32[]{:S(2)}) copy-start(bf16[128,512]{1,0:T(8,128)(2,1)S(1)} %collective-permute-done.3.rest_4_) | copy-start | bytes 393220
  12.8 7.1 %collective-permute-start.4 = (bf16[128,512]{1,0:T(8,128)(2,1)S(1)}, bf16[128,512]{1,0:T(8,128)(2,1)S(1)}, u32[]{:S(2)}, u32[]{:S(2)}) collective-permute-start(bf16[128,512]{1,0:T(8,128)(2,1)S(1)} %collective-permute-done.3.rest_4_), channel_id=1, source_target_pairs={{0,4},{4,0},{8,12},{12,8},{16,20},{20,16},{24,28},{28,24},{1,5},{5... | collective-permute-start | bytes 393224 | tf_op jit(solution)/shard_map/ppermute | solution.py:28
  14.5 7.4 %collective-permute-start.5 = (bf16[128,512]{1,0:T(8,128)(2,1)S(1)}, bf16[128,512]{1,0:T(8,128)(2,1)S(1)}, u32[]{:S(2)}, u32[]{:S(2)}) collective-permute-start(bf16[128,512]{1,0:T(8,128)(2,1)S(1)} %collective-permute-done.3.rest_4_), channel_id=1, source_target_pairs={{0,8},{4,12},{8,0},{12,4},{16,24},{20,28},{24,16},{28,20},{1,9},{5... | collective-permute-start | bytes 393224 | tf_op jit(solution)/shard_map/ppermute | solution.py:28
  15.9 8.3 %copy-start.6 = (bf16[128,512]{1,0:T(8,128)(2,1)}, bf16[128,512]{1,0:T(8,128)(2,1)S(1)}, u32[]{:S(2)}) copy-start(bf16[128,512]{1,0:T(8,128)(2,1)S(1)} %collective-permute-done.rest_1_) | copy-start | bytes 393220
  15.9 8.3 %collective-permute-start.6 = (bf16[128,512]{1,0:T(8,128)(2,1)S(1)}, bf16[128,512]{1,0:T(8,128)(2,1)S(1)}, u32[]{:S(2)}, u32[]{:S(2)}) collective-permute-start(bf16[128,512]{1,0:T(8,128)(2,1)S(1)} %collective-permute-done.3.rest_4_), channel_id=1, source_target_pairs={{0,12},{4,8},{8,4},{12,0},{16,28},{20,24},{24,20},{28,16},{1,13},{... | collective-permute-start | bytes 393224 | tf_op jit(solution)/shard_map/ppermute | solution.py:28
  19.3 4.9 %copy-start.8 = (bf16[128,512]{1,0:T(8,128)(2,1)}, bf16[128,512]{1,0:T(8,128)(2,1)S(1)}, u32[]{:S(2)}) copy-start(bf16[128,512]{1,0:T(8,128)(2,1)S(1)} %collective-permute-done.2.rest_3_) | copy-start | bytes 393220
  29.0 6.2 %copy-start.3 = (bf16[2,128,512]{2,1,0:T(8,128)(2,1)S(1)}, bf16[2,128,512]{2,1,0:T(8,128)(2,1)}, u32[]{:S(2)}) copy-start(bf16[2,128,512]{2,1,0:T(8,128)(2,1)} %shard_map.109) | copy-start | bytes 786436
  29.0 8.2 %collective-permute-start.8 = (bf16[256,512]{1,0:T(8,128)(2,1)}, bf16[256,512]{1,0:T(8,128)(2,1)S(1)}, u32[]{:S(2)}, u32[]{:S(2)}) collective-permute-start(bf16[256,512]{1,0:T(8,128)(2,1)} %bitcast.42), channel_id=1, source_target_pairs={{0,2},{1,3},{2,0},{3,1},{4,6},{5,7},{6,4},{7,5},{8,10},{9,11},{10,... | collective-permute-start | bytes 786440 | tf_op jit(solution)/shard_map/ppermute | solution.py:28
  34.6 7.8 %collective-permute-start.11 = (bf16[256,512]{1,0:T(8,128)(2,1)}, bf16[256,512]{1,0:T(8,128)(2,1)S(1)}, u32[]{:S(2)}, u32[]{:S(2)}) collective-permute-start(bf16[256,512]{1,0:T(8,128)(2,1)} %bitcast.39), channel_id=1, source_target_pairs={{0,2},{1,3},{2,0},{3,1},{4,6},{5,7},{6,4},{7,5},{8,10},{9,11},{10,... | collective-permute-start | bytes 786440 | tf_op jit(solution)/shard_map/ppermute | solution.py:28
  35.2 8.0 %collective-permute-start.7 = (bf16[256,512]{1,0:T(8,128)(2,1)S(1)}, bf16[256,512]{1,0:T(8,128)(2,1)S(1)}, u32[]{:S(2)}, u32[]{:S(2)}) collective-permute-start(bf16[256,512]{1,0:T(8,128)(2,1)S(1)} %bitcast.43), channel_id=1, source_target_pairs={{0,1},{1,0},{2,3},{3,2},{4,5},{5,4},{6,7},{7,6},{8,9},{9,8},{10,11... | collective-permute-start | bytes 786440 | tf_op jit(solution)/shard_map/ppermute | solution.py:28
  35.2 8.7 %collective-permute-start.10 = (bf16[256,512]{1,0:T(8,128)(2,1)}, bf16[256,512]{1,0:T(8,128)(2,1)S(1)}, u32[]{:S(2)}, u32[]{:S(2)}) collective-permute-start(bf16[256,512]{1,0:T(8,128)(2,1)} %bitcast.40), channel_id=1, source_target_pairs={{0,1},{1,0},{2,3},{3,2},{4,5},{5,4},{6,7},{7,6},{8,9},{9,8},{10,11... | collective-permute-start | bytes 786440 | tf_op jit(solution)/shard_map/ppermute | solution.py:28
  37.2 7.7 %collective-permute-start.9 = (bf16[256,512]{1,0:T(8,128)(2,1)S(1)}, bf16[256,512]{1,0:T(8,128)(2,1)S(1)}, u32[]{:S(2)}, u32[]{:S(2)}) collective-permute-start(bf16[256,512]{1,0:T(8,128)(2,1)S(1)} %collective-permute-done.8), channel_id=1, source_target_pairs={{0,1},{1,0},{2,3},{3,2},{4,5},{5,4},{6,7},{7,6},{8,9},{9,8},{10,11... | collective-permute-start | bytes 786440 | tf_op jit(solution)/shard_map/ppermute | solution.py:28
  42.5 2.8 %collective-permute-start.12 = (bf16[256,512]{1,0:T(8,128)(2,1)S(1)}, bf16[256,512]{1,0:T(8,128)(2,1)S(1)}, u32[]{:S(2)}, u32[]{:S(2)}) collective-permute-start(bf16[256,512]{1,0:T(8,128)(2,1)S(1)} %collective-permute-done.11), channel_id=1, source_target_pairs={{0,1},{1,0},{2,3},{3,2},{4,5},{5,4},{6,7},{7,6},{8,9},{9,8},{10,11... | collective-permute-start | bytes 786440 | tf_op jit(solution)/shard_map/ppermute | solution.py:28
  45.2 4.9 %copy-start.4 = (bf16[4,128,576]{1,2,0:T(8,128)(2,1)S(1)}, bf16[4,128,576]{1,2,0:T(8,128)(2,1)}, u32[]{:S(2)}) copy-start(bf16[4,128,576]{1,2,0:T(8,128)(2,1)} %param.11) | copy-start | bytes 1769476
  45.2 4.9 %copy-start.12 = (f32[576]{0:T(1024)S(1)}, f32[576]{0:T(1024)}, u32[]{:S(2)}) copy-start(f32[576]{0:T(1024)} %param.19) | copy-start | bytes 6916
  45.9 3.1 %collective-permute-start.13 = (f32[4,128]{1,0:T(4,128)S(1)}, f32[4,128]{1,0:T(4,128)S(1)}, u32[]{:S(2)}, u32[]{:S(2)}) collective-permute-start(f32[4,128]{1,0:T(4,128)S(1)} %bitcast.45), channel_id=1, source_target_pairs={{0,1},{1,2},{2,3},{3,0},{4,5},{5,6},{6,7},{7,4},{8,9},{9,10},{10,1... | collective-permute-start | bytes 6152 | tf_op jit(solution)/shard_map/ppermute | solution.py:24
  46.4 3.6 %collective-permute-start.14 = (f32[4,128]{1,0:T(4,128)S(1)}, f32[4,128]{1,0:T(4,128)S(1)}, u32[]{:S(2)}, u32[]{:S(2)}) collective-permute-start(f32[4,128]{1,0:T(4,128)S(1)} %bitcast.46), channel_id=1, source_target_pairs={{0,2},{1,3},{2,0},{3,1},{4,6},{5,7},{6,4},{7,5},{8,10},{9,11},{10,... | collective-permute-start | bytes 6152 | tf_op jit(solution)/shard_map/ppermute | solution.py:24
  47.9 2.3 %collective-permute-start.15 = (f32[4,128]{1,0:T(4,128)S(1)}, f32[4,128]{1,0:T(4,128)S(1)}, u32[]{:S(2)}, u32[]{:S(2)}) collective-permute-start(f32[4,128]{1,0:T(4,128)S(1)} %bitcast.47), channel_id=1, source_target_pairs={{0,3},{1,0},{2,1},{3,2},{4,7},{5,4},{6,5},{7,6},{8,11},{9,8},{10,9... | collective-permute-start | bytes 6152 | tf_op jit(solution)/shard_map/ppermute | solution.py:24
  (5 other events, 13.2 us)

commit v16 on v15

--- a/solution.py
+++ b/solution.py
@@ -71,44 +71,45 @@
 
 def attention_kernel(limit_ref, flag_ref, qkv_ref, cos_ref, sin_ref, *rest):
     page_refs, out_ref = rest[:-1], rest[-1]
-    slots = qkv_ref.shape[1]
+    count, slots = qkv_ref.shape[0], qkv_ref.shape[1]
     per_group = qkv_ref.shape[2] // HD - 2
     half = HD // 2
     cosine = cos_ref[...]
     sine = sin_ref[...]
-    values_in = qkv_ref[0].astype(jnp.float32)
+    pages = [ref[...] for ref in page_refs]
+    prefix_keys = [page[:, :HD] for page in pages]
+    prefix_values = [page[:, HD:] for page in pages]
+    prefix_len = len(pages) * pages[0].shape[0]
+    flag = flag_ref[...]
 
     def rope(part):
         first = part[:, :half]
         second = part[:, half:]
         return jnp.concatenate([first * cosine - second * sine, second * cosine + first * sine], -1)
 
-    queries = jnp.concatenate(
-        [(rope(values_in[:, q * HD:(q + 1) * HD]) * HD ** (-0.5)).astype(jnp.bfloat16)
-         for q in range(per_group)], 0)
-    fresh_keys = rope(values_in[:, per_group * HD:(per_group + 1) * HD]).astype(jnp.bfloat16)
-    fresh_values = values_in[:, (per_group + 1) * HD:].astype(jnp.bfloat16)
-    pages = [ref[...] for ref in page_refs]
-    keys = jnp.concatenate([page[:, :HD] for page in pages] + [fresh_keys], 0)
-    values = jnp.concatenate([page[:, HD:] for page in pages] + [fresh_values], 0)
-    prefix_len = len(pages) * pages[0].shape[0]
-    key_count = keys.shape[0]
-    rows = queries.shape[0]
-
-    scores = lax.dot_general(queries, keys, (((1,), (1,)), ((), ())),
-                             preferred_element_type=jnp.float32)
-    column = lax.broadcasted_iota(jnp.int32, (rows, key_count), 1)
-    slot = lax.broadcasted_iota(jnp.int32, (rows, key_count), 0) % slots
-    suffix_pos = column - prefix_len
-    limit = limit_ref[0]
-    suffix_ok = (suffix_pos <= slot) & (suffix_pos < limit)
-    exps = capped_exp(scores) * flag_ref[...]
-    raw = jnp.where(suffix_ok, exps, 0.0)
-    totals = jnp.sum(raw, -1, keepdims=True)
-    weights = (raw / totals).astype(jnp.bfloat16)
-    attended = jnp.dot(weights, values, preferred_element_type=jnp.float32).astype(jnp.bfloat16)
-    out_ref[0] = jnp.concatenate(
-        [attended[q * slots:(q + 1) * slots] for q in range(per_group)], 1)
+    for request in range(count):
+        values_in = qkv_ref[request].astype(jnp.float32)
+        queries = jnp.concatenate(
+            [(rope(values_in[:, q * HD:(q + 1) * HD]) * HD ** (-0.5)).astype(jnp.bfloat16)
+             for q in range(per_group)], 0)
+        fresh_keys = rope(values_in[:, per_group * HD:(per_group + 1) * HD]).astype(jnp.bfloat16)
+        fresh_values = values_in[:, (per_group + 1) * HD:].astype(jnp.bfloat16)
+        keys = jnp.concatenate(prefix_keys + [fresh_keys], 0)
+        values = jnp.concatenate(prefix_values + [fresh_values], 0)
+        key_count = keys.shape[0]
+        rows = queries.shape[0]
+        scores = lax.dot_general(queries, keys, (((1,), (1,)), ((), ())),
+                                 preferred_element_type=jnp.float32)
+        column = lax.broadcasted_iota(jnp.int32, (rows, key_count), 1)
+        slot = lax.broadcasted_iota(jnp.int32, (rows, key_count), 0) % slots
+        suffix_pos = column - prefix_len
+        suffix_ok = (suffix_pos <= slot) & (suffix_pos < limit_ref[request])
+        raw = jnp.where(suffix_ok, capped_exp(scores) * flag, 0.0)
+        totals = jnp.sum(raw, -1, keepdims=True)
+        weights = (raw / totals).astype(jnp.bfloat16)
+        attended = jnp.dot(weights, values, preferred_element_type=jnp.float32).astype(jnp.bfloat16)
+        out_ref[request] = jnp.concatenate(
+            [attended[q * slots:(q + 1) * slots] for q in range(per_group)], 1)
 
 
 def attend(qkv, cosine, sine, blocks, lengths, valid, offset, count):
@@ -124,16 +125,17 @@
         [jnp.broadcast_to(jnp.full((requests, 1), prefix_len + slots, jnp.int32), (requests, prefix_len)),
          jnp.broadcast_to(lengths[:, None], (requests, slots))], 1)
     limits = limits[:, None, :]
+    chunk = offset // count
     full = lambda shape: pl.BlockSpec(shape, lambda r: (0,) * len(shape))
     return pl.pallas_call(
         attention_kernel,
-        grid=(count,),
-        in_specs=[pl.BlockSpec((1, 1, key_count), lambda r: (r + offset, 0, 0)),
+        grid=(1,),
+        in_specs=[pl.BlockSpec((count, 1, key_count), lambda r: (chunk, 0, 0)),
                   full((1, key_count)),
-                  pl.BlockSpec((1, slots, width), lambda r: (r + offset, 0, 0)),
+                  pl.BlockSpec((count, slots, width), lambda r: (chunk, 0, 0)),
                   full(cosine.shape), full(sine.shape)]
                  + [full((page_len, page_width)) for _ in blocks],
-        out_specs=pl.BlockSpec((1, slots, per_group * HD), lambda r: (r, 0, 0)),
+        out_specs=pl.BlockSpec((count, slots, per_group * HD), lambda r: (0, 0, 0)),
         out_shape=jax.ShapeDtypeStruct((count, slots, per_group * HD), jnp.bfloat16),
     )(limits, flags, qkv, cosine, sine, *blocks)
 

time: 51.7 us -> 51.3 us (level)
  Pallas kernels: 8.27 us -> 7.54 us
    pallas_call x2, Pallas kernels: 8.27 us -> 7.54 us  [attend(): pl.pallas_call(attention_kernel, grid=(1,), in_specs=[pl.BlockSpec((count...]
  transfers between devices with their start and end apart: 16 -> 16, of which waited for: 7 -> 7; matrix products, arithmetic and copies ran while one was open for 12% -> 13% of each run, Pallas kernels for 8% -> 7%
where the time goes in v16:
time: 51.3 us; the launch traced here: 50.8 us
  starting transfers between devices  17.7 us (35%)
  waiting for transfers between devices  13.3 us (26%)
  Pallas kernels  7.54 us (15%)
  other arithmetic  5.64 us (11%)
  local copies, waits for them, and re-layouts  3.02 us (6%)
  matrix products  2.79 us (5%)
  between operations  0.91 us (2%)
    ppermute x13, starting transfers between devices, swapped(): return lax.ppermute(value, axis, [(i, i ^ mask) for i in range(size)])  14.7 us
    ppermute x13, waiting for transfers between devices, swapped(): return lax.ppermute(value, axis, [(i, i ^ mask) for i in range(size)])  12 us
    pallas_call x2, Pallas kernels, attend(): pl.pallas_call(attention_kernel, grid=(1,), in_specs=[pl.BlockSpec((count...  7.54 us
    ppermute x3, starting transfers between devices, shifted(): lax.ppermute(value, axis, [(i, (i + shift) % size) for i in range(size)])  2.96 us
    dot_general x8, matrix products, project(): term = jnp.dot(block, rows, preferred_element_type=jnp.float32)  2.79 us
    reduce_sum x1, other arithmetic, gather_prefix(): slot = jnp.sum(jnp.where(mine, page_slot, 0))  1.54 us
    ppermute x3, waiting for transfers between devices, shifted(): lax.ppermute(value, axis, [(i, (i + shift) % size) for i in range(size)])  1.24 us
    convert_element_type x1, other arithmetic, on_device(): return ((source + branch) * live_mask[..., None]).astype(jnp.bfloat16)  1.1 us
  transfers between devices with their start and end apart: 16, of which 7 were waited for; matrix products, arithmetic and copies ran while one was open for 13% of the time, Pallas kernels for 7%

profile of v16, /device:TPU:0, one launch (start us, length us, event | category | flops | bytes accessed | tf_op | source)
XLA Modules:
  0.0 50.8 jit_solution(3864188154561643902)
XLA Ops:
  0.0 1.5 %fusion.28 = s32[]{:T(128)} fusion(s32[8]{0:T(128)} %param.15, s32[8]{0:T(128)} %param.14, s32[]{:T(128)} %axis_index.27), kind=kLoop, calls=%fused_computation.43 | loop fusion | flops 23 | bytes 72 | tf_op jit(solution)/shard_map/reduce_sum | solution.py:36
  2.2 1.0 %select_bitcast_fusion.rest_0_ = bf16[128,512]{1,0:T(8,128)(2,1)S(1)} fusion(bf16[2,128,1,512]{3,1,2,0:T(8,128)(2,1)} %param.13, pred[]{:T(512)S(6)} %eq.43), kind=kLoop, calls=%fused_computation.26 | loop fusion | flops 65536 | bytes 393217 | tf_op jit(solution)/shard_map/jit(_where)/select_n | solution.py:39
  3.2 5.1 %collective-permute-start.3 = (bf16[128,512]{1,0:T(8,128)(2,1)S(1)}, bf16[128,512]{1,0:T(8,128)(2,1)S(1)}, u32[]{:S(2)}, u32[]{:S(2)}) collective-permute-start(bf16[128,512]{1,0:T(8,128)(2,1)S(1)} %select_bitcast_fusion.rest_0_), channel_id=1, source_target_pairs={{0,24},{4,28},{8,16},{12,20},{16,8},{20,12},{24,0},{28,4},{1,25},{... | collective-permute-start | bytes 393224 | tf_op jit(solution)/shard_map/ppermute | solution.py:28
  8.4 1.5 %collective-permute-start = (bf16[128,512]{1,0:T(8,128)(2,1)S(1)}, bf16[128,512]{1,0:T(8,128)(2,1)S(1)}, u32[]{:S(2)}, u32[]{:S(2)}) collective-permute-start(bf16[128,512]{1,0:T(8,128)(2,1)S(1)} %select_bitcast_fusion.rest_0_), channel_id=1, source_target_pairs={{0,4},{4,0},{8,12},{12,8},{16,20},{20,16},{24,28},{28,24},{1,5},{5... | collective-permute-start | bytes 393224 | tf_op jit(solution)/shard_map/ppermute | solution.py:28
  9.9 2.0 %collective-permute-start.2 = (bf16[128,512]{1,0:T(8,128)(2,1)S(1)}, bf16[128,512]{1,0:T(8,128)(2,1)S(1)}, u32[]{:S(2)}, u32[]{:S(2)}) collective-permute-start(bf16[128,512]{1,0:T(8,128)(2,1)S(1)} %select_bitcast_fusion.rest_0_), channel_id=1, source_target_pairs={{0,12},{4,8},{8,4},{12,0},{16,28},{20,24},{24,20},{28,16},{1,13},{... | collective-permute-start | bytes 393224 | tf_op jit(solution)/shard_map/ppermute | solution.py:28
  11.9 0.8 %compare_reduce_fusion = pred[8]{0:T(512)(128)(4,1)S(1)} fusion(s32[8]{0:T(128)} %param.14, s32[8]{0:T(128)S(1)} %stack.35), kind=kLoop, calls=%fused_computation.27 | loop fusion | flops 120 | bytes 72 | tf_op jit(solution)/shard_map/reduce_or | solution.py:55
  12.8 1.7 %collective-permute-start.4 = (bf16[128,512]{1,0:T(8,128)(2,1)S(1)}, bf16[128,512]{1,0:T(8,128)(2,1)S(1)}, u32[]{:S(2)}, u32[]{:S(2)}) collective-permute-start(bf16[128,512]{1,0:T(8,128)(2,1)S(1)} %collective-permute-done.3.rest_4_), channel_id=1, source_target_pairs={{0,4},{4,0},{8,12},{12,8},{16,20},{20,16},{24,28},{28,24},{1,5},{5... | collective-permute-start | bytes 393224 | tf_op jit(solution)/shard_map/ppermute | solution.py:28
  14.5 1.5 %collective-permute-start.5 = (bf16[128,512]{1,0:T(8,128)(2,1)S(1)}, bf16[128,512]{1,0:T(8,128)(2,1)S(1)}, u32[]{:S(2)}, u32[]{:S(2)}) collective-permute-start(bf16[128,512]{1,0:T(8,128)(2,1)S(1)} %collective-permute-done.3.rest_4_), channel_id=1, source_target_pairs={{0,8},{4,12},{8,0},{12,4},{16,24},{20,28},{24,16},{28,20},{1,9},{5... | collective-permute-start | bytes 393224 | tf_op jit(solution)/shard_map/ppermute | solution.py:28
  16.4 0.6 %broadcast_in_dim.29.flag_ref = f32[1,1152]{1,0:T(1,128)} reshape(f32[1152]{0:T(1024)S(1)} %concatenate.12) | data formatting | bytes 9216 | tf_op jit(solution)/shard_map/broadcast_in_dim | solution.py:123
  17.0 0.7 %dynamic_slice.19 = s32[4]{0:T(128)S(1)} dynamic-slice(s32[32]{0:T(128)} %param.17, s32[]{:T(128)S(6)} %select_n.37), dynamic_slice_sizes={4} | dynamic-slice | bytes 36 | tf_op jit(solution)/shard_map/dynamic_slice | solution.py:172
  17.8 0.8 %select_reduce_fusion = s32[4]{0:T(128)S(1)} fusion(s32[32]{0:T(128)} %param.16, s32[4]{0:T(128)S(1)} %dynamic_slice.19), kind=kLoop, calls=%fused_computation.31 | loop fusion | flops 380 | bytes 160 | tf_op jit(solution)/shard_map/reduce_sum | solution.py:174
  18.7 0.6 %broadcast_in_dim.27.limit_ref = s32[4,1,1152]{2,1,0:T(1,128)} reshape(s32[4,1152]{1,0:T(4,128)S(1)} %concatenate.11) | data formatting | bytes 36864 | tf_op jit(solution)/shard_map/broadcast_in_dim | solution.py:127
  19.3 0.6 %collective-permute-done.4.rest_5_ = bf16[128,512]{1,0:T(8,128)(2,1)S(1)} collective-permute-done((bf16[128,512]{1,0:T(8,128)(2,1)S(1)}, bf16[128,512]{1,0:T(8,128)(2,1)S(1)}, u32[]{:S(2)}, u32[]{:S(2)}) %collective-permute-start.4) | collective-permute-done | bytes 131104 | tf_op jit(solution)/shard_map/ppermute | solution.py:28
  19.9 1.9 %collective-permute-done.5.rest_6_ = bf16[128,512]{1,0:T(8,128)(2,1)S(1)} collective-permute-done((bf16[128,512]{1,0:T(8,128)(2,1)S(1)}, bf16[128,512]{1,0:T(8,128)(2,1)S(1)}, u32[]{:S(2)}, u32[]{:S(2)}) %collective-permute-start.5) | collective-permute-done | bytes 131104 | tf_op jit(solution)/shard_map/ppermute | solution.py:28
  21.9 2.3 %collective-permute-done.6.rest_7_ = bf16[128,512]{1,0:T(8,128)(2,1)S(1)} collective-permute-done((bf16[128,512]{1,0:T(8,128)(2,1)S(1)}, bf16[128,512]{1,0:T(8,128)(2,1)S(1)}, u32[]{:S(2)}, u32[]{:S(2)}) %collective-permute-start.6) | collective-permute-done | bytes 131104 | tf_op jit(solution)/shard_map/ppermute | solution.py:28
  24.8 3.8 %shard_map.109 = bf16[2,128,512]{2,1,0:T(8,128)(2,1)} custom-call(s32[4,1,1152]{2,1,0:T(1,128)} %broadcast_in_dim.27.limit_ref, f32[1,1152]{1,0:T(1,128)} %broadcast_in_dim.29.flag_ref, bf16[4,128,1024]{2,1,0:T(8,128)(2,1)} %bitcast.37, f32[128,128]{1,0:T(8,128)} %constant.44.clone.cos_ref, f32[128,128]{1,0:T(8,128)} %constant.45.clone.sin_ref, ...), custom_call_target="tpu_custom_call" | custom-call | tf_op jit(solution)/shard_map/pallas_call | solution.py:130
  28.6 1.4 %collective-permute-start.8 = (bf16[256,512]{1,0:T(8,128)(2,1)}, bf16[256,512]{1,0:T(8,128)(2,1)S(1)}, u32[]{:S(2)}, u32[]{:S(2)}) collective-permute-start(bf16[256,512]{1,0:T(8,128)(2,1)} %bitcast.42), channel_id=1, source_target_pairs={{0,2},{1,3},{2,0},{3,1},{4,6},{5,7},{6,4},{7,5},{8,10},{9,11},{10,... | collective-permute-start | bytes 786440 | tf_op jit(solution)/shard_map/ppermute | solution.py:28
  30.1 3.8 %shard_map.110 = bf16[2,128,512]{2,1,0:T(8,128)(2,1)} custom-call(s32[4,1,1152]{2,1,0:T(1,128)} %broadcast_in_dim.27.limit_ref, f32[1,1152]{1,0:T(1,128)} %broadcast_in_dim.29.flag_ref, bf16[4,128,1024]{2,1,0:T(8,128)(2,1)} %bitcast.38, f32[128,128]{1,0:T(8,128)} %constant.44.clone.cos_ref, f32[128,128]{1,0:T(8,128)} %constant.45.clone.sin_ref, ...), custom_call_target="tpu_custom_call" | custom-call | tf_op jit(solution)/shard_map/pallas_call | solution.py:130
  34.9 2.2 %collective-permute-done.8 = bf16[256,512]{1,0:T(8,128)(2,1)S(1)} collective-permute-done((bf16[256,512]{1,0:T(8,128)(2,1)}, bf16[256,512]{1,0:T(8,128)(2,1)S(1)}, u32[]{:S(2)}, u32[]{:S(2)}) %collective-permute-start.8) | collective-permute-done | bytes 262176 | tf_op jit(solution)/shard_map/ppermute | solution.py:28
  37.1 4.9 %collective-permute-done.11 = bf16[256,512]{1,0:T(8,128)(2,1)S(1)} collective-permute-done((bf16[256,512]{1,0:T(8,128)(2,1)}, bf16[256,512]{1,0:T(8,128)(2,1)S(1)}, u32[]{:S(2)}, u32[]{:S(2)}) %collective-permute-start.11) | collective-permute-done | bytes 262176 | tf_op jit(solution)/shard_map/ppermute | solution.py:28
  46.0 1.4 %collective-permute-start.14 = (f32[4,128]{1,0:T(4,128)S(1)}, f32[4,128]{1,0:T(4,128)S(1)}, u32[]{:S(2)}, u32[]{:S(2)}) collective-permute-start(f32[4,128]{1,0:T(4,128)S(1)} %bitcast.46), channel_id=1, source_target_pairs={{0,2},{1,3},{2,0},{3,1},{4,6},{5,7},{6,4},{7,5},{8,10},{9,11},{10,... | collective-permute-start | bytes 6152 | tf_op jit(solution)/shard_map/ppermute | solution.py:24
  47.4 1.0 %collective-permute-start.15 = (f32[4,128]{1,0:T(4,128)S(1)}, f32[4,128]{1,0:T(4,128)S(1)}, u32[]{:S(2)}, u32[]{:S(2)}) collective-permute-start(f32[4,128]{1,0:T(4,128)S(1)} %bitcast.47), channel_id=1, source_target_pairs={{0,3},{1,0},{2,1},{3,2},{4,7},{5,4},{6,5},{7,6},{8,11},{9,8},{10,9... | collective-permute-start | bytes 6152 | tf_op jit(solution)/shard_map/ppermute | solution.py:24
  48.5 1.1 %collective-permute-done.14 = f32[4,128]{1,0:T(4,128)S(1)} collective-permute-done((f32[4,128]{1,0:T(4,128)S(1)}, f32[4,128]{1,0:T(4,128)S(1)}, u32[]{:S(2)}, u32[]{:S(2)}) %collective-permute-start.14) | collective-permute-done | bytes 2080 | tf_op jit(solution)/shard_map/ppermute | solution.py:24
  49.7 1.1 %fusion.5 = bf16[4,128,576]{1,2,0:T(8,128)(2,1)} fusion(f32[72,4,8,128]{3,2,1,0:T(8,128)S(1)} %get-tuple-element.6, bf16[4,128,576]{1,2,0:T(8,128)(2,1)S(1)} %copy-done.4, f32[4,128]{1,0:T(4,128)S(1)} %fusion.19, f32[576]{0:T(1024)S(1)} %copy-done.12, f32[4,128]{1,0:T(4,128)S(1)} %add_rsqrt_fusion), kind=kLoop, calls=%fused_computation.10 | loop fusion | flops 1769472 | bytes 2365696 | tf_op jit(solution)/shard_map/convert_element_type | solution.py:196
  (61 shorter events, 6.5 us)
Async XLA Ops:
  0.0 42.1 %copy-start = (bf16[2048,576]{0,1:T(8,128)(2,1)S(1)}, bf16[2048,576]{0,1:T(8,128)(2,1)}, u32[]{:S(2)}) copy-start(bf16[2048,576]{0,1:T(8,128)(2,1)} %param.18) | copy-start | bytes 7077892
  3.2 21.0 %copy-start.1 = (bf16[128,512]{1,0:T(8,128)(2,1)}, bf16[128,512]{1,0:T(8,128)(2,1)S(1)}, u32[]{:S(2)}) copy-start(bf16[128,512]{1,0:T(8,128)(2,1)S(1)} %select_bitcast_fusion.rest_0_) | copy-start | bytes 393220
  3.2 9.6 %collective-permute-start.3 = (bf16[128,512]{1,0:T(8,128)(2,1)S(1)}, bf16[128,512]{1,0:T(8,128)(2,1)S(1)}, u32[]{:S(2)}, u32[]{:S(2)}) collective-permute-start(bf16[128,512]{1,0:T(8,128)(2,1)S(1)} %select_bitcast_fusion.rest_0_), channel_id=1, source_target_pairs={{0,24},{4,28},{8,16},{12,20},{16,8},{20,12},{24,0},{28,4},{1,25},{... | collective-permute-start | bytes 393224 | tf_op jit(solution)/shard_map/ppermute | solution.py:28
  8.4 7.5 %collective-permute-start = (bf16[128,512]{1,0:T(8,128)(2,1)S(1)}, bf16[128,512]{1,0:T(8,128)(2,1)S(1)}, u32[]{:S(2)}, u32[]{:S(2)}) collective-permute-start(bf16[128,512]{1,0:T(8,128)(2,1)S(1)} %select_bitcast_fusion.rest_0_), channel_id=1, source_target_pairs={{0,4},{4,0},{8,12},{12,8},{16,20},{20,16},{24,28},{28,24},{1,5},{5... | collective-permute-start | bytes 393224 | tf_op jit(solution)/shard_map/ppermute | solution.py:28
  9.9 9.4 %collective-permute-start.1 = (bf16[128,512]{1,0:T(8,128)(2,1)S(1)}, bf16[128,512]{1,0:T(8,128)(2,1)S(1)}, u32[]{:S(2)}, u32[]{:S(2)}) collective-permute-start(bf16[128,512]{1,0:T(8,128)(2,1)S(1)} %select_bitcast_fusion.rest_0_), channel_id=1, source_target_pairs={{0,8},{4,12},{8,0},{12,4},{16,24},{20,28},{24,16},{28,20},{1,9},{5... | collective-permute-start | bytes 393224 | tf_op jit(solution)/shard_map/ppermute | solution.py:28
  9.9 9.4 %collective-permute-start.2 = (bf16[128,512]{1,0:T(8,128)(2,1)S(1)}, bf16[128,512]{1,0:T(8,128)(2,1)S(1)}, u32[]{:S(2)}, u32[]{:S(2)}) collective-permute-start(bf16[128,512]{1,0:T(8,128)(2,1)S(1)} %select_bitcast_fusion.rest_0_), channel_id=1, source_target_pairs={{0,12},{4,8},{8,4},{12,0},{16,28},{20,24},{24,20},{28,16},{1,13},{... | collective-permute-start | bytes 393224 | tf_op jit(solution)/shard_map/ppermute | solution.py:28
  12.8 11.4 %copy-start.5 = (bf16[128,512]{1,0:T(8,128)(2,1)}, bf16[128,512]{1,0:T(8,128)(2,1)S(1)}, u32[]{:S(2)}) copy-start(bf16[128,512]{1,0:T(8,128)(2,1)S(1)} %collective-permute-done.3.rest_4_) | copy-start | bytes 393220
  12.8 7.1 %collective-permute-start.4 = (bf16[128,512]{1,0:T(8,128)(2,1)S(1)}, bf16[128,512]{1,0:T(8,128)(2,1)S(1)}, u32[]{:S(2)}, u32[]{:S(2)}) collective-permute-start(bf16[128,512]{1,0:T(8,128)(2,1)S(1)} %collective-permute-done.3.rest_4_), channel_id=1, source_target_pairs={{0,4},{4,0},{8,12},{12,8},{16,20},{20,16},{24,28},{28,24},{1,5},{5... | collective-permute-start | bytes 393224 | tf_op jit(solution)/shard_map/ppermute | solution.py:28
  14.5 7.4 %collective-permute-start.5 = (bf16[128,512]{1,0:T(8,128)(2,1)S(1)}, bf16[128,512]{1,0:T(8,128)(2,1)S(1)}, u32[]{:S(2)}, u32[]{:S(2)}) collective-permute-start(bf16[128,512]{1,0:T(8,128)(2,1)S(1)} %collective-permute-done.3.rest_4_), channel_id=1, source_target_pairs={{0,8},{4,12},{8,0},{12,4},{16,24},{20,28},{24,16},{28,20},{1,9},{5... | collective-permute-start | bytes 393224 | tf_op jit(solution)/shard_map/ppermute | solution.py:28
  15.9 8.3 %copy-start.6 = (bf16[128,512]{1,0:T(8,128)(2,1)}, bf16[128,512]{1,0:T(8,128)(2,1)S(1)}, u32[]{:S(2)}) copy-start(bf16[128,512]{1,0:T(8,128)(2,1)S(1)} %collective-permute-done.rest_1_) | copy-start | bytes 393220
  15.9 8.3 %collective-permute-start.6 = (bf16[128,512]{1,0:T(8,128)(2,1)S(1)}, bf16[128,512]{1,0:T(8,128)(2,1)S(1)}, u32[]{:S(2)}, u32[]{:S(2)}) collective-permute-start(bf16[128,512]{1,0:T(8,128)(2,1)S(1)} %collective-permute-done.3.rest_4_), channel_id=1, source_target_pairs={{0,12},{4,8},{8,4},{12,0},{16,28},{20,24},{24,20},{28,16},{1,13},{... | collective-permute-start | bytes 393224 | tf_op jit(solution)/shard_map/ppermute | solution.py:28
  19.3 4.9 %copy-start.8 = (bf16[128,512]{1,0:T(8,128)(2,1)}, bf16[128,512]{1,0:T(8,128)(2,1)S(1)}, u32[]{:S(2)}) copy-start(bf16[128,512]{1,0:T(8,128)(2,1)S(1)} %collective-permute-done.2.rest_3_) | copy-start | bytes 393220
  28.6 5.8 %copy-start.3 = (bf16[2,128,512]{2,1,0:T(8,128)(2,1)S(1)}, bf16[2,128,512]{2,1,0:T(8,128)(2,1)}, u32[]{:S(2)}) copy-start(bf16[2,128,512]{2,1,0:T(8,128)(2,1)} %shard_map.109) | copy-start | bytes 786436
  28.6 8.5 %collective-permute-start.8 = (bf16[256,512]{1,0:T(8,128)(2,1)}, bf16[256,512]{1,0:T(8,128)(2,1)S(1)}, u32[]{:S(2)}, u32[]{:S(2)}) collective-permute-start(bf16[256,512]{1,0:T(8,128)(2,1)} %bitcast.42), channel_id=1, source_target_pairs={{0,2},{1,3},{2,0},{3,1},{4,6},{5,7},{6,4},{7,5},{8,10},{9,11},{10,... | collective-permute-start | bytes 786440 | tf_op jit(solution)/shard_map/ppermute | solution.py:28
  33.8 8.2 %collective-permute-start.11 = (bf16[256,512]{1,0:T(8,128)(2,1)}, bf16[256,512]{1,0:T(8,128)(2,1)S(1)}, u32[]{:S(2)}, u32[]{:S(2)}) collective-permute-start(bf16[256,512]{1,0:T(8,128)(2,1)} %bitcast.39), channel_id=1, source_target_pairs={{0,2},{1,3},{2,0},{3,1},{4,6},{5,7},{6,4},{7,5},{8,10},{9,11},{10,... | collective-permute-start | bytes 786440 | tf_op jit(solution)/shard_map/ppermute | solution.py:28
  34.4 8.3 %collective-permute-start.7 = (bf16[256,512]{1,0:T(8,128)(2,1)S(1)}, bf16[256,512]{1,0:T(8,128)(2,1)S(1)}, u32[]{:S(2)}, u32[]{:S(2)}) collective-permute-start(bf16[256,512]{1,0:T(8,128)(2,1)S(1)} %bitcast.43), channel_id=1, source_target_pairs={{0,1},{1,0},{2,3},{3,2},{4,5},{5,4},{6,7},{7,6},{8,9},{9,8},{10,11... | collective-permute-start | bytes 786440 | tf_op jit(solution)/shard_map/ppermute | solution.py:28
  34.4 9.1 %collective-permute-start.10 = (bf16[256,512]{1,0:T(8,128)(2,1)}, bf16[256,512]{1,0:T(8,128)(2,1)S(1)}, u32[]{:S(2)}, u32[]{:S(2)}) collective-permute-start(bf16[256,512]{1,0:T(8,128)(2,1)} %bitcast.40), channel_id=1, source_target_pairs={{0,1},{1,0},{2,3},{3,2},{4,5},{5,4},{6,7},{7,6},{8,9},{9,8},{10,11... | collective-permute-start | bytes 786440 | tf_op jit(solution)/shard_map/ppermute | solution.py:28
  37.1 7.3 %collective-permute-start.9 = (bf16[256,512]{1,0:T(8,128)(2,1)S(1)}, bf16[256,512]{1,0:T(8,128)(2,1)S(1)}, u32[]{:S(2)}, u32[]{:S(2)}) collective-permute-start(bf16[256,512]{1,0:T(8,128)(2,1)S(1)} %collective-permute-done.8), channel_id=1, source_target_pairs={{0,1},{1,0},{2,3},{3,2},{4,5},{5,4},{6,7},{7,6},{8,9},{9,8},{10,11... | collective-permute-start | bytes 786440 | tf_op jit(solution)/shard_map/ppermute | solution.py:28
  42.1 2.8 %collective-permute-start.12 = (bf16[256,512]{1,0:T(8,128)(2,1)S(1)}, bf16[256,512]{1,0:T(8,128)(2,1)S(1)}, u32[]{:S(2)}, u32[]{:S(2)}) collective-permute-start(bf16[256,512]{1,0:T(8,128)(2,1)S(1)} %collective-permute-done.11), channel_id=1, source_target_pairs={{0,1},{1,0},{2,3},{3,2},{4,5},{5,4},{6,7},{7,6},{8,9},{9,8},{10,11... | collective-permute-start | bytes 786440 | tf_op jit(solution)/shard_map/ppermute | solution.py:28
  44.8 4.9 %copy-start.4 = (bf16[4,128,576]{1,2,0:T(8,128)(2,1)S(1)}, bf16[4,128,576]{1,2,0:T(8,128)(2,1)}, u32[]{:S(2)}) copy-start(bf16[4,128,576]{1,2,0:T(8,128)(2,1)} %param.11) | copy-start | bytes 1769476
  44.8 4.9 %copy-start.12 = (f32[576]{0:T(1024)S(1)}, f32[576]{0:T(1024)}, u32[]{:S(2)}) copy-start(f32[576]{0:T(1024)} %param.19) | copy-start | bytes 6916
  45.4 3.1 %collective-permute-start.13 = (f32[4,128]{1,0:T(4,128)S(1)}, f32[4,128]{1,0:T(4,128)S(1)}, u32[]{:S(2)}, u32[]{:S(2)}) collective-permute-start(f32[4,128]{1,0:T(4,128)S(1)} %bitcast.45), channel_id=1, source_target_pairs={{0,1},{1,2},{2,3},{3,0},{4,5},{5,6},{6,7},{7,4},{8,9},{9,10},{10,1... | collective-permute-start | bytes 6152 | tf_op jit(solution)/shard_map/ppermute | solution.py:24
  46.0 3.6 %collective-permute-start.14 = (f32[4,128]{1,0:T(4,128)S(1)}, f32[4,128]{1,0:T(4,128)S(1)}, u32[]{:S(2)}, u32[]{:S(2)}) collective-permute-start(f32[4,128]{1,0:T(4,128)S(1)} %bitcast.46), channel_id=1, source_target_pairs={{0,2},{1,3},{2,0},{3,1},{4,6},{5,7},{6,4},{7,5},{8,10},{9,11},{10,... | collective-permute-start | bytes 6152 | tf_op jit(solution)/shard_map/ppermute | solution.py:24
  47.4 2.3 %collective-permute-start.15 = (f32[4,128]{1,0:T(4,128)S(1)}, f32[4,128]{1,0:T(4,128)S(1)}, u32[]{:S(2)}, u32[]{:S(2)}) collective-permute-start(f32[4,128]{1,0:T(4,128)S(1)} %bitcast.47), channel_id=1, source_target_pairs={{0,3},{1,0},{2,1},{3,2},{4,7},{5,4},{6,5},{7,6},{8,11},{9,8},{10,9... | collective-permute-start | bytes 6152 | tf_op jit(solution)/shard_map/ppermute | solution.py:24
  (5 other events, 13.2 us)

commit v17 on v16

--- a/solution.py
+++ b/solution.py
@@ -87,27 +87,35 @@
         second = part[:, half:]
         return jnp.concatenate([first * cosine - second * sine, second * cosine + first * sine], -1)
 
+    queries, fresh = [], []
     for request in range(count):
         values_in = qkv_ref[request].astype(jnp.float32)
-        queries = jnp.concatenate(
+        queries.append(jnp.concatenate(
             [(rope(values_in[:, q * HD:(q + 1) * HD]) * HD ** (-0.5)).astype(jnp.bfloat16)
-             for q in range(per_group)], 0)
-        fresh_keys = rope(values_in[:, per_group * HD:(per_group + 1) * HD]).astype(jnp.bfloat16)
-        fresh_values = values_in[:, (per_group + 1) * HD:].astype(jnp.bfloat16)
-        keys = jnp.concatenate(prefix_keys + [fresh_keys], 0)
-        values = jnp.concatenate(prefix_values + [fresh_values], 0)
-        key_count = keys.shape[0]
-        rows = queries.shape[0]
-        scores = lax.dot_general(queries, keys, (((1,), (1,)), ((), ())),
+             for q in range(per_group)], 0))
+        fresh.append((rope(values_in[:, per_group * HD:(per_group + 1) * HD]).astype(jnp.bfloat16),
+                      values_in[:, (per_group + 1) * HD:].astype(jnp.bfloat16)))
+    rows = queries[0].shape[0]
+    contract = (((1,), (1,)), ((), ()))
+    prefix_raw = capped_exp(lax.dot_general(
+        jnp.concatenate(queries, 0), jnp.concatenate(prefix_keys, 0), contract,
+        preferred_element_type=jnp.float32)) * flag[:, :prefix_len]
+    prefix_value_rows = jnp.concatenate(prefix_values, 0)
+    for request in range(count):
+        fresh_keys, fresh_values = fresh[request]
+        scores = lax.dot_general(queries[request], fresh_keys, contract,
                                  preferred_element_type=jnp.float32)
-        column = lax.broadcasted_iota(jnp.int32, (rows, key_count), 1)
-        slot = lax.broadcasted_iota(jnp.int32, (rows, key_count), 0) % slots
-        suffix_pos = column - prefix_len
-        suffix_ok = (suffix_pos <= slot) & (suffix_pos < limit_ref[request])
-        raw = jnp.where(suffix_ok, capped_exp(scores) * flag, 0.0)
-        totals = jnp.sum(raw, -1, keepdims=True)
-        weights = (raw / totals).astype(jnp.bfloat16)
-        attended = jnp.dot(weights, values, preferred_element_type=jnp.float32).astype(jnp.bfloat16)
+        column = lax.broadcasted_iota(jnp.int32, scores.shape, 1)
+        slot = lax.broadcasted_iota(jnp.int32, scores.shape, 0) % slots
+        allowed = (column <= slot) & (column < limit_ref[request][:, prefix_len:])
+        suffix_raw = jnp.where(allowed, capped_exp(scores), 0.0)
+        page_raw = prefix_raw[request * rows:(request + 1) * rows]
+        totals = jnp.sum(page_raw, -1, keepdims=True) + jnp.sum(suffix_raw, -1, keepdims=True)
+        attended = jnp.dot((page_raw / totals).astype(jnp.bfloat16), prefix_value_rows,
+                           preferred_element_type=jnp.float32)
+        attended = attended + jnp.dot((suffix_raw / totals).astype(jnp.bfloat16), fresh_values,
+                                      preferred_element_type=jnp.float32)
+        attended = attended.astype(jnp.bfloat16)
         out_ref[request] = jnp.concatenate(
             [attended[q * slots:(q + 1) * slots] for q in range(per_group)], 1)
 

time: 51.3 us -> 51.2 us (level)
  no operation moved by 1% of the time
where the time goes in v17:
time: 51.2 us; the launch traced here: 50.7 us
  starting transfers between devices  17.7 us (35%)
  waiting for transfers between devices  13.4 us (26%)
  Pallas kernels  7.32 us (14%)
  other arithmetic  5.64 us (11%)
  local copies, waits for them, and re-layouts  3.02 us (6%)
  matrix products  2.78 us (5%)
  between operations  0.92 us (2%)
    ppermute x13, starting transfers between devices, swapped(): return lax.ppermute(value, axis, [(i, i ^ mask) for i in range(size)])  14.7 us
    ppermute x13, waiting for transfers between devices, swapped(): return lax.ppermute(value, axis, [(i, i ^ mask) for i in range(size)])  12.1 us
    pallas_call x2, Pallas kernels, attend(): pl.pallas_call(attention_kernel, grid=(1,), in_specs=[pl.BlockSpec((count...  7.32 us
    ppermute x3, starting transfers between devices, shifted(): lax.ppermute(value, axis, [(i, (i + shift) % size) for i in range(size)])  2.97 us
    dot_general x8, matrix products, project(): term = jnp.dot(block, rows, preferred_element_type=jnp.float32)  2.78 us
    reduce_sum x1, other arithmetic, gather_prefix(): slot = jnp.sum(jnp.where(mine, page_slot, 0))  1.54 us
    ppermute x3, waiting for transfers between devices, shifted(): lax.ppermute(value, axis, [(i, (i + shift) % size) for i in range(size)])  1.24 us
    convert_element_type x1, other arithmetic, on_device(): return ((source + branch) * live_mask[..., None]).astype(jnp.bfloat16)  1.1 us
  transfers between devices with their start and end apart: 16, of which 7 were waited for; matrix products, arithmetic and copies ran while one was open for 13% of the time, Pallas kernels for 7%

profile of v17, /device:TPU:0, one launch (start us, length us, event | category | flops | bytes accessed | tf_op | source)
XLA Modules:
  0.0 50.7 jit_solution(13701929342286160060)
XLA Ops:
  0.0 1.5 %fusion.28 = s32[]{:T(128)} fusion(s32[8]{0:T(128)} %param.15, s32[8]{0:T(128)} %param.14, s32[]{:T(128)} %axis_index.27), kind=kLoop, calls=%fused_computation.43 | loop fusion | flops 23 | bytes 72 | tf_op jit(solution)/shard_map/reduce_sum | solution.py:36
  2.2 1.0 %select_bitcast_fusion.rest_0_ = bf16[128,512]{1,0:T(8,128)(2,1)S(1)} fusion(bf16[2,128,1,512]{3,1,2,0:T(8,128)(2,1)} %param.13, pred[]{:T(512)S(6)} %eq.43), kind=kLoop, calls=%fused_computation.26 | loop fusion | flops 65536 | bytes 393217 | tf_op jit(solution)/shard_map/jit(_where)/select_n | solution.py:39
  3.2 5.1 %collective-permute-start.3 = (bf16[128,512]{1,0:T(8,128)(2,1)S(1)}, bf16[128,512]{1,0:T(8,128)(2,1)S(1)}, u32[]{:S(2)}, u32[]{:S(2)}) collective-permute-start(bf16[128,512]{1,0:T(8,128)(2,1)S(1)} %select_bitcast_fusion.rest_0_), channel_id=1, source_target_pairs={{0,24},{4,28},{8,16},{12,20},{16,8},{20,12},{24,0},{28,4},{1,25},{... | collective-permute-start | bytes 393224 | tf_op jit(solution)/shard_map/ppermute | solution.py:28
  8.4 1.5 %collective-permute-start = (bf16[128,512]{1,0:T(8,128)(2,1)S(1)}, bf16[128,512]{1,0:T(8,128)(2,1)S(1)}, u32[]{:S(2)}, u32[]{:S(2)}) collective-permute-start(bf16[128,512]{1,0:T(8,128)(2,1)S(1)} %select_bitcast_fusion.rest_0_), channel_id=1, source_target_pairs={{0,4},{4,0},{8,12},{12,8},{16,20},{20,16},{24,28},{28,24},{1,5},{5... | collective-permute-start | bytes 393224 | tf_op jit(solution)/shard_map/ppermute | solution.py:28
  9.9 2.0 %collective-permute-start.2 = (bf16[128,512]{1,0:T(8,128)(2,1)S(1)}, bf16[128,512]{1,0:T(8,128)(2,1)S(1)}, u32[]{:S(2)}, u32[]{:S(2)}) collective-permute-start(bf16[128,512]{1,0:T(8,128)(2,1)S(1)} %select_bitcast_fusion.rest_0_), channel_id=1, source_target_pairs={{0,12},{4,8},{8,4},{12,0},{16,28},{20,24},{24,20},{28,16},{1,13},{... | collective-permute-start | bytes 393224 | tf_op jit(solution)/shard_map/ppermute | solution.py:28
  11.9 0.8 %compare_reduce_fusion = pred[8]{0:T(512)(128)(4,1)S(1)} fusion(s32[8]{0:T(128)} %param.14, s32[8]{0:T(128)S(1)} %stack.35), kind=kLoop, calls=%fused_computation.27 | loop fusion | flops 120 | bytes 72 | tf_op jit(solution)/shard_map/reduce_or | solution.py:55
  12.8 1.7 %collective-permute-start.4 = (bf16[128,512]{1,0:T(8,128)(2,1)S(1)}, bf16[128,512]{1,0:T(8,128)(2,1)S(1)}, u32[]{:S(2)}, u32[]{:S(2)}) collective-permute-start(bf16[128,512]{1,0:T(8,128)(2,1)S(1)} %collective-permute-done.3.rest_4_), channel_id=1, source_target_pairs={{0,4},{4,0},{8,12},{12,8},{16,20},{20,16},{24,28},{28,24},{1,5},{5... | collective-permute-start | bytes 393224 | tf_op jit(solution)/shard_map/ppermute | solution.py:28
  14.5 1.5 %collective-permute-start.5 = (bf16[128,512]{1,0:T(8,128)(2,1)S(1)}, bf16[128,512]{1,0:T(8,128)(2,1)S(1)}, u32[]{:S(2)}, u32[]{:S(2)}) collective-permute-start(bf16[128,512]{1,0:T(8,128)(2,1)S(1)} %collective-permute-done.3.rest_4_), channel_id=1, source_target_pairs={{0,8},{4,12},{8,0},{12,4},{16,24},{20,28},{24,16},{28,20},{1,9},{5... | collective-permute-start | bytes 393224 | tf_op jit(solution)/shard_map/ppermute | solution.py:28
  16.4 0.6 %broadcast_in_dim.29.flag_ref = f32[1,1152]{1,0:T(1,128)} reshape(f32[1152]{0:T(1024)S(1)} %concatenate.12) | data formatting | bytes 9216 | tf_op jit(solution)/shard_map/broadcast_in_dim | solution.py:131
  17.0 0.7 %dynamic_slice.19 = s32[4]{0:T(128)S(1)} dynamic-slice(s32[32]{0:T(128)} %param.17, s32[]{:T(128)S(6)} %select_n.37), dynamic_slice_sizes={4} | dynamic-slice | bytes 36 | tf_op jit(solution)/shard_map/dynamic_slice | solution.py:180
  17.8 0.8 %select_reduce_fusion = s32[4]{0:T(128)S(1)} fusion(s32[32]{0:T(128)} %param.16, s32[4]{0:T(128)S(1)} %dynamic_slice.19), kind=kLoop, calls=%fused_computation.31 | loop fusion | flops 380 | bytes 160 | tf_op jit(solution)/shard_map/reduce_sum | solution.py:182
  18.7 0.6 %broadcast_in_dim.27.limit_ref = s32[4,1,1152]{2,1,0:T(1,128)} reshape(s32[4,1152]{1,0:T(4,128)S(1)} %concatenate.11) | data formatting | bytes 36864 | tf_op jit(solution)/shard_map/broadcast_in_dim | solution.py:135
  19.3 0.6 %collective-permute-done.4.rest_5_ = bf16[128,512]{1,0:T(8,128)(2,1)S(1)} collective-permute-done((bf16[128,512]{1,0:T(8,128)(2,1)S(1)}, bf16[128,512]{1,0:T(8,128)(2,1)S(1)}, u32[]{:S(2)}, u32[]{:S(2)}) %collective-permute-start.4) | collective-permute-done | bytes 131104 | tf_op jit(solution)/shard_map/ppermute | solution.py:28
  19.9 1.9 %collective-permute-done.5.rest_6_ = bf16[128,512]{1,0:T(8,128)(2,1)S(1)} collective-permute-done((bf16[128,512]{1,0:T(8,128)(2,1)S(1)}, bf16[128,512]{1,0:T(8,128)(2,1)S(1)}, u32[]{:S(2)}, u32[]{:S(2)}) %collective-permute-start.5) | collective-permute-done | bytes 131104 | tf_op jit(solution)/shard_map/ppermute | solution.py:28
  21.9 2.3 %collective-permute-done.6.rest_7_ = bf16[128,512]{1,0:T(8,128)(2,1)S(1)} collective-permute-done((bf16[128,512]{1,0:T(8,128)(2,1)S(1)}, bf16[128,512]{1,0:T(8,128)(2,1)S(1)}, u32[]{:S(2)}, u32[]{:S(2)}) %collective-permute-start.6) | collective-permute-done | bytes 131104 | tf_op jit(solution)/shard_map/ppermute | solution.py:28
  24.8 3.7 %shard_map.109 = bf16[2,128,512]{2,1,0:T(8,128)(2,1)} custom-call(s32[4,1,1152]{2,1,0:T(1,128)} %broadcast_in_dim.27.limit_ref, f32[1,1152]{1,0:T(1,128)} %broadcast_in_dim.29.flag_ref, bf16[4,128,1024]{2,1,0:T(8,128)(2,1)} %bitcast.37, f32[128,128]{1,0:T(8,128)} %constant.44.clone.cos_ref, f32[128,128]{1,0:T(8,128)} %constant.45.clone.sin_ref, ...), custom_call_target="tpu_custom_call" | custom-call | tf_op jit(solution)/shard_map/pallas_call | solution.py:138
  28.5 1.4 %collective-permute-start.8 = (bf16[256,512]{1,0:T(8,128)(2,1)}, bf16[256,512]{1,0:T(8,128)(2,1)S(1)}, u32[]{:S(2)}, u32[]{:S(2)}) collective-permute-start(bf16[256,512]{1,0:T(8,128)(2,1)} %bitcast.42), channel_id=1, source_target_pairs={{0,2},{1,3},{2,0},{3,1},{4,6},{5,7},{6,4},{7,5},{8,10},{9,11},{10,... | collective-permute-start | bytes 786440 | tf_op jit(solution)/shard_map/ppermute | solution.py:28
  30.0 3.7 %shard_map.110 = bf16[2,128,512]{2,1,0:T(8,128)(2,1)} custom-call(s32[4,1,1152]{2,1,0:T(1,128)} %broadcast_in_dim.27.limit_ref, f32[1,1152]{1,0:T(1,128)} %broadcast_in_dim.29.flag_ref, bf16[4,128,1024]{2,1,0:T(8,128)(2,1)} %bitcast.38, f32[128,128]{1,0:T(8,128)} %constant.44.clone.cos_ref, f32[128,128]{1,0:T(8,128)} %constant.45.clone.sin_ref, ...), custom_call_target="tpu_custom_call" | custom-call | tf_op jit(solution)/shard_map/pallas_call | solution.py:138
  34.7 2.4 %collective-permute-done.8 = bf16[256,512]{1,0:T(8,128)(2,1)S(1)} collective-permute-done((bf16[256,512]{1,0:T(8,128)(2,1)}, bf16[256,512]{1,0:T(8,128)(2,1)S(1)}, u32[]{:S(2)}, u32[]{:S(2)}) %collective-permute-start.8) | collective-permute-done | bytes 262176 | tf_op jit(solution)/shard_map/ppermute | solution.py:28
  37.1 4.8 %collective-permute-done.11 = bf16[256,512]{1,0:T(8,128)(2,1)S(1)} collective-permute-done((bf16[256,512]{1,0:T(8,128)(2,1)}, bf16[256,512]{1,0:T(8,128)(2,1)S(1)}, u32[]{:S(2)}, u32[]{:S(2)}) %collective-permute-start.11) | collective-permute-done | bytes 262176 | tf_op jit(solution)/shard_map/ppermute | solution.py:28
  45.9 1.4 %collective-permute-start.14 = (f32[4,128]{1,0:T(4,128)S(1)}, f32[4,128]{1,0:T(4,128)S(1)}, u32[]{:S(2)}, u32[]{:S(2)}) collective-permute-start(f32[4,128]{1,0:T(4,128)S(1)} %bitcast.46), channel_id=1, source_target_pairs={{0,2},{1,3},{2,0},{3,1},{4,6},{5,7},{6,4},{7,5},{8,10},{9,11},{10,... | collective-permute-start | bytes 6152 | tf_op jit(solution)/shard_map/ppermute | solution.py:24
  47.3 1.0 %collective-permute-start.15 = (f32[4,128]{1,0:T(4,128)S(1)}, f32[4,128]{1,0:T(4,128)S(1)}, u32[]{:S(2)}, u32[]{:S(2)}) collective-permute-start(f32[4,128]{1,0:T(4,128)S(1)} %bitcast.47), channel_id=1, source_target_pairs={{0,3},{1,0},{2,1},{3,2},{4,7},{5,4},{6,5},{7,6},{8,11},{9,8},{10,9... | collective-permute-start | bytes 6152 | tf_op jit(solution)/shard_map/ppermute | solution.py:24
  48.4 1.1 %collective-permute-done.14 = f32[4,128]{1,0:T(4,128)S(1)} collective-permute-done((f32[4,128]{1,0:T(4,128)S(1)}, f32[4,128]{1,0:T(4,128)S(1)}, u32[]{:S(2)}, u32[]{:S(2)}) %collective-permute-start.14) | collective-permute-done | bytes 2080 | tf_op jit(solution)/shard_map/ppermute | solution.py:24
  49.6 1.1 %fusion.5 = bf16[4,128,576]{1,2,0:T(8,128)(2,1)} fusion(f32[72,4,8,128]{3,2,1,0:T(8,128)S(1)} %get-tuple-element.6, bf16[4,128,576]{1,2,0:T(8,128)(2,1)S(1)} %copy-done.4, f32[4,128]{1,0:T(4,128)S(1)} %fusion.19, f32[576]{0:T(1024)S(1)} %copy-done.12, f32[4,128]{1,0:T(4,128)S(1)} %add_rsqrt_fusion), kind=kLoop, calls=%fused_computation.10 | loop fusion | flops 1769472 | bytes 2365696 | tf_op jit(solution)/shard_map/convert_element_type | solution.py:204
  (61 shorter events, 6.5 us)
Async XLA Ops:
  0.0 42.0 %copy-start = (bf16[2048,576]{0,1:T(8,128)(2,1)S(1)}, bf16[2048,576]{0,1:T(8,128)(2,1)}, u32[]{:S(2)}) copy-start(bf16[2048,576]{0,1:T(8,128)(2,1)} %param.18) | copy-start | bytes 7077892
  3.2 21.0 %copy-start.1 = (bf16[128,512]{1,0:T(8,128)(2,1)}, bf16[128,512]{1,0:T(8,128)(2,1)S(1)}, u32[]{:S(2)}) copy-start(bf16[128,512]{1,0:T(8,128)(2,1)S(1)} %select_bitcast_fusion.rest_0_) | copy-start | bytes 393220
  3.2 9.6 %collective-permute-start.3 = (bf16[128,512]{1,0:T(8,128)(2,1)S(1)}, bf16[128,512]{1,0:T(8,128)(2,1)S(1)}, u32[]{:S(2)}, u32[]{:S(2)}) collective-permute-start(bf16[128,512]{1,0:T(8,128)(2,1)S(1)} %select_bitcast_fusion.rest_0_), channel_id=1, source_target_pairs={{0,24},{4,28},{8,16},{12,20},{16,8},{20,12},{24,0},{28,4},{1,25},{... | collective-permute-start | bytes 393224 | tf_op jit(solution)/shard_map/ppermute | solution.py:28
  8.4 7.5 %collective-permute-start = (bf16[128,512]{1,0:T(8,128)(2,1)S(1)}, bf16[128,512]{1,0:T(8,128)(2,1)S(1)}, u32[]{:S(2)}, u32[]{:S(2)}) collective-permute-start(bf16[128,512]{1,0:T(8,128)(2,1)S(1)} %select_bitcast_fusion.rest_0_), channel_id=1, source_target_pairs={{0,4},{4,0},{8,12},{12,8},{16,20},{20,16},{24,28},{28,24},{1,5},{5... | collective-permute-start | bytes 393224 | tf_op jit(solution)/shard_map/ppermute | solution.py:28
  9.9 9.4 %collective-permute-start.1 = (bf16[128,512]{1,0:T(8,128)(2,1)S(1)}, bf16[128,512]{1,0:T(8,128)(2,1)S(1)}, u32[]{:S(2)}, u32[]{:S(2)}) collective-permute-start(bf16[128,512]{1,0:T(8,128)(2,1)S(1)} %select_bitcast_fusion.rest_0_), channel_id=1, source_target_pairs={{0,8},{4,12},{8,0},{12,4},{16,24},{20,28},{24,16},{28,20},{1,9},{5... | collective-permute-start | bytes 393224 | tf_op jit(solution)/shard_map/ppermute | solution.py:28
  9.9 9.4 %collective-permute-start.2 = (bf16[128,512]{1,0:T(8,128)(2,1)S(1)}, bf16[128,512]{1,0:T(8,128)(2,1)S(1)}, u32[]{:S(2)}, u32[]{:S(2)}) collective-permute-start(bf16[128,512]{1,0:T(8,128)(2,1)S(1)} %select_bitcast_fusion.rest_0_), channel_id=1, source_target_pairs={{0,12},{4,8},{8,4},{12,0},{16,28},{20,24},{24,20},{28,16},{1,13},{... | collective-permute-start | bytes 393224 | tf_op jit(solution)/shard_map/ppermute | solution.py:28
  12.8 11.4 %copy-start.5 = (bf16[128,512]{1,0:T(8,128)(2,1)}, bf16[128,512]{1,0:T(8,128)(2,1)S(1)}, u32[]{:S(2)}) copy-start(bf16[128,512]{1,0:T(8,128)(2,1)S(1)} %collective-permute-done.3.rest_4_) | copy-start | bytes 393220
  12.8 7.1 %collective-permute-start.4 = (bf16[128,512]{1,0:T(8,128)(2,1)S(1)}, bf16[128,512]{1,0:T(8,128)(2,1)S(1)}, u32[]{:S(2)}, u32[]{:S(2)}) collective-permute-start(bf16[128,512]{1,0:T(8,128)(2,1)S(1)} %collective-permute-done.3.rest_4_), channel_id=1, source_target_pairs={{0,4},{4,0},{8,12},{12,8},{16,20},{20,16},{24,28},{28,24},{1,5},{5... | collective-permute-start | bytes 393224 | tf_op jit(solution)/shard_map/ppermute | solution.py:28
  14.5 7.4 %collective-permute-start.5 = (bf16[128,512]{1,0:T(8,128)(2,1)S(1)}, bf16[128,512]{1,0:T(8,128)(2,1)S(1)}, u32[]{:S(2)}, u32[]{:S(2)}) collective-permute-start(bf16[128,512]{1,0:T(8,128)(2,1)S(1)} %collective-permute-done.3.rest_4_), channel_id=1, source_target_pairs={{0,8},{4,12},{8,0},{12,4},{16,24},{20,28},{24,16},{28,20},{1,9},{5... | collective-permute-start | bytes 393224 | tf_op jit(solution)/shard_map/ppermute | solution.py:28
  15.9 8.3 %copy-start.6 = (bf16[128,512]{1,0:T(8,128)(2,1)}, bf16[128,512]{1,0:T(8,128)(2,1)S(1)}, u32[]{:S(2)}) copy-start(bf16[128,512]{1,0:T(8,128)(2,1)S(1)} %collective-permute-done.rest_1_) | copy-start | bytes 393220
  15.9 8.3 %collective-permute-start.6 = (bf16[128,512]{1,0:T(8,128)(2,1)S(1)}, bf16[128,512]{1,0:T(8,128)(2,1)S(1)}, u32[]{:S(2)}, u32[]{:S(2)}) collective-permute-start(bf16[128,512]{1,0:T(8,128)(2,1)S(1)} %collective-permute-done.3.rest_4_), channel_id=1, source_target_pairs={{0,12},{4,8},{8,4},{12,0},{16,28},{20,24},{24,20},{28,16},{1,13},{... | collective-permute-start | bytes 393224 | tf_op jit(solution)/shard_map/ppermute | solution.py:28
  19.3 4.9 %copy-start.8 = (bf16[128,512]{1,0:T(8,128)(2,1)}, bf16[128,512]{1,0:T(8,128)(2,1)S(1)}, u32[]{:S(2)}) copy-start(bf16[128,512]{1,0:T(8,128)(2,1)S(1)} %collective-permute-done.2.rest_3_) | copy-start | bytes 393220
  28.5 5.7 %copy-start.3 = (bf16[2,128,512]{2,1,0:T(8,128)(2,1)S(1)}, bf16[2,128,512]{2,1,0:T(8,128)(2,1)}, u32[]{:S(2)}) copy-start(bf16[2,128,512]{2,1,0:T(8,128)(2,1)} %shard_map.109) | copy-start | bytes 786436
  28.5 8.6 %collective-permute-start.8 = (bf16[256,512]{1,0:T(8,128)(2,1)}, bf16[256,512]{1,0:T(8,128)(2,1)S(1)}, u32[]{:S(2)}, u32[]{:S(2)}) collective-permute-start(bf16[256,512]{1,0:T(8,128)(2,1)} %bitcast.42), channel_id=1, source_target_pairs={{0,2},{1,3},{2,0},{3,1},{4,6},{5,7},{6,4},{7,5},{8,10},{9,11},{10,... | collective-permute-start | bytes 786440 | tf_op jit(solution)/shard_map/ppermute | solution.py:28
  33.6 8.3 %collective-permute-start.11 = (bf16[256,512]{1,0:T(8,128)(2,1)}, bf16[256,512]{1,0:T(8,128)(2,1)S(1)}, u32[]{:S(2)}, u32[]{:S(2)}) collective-permute-start(bf16[256,512]{1,0:T(8,128)(2,1)} %bitcast.39), channel_id=1, source_target_pairs={{0,2},{1,3},{2,0},{3,1},{4,6},{5,7},{6,4},{7,5},{8,10},{9,11},{10,... | collective-permute-start | bytes 786440 | tf_op jit(solution)/shard_map/ppermute | solution.py:28
  34.2 8.5 %collective-permute-start.7 = (bf16[256,512]{1,0:T(8,128)(2,1)S(1)}, bf16[256,512]{1,0:T(8,128)(2,1)S(1)}, u32[]{:S(2)}, u32[]{:S(2)}) collective-permute-start(bf16[256,512]{1,0:T(8,128)(2,1)S(1)} %bitcast.43), channel_id=1, source_target_pairs={{0,1},{1,0},{2,3},{3,2},{4,5},{5,4},{6,7},{7,6},{8,9},{9,8},{10,11... | collective-permute-start | bytes 786440 | tf_op jit(solution)/shard_map/ppermute | solution.py:28
  34.2 9.2 %collective-permute-start.10 = (bf16[256,512]{1,0:T(8,128)(2,1)}, bf16[256,512]{1,0:T(8,128)(2,1)S(1)}, u32[]{:S(2)}, u32[]{:S(2)}) collective-permute-start(bf16[256,512]{1,0:T(8,128)(2,1)} %bitcast.40), channel_id=1, source_target_pairs={{0,1},{1,0},{2,3},{3,2},{4,5},{5,4},{6,7},{7,6},{8,9},{9,8},{10,11... | collective-permute-start | bytes 786440 | tf_op jit(solution)/shard_map/ppermute | solution.py:28
  37.1 7.2 %collective-permute-start.9 = (bf16[256,512]{1,0:T(8,128)(2,1)S(1)}, bf16[256,512]{1,0:T(8,128)(2,1)S(1)}, u32[]{:S(2)}, u32[]{:S(2)}) collective-permute-start(bf16[256,512]{1,0:T(8,128)(2,1)S(1)} %collective-permute-done.8), channel_id=1, source_target_pairs={{0,1},{1,0},{2,3},{3,2},{4,5},{5,4},{6,7},{7,6},{8,9},{9,8},{10,11... | collective-permute-start | bytes 786440 | tf_op jit(solution)/shard_map/ppermute | solution.py:28
  41.9 2.8 %collective-permute-start.12 = (bf16[256,512]{1,0:T(8,128)(2,1)S(1)}, bf16[256,512]{1,0:T(8,128)(2,1)S(1)}, u32[]{:S(2)}, u32[]{:S(2)}) collective-permute-start(bf16[256,512]{1,0:T(8,128)(2,1)S(1)} %collective-permute-done.11), channel_id=1, source_target_pairs={{0,1},{1,0},{2,3},{3,2},{4,5},{5,4},{6,7},{7,6},{8,9},{9,8},{10,11... | collective-permute-start | bytes 786440 | tf_op jit(solution)/shard_map/ppermute | solution.py:28
  44.7 4.9 %copy-start.4 = (bf16[4,128,576]{1,2,0:T(8,128)(2,1)S(1)}, bf16[4,128,576]{1,2,0:T(8,128)(2,1)}, u32[]{:S(2)}) copy-start(bf16[4,128,576]{1,2,0:T(8,128)(2,1)} %param.11) | copy-start | bytes 1769476
  44.7 4.9 %copy-start.12 = (f32[576]{0:T(1024)S(1)}, f32[576]{0:T(1024)}, u32[]{:S(2)}) copy-start(f32[576]{0:T(1024)} %param.19) | copy-start | bytes 6916
  45.3 3.1 %collective-permute-start.13 = (f32[4,128]{1,0:T(4,128)S(1)}, f32[4,128]{1,0:T(4,128)S(1)}, u32[]{:S(2)}, u32[]{:S(2)}) collective-permute-start(f32[4,128]{1,0:T(4,128)S(1)} %bitcast.45), channel_id=1, source_target_pairs={{0,1},{1,2},{2,3},{3,0},{4,5},{5,6},{6,7},{7,4},{8,9},{9,10},{10,1... | collective-permute-start | bytes 6152 | tf_op jit(solution)/shard_map/ppermute | solution.py:24
  45.9 3.6 %collective-permute-start.14 = (f32[4,128]{1,0:T(4,128)S(1)}, f32[4,128]{1,0:T(4,128)S(1)}, u32[]{:S(2)}, u32[]{:S(2)}) collective-permute-start(f32[4,128]{1,0:T(4,128)S(1)} %bitcast.46), channel_id=1, source_target_pairs={{0,2},{1,3},{2,0},{3,1},{4,6},{5,7},{6,4},{7,5},{8,10},{9,11},{10,... | collective-permute-start | bytes 6152 | tf_op jit(solution)/shard_map/ppermute | solution.py:24
  47.3 2.3 %collective-permute-start.15 = (f32[4,128]{1,0:T(4,128)S(1)}, f32[4,128]{1,0:T(4,128)S(1)}, u32[]{:S(2)}, u32[]{:S(2)}) collective-permute-start(f32[4,128]{1,0:T(4,128)S(1)} %bitcast.47), channel_id=1, source_target_pairs={{0,3},{1,0},{2,1},{3,2},{4,7},{5,4},{6,5},{7,6},{8,11},{9,8},{10,9... | collective-permute-start | bytes 6152 | tf_op jit(solution)/shard_map/ppermute | solution.py:24
  (5 other events, 13.2 us)

commit v18 on v16

--- a/solution.py
+++ b/solution.py
@@ -139,23 +139,24 @@
         out_shape=jax.ShapeDtypeStruct((count, slots, per_group * HD), jnp.bfloat16),
     )(limits, flags, qkv, cosine, sine, *blocks)
 
-def project(own, w_out, tp_index, n_tp, group_width):
+def exchange(own, tp_index, n_tp):
     if n_tp == 4:
         near = swapped(own, "tp", n_tp, 1)
         far = swapped(own, "tp", n_tp, 2)
         farther = swapped(far, "tp", n_tp, 1)
-        parts = [(own, tp_index), (near, tp_index ^ 1), (far, tp_index ^ 2), (farther, tp_index ^ 3)]
-    else:
-        parts = [(own, tp_index)]
-        for shift in range(1, n_tp):
-            parts.append((shifted(own, "tp", n_tp, shift), (tp_index - shift) % n_tp))
-    projected = None
+        return [(own, tp_index), (near, tp_index ^ 1), (far, tp_index ^ 2), (farther, tp_index ^ 3)]
+    parts = [(own, tp_index)]
+    for shift in range(1, n_tp):
+        parts.append((shifted(own, "tp", n_tp, shift), (tp_index - shift) % n_tp))
+    return parts
+
+
+def products(parts, w_out, group_width, projected=None):
     for block, group in parts:
         rows = lax.dynamic_slice_in_dim(w_out, group * group_width, group_width, 0)
         term = jnp.dot(block, rows, preferred_element_type=jnp.float32)
         projected = term if projected is None else projected + term
     return projected
-
 
 def on_device(
     hidden, qkv, page_store, page_owner, page_slot, lengths, request_perm, w_out, post_gain,
@@ -179,12 +180,19 @@
     cosine, sine = static_tables(prefix_len + np.arange(slots), HD)
     group_width = per_group * HD
     chunk = max(1, requests // 2)
+    qkv_rows = qkv[:, :, 0]
     projected_parts = []
+    pending = None
     for start in range(0, requests, chunk):
-        attended = attend(qkv[:, :, 0], jnp.asarray(cosine), jnp.asarray(sine), blocks,
+        if pending is not None:
+            early, late = pending
+            early, qkv_rows = lax.optimization_barrier((early, qkv_rows))
+            projected_parts.append(products(late, w_out, group_width, early))
+        attended = attend(qkv_rows, jnp.asarray(cosine), jnp.asarray(sine), blocks,
                           my_lengths, valid.astype(jnp.int32), start, chunk)
-        own = attended.reshape(chunk * slots, per_group * HD)
-        projected_parts.append(project(own, w_out, tp_index, n_tp, group_width))
+        parts = exchange(attended.reshape(chunk * slots, per_group * HD), tp_index, n_tp)
+        pending = (products(parts[:2], w_out, group_width), parts[2:])
+    projected_parts.append(products(pending[1], w_out, group_width, pending[0]))
     projected = jnp.concatenate(projected_parts, 0).reshape(requests, slots, local_width)
 
     squares = jnp.sum(projected * projected, -1)

time: 51.3 us -> 52.1 us (1.016)
  matrix products: 2.79 us -> 3.75 us
  starting transfers between devices: 17.7 us -> 18.3 us
    dot_general x8, matrix products: 2.79 us -> 3.75 us  [products(): term = jnp.dot(block, rows, preferred_element_type=jnp.float32)]
    ppermute x13, starting transfers between devices: 14.7 us -> 15.3 us  [swapped(): return lax.ppermute(value, axis, [(i, i ^ mask) for i in range(size)])]
  transfers between devices with their start and end apart: 16 -> 16, of which waited for: 7 -> 8; matrix products, arithmetic and copies ran while one was open for 13% -> 14% of each run, Pallas kernels for 7% -> 7%
where the time goes in v18:
time: 52.1 us; the launch traced here: 51.7 us
  starting transfers between devices  18.3 us (35%)
  waiting for transfers between devices  13 us (25%)
  Pallas kernels  7.53 us (14%)
  other arithmetic  5.54 us (11%)
  matrix products  3.75 us (7%)
  local copies, waits for them, and re-layouts  2.82 us (5%)
  between operations  0.76 us (1%)
    ppermute x13, starting transfers between devices, swapped(): return lax.ppermute(value, axis, [(i, i ^ mask) for i in range(size)])  15.3 us
    ppermute x13, waiting for transfers between devices, swapped(): return lax.ppermute(value, axis, [(i, i ^ mask) for i in range(size)])  11.8 us
    pallas_call x2, Pallas kernels, attend(): pl.pallas_call(attention_kernel, grid=(1,), in_specs=[pl.BlockSpec((count...  7.53 us
    dot_general x8, matrix products, products(): term = jnp.dot(block, rows, preferred_element_type=jnp.float32)  3.75 us
    ppermute x3, starting transfers between devices, shifted(): lax.ppermute(value, axis, [(i, (i + shift) % size) for i in range(size)])  2.95 us
    reduce_sum x1, other arithmetic, gather_prefix(): slot = jnp.sum(jnp.where(mine, page_slot, 0))  1.43 us
    ppermute x3, waiting for transfers between devices, shifted(): lax.ppermute(value, axis, [(i, (i + shift) % size) for i in range(size)])  1.24 us
    convert_element_type x1, other arithmetic, on_device(): return ((source + branch) * live_mask[..., None]).astype(jnp.bfloat16)  1.1 us
  transfers between devices with their start and end apart: 16, of which 8 were waited for; matrix products, arithmetic and copies ran while one was open for 14% of the time, Pallas kernels for 7%

profile of v18, /device:TPU:0, one launch (start us, length us, event | category | flops | bytes accessed | tf_op | source)
XLA Modules:
  0.0 51.7 jit_solution(3048998791511530050)
XLA Ops:
  0.0 1.4 %fusion.26 = s32[]{:T(128)} fusion(s32[8]{0:T(128)} %param.15, s32[8]{0:T(128)} %param.14, s32[]{:T(128)} %axis_index.27), kind=kLoop, calls=%fused_computation.42 | loop fusion | flops 23 | bytes 72 | tf_op jit(solution)/shard_map/reduce_sum | solution.py:36
  2.0 1.0 %select_bitcast_fusion.rest_0_ = bf16[128,512]{1,0:T(8,128)(2,1)S(1)} fusion(bf16[2,128,1,512]{3,1,2,0:T(8,128)(2,1)} %param.13, pred[]{:T(512)S(6)} %eq.43), kind=kLoop, calls=%fused_computation.25 | loop fusion | flops 65536 | bytes 393217 | tf_op jit(solution)/shard_map/jit(_where)/select_n | solution.py:39
  3.0 5.1 %collective-permute-start.3 = (bf16[128,512]{1,0:T(8,128)(2,1)S(1)}, bf16[128,512]{1,0:T(8,128)(2,1)S(1)}, u32[]{:S(2)}, u32[]{:S(2)}) collective-permute-start(bf16[128,512]{1,0:T(8,128)(2,1)S(1)} %select_bitcast_fusion.rest_0_), channel_id=1, source_target_pairs={{0,24},{4,28},{8,16},{12,20},{16,8},{20,12},{24,0},{28,4},{1,25},{... | collective-permute-start | bytes 393224 | tf_op jit(solution)/shard_map/ppermute | solution.py:28
  8.1 1.5 %collective-permute-start = (bf16[128,512]{1,0:T(8,128)(2,1)S(1)}, bf16[128,512]{1,0:T(8,128)(2,1)S(1)}, u32[]{:S(2)}, u32[]{:S(2)}) collective-permute-start(bf16[128,512]{1,0:T(8,128)(2,1)S(1)} %select_bitcast_fusion.rest_0_), channel_id=1, source_target_pairs={{0,4},{4,0},{8,12},{12,8},{16,20},{20,16},{24,28},{28,24},{1,5},{5... | collective-permute-start | bytes 393224 | tf_op jit(solution)/shard_map/ppermute | solution.py:28
  9.6 2.0 %collective-permute-start.2 = (bf16[128,512]{1,0:T(8,128)(2,1)S(1)}, bf16[128,512]{1,0:T(8,128)(2,1)S(1)}, u32[]{:S(2)}, u32[]{:S(2)}) collective-permute-start(bf16[128,512]{1,0:T(8,128)(2,1)S(1)} %select_bitcast_fusion.rest_0_), channel_id=1, source_target_pairs={{0,12},{4,8},{8,4},{12,0},{16,28},{20,24},{24,20},{28,16},{1,13},{... | collective-permute-start | bytes 393224 | tf_op jit(solution)/shard_map/ppermute | solution.py:28
  11.7 0.8 %compare_reduce_fusion = pred[8]{0:T(512)(128)(4,1)S(1)} fusion(s32[8]{0:T(128)} %param.14, s32[8]{0:T(128)S(1)} %stack.35), kind=kLoop, calls=%fused_computation.26 | loop fusion | flops 120 | bytes 72 | tf_op jit(solution)/shard_map/reduce_or | solution.py:55
  12.6 1.7 %collective-permute-start.4 = (bf16[128,512]{1,0:T(8,128)(2,1)S(1)}, bf16[128,512]{1,0:T(8,128)(2,1)S(1)}, u32[]{:S(2)}, u32[]{:S(2)}) collective-permute-start(bf16[128,512]{1,0:T(8,128)(2,1)S(1)} %collective-permute-done.3.rest_4_), channel_id=1, source_target_pairs={{0,4},{4,0},{8,12},{12,8},{16,20},{20,16},{24,28},{28,24},{1,5},{5... | collective-permute-start | bytes 393224 | tf_op jit(solution)/shard_map/ppermute | solution.py:28
  14.2 1.5 %collective-permute-start.5 = (bf16[128,512]{1,0:T(8,128)(2,1)S(1)}, bf16[128,512]{1,0:T(8,128)(2,1)S(1)}, u32[]{:S(2)}, u32[]{:S(2)}) collective-permute-start(bf16[128,512]{1,0:T(8,128)(2,1)S(1)} %collective-permute-done.3.rest_4_), channel_id=1, source_target_pairs={{0,8},{4,12},{8,0},{12,4},{16,24},{20,28},{24,16},{28,20},{1,9},{5... | collective-permute-start | bytes 393224 | tf_op jit(solution)/shard_map/ppermute | solution.py:28
  16.8 0.7 %dynamic_slice.19 = s32[4]{0:T(128)S(1)} dynamic-slice(s32[32]{0:T(128)} %param.17, s32[]{:T(128)S(6)} %select_n.37), dynamic_slice_sizes={4} | dynamic-slice | bytes 36 | tf_op jit(solution)/shard_map/dynamic_slice | solution.py:173
  17.5 0.8 %select_reduce_fusion = s32[4]{0:T(128)S(1)} fusion(s32[32]{0:T(128)} %param.16, s32[4]{0:T(128)S(1)} %dynamic_slice.19), kind=kLoop, calls=%fused_computation.30 | loop fusion | flops 380 | bytes 160 | tf_op jit(solution)/shard_map/reduce_sum | solution.py:175
  18.4 0.6 %broadcast_in_dim.27.limit_ref = s32[4,1,1152]{2,1,0:T(1,128)} reshape(s32[4,1152]{1,0:T(4,128)S(1)} %concatenate.11) | data formatting | bytes 36864 | tf_op jit(solution)/shard_map/broadcast_in_dim | solution.py:127
  19.1 0.6 %collective-permute-done.4.rest_5_ = bf16[128,512]{1,0:T(8,128)(2,1)S(1)} collective-permute-done((bf16[128,512]{1,0:T(8,128)(2,1)S(1)}, bf16[128,512]{1,0:T(8,128)(2,1)S(1)}, u32[]{:S(2)}, u32[]{:S(2)}) %collective-permute-start.4) | collective-permute-done | bytes 131104 | tf_op jit(solution)/shard_map/ppermute | solution.py:28
  19.7 1.9 %collective-permute-done.5.rest_6_ = bf16[128,512]{1,0:T(8,128)(2,1)S(1)} collective-permute-done((bf16[128,512]{1,0:T(8,128)(2,1)S(1)}, bf16[128,512]{1,0:T(8,128)(2,1)S(1)}, u32[]{:S(2)}, u32[]{:S(2)}) %collective-permute-start.5) | collective-permute-done | bytes 131104 | tf_op jit(solution)/shard_map/ppermute | solution.py:28
  21.6 2.3 %collective-permute-done.6.rest_7_ = bf16[128,512]{1,0:T(8,128)(2,1)S(1)} collective-permute-done((bf16[128,512]{1,0:T(8,128)(2,1)S(1)}, bf16[128,512]{1,0:T(8,128)(2,1)S(1)}, u32[]{:S(2)}, u32[]{:S(2)}) %collective-permute-start.6) | collective-permute-done | bytes 131104 | tf_op jit(solution)/shard_map/ppermute | solution.py:28
  24.6 3.8 %shard_map.109 = bf16[2,128,512]{2,1,0:T(8,128)(2,1)} custom-call(s32[4,1,1152]{2,1,0:T(1,128)} %broadcast_in_dim.27.limit_ref, f32[1,1152]{1,0:T(1,128)} %broadcast_in_dim.29.flag_ref, bf16[4,128,1024]{2,1,0:T(8,128)(2,1)} %bitcast.37, f32[128,128]{1,0:T(8,128)} %constant.44.clone.cos_ref, f32[128,128]{1,0:T(8,128)} %constant.45.clone.sin_ref, ...), custom_call_target="tpu_custom_call" | custom-call | tf_op jit(solution)/shard_map/pallas_call | solution.py:130
  28.4 1.4 %collective-permute-start.8 = (bf16[256,512]{1,0:T(8,128)(2,1)}, bf16[256,512]{1,0:T(8,128)(2,1)S(1)}, u32[]{:S(2)}, u32[]{:S(2)}) collective-permute-start(bf16[256,512]{1,0:T(8,128)(2,1)} %bitcast.40), channel_id=1, source_target_pairs={{0,2},{1,3},{2,0},{3,1},{4,6},{5,7},{6,4},{7,5},{8,10},{9,11},{10,... | collective-permute-start | bytes 786440 | tf_op jit(solution)/shard_map/ppermute | solution.py:28
  30.5 1.3 %convolution_add_fusion.4 = f32[256,576]{0,1:T(8,128)S(1)} fusion(f32[256,576]{0,1:T(8,128)S(1)} %fusion.13, bf16[256,512]{1,0:T(8,128)(2,1)} %bitcast.41, bf16[2048,576]{0,1:T(8,128)(2,1)S(1)} %copy-done, s32[]{:T(128)S(6)} %select_n.43), kind=kOutput, calls=%fused_computation.4 | convolution fusion | flops 151142400 | bytes 2031620 | tf_op jit(solution)/shard_map/dot_general | solution.py:157
  31.8 3.8 %shard_map.110 = bf16[2,128,512]{2,1,0:T(8,128)(2,1)} custom-call(s32[4,1,1152]{2,1,0:T(1,128)} %broadcast_in_dim.27.limit_ref, f32[1,1152]{1,0:T(1,128)} %broadcast_in_dim.29.flag_ref, bf16[4,128,1024]{2,1,0:T(8,128)(2,1)} %bitcast.38, f32[128,128]{1,0:T(8,128)} %constant.44.clone.cos_ref, f32[128,128]{1,0:T(8,128)} %constant.45.clone.sin_ref, ...), custom_call_target="tpu_custom_call" | custom-call | tf_op jit(solution)/shard_map/pallas_call | solution.py:130
  35.6 1.4 %collective-permute-start.11 = (bf16[256,512]{1,0:T(8,128)(2,1)}, bf16[256,512]{1,0:T(8,128)(2,1)S(1)}, u32[]{:S(2)}, u32[]{:S(2)}) collective-permute-start(bf16[256,512]{1,0:T(8,128)(2,1)} %bitcast.42), channel_id=1, source_target_pairs={{0,2},{1,3},{2,0},{3,1},{4,6},{5,7},{6,4},{7,5},{8,10},{9,11},{10,... | collective-permute-start | bytes 786440 | tf_op jit(solution)/shard_map/ppermute | solution.py:28
  37.9 6.2 %collective-permute-done.11 = bf16[256,512]{1,0:T(8,128)(2,1)S(1)} collective-permute-done((bf16[256,512]{1,0:T(8,128)(2,1)}, bf16[256,512]{1,0:T(8,128)(2,1)S(1)}, u32[]{:S(2)}, u32[]{:S(2)}) %collective-permute-start.11) | collective-permute-done | bytes 262176 | tf_op jit(solution)/shard_map/ppermute | solution.py:28
  46.8 1.4 %collective-permute-start.14 = (f32[4,128]{1,0:T(4,128)S(1)}, f32[4,128]{1,0:T(4,128)S(1)}, u32[]{:S(2)}, u32[]{:S(2)}) collective-permute-start(f32[4,128]{1,0:T(4,128)S(1)} %bitcast.46), channel_id=1, source_target_pairs={{0,2},{1,3},{2,0},{3,1},{4,6},{5,7},{6,4},{7,5},{8,10},{9,11},{10,... | collective-permute-start | bytes 6152 | tf_op jit(solution)/shard_map/ppermute | solution.py:24
  48.2 1.0 %collective-permute-start.15 = (f32[4,128]{1,0:T(4,128)S(1)}, f32[4,128]{1,0:T(4,128)S(1)}, u32[]{:S(2)}, u32[]{:S(2)}) collective-permute-start(f32[4,128]{1,0:T(4,128)S(1)} %bitcast.47), channel_id=1, source_target_pairs={{0,3},{1,0},{2,1},{3,2},{4,7},{5,4},{6,5},{7,6},{8,11},{9,8},{10,9... | collective-permute-start | bytes 6152 | tf_op jit(solution)/shard_map/ppermute | solution.py:24
  49.3 1.0 %collective-permute-done.14 = f32[4,128]{1,0:T(4,128)S(1)} collective-permute-done((f32[4,128]{1,0:T(4,128)S(1)}, f32[4,128]{1,0:T(4,128)S(1)}, u32[]{:S(2)}, u32[]{:S(2)}) %collective-permute-start.14) | collective-permute-done | bytes 2080 | tf_op jit(solution)/shard_map/ppermute | solution.py:24
  50.6 1.1 %fusion.4 = bf16[4,128,576]{1,2,0:T(8,128)(2,1)} fusion(f32[72,4,8,128]{3,2,1,0:T(8,128)S(1)} %get-tuple-element.10, bf16[4,128,576]{1,2,0:T(8,128)(2,1)S(1)} %copy-done.3, f32[4,128]{1,0:T(4,128)S(1)} %fusion.17, f32[576]{0:T(1024)S(1)} %copy-done.11, f32[4,128]{1,0:T(4,128)S(1)} %add_rsqrt_fusion), kind=kLoop, calls=%fused_computation.10 | loop fusion | flops 1769472 | bytes 2365696 | tf_op jit(solution)/shard_map/convert_element_type | solution.py:204
  (59 shorter events, 6.3 us)
Async XLA Ops:
  0.0 30.1 %copy-start = (bf16[2048,576]{0,1:T(8,128)(2,1)S(1)}, bf16[2048,576]{0,1:T(8,128)(2,1)}, u32[]{:S(2)}) copy-start(bf16[2048,576]{0,1:T(8,128)(2,1)} %param.18) | copy-start | bytes 7077892
  3.0 21.0 %copy-start.1 = (bf16[128,512]{1,0:T(8,128)(2,1)}, bf16[128,512]{1,0:T(8,128)(2,1)S(1)}, u32[]{:S(2)}) copy-start(bf16[128,512]{1,0:T(8,128)(2,1)S(1)} %select_bitcast_fusion.rest_0_) | copy-start | bytes 393220
  3.0 9.6 %collective-permute-start.3 = (bf16[128,512]{1,0:T(8,128)(2,1)S(1)}, bf16[128,512]{1,0:T(8,128)(2,1)S(1)}, u32[]{:S(2)}, u32[]{:S(2)}) collective-permute-start(bf16[128,512]{1,0:T(8,128)(2,1)S(1)} %select_bitcast_fusion.rest_0_), channel_id=1, source_target_pairs={{0,24},{4,28},{8,16},{12,20},{16,8},{20,12},{24,0},{28,4},{1,25},{... | collective-permute-start | bytes 393224 | tf_op jit(solution)/shard_map/ppermute | solution.py:28
  8.1 7.5 %collective-permute-start = (bf16[128,512]{1,0:T(8,128)(2,1)S(1)}, bf16[128,512]{1,0:T(8,128)(2,1)S(1)}, u32[]{:S(2)}, u32[]{:S(2)}) collective-permute-start(bf16[128,512]{1,0:T(8,128)(2,1)S(1)} %select_bitcast_fusion.rest_0_), channel_id=1, source_target_pairs={{0,4},{4,0},{8,12},{12,8},{16,20},{20,16},{24,28},{28,24},{1,5},{5... | collective-permute-start | bytes 393224 | tf_op jit(solution)/shard_map/ppermute | solution.py:28
  9.6 9.4 %collective-permute-start.1 = (bf16[128,512]{1,0:T(8,128)(2,1)S(1)}, bf16[128,512]{1,0:T(8,128)(2,1)S(1)}, u32[]{:S(2)}, u32[]{:S(2)}) collective-permute-start(bf16[128,512]{1,0:T(8,128)(2,1)S(1)} %select_bitcast_fusion.rest_0_), channel_id=1, source_target_pairs={{0,8},{4,12},{8,0},{12,4},{16,24},{20,28},{24,16},{28,20},{1,9},{5... | collective-permute-start | bytes 393224 | tf_op jit(solution)/shard_map/ppermute | solution.py:28
  9.6 9.4 %collective-permute-start.2 = (bf16[128,512]{1,0:T(8,128)(2,1)S(1)}, bf16[128,512]{1,0:T(8,128)(2,1)S(1)}, u32[]{:S(2)}, u32[]{:S(2)}) collective-permute-start(bf16[128,512]{1,0:T(8,128)(2,1)S(1)} %select_bitcast_fusion.rest_0_), channel_id=1, source_target_pairs={{0,12},{4,8},{8,4},{12,0},{16,28},{20,24},{24,20},{28,16},{1,13},{... | collective-permute-start | bytes 393224 | tf_op jit(solution)/shard_map/ppermute | solution.py:28
  12.6 11.4 %copy-start.4 = (bf16[128,512]{1,0:T(8,128)(2,1)}, bf16[128,512]{1,0:T(8,128)(2,1)S(1)}, u32[]{:S(2)}) copy-start(bf16[128,512]{1,0:T(8,128)(2,1)S(1)} %collective-permute-done.3.rest_4_) | copy-start | bytes 393220
  12.6 7.1 %collective-permute-start.4 = (bf16[128,512]{1,0:T(8,128)(2,1)S(1)}, bf16[128,512]{1,0:T(8,128)(2,1)S(1)}, u32[]{:S(2)}, u32[]{:S(2)}) collective-permute-start(bf16[128,512]{1,0:T(8,128)(2,1)S(1)} %collective-permute-done.3.rest_4_), channel_id=1, source_target_pairs={{0,4},{4,0},{8,12},{12,8},{16,20},{20,16},{24,28},{28,24},{1,5},{5... | collective-permute-start | bytes 393224 | tf_op jit(solution)/shard_map/ppermute | solution.py:28
  14.2 7.4 %collective-permute-start.5 = (bf16[128,512]{1,0:T(8,128)(2,1)S(1)}, bf16[128,512]{1,0:T(8,128)(2,1)S(1)}, u32[]{:S(2)}, u32[]{:S(2)}) collective-permute-start(bf16[128,512]{1,0:T(8,128)(2,1)S(1)} %collective-permute-done.3.rest_4_), channel_id=1, source_target_pairs={{0,8},{4,12},{8,0},{12,4},{16,24},{20,28},{24,16},{28,20},{1,9},{5... | collective-permute-start | bytes 393224 | tf_op jit(solution)/shard_map/ppermute | solution.py:28
  15.7 8.3 %copy-start.5 = (bf16[128,512]{1,0:T(8,128)(2,1)}, bf16[128,512]{1,0:T(8,128)(2,1)S(1)}, u32[]{:S(2)}) copy-start(bf16[128,512]{1,0:T(8,128)(2,1)S(1)} %collective-permute-done.rest_1_) | copy-start | bytes 393220
  15.7 8.3 %collective-permute-start.6 = (bf16[128,512]{1,0:T(8,128)(2,1)S(1)}, bf16[128,512]{1,0:T(8,128)(2,1)S(1)}, u32[]{:S(2)}, u32[]{:S(2)}) collective-permute-start(bf16[128,512]{1,0:T(8,128)(2,1)S(1)} %collective-permute-done.3.rest_4_), channel_id=1, source_target_pairs={{0,12},{4,8},{8,4},{12,0},{16,28},{20,24},{24,20},{28,16},{1,13},{... | collective-permute-start | bytes 393224 | tf_op jit(solution)/shard_map/ppermute | solution.py:28
  19.1 4.9 %copy-start.7 = (bf16[128,512]{1,0:T(8,128)(2,1)}, bf16[128,512]{1,0:T(8,128)(2,1)S(1)}, u32[]{:S(2)}) copy-start(bf16[128,512]{1,0:T(8,128)(2,1)S(1)} %collective-permute-done.2.rest_3_) | copy-start | bytes 393220
  28.4 1.7 %collective-permute-start.7 = (bf16[256,512]{1,0:T(8,128)(2,1)}, bf16[256,512]{1,0:T(8,128)(2,1)S(1)}, u32[]{:S(2)}, u32[]{:S(2)}) collective-permute-start(bf16[256,512]{1,0:T(8,128)(2,1)} %bitcast.39), channel_id=1, source_target_pairs={{0,1},{1,0},{2,3},{3,2},{4,5},{5,4},{6,7},{7,6},{8,9},{9,8},{10,11... | collective-permute-start | bytes 786440 | tf_op jit(solution)/shard_map/ppermute | solution.py:28
  28.4 8.9 %collective-permute-start.8 = (bf16[256,512]{1,0:T(8,128)(2,1)}, bf16[256,512]{1,0:T(8,128)(2,1)S(1)}, u32[]{:S(2)}, u32[]{:S(2)}) collective-permute-start(bf16[256,512]{1,0:T(8,128)(2,1)} %bitcast.40), channel_id=1, source_target_pairs={{0,2},{1,3},{2,0},{3,1},{4,6},{5,7},{6,4},{7,5},{8,10},{9,11},{10,... | collective-permute-start | bytes 786440 | tf_op jit(solution)/shard_map/ppermute | solution.py:28
  35.6 8.6 %collective-permute-start.11 = (bf16[256,512]{1,0:T(8,128)(2,1)}, bf16[256,512]{1,0:T(8,128)(2,1)S(1)}, u32[]{:S(2)}, u32[]{:S(2)}) collective-permute-start(bf16[256,512]{1,0:T(8,128)(2,1)} %bitcast.42), channel_id=1, source_target_pairs={{0,2},{1,3},{2,0},{3,1},{4,6},{5,7},{6,4},{7,5},{8,10},{9,11},{10,... | collective-permute-start | bytes 786440 | tf_op jit(solution)/shard_map/ppermute | solution.py:28
  37.0 7.8 %copy-start.2 = (bf16[2,128,512]{2,1,0:T(8,128)(2,1)S(1)}, bf16[2,128,512]{2,1,0:T(8,128)(2,1)}, u32[]{:S(2)}) copy-start(bf16[2,128,512]{2,1,0:T(8,128)(2,1)} %shard_map.110) | copy-start | bytes 786436
  37.0 7.5 %collective-permute-start.10 = (bf16[256,512]{1,0:T(8,128)(2,1)}, bf16[256,512]{1,0:T(8,128)(2,1)S(1)}, u32[]{:S(2)}, u32[]{:S(2)}) collective-permute-start(bf16[256,512]{1,0:T(8,128)(2,1)} %bitcast.43), channel_id=1, source_target_pairs={{0,1},{1,0},{2,3},{3,2},{4,5},{5,4},{6,7},{7,6},{8,9},{9,8},{10,11... | collective-permute-start | bytes 786440 | tf_op jit(solution)/shard_map/ppermute | solution.py:28
  37.3 7.9 %collective-permute-start.9 = (bf16[256,512]{1,0:T(8,128)(2,1)S(1)}, bf16[256,512]{1,0:T(8,128)(2,1)S(1)}, u32[]{:S(2)}, u32[]{:S(2)}) collective-permute-start(bf16[256,512]{1,0:T(8,128)(2,1)S(1)} %collective-permute-done.8), channel_id=1, source_target_pairs={{0,1},{1,0},{2,3},{3,2},{4,5},{5,4},{6,7},{7,6},{8,9},{9,8},{10,11... | collective-permute-start | bytes 786440 | tf_op jit(solution)/shard_map/ppermute | solution.py:28
  44.1 1.5 %collective-permute-start.12 = (bf16[256,512]{1,0:T(8,128)(2,1)S(1)}, bf16[256,512]{1,0:T(8,128)(2,1)S(1)}, u32[]{:S(2)}, u32[]{:S(2)}) collective-permute-start(bf16[256,512]{1,0:T(8,128)(2,1)S(1)} %collective-permute-done.11), channel_id=1, source_target_pairs={{0,1},{1,0},{2,3},{3,2},{4,5},{5,4},{6,7},{7,6},{8,9},{9,8},{10,11... | collective-permute-start | bytes 786440 | tf_op jit(solution)/shard_map/ppermute | solution.py:28
  45.6 5.0 %copy-start.3 = (bf16[4,128,576]{1,2,0:T(8,128)(2,1)S(1)}, bf16[4,128,576]{1,2,0:T(8,128)(2,1)}, u32[]{:S(2)}) copy-start(bf16[4,128,576]{1,2,0:T(8,128)(2,1)} %param.11) | copy-start | bytes 1769476
  45.6 4.9 %copy-start.11 = (f32[576]{0:T(1024)S(1)}, f32[576]{0:T(1024)}, u32[]{:S(2)}) copy-start(f32[576]{0:T(1024)} %param.19) | copy-start | bytes 6916
  46.3 3.1 %collective-permute-start.13 = (f32[4,128]{1,0:T(4,128)S(1)}, f32[4,128]{1,0:T(4,128)S(1)}, u32[]{:S(2)}, u32[]{:S(2)}) collective-permute-start(f32[4,128]{1,0:T(4,128)S(1)} %bitcast.45), channel_id=1, source_target_pairs={{0,1},{1,2},{2,3},{3,0},{4,5},{5,6},{6,7},{7,4},{8,9},{9,10},{10,1... | collective-permute-start | bytes 6152 | tf_op jit(solution)/shard_map/ppermute | solution.py:24
  46.8 3.6 %collective-permute-start.14 = (f32[4,128]{1,0:T(4,128)S(1)}, f32[4,128]{1,0:T(4,128)S(1)}, u32[]{:S(2)}, u32[]{:S(2)}) collective-permute-start(f32[4,128]{1,0:T(4,128)S(1)} %bitcast.46), channel_id=1, source_target_pairs={{0,2},{1,3},{2,0},{3,1},{4,6},{5,7},{6,4},{7,5},{8,10},{9,11},{10,... | collective-permute-start | bytes 6152 | tf_op jit(solution)/shard_map/ppermute | solution.py:24
  48.2 2.3 %collective-permute-start.15 = (f32[4,128]{1,0:T(4,128)S(1)}, f32[4,128]{1,0:T(4,128)S(1)}, u32[]{:S(2)}, u32[]{:S(2)}) collective-permute-start(f32[4,128]{1,0:T(4,128)S(1)} %bitcast.47), channel_id=1, source_target_pairs={{0,3},{1,0},{2,1},{3,2},{4,7},{5,4},{6,5},{7,6},{8,11},{9,8},{10,9... | collective-permute-start | bytes 6152 | tf_op jit(solution)/shard_map/ppermute | solution.py:24
  (4 other events, 12.2 us)

commit v19 on v16

--- a/solution.py
+++ b/solution.py
@@ -70,30 +70,41 @@
 
 
 def attention_kernel(limit_ref, flag_ref, qkv_ref, cos_ref, sin_ref, *rest):
-    page_refs, out_ref = rest[:-1], rest[-1]
+    page_count = (len(rest) - 3)
+    page_refs, out_ref, page_scratch, page_sems = rest[:page_count], rest[page_count], rest[-2], rest[-1]
+    copies = [pltpu.make_async_copy(ref, page_scratch.at[index], page_sems.at[index])
+              for index, ref in enumerate(page_refs)]
+    for copy in copies:
+        copy.start()
     count, slots = qkv_ref.shape[0], qkv_ref.shape[1]
     per_group = qkv_ref.shape[2] // HD - 2
     half = HD // 2
     cosine = cos_ref[...]
     sine = sin_ref[...]
-    pages = [ref[...] for ref in page_refs]
+    def rope(part):
+        first = part[:, :half]
+        second = part[:, half:]
+        return jnp.concatenate([first * cosine - second * sine, second * cosine + first * sine], -1)
+
+    ropes = []
+    for request in range(count):
+        values_in = qkv_ref[request].astype(jnp.float32)
+        ropes.append((
+            jnp.concatenate(
+                [(rope(values_in[:, q * HD:(q + 1) * HD]) * HD ** (-0.5)).astype(jnp.bfloat16)
+                 for q in range(per_group)], 0),
+            rope(values_in[:, per_group * HD:(per_group + 1) * HD]).astype(jnp.bfloat16),
+            values_in[:, (per_group + 1) * HD:].astype(jnp.bfloat16)))
+    for copy in copies:
+        copy.wait()
+    pages = [page_scratch[index] for index in range(page_count)]
     prefix_keys = [page[:, :HD] for page in pages]
     prefix_values = [page[:, HD:] for page in pages]
     prefix_len = len(pages) * pages[0].shape[0]
     flag = flag_ref[...]
 
-    def rope(part):
-        first = part[:, :half]
-        second = part[:, half:]
-        return jnp.concatenate([first * cosine - second * sine, second * cosine + first * sine], -1)
-
     for request in range(count):
-        values_in = qkv_ref[request].astype(jnp.float32)
-        queries = jnp.concatenate(
-            [(rope(values_in[:, q * HD:(q + 1) * HD]) * HD ** (-0.5)).astype(jnp.bfloat16)
-             for q in range(per_group)], 0)
-        fresh_keys = rope(values_in[:, per_group * HD:(per_group + 1) * HD]).astype(jnp.bfloat16)
-        fresh_values = values_in[:, (per_group + 1) * HD:].astype(jnp.bfloat16)
+        queries, fresh_keys, fresh_values = ropes[request]
         keys = jnp.concatenate(prefix_keys + [fresh_keys], 0)
         values = jnp.concatenate(prefix_values + [fresh_values], 0)
         key_count = keys.shape[0]
@@ -134,8 +145,10 @@
                   full((1, key_count)),
                   pl.BlockSpec((count, slots, width), lambda r: (chunk, 0, 0)),
                   full(cosine.shape), full(sine.shape)]
-                 + [full((page_len, page_width)) for _ in blocks],
+                 + [pl.BlockSpec(memory_space=pl.ANY) for _ in blocks],
         out_specs=pl.BlockSpec((count, slots, per_group * HD), lambda r: (0, 0, 0)),
+        scratch_shapes=[pltpu.VMEM((len(blocks), page_len, page_width), jnp.bfloat16),
+                        pltpu.SemaphoreType.DMA((len(blocks),))],
         out_shape=jax.ShapeDtypeStruct((count, slots, per_group * HD), jnp.bfloat16),
     )(limits, flags, qkv, cosine, sine, *blocks)
 

time: 51.3 us -> 52.5 us (1.023)
  Pallas kernels: 7.54 us -> 9.23 us
  waiting for transfers between devices: 13.3 us -> 12.7 us
    pallas_call x2, Pallas kernels: 7.54 us -> 9.23 us  [attend(): pl.pallas_call(attention_kernel, grid=(1,), in_specs=[pl.BlockSpec((count...]
    ppermute x13, waiting for transfers between devices: 12 us -> 11.3 us  [swapped(): return lax.ppermute(value, axis, [(i, i ^ mask) for i in range(size)])]
  transfers between devices with their start and end apart: 16 -> 16, of which waited for: 7 -> 7; matrix products, arithmetic and copies ran while one was open for 13% -> 12% of each run, Pallas kernels for 7% -> 9%
where the time goes in v19:
time: 52.5 us; the launch traced here: 51.9 us
  starting transfers between devices  17.6 us (34%)
  waiting for transfers between devices  12.7 us (24%)
  Pallas kernels  9.23 us (18%)
  other arithmetic  5.64 us (11%)
  local copies, waits for them, and re-layouts  3.03 us (6%)
  matrix products  2.8 us (5%)
  between operations  0.95 us (2%)
    ppermute x13, starting transfers between devices, swapped(): return lax.ppermute(value, axis, [(i, i ^ mask) for i in range(size)])  14.9 us
    ppermute x13, waiting for transfers between devices, swapped(): return lax.ppermute(value, axis, [(i, i ^ mask) for i in range(size)])  11.3 us
    pallas_call x2, Pallas kernels, attend(): pl.pallas_call(attention_kernel, grid=(1,), in_specs=[pl.BlockSpec((count...  9.23 us
    dot_general x8, matrix products, project(): term = jnp.dot(block, rows, preferred_element_type=jnp.float32)  2.8 us
    ppermute x3, starting transfers between devices, shifted(): lax.ppermute(value, axis, [(i, (i + shift) % size) for i in range(size)])  2.71 us
    reduce_sum x1, other arithmetic, gather_prefix(): slot = jnp.sum(jnp.where(mine, page_slot, 0))  1.54 us
    ppermute x3, waiting for transfers between devices, shifted(): lax.ppermute(value, axis, [(i, (i + shift) % size) for i in range(size)])  1.33 us
    convert_element_type x1, other arithmetic, on_device(): return ((source + branch) * live_mask[..., None]).astype(jnp.bfloat16)  1.1 us
  transfers between devices with their start and end apart: 16, of which 7 were waited for; matrix products, arithmetic and copies ran while one was open for 12% of the time, Pallas kernels for 9%

profile of v19, /device:TPU:0, one launch (start us, length us, event | category | flops | bytes accessed | tf_op | source)
XLA Modules:
  0.0 51.9 jit_solution(7067786113003744521)
XLA Ops:
  0.0 1.5 %fusion.28 = s32[]{:T(128)} fusion(s32[8]{0:T(128)} %param.15, s32[8]{0:T(128)} %param.14, s32[]{:T(128)} %axis_index.27), kind=kLoop, calls=%fused_computation.43 | loop fusion | flops 23 | bytes 72 | tf_op jit(solution)/shard_map/reduce_sum | solution.py:36
  2.2 1.0 %select_bitcast_fusion.rest_0_ = bf16[128,512]{1,0:T(8,128)(2,1)S(1)} fusion(bf16[2,128,1,512]{3,1,2,0:T(8,128)(2,1)} %param.13, pred[]{:T(512)S(6)} %eq.43), kind=kLoop, calls=%fused_computation.26 | loop fusion | flops 65536 | bytes 393217 | tf_op jit(solution)/shard_map/jit(_where)/select_n | solution.py:39
  3.2 5.1 %collective-permute-start.3 = (bf16[128,512]{1,0:T(8,128)(2,1)S(1)}, bf16[128,512]{1,0:T(8,128)(2,1)S(1)}, u32[]{:S(2)}, u32[]{:S(2)}) collective-permute-start(bf16[128,512]{1,0:T(8,128)(2,1)S(1)} %select_bitcast_fusion.rest_0_), channel_id=1, source_target_pairs={{0,24},{4,28},{8,16},{12,20},{16,8},{20,12},{24,0},{28,4},{1,25},{... | collective-permute-start | bytes 393224 | tf_op jit(solution)/shard_map/ppermute | solution.py:28
  8.4 1.5 %collective-permute-start = (bf16[128,512]{1,0:T(8,128)(2,1)S(1)}, bf16[128,512]{1,0:T(8,128)(2,1)S(1)}, u32[]{:S(2)}, u32[]{:S(2)}) collective-permute-start(bf16[128,512]{1,0:T(8,128)(2,1)S(1)} %select_bitcast_fusion.rest_0_), channel_id=1, source_target_pairs={{0,4},{4,0},{8,12},{12,8},{16,20},{20,16},{24,28},{28,24},{1,5},{5... | collective-permute-start | bytes 393224 | tf_op jit(solution)/shard_map/ppermute | solution.py:28
  9.9 2.0 %collective-permute-start.2 = (bf16[128,512]{1,0:T(8,128)(2,1)S(1)}, bf16[128,512]{1,0:T(8,128)(2,1)S(1)}, u32[]{:S(2)}, u32[]{:S(2)}) collective-permute-start(bf16[128,512]{1,0:T(8,128)(2,1)S(1)} %select_bitcast_fusion.rest_0_), channel_id=1, source_target_pairs={{0,12},{4,8},{8,4},{12,0},{16,28},{20,24},{24,20},{28,16},{1,13},{... | collective-permute-start | bytes 393224 | tf_op jit(solution)/shard_map/ppermute | solution.py:28
  11.9 0.8 %compare_reduce_fusion = pred[8]{0:T(512)(128)(4,1)S(1)} fusion(s32[8]{0:T(128)} %param.14, s32[8]{0:T(128)S(1)} %stack.35), kind=kLoop, calls=%fused_computation.27 | loop fusion | flops 120 | bytes 72 | tf_op jit(solution)/shard_map/reduce_or | solution.py:55
  12.8 1.7 %collective-permute-start.4 = (bf16[128,512]{1,0:T(8,128)(2,1)S(1)}, bf16[128,512]{1,0:T(8,128)(2,1)S(1)}, u32[]{:S(2)}, u32[]{:S(2)}) collective-permute-start(bf16[128,512]{1,0:T(8,128)(2,1)S(1)} %collective-permute-done.3.rest_4_), channel_id=1, source_target_pairs={{0,4},{4,0},{8,12},{12,8},{16,20},{20,16},{24,28},{28,24},{1,5},{5... | collective-permute-start | bytes 393224 | tf_op jit(solution)/shard_map/ppermute | solution.py:28
  14.5 1.5 %collective-permute-start.5 = (bf16[128,512]{1,0:T(8,128)(2,1)S(1)}, bf16[128,512]{1,0:T(8,128)(2,1)S(1)}, u32[]{:S(2)}, u32[]{:S(2)}) collective-permute-start(bf16[128,512]{1,0:T(8,128)(2,1)S(1)} %collective-permute-done.3.rest_4_), channel_id=1, source_target_pairs={{0,8},{4,12},{8,0},{12,4},{16,24},{20,28},{24,16},{28,20},{1,9},{5... | collective-permute-start | bytes 393224 | tf_op jit(solution)/shard_map/ppermute | solution.py:28
  16.4 0.6 %broadcast_in_dim.29.flag_ref = f32[1,1152]{1,0:T(1,128)} reshape(f32[1152]{0:T(1024)S(1)} %concatenate.12) | data formatting | bytes 9216 | tf_op jit(solution)/shard_map/broadcast_in_dim | solution.py:134
  17.0 0.7 %dynamic_slice.19 = s32[4]{0:T(128)S(1)} dynamic-slice(s32[32]{0:T(128)} %param.17, s32[]{:T(128)S(6)} %select_n.37), dynamic_slice_sizes={4} | dynamic-slice | bytes 36 | tf_op jit(solution)/shard_map/dynamic_slice | solution.py:185
  17.8 0.8 %select_reduce_fusion = s32[4]{0:T(128)S(1)} fusion(s32[32]{0:T(128)} %param.16, s32[4]{0:T(128)S(1)} %dynamic_slice.19), kind=kLoop, calls=%fused_computation.31 | loop fusion | flops 380 | bytes 160 | tf_op jit(solution)/shard_map/reduce_sum | solution.py:187
  18.7 0.6 %broadcast_in_dim.27.limit_ref = s32[4,1,1152]{2,1,0:T(1,128)} reshape(s32[4,1152]{1,0:T(4,128)S(1)} %concatenate.11) | data formatting | bytes 36864 | tf_op jit(solution)/shard_map/broadcast_in_dim | solution.py:138
  19.3 0.6 %collective-permute-done.4.rest_5_ = bf16[128,512]{1,0:T(8,128)(2,1)S(1)} collective-permute-done((bf16[128,512]{1,0:T(8,128)(2,1)S(1)}, bf16[128,512]{1,0:T(8,128)(2,1)S(1)}, u32[]{:S(2)}, u32[]{:S(2)}) %collective-permute-start.4) | collective-permute-done | bytes 131104 | tf_op jit(solution)/shard_map/ppermute | solution.py:28
  19.9 1.9 %collective-permute-done.5.rest_6_ = bf16[128,512]{1,0:T(8,128)(2,1)S(1)} collective-permute-done((bf16[128,512]{1,0:T(8,128)(2,1)S(1)}, bf16[128,512]{1,0:T(8,128)(2,1)S(1)}, u32[]{:S(2)}, u32[]{:S(2)}) %collective-permute-start.5) | collective-permute-done | bytes 131104 | tf_op jit(solution)/shard_map/ppermute | solution.py:28
  21.9 2.3 %collective-permute-done.6.rest_7_ = bf16[128,512]{1,0:T(8,128)(2,1)S(1)} collective-permute-done((bf16[128,512]{1,0:T(8,128)(2,1)S(1)}, bf16[128,512]{1,0:T(8,128)(2,1)S(1)}, u32[]{:S(2)}, u32[]{:S(2)}) %collective-permute-start.6) | collective-permute-done | bytes 131104 | tf_op jit(solution)/shard_map/ppermute | solution.py:28
  24.8 4.6 %shard_map.109 = bf16[2,128,512]{2,1,0:T(8,128)(2,1)} custom-call(s32[4,1,1152]{2,1,0:T(1,128)} %broadcast_in_dim.27.limit_ref, f32[1,1152]{1,0:T(1,128)} %broadcast_in_dim.29.flag_ref, bf16[4,128,1024]{2,1,0:T(8,128)(2,1)} %bitcast.37, f32[128,128]{1,0:T(8,128)} %constant.44.clone.cos_ref, f32[128,128]{1,0:T(8,128)} %constant.45.clone.sin_ref, ...), custom_call_target="tpu_custom_call" | custom-call | tf_op jit(solution)/shard_map/pallas_call | solution.py:141
  29.5 1.5 %collective-permute-start.8 = (bf16[256,512]{1,0:T(8,128)(2,1)}, bf16[256,512]{1,0:T(8,128)(2,1)S(1)}, u32[]{:S(2)}, u32[]{:S(2)}) collective-permute-start(bf16[256,512]{1,0:T(8,128)(2,1)} %bitcast.42), channel_id=1, source_target_pairs={{0,2},{1,3},{2,0},{3,1},{4,6},{5,7},{6,4},{7,5},{8,10},{9,11},{10,... | collective-permute-start | bytes 786440 | tf_op jit(solution)/shard_map/ppermute | solution.py:28
  31.0 4.6 %shard_map.110 = bf16[2,128,512]{2,1,0:T(8,128)(2,1)} custom-call(s32[4,1,1152]{2,1,0:T(1,128)} %broadcast_in_dim.27.limit_ref, f32[1,1152]{1,0:T(1,128)} %broadcast_in_dim.29.flag_ref, bf16[4,128,1024]{2,1,0:T(8,128)(2,1)} %bitcast.38, f32[128,128]{1,0:T(8,128)} %constant.44.clone.cos_ref, f32[128,128]{1,0:T(8,128)} %constant.45.clone.sin_ref, ...), custom_call_target="tpu_custom_call" | custom-call | tf_op jit(solution)/shard_map/pallas_call | solution.py:141
  35.6 0.6 %collective-permute-start.11 = (bf16[256,512]{1,0:T(8,128)(2,1)}, bf16[256,512]{1,0:T(8,128)(2,1)S(1)}, u32[]{:S(2)}, u32[]{:S(2)}) collective-permute-start(bf16[256,512]{1,0:T(8,128)(2,1)} %bitcast.39), channel_id=1, source_target_pairs={{0,2},{1,3},{2,0},{3,1},{4,6},{5,7},{6,4},{7,5},{8,10},{9,11},{10,... | collective-permute-start | bytes 786440 | tf_op jit(solution)/shard_map/ppermute | solution.py:28
  37.4 5.8 %collective-permute-done.11 = bf16[256,512]{1,0:T(8,128)(2,1)S(1)} collective-permute-done((bf16[256,512]{1,0:T(8,128)(2,1)}, bf16[256,512]{1,0:T(8,128)(2,1)S(1)}, u32[]{:S(2)}, u32[]{:S(2)}) %collective-permute-start.11) | collective-permute-done | bytes 262176 | tf_op jit(solution)/shard_map/ppermute | solution.py:28
  47.2 1.2 %collective-permute-start.14 = (f32[4,128]{1,0:T(4,128)S(1)}, f32[4,128]{1,0:T(4,128)S(1)}, u32[]{:S(2)}, u32[]{:S(2)}) collective-permute-start(f32[4,128]{1,0:T(4,128)S(1)} %bitcast.46), channel_id=1, source_target_pairs={{0,2},{1,3},{2,0},{3,1},{4,6},{5,7},{6,4},{7,5},{8,10},{9,11},{10,... | collective-permute-start | bytes 6152 | tf_op jit(solution)/shard_map/ppermute | solution.py:24
  48.4 1.0 %collective-permute-start.15 = (f32[4,128]{1,0:T(4,128)S(1)}, f32[4,128]{1,0:T(4,128)S(1)}, u32[]{:S(2)}, u32[]{:S(2)}) collective-permute-start(f32[4,128]{1,0:T(4,128)S(1)} %bitcast.47), channel_id=1, source_target_pairs={{0,3},{1,0},{2,1},{3,2},{4,7},{5,4},{6,5},{7,6},{8,11},{9,8},{10,9... | collective-permute-start | bytes 6152 | tf_op jit(solution)/shard_map/ppermute | solution.py:24
  49.7 1.1 %collective-permute-done.14 = f32[4,128]{1,0:T(4,128)S(1)} collective-permute-done((f32[4,128]{1,0:T(4,128)S(1)}, f32[4,128]{1,0:T(4,128)S(1)}, u32[]{:S(2)}, u32[]{:S(2)}) %collective-permute-start.14) | collective-permute-done | bytes 2080 | tf_op jit(solution)/shard_map/ppermute | solution.py:24
  50.8 1.1 %fusion.5 = bf16[4,128,576]{1,2,0:T(8,128)(2,1)} fusion(f32[72,4,8,128]{3,2,1,0:T(8,128)S(1)} %get-tuple-element.6, bf16[4,128,576]{1,2,0:T(8,128)(2,1)S(1)} %copy-done.4, f32[4,128]{1,0:T(4,128)S(1)} %fusion.19, f32[576]{0:T(1024)S(1)} %copy-done.12, f32[4,128]{1,0:T(4,128)S(1)} %add_rsqrt_fusion), kind=kLoop, calls=%fused_computation.10 | loop fusion | flops 1769472 | bytes 2365696 | tf_op jit(solution)/shard_map/convert_element_type | solution.py:209
  (61 shorter events, 6.6 us)
Async XLA Ops:
  0.0 43.2 %copy-start = (bf16[2048,576]{0,1:T(8,128)(2,1)S(1)}, bf16[2048,576]{0,1:T(8,128)(2,1)}, u32[]{:S(2)}) copy-start(bf16[2048,576]{0,1:T(8,128)(2,1)} %param.18) | copy-start | bytes 7077892
  3.2 21.0 %copy-start.1 = (bf16[128,512]{1,0:T(8,128)(2,1)}, bf16[128,512]{1,0:T(8,128)(2,1)S(1)}, u32[]{:S(2)}) copy-start(bf16[128,512]{1,0:T(8,128)(2,1)S(1)} %select_bitcast_fusion.rest_0_) | copy-start | bytes 393220
  3.2 9.6 %collective-permute-start.3 = (bf16[128,512]{1,0:T(8,128)(2,1)S(1)}, bf16[128,512]{1,0:T(8,128)(2,1)S(1)}, u32[]{:S(2)}, u32[]{:S(2)}) collective-permute-start(bf16[128,512]{1,0:T(8,128)(2,1)S(1)} %select_bitcast_fusion.rest_0_), channel_id=1, source_target_pairs={{0,24},{4,28},{8,16},{12,20},{16,8},{20,12},{24,0},{28,4},{1,25},{... | collective-permute-start | bytes 393224 | tf_op jit(solution)/shard_map/ppermute | solution.py:28
  8.4 7.5 %collective-permute-start = (bf16[128,512]{1,0:T(8,128)(2,1)S(1)}, bf16[128,512]{1,0:T(8,128)(2,1)S(1)}, u32[]{:S(2)}, u32[]{:S(2)}) collective-permute-start(bf16[128,512]{1,0:T(8,128)(2,1)S(1)} %select_bitcast_fusion.rest_0_), channel_id=1, source_target_pairs={{0,4},{4,0},{8,12},{12,8},{16,20},{20,16},{24,28},{28,24},{1,5},{5... | collective-permute-start | bytes 393224 | tf_op jit(solution)/shard_map/ppermute | solution.py:28
  9.9 9.4 %collective-permute-start.1 = (bf16[128,512]{1,0:T(8,128)(2,1)S(1)}, bf16[128,512]{1,0:T(8,128)(2,1)S(1)}, u32[]{:S(2)}, u32[]{:S(2)}) collective-permute-start(bf16[128,512]{1,0:T(8,128)(2,1)S(1)} %select_bitcast_fusion.rest_0_), channel_id=1, source_target_pairs={{0,8},{4,12},{8,0},{12,4},{16,24},{20,28},{24,16},{28,20},{1,9},{5... | collective-permute-start | bytes 393224 | tf_op jit(solution)/shard_map/ppermute | solution.py:28
  9.9 9.4 %collective-permute-start.2 = (bf16[128,512]{1,0:T(8,128)(2,1)S(1)}, bf16[128,512]{1,0:T(8,128)(2,1)S(1)}, u32[]{:S(2)}, u32[]{:S(2)}) collective-permute-start(bf16[128,512]{1,0:T(8,128)(2,1)S(1)} %select_bitcast_fusion.rest_0_), channel_id=1, source_target_pairs={{0,12},{4,8},{8,4},{12,0},{16,28},{20,24},{24,20},{28,16},{1,13},{... | collective-permute-start | bytes 393224 | tf_op jit(solution)/shard_map/ppermute | solution.py:28
  12.8 11.4 %copy-start.5 = (bf16[128,512]{1,0:T(8,128)(2,1)}, bf16[128,512]{1,0:T(8,128)(2,1)S(1)}, u32[]{:S(2)}) copy-start(bf16[128,512]{1,0:T(8,128)(2,1)S(1)} %collective-permute-done.3.rest_4_) | copy-start | bytes 393220
  12.8 7.1 %collective-permute-start.4 = (bf16[128,512]{1,0:T(8,128)(2,1)S(1)}, bf16[128,512]{1,0:T(8,128)(2,1)S(1)}, u32[]{:S(2)}, u32[]{:S(2)}) collective-permute-start(bf16[128,512]{1,0:T(8,128)(2,1)S(1)} %collective-permute-done.3.rest_4_), channel_id=1, source_target_pairs={{0,4},{4,0},{8,12},{12,8},{16,20},{20,16},{24,28},{28,24},{1,5},{5... | collective-permute-start | bytes 393224 | tf_op jit(solution)/shard_map/ppermute | solution.py:28
  14.5 7.4 %collective-permute-start.5 = (bf16[128,512]{1,0:T(8,128)(2,1)S(1)}, bf16[128,512]{1,0:T(8,128)(2,1)S(1)}, u32[]{:S(2)}, u32[]{:S(2)}) collective-permute-start(bf16[128,512]{1,0:T(8,128)(2,1)S(1)} %collective-permute-done.3.rest_4_), channel_id=1, source_target_pairs={{0,8},{4,12},{8,0},{12,4},{16,24},{20,28},{24,16},{28,20},{1,9},{5... | collective-permute-start | bytes 393224 | tf_op jit(solution)/shard_map/ppermute | solution.py:28
  15.9 8.3 %copy-start.6 = (bf16[128,512]{1,0:T(8,128)(2,1)}, bf16[128,512]{1,0:T(8,128)(2,1)S(1)}, u32[]{:S(2)}) copy-start(bf16[128,512]{1,0:T(8,128)(2,1)S(1)} %collective-permute-done.rest_1_) | copy-start | bytes 393220
  15.9 8.3 %collective-permute-start.6 = (bf16[128,512]{1,0:T(8,128)(2,1)S(1)}, bf16[128,512]{1,0:T(8,128)(2,1)S(1)}, u32[]{:S(2)}, u32[]{:S(2)}) collective-permute-start(bf16[128,512]{1,0:T(8,128)(2,1)S(1)} %collective-permute-done.3.rest_4_), channel_id=1, source_target_pairs={{0,12},{4,8},{8,4},{12,0},{16,28},{20,24},{24,20},{28,16},{1,13},{... | collective-permute-start | bytes 393224 | tf_op jit(solution)/shard_map/ppermute | solution.py:28
  19.3 4.9 %copy-start.7 = (bf16[128,512]{1,0:T(8,128)(2,1)}, bf16[128,512]{1,0:T(8,128)(2,1)S(1)}, u32[]{:S(2)}) copy-start(bf16[128,512]{1,0:T(8,128)(2,1)S(1)} %collective-permute-done.1.rest_2_) | copy-start | bytes 393220
  19.3 4.9 %copy-start.8 = (bf16[128,512]{1,0:T(8,128)(2,1)}, bf16[128,512]{1,0:T(8,128)(2,1)S(1)}, u32[]{:S(2)}) copy-start(bf16[128,512]{1,0:T(8,128)(2,1)S(1)} %collective-permute-done.2.rest_3_) | copy-start | bytes 393220
  29.5 6.8 %copy-start.3 = (bf16[2,128,512]{2,1,0:T(8,128)(2,1)S(1)}, bf16[2,128,512]{2,1,0:T(8,128)(2,1)}, u32[]{:S(2)}) copy-start(bf16[2,128,512]{2,1,0:T(8,128)(2,1)} %shard_map.109) | copy-start | bytes 786436
  29.5 7.9 %collective-permute-start.8 = (bf16[256,512]{1,0:T(8,128)(2,1)}, bf16[256,512]{1,0:T(8,128)(2,1)S(1)}, u32[]{:S(2)}, u32[]{:S(2)}) collective-permute-start(bf16[256,512]{1,0:T(8,128)(2,1)} %bitcast.42), channel_id=1, source_target_pairs={{0,2},{1,3},{2,0},{3,1},{4,6},{5,7},{6,4},{7,5},{8,10},{9,11},{10,... | collective-permute-start | bytes 786440 | tf_op jit(solution)/shard_map/ppermute | solution.py:28
  35.6 7.6 %collective-permute-start.11 = (bf16[256,512]{1,0:T(8,128)(2,1)}, bf16[256,512]{1,0:T(8,128)(2,1)S(1)}, u32[]{:S(2)}, u32[]{:S(2)}) collective-permute-start(bf16[256,512]{1,0:T(8,128)(2,1)} %bitcast.39), channel_id=1, source_target_pairs={{0,2},{1,3},{2,0},{3,1},{4,6},{5,7},{6,4},{7,5},{8,10},{9,11},{10,... | collective-permute-start | bytes 786440 | tf_op jit(solution)/shard_map/ppermute | solution.py:28
  36.3 7.7 %collective-permute-start.7 = (bf16[256,512]{1,0:T(8,128)(2,1)S(1)}, bf16[256,512]{1,0:T(8,128)(2,1)S(1)}, u32[]{:S(2)}, u32[]{:S(2)}) collective-permute-start(bf16[256,512]{1,0:T(8,128)(2,1)S(1)} %bitcast.43), channel_id=1, source_target_pairs={{0,1},{1,0},{2,3},{3,2},{4,5},{5,4},{6,7},{7,6},{8,9},{9,8},{10,11... | collective-permute-start | bytes 786440 | tf_op jit(solution)/shard_map/ppermute | solution.py:28
  36.3 8.4 %collective-permute-start.10 = (bf16[256,512]{1,0:T(8,128)(2,1)}, bf16[256,512]{1,0:T(8,128)(2,1)S(1)}, u32[]{:S(2)}, u32[]{:S(2)}) collective-permute-start(bf16[256,512]{1,0:T(8,128)(2,1)} %bitcast.40), channel_id=1, source_target_pairs={{0,1},{1,0},{2,3},{3,2},{4,5},{5,4},{6,7},{7,6},{8,9},{9,8},{10,11... | collective-permute-start | bytes 786440 | tf_op jit(solution)/shard_map/ppermute | solution.py:28
  37.4 8.2 %collective-permute-start.9 = (bf16[256,512]{1,0:T(8,128)(2,1)S(1)}, bf16[256,512]{1,0:T(8,128)(2,1)S(1)}, u32[]{:S(2)}, u32[]{:S(2)}) collective-permute-start(bf16[256,512]{1,0:T(8,128)(2,1)S(1)} %collective-permute-done.8), channel_id=1, source_target_pairs={{0,1},{1,0},{2,3},{3,2},{4,5},{5,4},{6,7},{7,6},{8,9},{9,8},{10,11... | collective-permute-start | bytes 786440 | tf_op jit(solution)/shard_map/ppermute | solution.py:28
  43.2 2.8 %collective-permute-start.12 = (bf16[256,512]{1,0:T(8,128)(2,1)S(1)}, bf16[256,512]{1,0:T(8,128)(2,1)S(1)}, u32[]{:S(2)}, u32[]{:S(2)}) collective-permute-start(bf16[256,512]{1,0:T(8,128)(2,1)S(1)} %collective-permute-done.11), channel_id=1, source_target_pairs={{0,1},{1,0},{2,3},{3,2},{4,5},{5,4},{6,7},{7,6},{8,9},{9,8},{10,11... | collective-permute-start | bytes 786440 | tf_op jit(solution)/shard_map/ppermute | solution.py:28
  46.0 4.8 %copy-start.4 = (bf16[4,128,576]{1,2,0:T(8,128)(2,1)S(1)}, bf16[4,128,576]{1,2,0:T(8,128)(2,1)}, u32[]{:S(2)}) copy-start(bf16[4,128,576]{1,2,0:T(8,128)(2,1)} %param.11) | copy-start | bytes 1769476
  46.6 3.1 %collective-permute-start.13 = (f32[4,128]{1,0:T(4,128)S(1)}, f32[4,128]{1,0:T(4,128)S(1)}, u32[]{:S(2)}, u32[]{:S(2)}) collective-permute-start(f32[4,128]{1,0:T(4,128)S(1)} %bitcast.45), channel_id=1, source_target_pairs={{0,1},{1,2},{2,3},{3,0},{4,5},{5,6},{6,7},{7,4},{8,9},{9,10},{10,1... | collective-permute-start | bytes 6152 | tf_op jit(solution)/shard_map/ppermute | solution.py:24
  47.2 3.6 %collective-permute-start.14 = (f32[4,128]{1,0:T(4,128)S(1)}, f32[4,128]{1,0:T(4,128)S(1)}, u32[]{:S(2)}, u32[]{:S(2)}) collective-permute-start(f32[4,128]{1,0:T(4,128)S(1)} %bitcast.46), channel_id=1, source_target_pairs={{0,2},{1,3},{2,0},{3,1},{4,6},{5,7},{6,4},{7,5},{8,10},{9,11},{10,... | collective-permute-start | bytes 6152 | tf_op jit(solution)/shard_map/ppermute | solution.py:24
  48.4 2.4 %collective-permute-start.15 = (f32[4,128]{1,0:T(4,128)S(1)}, f32[4,128]{1,0:T(4,128)S(1)}, u32[]{:S(2)}, u32[]{:S(2)}) collective-permute-start(f32[4,128]{1,0:T(4,128)S(1)} %bitcast.47), channel_id=1, source_target_pairs={{0,3},{1,0},{2,1},{3,2},{4,7},{5,4},{6,5},{7,6},{8,11},{9,8},{10,9... | collective-permute-start | bytes 6152 | tf_op jit(solution)/shard_map/ppermute | solution.py:24
  (5 other events, 13.0 us)

commit v20 on v16

--- a/solution.py
+++ b/solution.py
@@ -188,9 +188,13 @@
     projected = jnp.concatenate(projected_parts, 0).reshape(requests, slots, local_width)
 
     squares = jnp.sum(projected * projected, -1)
-    branch_total = squares
-    for shift in range(1, n_tp):
-        branch_total = branch_total + shifted(squares, "tp", n_tp, shift)
+    if n_tp == 4:
+        branch_total = squares + swapped(squares, "tp", n_tp, 2)
+        branch_total = branch_total + swapped(branch_total, "tp", n_tp, 1)
+    else:
+        branch_total = squares
+        for shift in range(1, n_tp):
+            branch_total = branch_total + shifted(squares, "tp", n_tp, shift)
     branch = projected * lax.rsqrt(branch_total / D + EPSILON)[..., None] * post_gain
     source = hidden.astype(jnp.float32)
     return ((source + branch) * live_mask[..., None]).astype(jnp.bfloat16)

time: 51.3 us -> 51.4 us (level)
  waiting for transfers between devices: 13.3 us -> 15.2 us
  starting transfers between devices: 17.7 us -> 16.2 us
    ppermute x13 -> x15, waiting for transfers between devices: 12 us -> 15.2 us  [swapped(): return lax.ppermute(value, axis, [(i, i ^ mask) for i in range(size)])]
    ppermute x3 -> x0, starting transfers between devices: 2.96 us -> none  [shifted(): lax.ppermute(value, axis, [(i, (i + shift) % size) for i in range(size)])]
    ppermute x13 -> x15, starting transfers between devices: 14.7 us -> 16.2 us  [swapped(): return lax.ppermute(value, axis, [(i, i ^ mask) for i in range(size)])]
    ppermute x3 -> x0, waiting for transfers between devices: 1.24 us -> none  [shifted(): lax.ppermute(value, axis, [(i, (i + shift) % size) for i in range(size)])]
  transfers between devices with their start and end apart: 16 -> 15, of which waited for: 7 -> 7; matrix products, arithmetic and copies ran while one was open for 13% -> 12% of each run, Pallas kernels for 7% -> 7%
where the time goes in v20:
time: 51.4 us; the launch traced here: 51.1 us
  starting transfers between devices  16.2 us (32%)
  waiting for transfers between devices  15.2 us (30%)
  Pallas kernels  7.52 us (15%)
  other arithmetic  5.54 us (11%)
  local copies, waits for them, and re-layouts  3.03 us (6%)
  matrix products  2.78 us (5%)
  between operations  0.78 us (2%)
    ppermute x15, starting transfers between devices, swapped(): return lax.ppermute(value, axis, [(i, i ^ mask) for i in range(size)])  16.2 us
    ppermute x15, waiting for transfers between devices, swapped(): return lax.ppermute(value, axis, [(i, i ^ mask) for i in range(size)])  15.2 us
    pallas_call x2, Pallas kernels, attend(): pl.pallas_call(attention_kernel, grid=(1,), in_specs=[pl.BlockSpec((count...  7.52 us
    dot_general x8, matrix products, project(): term = jnp.dot(block, rows, preferred_element_type=jnp.float32)  2.78 us
    reduce_sum x1, other arithmetic, gather_prefix(): slot = jnp.sum(jnp.where(mine, page_slot, 0))  1.43 us
    convert_element_type x1, other arithmetic, on_device(): return ((source + branch) * live_mask[..., None]).astype(jnp.bfloat16)  1.1 us
  transfers between devices with their start and end apart: 15, of which 7 were waited for; matrix products, arithmetic and copies ran while one was open for 12% of the time, Pallas kernels for 7%

profile of v20, /device:TPU:0, one launch (start us, length us, event | category | flops | bytes accessed | tf_op | source)
XLA Modules:
  0.0 51.1 jit_solution(13214916500654799181)
XLA Ops:
  0.0 1.4 %fusion.28 = s32[]{:T(128)} fusion(s32[8]{0:T(128)} %param.15, s32[8]{0:T(128)} %param.14, s32[]{:T(128)} %axis_index.27), kind=kLoop, calls=%fused_computation.43 | loop fusion | flops 23 | bytes 72 | tf_op jit(solution)/shard_map/reduce_sum | solution.py:36
  2.0 1.0 %select_bitcast_fusion.rest_0_ = bf16[128,512]{1,0:T(8,128)(2,1)S(1)} fusion(bf16[2,128,1,512]{3,1,2,0:T(8,128)(2,1)} %param.13, pred[]{:T(512)S(6)} %eq.43), kind=kLoop, calls=%fused_computation.26 | loop fusion | flops 65536 | bytes 393217 | tf_op jit(solution)/shard_map/jit(_where)/select_n | solution.py:39
  3.0 5.1 %collective-permute-start.3 = (bf16[128,512]{1,0:T(8,128)(2,1)S(1)}, bf16[128,512]{1,0:T(8,128)(2,1)S(1)}, u32[]{:S(2)}, u32[]{:S(2)}) collective-permute-start(bf16[128,512]{1,0:T(8,128)(2,1)S(1)} %select_bitcast_fusion.rest_0_), channel_id=1, source_target_pairs={{0,24},{4,28},{8,16},{12,20},{16,8},{20,12},{24,0},{28,4},{1,25},{... | collective-permute-start | bytes 393224 | tf_op jit(solution)/shard_map/ppermute | solution.py:28
  8.1 1.5 %collective-permute-start = (bf16[128,512]{1,0:T(8,128)(2,1)S(1)}, bf16[128,512]{1,0:T(8,128)(2,1)S(1)}, u32[]{:S(2)}, u32[]{:S(2)}) collective-permute-start(bf16[128,512]{1,0:T(8,128)(2,1)S(1)} %select_bitcast_fusion.rest_0_), channel_id=1, source_target_pairs={{0,4},{4,0},{8,12},{12,8},{16,20},{20,16},{24,28},{28,24},{1,5},{5... | collective-permute-start | bytes 393224 | tf_op jit(solution)/shard_map/ppermute | solution.py:28
  9.6 2.0 %collective-permute-start.2 = (bf16[128,512]{1,0:T(8,128)(2,1)S(1)}, bf16[128,512]{1,0:T(8,128)(2,1)S(1)}, u32[]{:S(2)}, u32[]{:S(2)}) collective-permute-start(bf16[128,512]{1,0:T(8,128)(2,1)S(1)} %select_bitcast_fusion.rest_0_), channel_id=1, source_target_pairs={{0,12},{4,8},{8,4},{12,0},{16,28},{20,24},{24,20},{28,16},{1,13},{... | collective-permute-start | bytes 393224 | tf_op jit(solution)/shard_map/ppermute | solution.py:28
  11.7 0.8 %compare_reduce_fusion = pred[8]{0:T(512)(128)(4,1)S(1)} fusion(s32[8]{0:T(128)} %param.14, s32[8]{0:T(128)S(1)} %stack.35), kind=kLoop, calls=%fused_computation.27 | loop fusion | flops 120 | bytes 72 | tf_op jit(solution)/shard_map/reduce_or | solution.py:55
  12.6 1.7 %collective-permute-start.4 = (bf16[128,512]{1,0:T(8,128)(2,1)S(1)}, bf16[128,512]{1,0:T(8,128)(2,1)S(1)}, u32[]{:S(2)}, u32[]{:S(2)}) collective-permute-start(bf16[128,512]{1,0:T(8,128)(2,1)S(1)} %collective-permute-done.3.rest_4_), channel_id=1, source_target_pairs={{0,4},{4,0},{8,12},{12,8},{16,20},{20,16},{24,28},{28,24},{1,5},{5... | collective-permute-start | bytes 393224 | tf_op jit(solution)/shard_map/ppermute | solution.py:28
  14.2 1.5 %collective-permute-start.5 = (bf16[128,512]{1,0:T(8,128)(2,1)S(1)}, bf16[128,512]{1,0:T(8,128)(2,1)S(1)}, u32[]{:S(2)}, u32[]{:S(2)}) collective-permute-start(bf16[128,512]{1,0:T(8,128)(2,1)S(1)} %collective-permute-done.3.rest_4_), channel_id=1, source_target_pairs={{0,8},{4,12},{8,0},{12,4},{16,24},{20,28},{24,16},{28,20},{1,9},{5... | collective-permute-start | bytes 393224 | tf_op jit(solution)/shard_map/ppermute | solution.py:28
  16.2 0.6 %broadcast_in_dim.29.flag_ref = f32[1,1152]{1,0:T(1,128)} reshape(f32[1152]{0:T(1024)S(1)} %concatenate.12) | data formatting | bytes 9216 | tf_op jit(solution)/shard_map/broadcast_in_dim | solution.py:123
  16.8 0.7 %dynamic_slice.19 = s32[4]{0:T(128)S(1)} dynamic-slice(s32[32]{0:T(128)} %param.17, s32[]{:T(128)S(6)} %select_n.37), dynamic_slice_sizes={4} | dynamic-slice | bytes 36 | tf_op jit(solution)/shard_map/dynamic_slice | solution.py:172
  17.5 0.8 %select_reduce_fusion = s32[4]{0:T(128)S(1)} fusion(s32[32]{0:T(128)} %param.16, s32[4]{0:T(128)S(1)} %dynamic_slice.19), kind=kLoop, calls=%fused_computation.31 | loop fusion | flops 380 | bytes 160 | tf_op jit(solution)/shard_map/reduce_sum | solution.py:174
  18.4 0.6 %broadcast_in_dim.27.limit_ref = s32[4,1,1152]{2,1,0:T(1,128)} reshape(s32[4,1152]{1,0:T(4,128)S(1)} %concatenate.11) | data formatting | bytes 36864 | tf_op jit(solution)/shard_map/broadcast_in_dim | solution.py:127
  19.1 0.6 %collective-permute-done.4.rest_5_ = bf16[128,512]{1,0:T(8,128)(2,1)S(1)} collective-permute-done((bf16[128,512]{1,0:T(8,128)(2,1)S(1)}, bf16[128,512]{1,0:T(8,128)(2,1)S(1)}, u32[]{:S(2)}, u32[]{:S(2)}) %collective-permute-start.4) | collective-permute-done | bytes 131104 | tf_op jit(solution)/shard_map/ppermute | solution.py:28
  19.7 1.9 %collective-permute-done.5.rest_6_ = bf16[128,512]{1,0:T(8,128)(2,1)S(1)} collective-permute-done((bf16[128,512]{1,0:T(8,128)(2,1)S(1)}, bf16[128,512]{1,0:T(8,128)(2,1)S(1)}, u32[]{:S(2)}, u32[]{:S(2)}) %collective-permute-start.5) | collective-permute-done | bytes 131104 | tf_op jit(solution)/shard_map/ppermute | solution.py:28
  21.6 2.3 %collective-permute-done.6.rest_7_ = bf16[128,512]{1,0:T(8,128)(2,1)S(1)} collective-permute-done((bf16[128,512]{1,0:T(8,128)(2,1)S(1)}, bf16[128,512]{1,0:T(8,128)(2,1)S(1)}, u32[]{:S(2)}, u32[]{:S(2)}) %collective-permute-start.6) | collective-permute-done | bytes 131104 | tf_op jit(solution)/shard_map/ppermute | solution.py:28
  24.6 3.8 %shard_map.109 = bf16[2,128,512]{2,1,0:T(8,128)(2,1)} custom-call(s32[4,1,1152]{2,1,0:T(1,128)} %broadcast_in_dim.27.limit_ref, f32[1,1152]{1,0:T(1,128)} %broadcast_in_dim.29.flag_ref, bf16[4,128,1024]{2,1,0:T(8,128)(2,1)} %bitcast.39, f32[128,128]{1,0:T(8,128)} %constant.44.clone.cos_ref, f32[128,128]{1,0:T(8,128)} %constant.45.clone.sin_ref, ...), custom_call_target="tpu_custom_call" | custom-call | tf_op jit(solution)/shard_map/pallas_call | solution.py:130
  28.4 1.4 %collective-permute-start.8 = (bf16[256,512]{1,0:T(8,128)(2,1)}, bf16[256,512]{1,0:T(8,128)(2,1)S(1)}, u32[]{:S(2)}, u32[]{:S(2)}) collective-permute-start(bf16[256,512]{1,0:T(8,128)(2,1)} %bitcast.44), channel_id=1, source_target_pairs={{0,2},{1,3},{2,0},{3,1},{4,6},{5,7},{6,4},{7,5},{8,10},{9,11},{10,... | collective-permute-start | bytes 786440 | tf_op jit(solution)/shard_map/ppermute | solution.py:28
  29.8 3.8 %shard_map.110 = bf16[2,128,512]{2,1,0:T(8,128)(2,1)} custom-call(s32[4,1,1152]{2,1,0:T(1,128)} %broadcast_in_dim.27.limit_ref, f32[1,1152]{1,0:T(1,128)} %broadcast_in_dim.29.flag_ref, bf16[4,128,1024]{2,1,0:T(8,128)(2,1)} %bitcast.40, f32[128,128]{1,0:T(8,128)} %constant.44.clone.cos_ref, f32[128,128]{1,0:T(8,128)} %constant.45.clone.sin_ref, ...), custom_call_target="tpu_custom_call" | custom-call | tf_op jit(solution)/shard_map/pallas_call | solution.py:130
  34.7 2.2 %collective-permute-done.8 = bf16[256,512]{1,0:T(8,128)(2,1)S(1)} collective-permute-done((bf16[256,512]{1,0:T(8,128)(2,1)}, bf16[256,512]{1,0:T(8,128)(2,1)S(1)}, u32[]{:S(2)}, u32[]{:S(2)}) %collective-permute-start.8) | collective-permute-done | bytes 262176 | tf_op jit(solution)/shard_map/ppermute | solution.py:28
  36.9 4.9 %collective-permute-done.11 = bf16[256,512]{1,0:T(8,128)(2,1)S(1)} collective-permute-done((bf16[256,512]{1,0:T(8,128)(2,1)}, bf16[256,512]{1,0:T(8,128)(2,1)S(1)}, u32[]{:S(2)}, u32[]{:S(2)}) %collective-permute-start.11) | collective-permute-done | bytes 262176 | tf_op jit(solution)/shard_map/ppermute | solution.py:28
  45.2 1.5 %collective-permute-start.13 = (f32[4,128]{1,0:T(4,128)S(1)}, f32[4,128]{1,0:T(4,128)S(1)}, u32[]{:S(2)}, u32[]{:S(2)}) collective-permute-start(f32[4,128]{1,0:T(4,128)S(1)} %bitcast.47), channel_id=1, source_target_pairs={{0,2},{1,3},{2,0},{3,1},{4,6},{5,7},{6,4},{7,5},{8,10},{9,11},{10,... | collective-permute-start | bytes 6152 | tf_op jit(solution)/shard_map/ppermute | solution.py:28
  46.7 2.1 %collective-permute-done.13 = f32[4,128]{1,0:T(4,128)S(1)} collective-permute-done((f32[4,128]{1,0:T(4,128)S(1)}, f32[4,128]{1,0:T(4,128)S(1)}, u32[]{:S(2)}, u32[]{:S(2)}) %collective-permute-start.13) | collective-permute-done | bytes 2080 | tf_op jit(solution)/shard_map/ppermute | solution.py:28
  48.9 1.1 %collective-permute-done.14 = f32[4,128]{1,0:T(4,128)S(1)} collective-permute-done((f32[4,128]{1,0:T(4,128)S(1)}, f32[4,128]{1,0:T(4,128)S(1)}, u32[]{:S(2)}, u32[]{:S(2)}) %collective-permute-start.14) | collective-permute-done | bytes 2080 | tf_op jit(solution)/shard_map/ppermute | solution.py:28
  50.0 1.1 %fusion.5 = bf16[4,128,576]{1,2,0:T(8,128)(2,1)} fusion(f32[72,4,8,128]{3,2,1,0:T(8,128)S(1)} %get-tuple-element.6, bf16[4,128,576]{1,2,0:T(8,128)(2,1)S(1)} %copy-done.4, f32[4,128]{1,0:T(4,128)S(1)} %fusion.19, f32[576]{0:T(1024)S(1)} %copy-done.12, f32[4,128]{1,0:T(4,128)S(1)} %add_rsqrt_fusion), kind=kLoop, calls=%fused_computation.10 | loop fusion | flops 1769472 | bytes 2365696 | tf_op jit(solution)/shard_map/convert_element_type | solution.py:200
  (60 shorter events, 5.8 us)
Async XLA Ops:
  0.0 41.8 %copy-start = (bf16[2048,576]{0,1:T(8,128)(2,1)S(1)}, bf16[2048,576]{0,1:T(8,128)(2,1)}, u32[]{:S(2)}) copy-start(bf16[2048,576]{0,1:T(8,128)(2,1)} %param.18) | copy-start | bytes 7077892
  3.0 21.0 %copy-start.1 = (bf16[128,512]{1,0:T(8,128)(2,1)}, bf16[128,512]{1,0:T(8,128)(2,1)S(1)}, u32[]{:S(2)}) copy-start(bf16[128,512]{1,0:T(8,128)(2,1)S(1)} %select_bitcast_fusion.rest_0_) | copy-start | bytes 393220
  3.0 9.6 %collective-permute-start.3 = (bf16[128,512]{1,0:T(8,128)(2,1)S(1)}, bf16[128,512]{1,0:T(8,128)(2,1)S(1)}, u32[]{:S(2)}, u32[]{:S(2)}) collective-permute-start(bf16[128,512]{1,0:T(8,128)(2,1)S(1)} %select_bitcast_fusion.rest_0_), channel_id=1, source_target_pairs={{0,24},{4,28},{8,16},{12,20},{16,8},{20,12},{24,0},{28,4},{1,25},{... | collective-permute-start | bytes 393224 | tf_op jit(solution)/shard_map/ppermute | solution.py:28
  8.1 7.5 %collective-permute-start = (bf16[128,512]{1,0:T(8,128)(2,1)S(1)}, bf16[128,512]{1,0:T(8,128)(2,1)S(1)}, u32[]{:S(2)}, u32[]{:S(2)}) collective-permute-start(bf16[128,512]{1,0:T(8,128)(2,1)S(1)} %select_bitcast_fusion.rest_0_), channel_id=1, source_target_pairs={{0,4},{4,0},{8,12},{12,8},{16,20},{20,16},{24,28},{28,24},{1,5},{5... | collective-permute-start | bytes 393224 | tf_op jit(solution)/shard_map/ppermute | solution.py:28
  9.6 9.4 %collective-permute-start.1 = (bf16[128,512]{1,0:T(8,128)(2,1)S(1)}, bf16[128,512]{1,0:T(8,128)(2,1)S(1)}, u32[]{:S(2)}, u32[]{:S(2)}) collective-permute-start(bf16[128,512]{1,0:T(8,128)(2,1)S(1)} %select_bitcast_fusion.rest_0_), channel_id=1, source_target_pairs={{0,8},{4,12},{8,0},{12,4},{16,24},{20,28},{24,16},{28,20},{1,9},{5... | collective-permute-start | bytes 393224 | tf_op jit(solution)/shard_map/ppermute | solution.py:28
  9.6 9.4 %collective-permute-start.2 = (bf16[128,512]{1,0:T(8,128)(2,1)S(1)}, bf16[128,512]{1,0:T(8,128)(2,1)S(1)}, u32[]{:S(2)}, u32[]{:S(2)}) collective-permute-start(bf16[128,512]{1,0:T(8,128)(2,1)S(1)} %select_bitcast_fusion.rest_0_), channel_id=1, source_target_pairs={{0,12},{4,8},{8,4},{12,0},{16,28},{20,24},{24,20},{28,16},{1,13},{... | collective-permute-start | bytes 393224 | tf_op jit(solution)/shard_map/ppermute | solution.py:28
  12.6 11.4 %copy-start.5 = (bf16[128,512]{1,0:T(8,128)(2,1)}, bf16[128,512]{1,0:T(8,128)(2,1)S(1)}, u32[]{:S(2)}) copy-start(bf16[128,512]{1,0:T(8,128)(2,1)S(1)} %collective-permute-done.3.rest_4_) | copy-start | bytes 393220
  12.6 7.1 %collective-permute-start.4 = (bf16[128,512]{1,0:T(8,128)(2,1)S(1)}, bf16[128,512]{1,0:T(8,128)(2,1)S(1)}, u32[]{:S(2)}, u32[]{:S(2)}) collective-permute-start(bf16[128,512]{1,0:T(8,128)(2,1)S(1)} %collective-permute-done.3.rest_4_), channel_id=1, source_target_pairs={{0,4},{4,0},{8,12},{12,8},{16,20},{20,16},{24,28},{28,24},{1,5},{5... | collective-permute-start | bytes 393224 | tf_op jit(solution)/shard_map/ppermute | solution.py:28
  14.2 7.4 %collective-permute-start.5 = (bf16[128,512]{1,0:T(8,128)(2,1)S(1)}, bf16[128,512]{1,0:T(8,128)(2,1)S(1)}, u32[]{:S(2)}, u32[]{:S(2)}) collective-permute-start(bf16[128,512]{1,0:T(8,128)(2,1)S(1)} %collective-permute-done.3.rest_4_), channel_id=1, source_target_pairs={{0,8},{4,12},{8,0},{12,4},{16,24},{20,28},{24,16},{28,20},{1,9},{5... | collective-permute-start | bytes 393224 | tf_op jit(solution)/shard_map/ppermute | solution.py:28
  15.7 8.3 %copy-start.6 = (bf16[128,512]{1,0:T(8,128)(2,1)}, bf16[128,512]{1,0:T(8,128)(2,1)S(1)}, u32[]{:S(2)}) copy-start(bf16[128,512]{1,0:T(8,128)(2,1)S(1)} %collective-permute-done.rest_1_) | copy-start | bytes 393220
  15.7 8.3 %collective-permute-start.6 = (bf16[128,512]{1,0:T(8,128)(2,1)S(1)}, bf16[128,512]{1,0:T(8,128)(2,1)S(1)}, u32[]{:S(2)}, u32[]{:S(2)}) collective-permute-start(bf16[128,512]{1,0:T(8,128)(2,1)S(1)} %collective-permute-done.3.rest_4_), channel_id=1, source_target_pairs={{0,12},{4,8},{8,4},{12,0},{16,28},{20,24},{24,20},{28,16},{1,13},{... | collective-permute-start | bytes 393224 | tf_op jit(solution)/shard_map/ppermute | solution.py:28
  19.1 4.9 %copy-start.7 = (bf16[128,512]{1,0:T(8,128)(2,1)}, bf16[128,512]{1,0:T(8,128)(2,1)S(1)}, u32[]{:S(2)}) copy-start(bf16[128,512]{1,0:T(8,128)(2,1)S(1)} %collective-permute-done.1.rest_2_) | copy-start | bytes 393220
  19.1 4.9 %copy-start.8 = (bf16[128,512]{1,0:T(8,128)(2,1)}, bf16[128,512]{1,0:T(8,128)(2,1)S(1)}, u32[]{:S(2)}) copy-start(bf16[128,512]{1,0:T(8,128)(2,1)S(1)} %collective-permute-done.2.rest_3_) | copy-start | bytes 393220
  28.4 5.8 %copy-start.3 = (bf16[2,128,512]{2,1,0:T(8,128)(2,1)S(1)}, bf16[2,128,512]{2,1,0:T(8,128)(2,1)}, u32[]{:S(2)}) copy-start(bf16[2,128,512]{2,1,0:T(8,128)(2,1)} %shard_map.109) | copy-start | bytes 786436
  28.4 8.5 %collective-permute-start.8 = (bf16[256,512]{1,0:T(8,128)(2,1)}, bf16[256,512]{1,0:T(8,128)(2,1)S(1)}, u32[]{:S(2)}, u32[]{:S(2)}) collective-permute-start(bf16[256,512]{1,0:T(8,128)(2,1)} %bitcast.44), channel_id=1, source_target_pairs={{0,2},{1,3},{2,0},{3,1},{4,6},{5,7},{6,4},{7,5},{8,10},{9,11},{10,... | collective-permute-start | bytes 786440 | tf_op jit(solution)/shard_map/ppermute | solution.py:28
  33.6 8.2 %collective-permute-start.11 = (bf16[256,512]{1,0:T(8,128)(2,1)}, bf16[256,512]{1,0:T(8,128)(2,1)S(1)}, u32[]{:S(2)}, u32[]{:S(2)}) collective-permute-start(bf16[256,512]{1,0:T(8,128)(2,1)} %bitcast.41), channel_id=1, source_target_pairs={{0,2},{1,3},{2,0},{3,1},{4,6},{5,7},{6,4},{7,5},{8,10},{9,11},{10,... | collective-permute-start | bytes 786440 | tf_op jit(solution)/shard_map/ppermute | solution.py:28
  34.2 8.3 %collective-permute-start.7 = (bf16[256,512]{1,0:T(8,128)(2,1)S(1)}, bf16[256,512]{1,0:T(8,128)(2,1)S(1)}, u32[]{:S(2)}, u32[]{:S(2)}) collective-permute-start(bf16[256,512]{1,0:T(8,128)(2,1)S(1)} %bitcast.45), channel_id=1, source_target_pairs={{0,1},{1,0},{2,3},{3,2},{4,5},{5,4},{6,7},{7,6},{8,9},{9,8},{10,11... | collective-permute-start | bytes 786440 | tf_op jit(solution)/shard_map/ppermute | solution.py:28
  34.2 9.1 %collective-permute-start.10 = (bf16[256,512]{1,0:T(8,128)(2,1)}, bf16[256,512]{1,0:T(8,128)(2,1)S(1)}, u32[]{:S(2)}, u32[]{:S(2)}) collective-permute-start(bf16[256,512]{1,0:T(8,128)(2,1)} %bitcast.42), channel_id=1, source_target_pairs={{0,1},{1,0},{2,3},{3,2},{4,5},{5,4},{6,7},{7,6},{8,9},{9,8},{10,11... | collective-permute-start | bytes 786440 | tf_op jit(solution)/shard_map/ppermute | solution.py:28
  36.9 7.3 %collective-permute-start.9 = (bf16[256,512]{1,0:T(8,128)(2,1)S(1)}, bf16[256,512]{1,0:T(8,128)(2,1)S(1)}, u32[]{:S(2)}, u32[]{:S(2)}) collective-permute-start(bf16[256,512]{1,0:T(8,128)(2,1)S(1)} %collective-permute-done.8), channel_id=1, source_target_pairs={{0,1},{1,0},{2,3},{3,2},{4,5},{5,4},{6,7},{7,6},{8,9},{9,8},{10,11... | collective-permute-start | bytes 786440 | tf_op jit(solution)/shard_map/ppermute | solution.py:28
  41.8 2.8 %collective-permute-start.12 = (bf16[256,512]{1,0:T(8,128)(2,1)S(1)}, bf16[256,512]{1,0:T(8,128)(2,1)S(1)}, u32[]{:S(2)}, u32[]{:S(2)}) collective-permute-start(bf16[256,512]{1,0:T(8,128)(2,1)S(1)} %collective-permute-done.11), channel_id=1, source_target_pairs={{0,1},{1,0},{2,3},{3,2},{4,5},{5,4},{6,7},{7,6},{8,9},{9,8},{10,11... | collective-permute-start | bytes 786440 | tf_op jit(solution)/shard_map/ppermute | solution.py:28
  44.5 5.5 %copy-start.4 = (bf16[4,128,576]{1,2,0:T(8,128)(2,1)S(1)}, bf16[4,128,576]{1,2,0:T(8,128)(2,1)}, u32[]{:S(2)}) copy-start(bf16[4,128,576]{1,2,0:T(8,128)(2,1)} %param.11) | copy-start | bytes 1769476
  44.6 5.5 %copy-start.12 = (f32[576]{0:T(1024)S(1)}, f32[576]{0:T(1024)}, u32[]{:S(2)}) copy-start(f32[576]{0:T(1024)} %param.19) | copy-start | bytes 6916
  45.2 3.6 %collective-permute-start.13 = (f32[4,128]{1,0:T(4,128)S(1)}, f32[4,128]{1,0:T(4,128)S(1)}, u32[]{:S(2)}, u32[]{:S(2)}) collective-permute-start(f32[4,128]{1,0:T(4,128)S(1)} %bitcast.47), channel_id=1, source_target_pairs={{0,2},{1,3},{2,0},{3,1},{4,6},{5,7},{6,4},{7,5},{8,10},{9,11},{10,... | collective-permute-start | bytes 6152 | tf_op jit(solution)/shard_map/ppermute | solution.py:28
  48.8 1.2 %collective-permute-start.14 = (f32[4,128]{1,0:T(4,128)S(1)}, f32[4,128]{1,0:T(4,128)S(1)}, u32[]{:S(2)}, u32[]{:S(2)}) collective-permute-start(f32[4,128]{1,0:T(4,128)S(1)} %bitcast_add_fusion), channel_id=1, source_target_pairs={{0,1},{1,0},{2,3},{3,2},{4,5},{5,4},{6,7},{7,6},{8,9},{9,8},{10,11... | collective-permute-start | bytes 6152 | tf_op jit(solution)/shard_map/ppermute | solution.py:28
  (4 other events, 8.3 us)

commit v21 on v16

--- a/solution.py
+++ b/solution.py
@@ -100,13 +100,17 @@
         rows = queries.shape[0]
         scores = lax.dot_general(queries, keys, (((1,), (1,)), ((), ())),
                                  preferred_element_type=jnp.float32)
-        column = lax.broadcasted_iota(jnp.int32, (rows, key_count), 1)
-        slot = lax.broadcasted_iota(jnp.int32, (rows, key_count), 0) % slots
-        suffix_pos = column - prefix_len
-        suffix_ok = (suffix_pos <= slot) & (suffix_pos < limit_ref[request])
-        raw = jnp.where(suffix_ok, capped_exp(scores) * flag, 0.0)
-        totals = jnp.sum(raw, -1, keepdims=True)
-        weights = (raw / totals).astype(jnp.bfloat16)
+        exps = capped_exp(scores) * flag
+        suffix_shape = (rows, key_count - prefix_len)
+        column = lax.broadcasted_iota(jnp.int32, suffix_shape, 1)
+        slot = lax.broadcasted_iota(jnp.int32, suffix_shape, 0) % slots
+        allowed = (column <= slot) & (column < limit_ref[request][:, prefix_len:])
+        prefix_raw = exps[:, :prefix_len]
+        suffix_raw = jnp.where(allowed, exps[:, prefix_len:], 0.0)
+        totals = jnp.sum(prefix_raw, -1, keepdims=True) + jnp.sum(suffix_raw, -1, keepdims=True)
+        inverse = 1.0 / totals
+        weights = jnp.concatenate([(prefix_raw * inverse).astype(jnp.bfloat16),
+                                   (suffix_raw * inverse).astype(jnp.bfloat16)], 1)
         attended = jnp.dot(weights, values, preferred_element_type=jnp.float32).astype(jnp.bfloat16)
         out_ref[request] = jnp.concatenate(
             [attended[q * slots:(q + 1) * slots] for q in range(per_group)], 1)

time: 51.3 us -> 51.2 us (level)
  no operation moved by 1% of the time
where the time goes in v21:
time: 51.2 us; the launch traced here: 50.8 us
  starting transfers between devices  17.7 us (35%)
  waiting for transfers between devices  13.3 us (26%)
  Pallas kernels  7.4 us (14%)
  other arithmetic  5.64 us (11%)
  local copies, waits for them, and re-layouts  3.02 us (6%)
  matrix products  2.78 us (5%)
  between operations  0.92 us (2%)
    ppermute x13, starting transfers between devices, swapped(): return lax.ppermute(value, axis, [(i, i ^ mask) for i in range(size)])  14.7 us
    ppermute x13, waiting for transfers between devices, swapped(): return lax.ppermute(value, axis, [(i, i ^ mask) for i in range(size)])  12.1 us
    pallas_call x2, Pallas kernels, attend(): pl.pallas_call(attention_kernel, grid=(1,), in_specs=[pl.BlockSpec((count...  7.4 us
    ppermute x3, starting transfers between devices, shifted(): lax.ppermute(value, axis, [(i, (i + shift) % size) for i in range(size)])  2.96 us
    dot_general x8, matrix products, project(): term = jnp.dot(block, rows, preferred_element_type=jnp.float32)  2.78 us
    reduce_sum x1, other arithmetic, gather_prefix(): slot = jnp.sum(jnp.where(mine, page_slot, 0))  1.54 us
    ppermute x3, waiting for transfers between devices, shifted(): lax.ppermute(value, axis, [(i, (i + shift) % size) for i in range(size)])  1.24 us
    convert_element_type x1, other arithmetic, on_device(): return ((source + branch) * live_mask[..., None]).astype(jnp.bfloat16)  1.1 us
  transfers between devices with their start and end apart: 16, of which 7 were waited for; matrix products, arithmetic and copies ran while one was open for 13% of the time, Pallas kernels for 7%

profile of v21, /device:TPU:0, one launch (start us, length us, event | category | flops | bytes accessed | tf_op | source)
XLA Modules:
  0.0 50.8 jit_solution(11842775112923913520)
XLA Ops:
  0.0 1.5 %fusion.28 = s32[]{:T(128)} fusion(s32[8]{0:T(128)} %param.15, s32[8]{0:T(128)} %param.14, s32[]{:T(128)} %axis_index.27), kind=kLoop, calls=%fused_computation.43 | loop fusion | flops 23 | bytes 72 | tf_op jit(solution)/shard_map/reduce_sum | solution.py:36
  2.2 1.0 %select_bitcast_fusion.rest_0_ = bf16[128,512]{1,0:T(8,128)(2,1)S(1)} fusion(bf16[2,128,1,512]{3,1,2,0:T(8,128)(2,1)} %param.13, pred[]{:T(512)S(6)} %eq.43), kind=kLoop, calls=%fused_computation.26 | loop fusion | flops 65536 | bytes 393217 | tf_op jit(solution)/shard_map/jit(_where)/select_n | solution.py:39
  3.2 5.1 %collective-permute-start.3 = (bf16[128,512]{1,0:T(8,128)(2,1)S(1)}, bf16[128,512]{1,0:T(8,128)(2,1)S(1)}, u32[]{:S(2)}, u32[]{:S(2)}) collective-permute-start(bf16[128,512]{1,0:T(8,128)(2,1)S(1)} %select_bitcast_fusion.rest_0_), channel_id=1, source_target_pairs={{0,24},{4,28},{8,16},{12,20},{16,8},{20,12},{24,0},{28,4},{1,25},{... | collective-permute-start | bytes 393224 | tf_op jit(solution)/shard_map/ppermute | solution.py:28
  8.4 1.5 %collective-permute-start = (bf16[128,512]{1,0:T(8,128)(2,1)S(1)}, bf16[128,512]{1,0:T(8,128)(2,1)S(1)}, u32[]{:S(2)}, u32[]{:S(2)}) collective-permute-start(bf16[128,512]{1,0:T(8,128)(2,1)S(1)} %select_bitcast_fusion.rest_0_), channel_id=1, source_target_pairs={{0,4},{4,0},{8,12},{12,8},{16,20},{20,16},{24,28},{28,24},{1,5},{5... | collective-permute-start | bytes 393224 | tf_op jit(solution)/shard_map/ppermute | solution.py:28
  9.9 2.0 %collective-permute-start.2 = (bf16[128,512]{1,0:T(8,128)(2,1)S(1)}, bf16[128,512]{1,0:T(8,128)(2,1)S(1)}, u32[]{:S(2)}, u32[]{:S(2)}) collective-permute-start(bf16[128,512]{1,0:T(8,128)(2,1)S(1)} %select_bitcast_fusion.rest_0_), channel_id=1, source_target_pairs={{0,12},{4,8},{8,4},{12,0},{16,28},{20,24},{24,20},{28,16},{1,13},{... | collective-permute-start | bytes 393224 | tf_op jit(solution)/shard_map/ppermute | solution.py:28
  11.9 0.8 %compare_reduce_fusion = pred[8]{0:T(512)(128)(4,1)S(1)} fusion(s32[8]{0:T(128)} %param.14, s32[8]{0:T(128)S(1)} %stack.35), kind=kLoop, calls=%fused_computation.27 | loop fusion | flops 120 | bytes 72 | tf_op jit(solution)/shard_map/reduce_or | solution.py:55
  12.8 1.7 %collective-permute-start.4 = (bf16[128,512]{1,0:T(8,128)(2,1)S(1)}, bf16[128,512]{1,0:T(8,128)(2,1)S(1)}, u32[]{:S(2)}, u32[]{:S(2)}) collective-permute-start(bf16[128,512]{1,0:T(8,128)(2,1)S(1)} %collective-permute-done.3.rest_4_), channel_id=1, source_target_pairs={{0,4},{4,0},{8,12},{12,8},{16,20},{20,16},{24,28},{28,24},{1,5},{5... | collective-permute-start | bytes 393224 | tf_op jit(solution)/shard_map/ppermute | solution.py:28
  14.5 1.5 %collective-permute-start.5 = (bf16[128,512]{1,0:T(8,128)(2,1)S(1)}, bf16[128,512]{1,0:T(8,128)(2,1)S(1)}, u32[]{:S(2)}, u32[]{:S(2)}) collective-permute-start(bf16[128,512]{1,0:T(8,128)(2,1)S(1)} %collective-permute-done.3.rest_4_), channel_id=1, source_target_pairs={{0,8},{4,12},{8,0},{12,4},{16,24},{20,28},{24,16},{28,20},{1,9},{5... | collective-permute-start | bytes 393224 | tf_op jit(solution)/shard_map/ppermute | solution.py:28
  16.4 0.6 %broadcast_in_dim.29.flag_ref = f32[1,1152]{1,0:T(1,128)} reshape(f32[1152]{0:T(1024)S(1)} %concatenate.12) | data formatting | bytes 9216 | tf_op jit(solution)/shard_map/broadcast_in_dim | solution.py:127
  17.0 0.7 %dynamic_slice.19 = s32[4]{0:T(128)S(1)} dynamic-slice(s32[32]{0:T(128)} %param.17, s32[]{:T(128)S(6)} %select_n.37), dynamic_slice_sizes={4} | dynamic-slice | bytes 36 | tf_op jit(solution)/shard_map/dynamic_slice | solution.py:176
  17.8 0.8 %select_reduce_fusion = s32[4]{0:T(128)S(1)} fusion(s32[32]{0:T(128)} %param.16, s32[4]{0:T(128)S(1)} %dynamic_slice.19), kind=kLoop, calls=%fused_computation.31 | loop fusion | flops 380 | bytes 160 | tf_op jit(solution)/shard_map/reduce_sum | solution.py:178
  18.7 0.6 %broadcast_in_dim.27.limit_ref = s32[4,1,1152]{2,1,0:T(1,128)} reshape(s32[4,1152]{1,0:T(4,128)S(1)} %concatenate.11) | data formatting | bytes 36864 | tf_op jit(solution)/shard_map/broadcast_in_dim | solution.py:131
  19.3 0.6 %collective-permute-done.4.rest_5_ = bf16[128,512]{1,0:T(8,128)(2,1)S(1)} collective-permute-done((bf16[128,512]{1,0:T(8,128)(2,1)S(1)}, bf16[128,512]{1,0:T(8,128)(2,1)S(1)}, u32[]{:S(2)}, u32[]{:S(2)}) %collective-permute-start.4) | collective-permute-done | bytes 131104 | tf_op jit(solution)/shard_map/ppermute | solution.py:28
  19.9 1.9 %collective-permute-done.5.rest_6_ = bf16[128,512]{1,0:T(8,128)(2,1)S(1)} collective-permute-done((bf16[128,512]{1,0:T(8,128)(2,1)S(1)}, bf16[128,512]{1,0:T(8,128)(2,1)S(1)}, u32[]{:S(2)}, u32[]{:S(2)}) %collective-permute-start.5) | collective-permute-done | bytes 131104 | tf_op jit(solution)/shard_map/ppermute | solution.py:28
  21.9 2.3 %collective-permute-done.6.rest_7_ = bf16[128,512]{1,0:T(8,128)(2,1)S(1)} collective-permute-done((bf16[128,512]{1,0:T(8,128)(2,1)S(1)}, bf16[128,512]{1,0:T(8,128)(2,1)S(1)}, u32[]{:S(2)}, u32[]{:S(2)}) %collective-permute-start.6) | collective-permute-done | bytes 131104 | tf_op jit(solution)/shard_map/ppermute | solution.py:28
  24.8 3.7 %shard_map.109 = bf16[2,128,512]{2,1,0:T(8,128)(2,1)} custom-call(s32[4,1,1152]{2,1,0:T(1,128)} %broadcast_in_dim.27.limit_ref, f32[1,1152]{1,0:T(1,128)} %broadcast_in_dim.29.flag_ref, bf16[4,128,1024]{2,1,0:T(8,128)(2,1)} %bitcast.37, f32[128,128]{1,0:T(8,128)} %constant.44.clone.cos_ref, f32[128,128]{1,0:T(8,128)} %constant.45.clone.sin_ref, ...), custom_call_target="tpu_custom_call" | custom-call | tf_op jit(solution)/shard_map/pallas_call | solution.py:134
  28.6 1.4 %collective-permute-start.8 = (bf16[256,512]{1,0:T(8,128)(2,1)}, bf16[256,512]{1,0:T(8,128)(2,1)S(1)}, u32[]{:S(2)}, u32[]{:S(2)}) collective-permute-start(bf16[256,512]{1,0:T(8,128)(2,1)} %bitcast.42), channel_id=1, source_target_pairs={{0,2},{1,3},{2,0},{3,1},{4,6},{5,7},{6,4},{7,5},{8,10},{9,11},{10,... | collective-permute-start | bytes 786440 | tf_op jit(solution)/shard_map/ppermute | solution.py:28
  30.0 3.7 %shard_map.110 = bf16[2,128,512]{2,1,0:T(8,128)(2,1)} custom-call(s32[4,1,1152]{2,1,0:T(1,128)} %broadcast_in_dim.27.limit_ref, f32[1,1152]{1,0:T(1,128)} %broadcast_in_dim.29.flag_ref, bf16[4,128,1024]{2,1,0:T(8,128)(2,1)} %bitcast.38, f32[128,128]{1,0:T(8,128)} %constant.44.clone.cos_ref, f32[128,128]{1,0:T(8,128)} %constant.45.clone.sin_ref, ...), custom_call_target="tpu_custom_call" | custom-call | tf_op jit(solution)/shard_map/pallas_call | solution.py:134
  34.8 2.3 %collective-permute-done.8 = bf16[256,512]{1,0:T(8,128)(2,1)S(1)} collective-permute-done((bf16[256,512]{1,0:T(8,128)(2,1)}, bf16[256,512]{1,0:T(8,128)(2,1)S(1)}, u32[]{:S(2)}, u32[]{:S(2)}) %collective-permute-start.8) | collective-permute-done | bytes 262176 | tf_op jit(solution)/shard_map/ppermute | solution.py:28
  37.1 4.9 %collective-permute-done.11 = bf16[256,512]{1,0:T(8,128)(2,1)S(1)} collective-permute-done((bf16[256,512]{1,0:T(8,128)(2,1)}, bf16[256,512]{1,0:T(8,128)(2,1)S(1)}, u32[]{:S(2)}, u32[]{:S(2)}) %collective-permute-start.11) | collective-permute-done | bytes 262176 | tf_op jit(solution)/shard_map/ppermute | solution.py:28
  45.9 1.4 %collective-permute-start.14 = (f32[4,128]{1,0:T(4,128)S(1)}, f32[4,128]{1,0:T(4,128)S(1)}, u32[]{:S(2)}, u32[]{:S(2)}) collective-permute-start(f32[4,128]{1,0:T(4,128)S(1)} %bitcast.46), channel_id=1, source_target_pairs={{0,2},{1,3},{2,0},{3,1},{4,6},{5,7},{6,4},{7,5},{8,10},{9,11},{10,... | collective-permute-start | bytes 6152 | tf_op jit(solution)/shard_map/ppermute | solution.py:24
  47.4 1.0 %collective-permute-start.15 = (f32[4,128]{1,0:T(4,128)S(1)}, f32[4,128]{1,0:T(4,128)S(1)}, u32[]{:S(2)}, u32[]{:S(2)}) collective-permute-start(f32[4,128]{1,0:T(4,128)S(1)} %bitcast.47), channel_id=1, source_target_pairs={{0,3},{1,0},{2,1},{3,2},{4,7},{5,4},{6,5},{7,6},{8,11},{9,8},{10,9... | collective-permute-start | bytes 6152 | tf_op jit(solution)/shard_map/ppermute | solution.py:24
  48.4 1.1 %collective-permute-done.14 = f32[4,128]{1,0:T(4,128)S(1)} collective-permute-done((f32[4,128]{1,0:T(4,128)S(1)}, f32[4,128]{1,0:T(4,128)S(1)}, u32[]{:S(2)}, u32[]{:S(2)}) %collective-permute-start.14) | collective-permute-done | bytes 2080 | tf_op jit(solution)/shard_map/ppermute | solution.py:24
  49.7 1.1 %fusion.5 = bf16[4,128,576]{1,2,0:T(8,128)(2,1)} fusion(f32[72,4,8,128]{3,2,1,0:T(8,128)S(1)} %get-tuple-element.6, bf16[4,128,576]{1,2,0:T(8,128)(2,1)S(1)} %copy-done.4, f32[4,128]{1,0:T(4,128)S(1)} %fusion.19, f32[576]{0:T(1024)S(1)} %copy-done.12, f32[4,128]{1,0:T(4,128)S(1)} %add_rsqrt_fusion), kind=kLoop, calls=%fused_computation.10 | loop fusion | flops 1769472 | bytes 2365696 | tf_op jit(solution)/shard_map/convert_element_type | solution.py:200
  (61 shorter events, 6.5 us)
Async XLA Ops:
  0.0 42.0 %copy-start = (bf16[2048,576]{0,1:T(8,128)(2,1)S(1)}, bf16[2048,576]{0,1:T(8,128)(2,1)}, u32[]{:S(2)}) copy-start(bf16[2048,576]{0,1:T(8,128)(2,1)} %param.18) | copy-start | bytes 7077892
  3.2 21.0 %copy-start.1 = (bf16[128,512]{1,0:T(8,128)(2,1)}, bf16[128,512]{1,0:T(8,128)(2,1)S(1)}, u32[]{:S(2)}) copy-start(bf16[128,512]{1,0:T(8,128)(2,1)S(1)} %select_bitcast_fusion.rest_0_) | copy-start | bytes 393220
  3.2 9.6 %collective-permute-start.3 = (bf16[128,512]{1,0:T(8,128)(2,1)S(1)}, bf16[128,512]{1,0:T(8,128)(2,1)S(1)}, u32[]{:S(2)}, u32[]{:S(2)}) collective-permute-start(bf16[128,512]{1,0:T(8,128)(2,1)S(1)} %select_bitcast_fusion.rest_0_), channel_id=1, source_target_pairs={{0,24},{4,28},{8,16},{12,20},{16,8},{20,12},{24,0},{28,4},{1,25},{... | collective-permute-start | bytes 393224 | tf_op jit(solution)/shard_map/ppermute | solution.py:28
  8.4 7.5 %collective-permute-start = (bf16[128,512]{1,0:T(8,128)(2,1)S(1)}, bf16[128,512]{1,0:T(8,128)(2,1)S(1)}, u32[]{:S(2)}, u32[]{:S(2)}) collective-permute-start(bf16[128,512]{1,0:T(8,128)(2,1)S(1)} %select_bitcast_fusion.rest_0_), channel_id=1, source_target_pairs={{0,4},{4,0},{8,12},{12,8},{16,20},{20,16},{24,28},{28,24},{1,5},{5... | collective-permute-start | bytes 393224 | tf_op jit(solution)/shard_map/ppermute | solution.py:28
  9.9 9.4 %collective-permute-start.1 = (bf16[128,512]{1,0:T(8,128)(2,1)S(1)}, bf16[128,512]{1,0:T(8,128)(2,1)S(1)}, u32[]{:S(2)}, u32[]{:S(2)}) collective-permute-start(bf16[128,512]{1,0:T(8,128)(2,1)S(1)} %select_bitcast_fusion.rest_0_), channel_id=1, source_target_pairs={{0,8},{4,12},{8,0},{12,4},{16,24},{20,28},{24,16},{28,20},{1,9},{5... | collective-permute-start | bytes 393224 | tf_op jit(solution)/shard_map/ppermute | solution.py:28
  9.9 9.4 %collective-permute-start.2 = (bf16[128,512]{1,0:T(8,128)(2,1)S(1)}, bf16[128,512]{1,0:T(8,128)(2,1)S(1)}, u32[]{:S(2)}, u32[]{:S(2)}) collective-permute-start(bf16[128,512]{1,0:T(8,128)(2,1)S(1)} %select_bitcast_fusion.rest_0_), channel_id=1, source_target_pairs={{0,12},{4,8},{8,4},{12,0},{16,28},{20,24},{24,20},{28,16},{1,13},{... | collective-permute-start | bytes 393224 | tf_op jit(solution)/shard_map/ppermute | solution.py:28
  12.8 11.4 %copy-start.5 = (bf16[128,512]{1,0:T(8,128)(2,1)}, bf16[128,512]{1,0:T(8,128)(2,1)S(1)}, u32[]{:S(2)}) copy-start(bf16[128,512]{1,0:T(8,128)(2,1)S(1)} %collective-permute-done.3.rest_4_) | copy-start | bytes 393220
  12.8 7.1 %collective-permute-start.4 = (bf16[128,512]{1,0:T(8,128)(2,1)S(1)}, bf16[128,512]{1,0:T(8,128)(2,1)S(1)}, u32[]{:S(2)}, u32[]{:S(2)}) collective-permute-start(bf16[128,512]{1,0:T(8,128)(2,1)S(1)} %collective-permute-done.3.rest_4_), channel_id=1, source_target_pairs={{0,4},{4,0},{8,12},{12,8},{16,20},{20,16},{24,28},{28,24},{1,5},{5... | collective-permute-start | bytes 393224 | tf_op jit(solution)/shard_map/ppermute | solution.py:28
  14.5 7.4 %collective-permute-start.5 = (bf16[128,512]{1,0:T(8,128)(2,1)S(1)}, bf16[128,512]{1,0:T(8,128)(2,1)S(1)}, u32[]{:S(2)}, u32[]{:S(2)}) collective-permute-start(bf16[128,512]{1,0:T(8,128)(2,1)S(1)} %collective-permute-done.3.rest_4_), channel_id=1, source_target_pairs={{0,8},{4,12},{8,0},{12,4},{16,24},{20,28},{24,16},{28,20},{1,9},{5... | collective-permute-start | bytes 393224 | tf_op jit(solution)/shard_map/ppermute | solution.py:28
  15.9 8.3 %copy-start.6 = (bf16[128,512]{1,0:T(8,128)(2,1)}, bf16[128,512]{1,0:T(8,128)(2,1)S(1)}, u32[]{:S(2)}) copy-start(bf16[128,512]{1,0:T(8,128)(2,1)S(1)} %collective-permute-done.rest_1_) | copy-start | bytes 393220
  15.9 8.3 %collective-permute-start.6 = (bf16[128,512]{1,0:T(8,128)(2,1)S(1)}, bf16[128,512]{1,0:T(8,128)(2,1)S(1)}, u32[]{:S(2)}, u32[]{:S(2)}) collective-permute-start(bf16[128,512]{1,0:T(8,128)(2,1)S(1)} %collective-permute-done.3.rest_4_), channel_id=1, source_target_pairs={{0,12},{4,8},{8,4},{12,0},{16,28},{20,24},{24,20},{28,16},{1,13},{... | collective-permute-start | bytes 393224 | tf_op jit(solution)/shard_map/ppermute | solution.py:28
  19.3 4.9 %copy-start.8 = (bf16[128,512]{1,0:T(8,128)(2,1)}, bf16[128,512]{1,0:T(8,128)(2,1)S(1)}, u32[]{:S(2)}) copy-start(bf16[128,512]{1,0:T(8,128)(2,1)S(1)} %collective-permute-done.2.rest_3_) | copy-start | bytes 393220
  28.6 5.7 %copy-start.3 = (bf16[2,128,512]{2,1,0:T(8,128)(2,1)S(1)}, bf16[2,128,512]{2,1,0:T(8,128)(2,1)}, u32[]{:S(2)}) copy-start(bf16[2,128,512]{2,1,0:T(8,128)(2,1)} %shard_map.109) | copy-start | bytes 786436
  28.6 8.6 %collective-permute-start.8 = (bf16[256,512]{1,0:T(8,128)(2,1)}, bf16[256,512]{1,0:T(8,128)(2,1)S(1)}, u32[]{:S(2)}, u32[]{:S(2)}) collective-permute-start(bf16[256,512]{1,0:T(8,128)(2,1)} %bitcast.42), channel_id=1, source_target_pairs={{0,2},{1,3},{2,0},{3,1},{4,6},{5,7},{6,4},{7,5},{8,10},{9,11},{10,... | collective-permute-start | bytes 786440 | tf_op jit(solution)/shard_map/ppermute | solution.py:28
  33.7 8.3 %collective-permute-start.11 = (bf16[256,512]{1,0:T(8,128)(2,1)}, bf16[256,512]{1,0:T(8,128)(2,1)S(1)}, u32[]{:S(2)}, u32[]{:S(2)}) collective-permute-start(bf16[256,512]{1,0:T(8,128)(2,1)} %bitcast.39), channel_id=1, source_target_pairs={{0,2},{1,3},{2,0},{3,1},{4,6},{5,7},{6,4},{7,5},{8,10},{9,11},{10,... | collective-permute-start | bytes 786440 | tf_op jit(solution)/shard_map/ppermute | solution.py:28
  34.3 8.4 %collective-permute-start.7 = (bf16[256,512]{1,0:T(8,128)(2,1)S(1)}, bf16[256,512]{1,0:T(8,128)(2,1)S(1)}, u32[]{:S(2)}, u32[]{:S(2)}) collective-permute-start(bf16[256,512]{1,0:T(8,128)(2,1)S(1)} %bitcast.43), channel_id=1, source_target_pairs={{0,1},{1,0},{2,3},{3,2},{4,5},{5,4},{6,7},{7,6},{8,9},{9,8},{10,11... | collective-permute-start | bytes 786440 | tf_op jit(solution)/shard_map/ppermute | solution.py:28
  34.3 9.1 %collective-permute-start.10 = (bf16[256,512]{1,0:T(8,128)(2,1)}, bf16[256,512]{1,0:T(8,128)(2,1)S(1)}, u32[]{:S(2)}, u32[]{:S(2)}) collective-permute-start(bf16[256,512]{1,0:T(8,128)(2,1)} %bitcast.40), channel_id=1, source_target_pairs={{0,1},{1,0},{2,3},{3,2},{4,5},{5,4},{6,7},{7,6},{8,9},{9,8},{10,11... | collective-permute-start | bytes 786440 | tf_op jit(solution)/shard_map/ppermute | solution.py:28
  37.1 7.2 %collective-permute-start.9 = (bf16[256,512]{1,0:T(8,128)(2,1)S(1)}, bf16[256,512]{1,0:T(8,128)(2,1)S(1)}, u32[]{:S(2)}, u32[]{:S(2)}) collective-permute-start(bf16[256,512]{1,0:T(8,128)(2,1)S(1)} %collective-permute-done.8), channel_id=1, source_target_pairs={{0,1},{1,0},{2,3},{3,2},{4,5},{5,4},{6,7},{7,6},{8,9},{9,8},{10,11... | collective-permute-start | bytes 786440 | tf_op jit(solution)/shard_map/ppermute | solution.py:28
  42.0 2.8 %collective-permute-start.12 = (bf16[256,512]{1,0:T(8,128)(2,1)S(1)}, bf16[256,512]{1,0:T(8,128)(2,1)S(1)}, u32[]{:S(2)}, u32[]{:S(2)}) collective-permute-start(bf16[256,512]{1,0:T(8,128)(2,1)S(1)} %collective-permute-done.11), channel_id=1, source_target_pairs={{0,1},{1,0},{2,3},{3,2},{4,5},{5,4},{6,7},{7,6},{8,9},{9,8},{10,11... | collective-permute-start | bytes 786440 | tf_op jit(solution)/shard_map/ppermute | solution.py:28
  44.7 4.9 %copy-start.4 = (bf16[4,128,576]{1,2,0:T(8,128)(2,1)S(1)}, bf16[4,128,576]{1,2,0:T(8,128)(2,1)}, u32[]{:S(2)}) copy-start(bf16[4,128,576]{1,2,0:T(8,128)(2,1)} %param.11) | copy-start | bytes 1769476
  44.7 4.9 %copy-start.12 = (f32[576]{0:T(1024)S(1)}, f32[576]{0:T(1024)}, u32[]{:S(2)}) copy-start(f32[576]{0:T(1024)} %param.19) | copy-start | bytes 6916
  45.4 3.1 %collective-permute-start.13 = (f32[4,128]{1,0:T(4,128)S(1)}, f32[4,128]{1,0:T(4,128)S(1)}, u32[]{:S(2)}, u32[]{:S(2)}) collective-permute-start(f32[4,128]{1,0:T(4,128)S(1)} %bitcast.45), channel_id=1, source_target_pairs={{0,1},{1,2},{2,3},{3,0},{4,5},{5,6},{6,7},{7,4},{8,9},{9,10},{10,1... | collective-permute-start | bytes 6152 | tf_op jit(solution)/shard_map/ppermute | solution.py:24
  45.9 3.6 %collective-permute-start.14 = (f32[4,128]{1,0:T(4,128)S(1)}, f32[4,128]{1,0:T(4,128)S(1)}, u32[]{:S(2)}, u32[]{:S(2)}) collective-permute-start(f32[4,128]{1,0:T(4,128)S(1)} %bitcast.46), channel_id=1, source_target_pairs={{0,2},{1,3},{2,0},{3,1},{4,6},{5,7},{6,4},{7,5},{8,10},{9,11},{10,... | collective-permute-start | bytes 6152 | tf_op jit(solution)/shard_map/ppermute | solution.py:24
  47.4 2.3 %collective-permute-start.15 = (f32[4,128]{1,0:T(4,128)S(1)}, f32[4,128]{1,0:T(4,128)S(1)}, u32[]{:S(2)}, u32[]{:S(2)}) collective-permute-start(f32[4,128]{1,0:T(4,128)S(1)} %bitcast.47), channel_id=1, source_target_pairs={{0,3},{1,0},{2,1},{3,2},{4,7},{5,4},{6,5},{7,6},{8,11},{9,8},{10,9... | collective-permute-start | bytes 6152 | tf_op jit(solution)/shard_map/ppermute | solution.py:24
  (5 other events, 13.2 us)

commit v22 on v16

--- a/solution.py
+++ b/solution.py
@@ -179,13 +179,27 @@
     cosine, sine = static_tables(prefix_len + np.arange(slots), HD)
     group_width = per_group * HD
     chunk = max(1, requests // 2)
-    projected_parts = []
+    chunk_parts = []
     for start in range(0, requests, chunk):
         attended = attend(qkv[:, :, 0], jnp.asarray(cosine), jnp.asarray(sine), blocks,
                           my_lengths, valid.astype(jnp.int32), start, chunk)
         own = attended.reshape(chunk * slots, per_group * HD)
-        projected_parts.append(project(own, w_out, tp_index, n_tp, group_width))
-    projected = jnp.concatenate(projected_parts, 0).reshape(requests, slots, local_width)
+        if n_tp == 4:
+            near = swapped(own, "tp", n_tp, 1)
+            far = swapped(own, "tp", n_tp, 2)
+            chunk_parts.append([(own, tp_index), (near, tp_index ^ 1), (far, tp_index ^ 2),
+                                (swapped(far, "tp", n_tp, 1), tp_index ^ 3)])
+        else:
+            chunk_parts.append([(own, tp_index)] + [
+                (shifted(own, "tp", n_tp, shift), (tp_index - shift) % n_tp)
+                for shift in range(1, n_tp)])
+    projected = None
+    for number in range(n_tp):
+        block = jnp.concatenate([parts[number][0] for parts in chunk_parts], 0)
+        rows = lax.dynamic_slice_in_dim(w_out, chunk_parts[0][number][1] * group_width, group_width, 0)
+        term = jnp.dot(block, rows, preferred_element_type=jnp.float32)
+        projected = term if projected is None else projected + term
+    projected = projected.reshape(requests, slots, local_width)
 
     squares = jnp.sum(projected * projected, -1)
     branch_total = squares

time: 51.3 us -> 51.1 us (level)
    dot_general x8 -> x4, matrix products: 2.79 us -> 2.99 us  [on_device(): term = jnp.dot(block, rows, preferred_element_type=jnp.float32)]
  transfers between devices with their start and end apart: 16 -> 16, of which waited for: 7 -> 8; matrix products, arithmetic and copies ran while one was open for 13% -> 13% of each run, Pallas kernels for 7% -> 7%
where the time goes in v22:
time: 51.1 us; the launch traced here: 50.6 us
  starting transfers between devices  17.5 us (34%)
  waiting for transfers between devices  13.6 us (27%)
  Pallas kernels  7.54 us (15%)
  other arithmetic  5.39 us (11%)
  matrix products  2.99 us (6%)
  local copies, waits for them, and re-layouts  2.81 us (5%)
  between operations  0.88 us (2%)
    ppermute x13, starting transfers between devices, swapped(): return lax.ppermute(value, axis, [(i, i ^ mask) for i in range(size)])  14.5 us
    ppermute x13, waiting for transfers between devices, swapped(): return lax.ppermute(value, axis, [(i, i ^ mask) for i in range(size)])  12.3 us
    pallas_call x2, Pallas kernels, attend(): pl.pallas_call(attention_kernel, grid=(1,), in_specs=[pl.BlockSpec((count...  7.54 us
    dot_general x4, matrix products, on_device(): term = jnp.dot(block, rows, preferred_element_type=jnp.float32)  2.99 us
    ppermute x3, starting transfers between devices, shifted(): lax.ppermute(value, axis, [(i, (i + shift) % size) for i in range(size)])  2.96 us
    reduce_sum x1, other arithmetic, gather_prefix(): slot = jnp.sum(jnp.where(mine, page_slot, 0))  1.54 us
    ppermute x3, waiting for transfers between devices, shifted(): lax.ppermute(value, axis, [(i, (i + shift) % size) for i in range(size)])  1.24 us
    convert_element_type x1, other arithmetic, on_device(): return ((source + branch) * live_mask[..., None]).astype(jnp.bfloat16)  1.1 us
  transfers between devices with their start and end apart: 16, of which 8 were waited for; matrix products, arithmetic and copies ran while one was open for 13% of the time, Pallas kernels for 7%

profile of v22, /device:TPU:0, one launch (start us, length us, event | category | flops | bytes accessed | tf_op | source)
XLA Modules:
  0.0 50.6 jit_solution(12062433465320198653)
XLA Ops:
  0.0 1.5 %fusion.26 = s32[]{:T(128)} fusion(s32[8]{0:T(128)} %param.15, s32[8]{0:T(128)} %param.14, s32[]{:T(128)} %axis_index.27), kind=kLoop, calls=%fused_computation.39 | loop fusion | flops 23 | bytes 72 | tf_op jit(solution)/shard_map/reduce_sum | solution.py:36
  2.2 1.0 %select_bitcast_fusion.rest_0_ = bf16[128,512]{1,0:T(8,128)(2,1)S(1)} fusion(bf16[2,128,1,512]{3,1,2,0:T(8,128)(2,1)} %param.13, pred[]{:T(512)S(6)} %eq.43), kind=kLoop, calls=%fused_computation.26 | loop fusion | flops 65536 | bytes 393217 | tf_op jit(solution)/shard_map/jit(_where)/select_n | solution.py:39
  3.2 5.1 %collective-permute-start.3 = (bf16[128,512]{1,0:T(8,128)(2,1)S(1)}, bf16[128,512]{1,0:T(8,128)(2,1)S(1)}, u32[]{:S(2)}, u32[]{:S(2)}) collective-permute-start(bf16[128,512]{1,0:T(8,128)(2,1)S(1)} %select_bitcast_fusion.rest_0_), channel_id=1, source_target_pairs={{0,24},{4,28},{8,16},{12,20},{16,8},{20,12},{24,0},{28,4},{1,25},{... | collective-permute-start | bytes 393224 | tf_op jit(solution)/shard_map/ppermute | solution.py:28
  8.4 1.5 %collective-permute-start = (bf16[128,512]{1,0:T(8,128)(2,1)S(1)}, bf16[128,512]{1,0:T(8,128)(2,1)S(1)}, u32[]{:S(2)}, u32[]{:S(2)}) collective-permute-start(bf16[128,512]{1,0:T(8,128)(2,1)S(1)} %select_bitcast_fusion.rest_0_), channel_id=1, source_target_pairs={{0,4},{4,0},{8,12},{12,8},{16,20},{20,16},{24,28},{28,24},{1,5},{5... | collective-permute-start | bytes 393224 | tf_op jit(solution)/shard_map/ppermute | solution.py:28
  9.9 2.0 %collective-permute-start.2 = (bf16[128,512]{1,0:T(8,128)(2,1)S(1)}, bf16[128,512]{1,0:T(8,128)(2,1)S(1)}, u32[]{:S(2)}, u32[]{:S(2)}) collective-permute-start(bf16[128,512]{1,0:T(8,128)(2,1)S(1)} %select_bitcast_fusion.rest_0_), channel_id=1, source_target_pairs={{0,12},{4,8},{8,4},{12,0},{16,28},{20,24},{24,20},{28,16},{1,13},{... | collective-permute-start | bytes 393224 | tf_op jit(solution)/shard_map/ppermute | solution.py:28
  11.9 0.8 %compare_reduce_fusion = pred[8]{0:T(512)(128)(4,1)S(1)} fusion(s32[8]{0:T(128)} %param.14, s32[8]{0:T(128)S(1)} %stack.35), kind=kLoop, calls=%fused_computation.27 | loop fusion | flops 120 | bytes 72 | tf_op jit(solution)/shard_map/reduce_or | solution.py:55
  12.8 1.7 %collective-permute-start.4 = (bf16[128,512]{1,0:T(8,128)(2,1)S(1)}, bf16[128,512]{1,0:T(8,128)(2,1)S(1)}, u32[]{:S(2)}, u32[]{:S(2)}) collective-permute-start(bf16[128,512]{1,0:T(8,128)(2,1)S(1)} %collective-permute-done.3.rest_4_), channel_id=1, source_target_pairs={{0,4},{4,0},{8,12},{12,8},{16,20},{20,16},{24,28},{28,24},{1,5},{5... | collective-permute-start | bytes 393224 | tf_op jit(solution)/shard_map/ppermute | solution.py:28
  14.5 1.5 %collective-permute-start.5 = (bf16[128,512]{1,0:T(8,128)(2,1)S(1)}, bf16[128,512]{1,0:T(8,128)(2,1)S(1)}, u32[]{:S(2)}, u32[]{:S(2)}) collective-permute-start(bf16[128,512]{1,0:T(8,128)(2,1)S(1)} %collective-permute-done.3.rest_4_), channel_id=1, source_target_pairs={{0,8},{4,12},{8,0},{12,4},{16,24},{20,28},{24,16},{28,20},{1,9},{5... | collective-permute-start | bytes 393224 | tf_op jit(solution)/shard_map/ppermute | solution.py:28
  17.0 0.7 %dynamic_slice.15 = s32[4]{0:T(128)S(1)} dynamic-slice(s32[32]{0:T(128)} %param.17, s32[]{:T(128)S(6)} %select_n.33), dynamic_slice_sizes={4} | dynamic-slice | bytes 36 | tf_op jit(solution)/shard_map/dynamic_slice | solution.py:172
  17.8 0.8 %select_reduce_fusion = s32[4]{0:T(128)S(1)} fusion(s32[32]{0:T(128)} %param.16, s32[4]{0:T(128)S(1)} %dynamic_slice.15), kind=kLoop, calls=%fused_computation.31 | loop fusion | flops 380 | bytes 160 | tf_op jit(solution)/shard_map/reduce_sum | solution.py:174
  19.3 0.6 %collective-permute-done.4.rest_5_ = bf16[128,512]{1,0:T(8,128)(2,1)S(1)} collective-permute-done((bf16[128,512]{1,0:T(8,128)(2,1)S(1)}, bf16[128,512]{1,0:T(8,128)(2,1)S(1)}, u32[]{:S(2)}, u32[]{:S(2)}) %collective-permute-start.4) | collective-permute-done | bytes 131104 | tf_op jit(solution)/shard_map/ppermute | solution.py:28
  19.9 1.9 %collective-permute-done.5.rest_6_ = bf16[128,512]{1,0:T(8,128)(2,1)S(1)} collective-permute-done((bf16[128,512]{1,0:T(8,128)(2,1)S(1)}, bf16[128,512]{1,0:T(8,128)(2,1)S(1)}, u32[]{:S(2)}, u32[]{:S(2)}) %collective-permute-start.5) | collective-permute-done | bytes 131104 | tf_op jit(solution)/shard_map/ppermute | solution.py:28
  21.9 2.3 %collective-permute-done.6.rest_7_ = bf16[128,512]{1,0:T(8,128)(2,1)S(1)} collective-permute-done((bf16[128,512]{1,0:T(8,128)(2,1)S(1)}, bf16[128,512]{1,0:T(8,128)(2,1)S(1)}, u32[]{:S(2)}, u32[]{:S(2)}) %collective-permute-start.6) | collective-permute-done | bytes 131104 | tf_op jit(solution)/shard_map/ppermute | solution.py:28
  24.8 3.8 %shard_map.109 = bf16[2,128,512]{2,1,0:T(8,128)(2,1)} custom-call(s32[4,1,1152]{2,1,0:T(1,128)} %broadcast_in_dim.27.limit_ref, f32[1,1152]{1,0:T(1,128)} %broadcast_in_dim.29.flag_ref, bf16[4,128,1024]{2,1,0:T(8,128)(2,1)} %bitcast.30, f32[128,128]{1,0:T(8,128)} %constant.44.clone.cos_ref, f32[128,128]{1,0:T(8,128)} %constant.45.clone.sin_ref, ...), custom_call_target="tpu_custom_call" | custom-call | tf_op jit(solution)/shard_map/pallas_call | solution.py:130
  28.6 1.4 %collective-permute-start.9 = (bf16[256,512]{1,0:T(8,128)(2,1)}, bf16[256,512]{1,0:T(8,128)(2,1)S(1)}, u32[]{:S(2)}, u32[]{:S(2)}) collective-permute-start(bf16[256,512]{1,0:T(8,128)(2,1)} %bitcast.33), channel_id=1, source_target_pairs={{0,2},{1,3},{2,0},{3,1},{4,6},{5,7},{6,4},{7,5},{8,10},{9,11},{10,... | collective-permute-start | bytes 786440 | tf_op jit(solution)/shard_map/ppermute | solution.py:28
  30.1 3.8 %shard_map.110 = bf16[2,128,512]{2,1,0:T(8,128)(2,1)} custom-call(s32[4,1,1152]{2,1,0:T(1,128)} %broadcast_in_dim.27.limit_ref, f32[1,1152]{1,0:T(1,128)} %broadcast_in_dim.29.flag_ref, bf16[4,128,1024]{2,1,0:T(8,128)(2,1)} %bitcast.31, f32[128,128]{1,0:T(8,128)} %constant.44.clone.cos_ref, f32[128,128]{1,0:T(8,128)} %constant.45.clone.sin_ref, ...), custom_call_target="tpu_custom_call" | custom-call | tf_op jit(solution)/shard_map/pallas_call | solution.py:130
  34.7 3.2 %collective-permute-done.9 = bf16[256,512]{1,0:T(8,128)(2,1)S(1)} collective-permute-done((bf16[256,512]{1,0:T(8,128)(2,1)}, bf16[256,512]{1,0:T(8,128)(2,1)S(1)}, u32[]{:S(2)}, u32[]{:S(2)}) %collective-permute-start.9) | collective-permute-done | bytes 262176 | tf_op jit(solution)/shard_map/ppermute | solution.py:28
  37.9 1.5 %fusion.6 = f32[512,576]{0,1:T(8,128)S(1)} fusion(bf16[2048,576]{0,1:T(8,128)(2,1)S(1)} %copy-done, s32[]{:T(128)S(6)} %select_n.40, bf16[256,512]{1,0:T(8,128)(2,1)} %collective-permute-done.8, bf16[256,512]{1,0:T(8,128)(2,1)S(1)} %collective-permute-done.7), kind=kOutput, calls=%fused_computation.11 | convolution fusion | flops 303038464 | bytes 2293764 | tf_op jit(solution)/shard_map/dot_general | solution.py:200
  39.9 3.3 %collective-permute-done.10 = bf16[256,512]{1,0:T(8,128)(2,1)S(1)} collective-permute-done((bf16[256,512]{1,0:T(8,128)(2,1)}, bf16[256,512]{1,0:T(8,128)(2,1)S(1)}, u32[]{:S(2)}, u32[]{:S(2)}) %collective-permute-start.10) | collective-permute-done | bytes 262176 | tf_op jit(solution)/shard_map/ppermute | solution.py:28
  43.7 1.0 %collective-permute-done.12 = bf16[256,512]{1,0:T(8,128)(2,1)S(1)} collective-permute-done((bf16[256,512]{1,0:T(8,128)(2,1)S(1)}, bf16[256,512]{1,0:T(8,128)(2,1)S(1)}, u32[]{:S(2)}, u32[]{:S(2)}) %collective-permute-start.12) | collective-permute-done | bytes 262176 | tf_op jit(solution)/shard_map/ppermute | solution.py:28
  45.4 1.4 %collective-permute-start.14 = (f32[4,128]{1,0:T(4,128)S(1)}, f32[4,128]{1,0:T(4,128)S(1)}, u32[]{:S(2)}, u32[]{:S(2)}) collective-permute-start(f32[4,128]{1,0:T(4,128)S(1)} %bitcast.39), channel_id=1, source_target_pairs={{0,2},{1,3},{2,0},{3,1},{4,6},{5,7},{6,4},{7,5},{8,10},{9,11},{10,... | collective-permute-start | bytes 6152 | tf_op jit(solution)/shard_map/ppermute | solution.py:24
  46.9 1.3 %collective-permute-start.15 = (f32[4,128]{1,0:T(4,128)S(1)}, f32[4,128]{1,0:T(4,128)S(1)}, u32[]{:S(2)}, u32[]{:S(2)}) collective-permute-start(f32[4,128]{1,0:T(4,128)S(1)} %bitcast.40), channel_id=1, source_target_pairs={{0,3},{1,0},{2,1},{3,2},{4,7},{5,4},{6,5},{7,6},{8,11},{9,8},{10,9... | collective-permute-start | bytes 6152 | tf_op jit(solution)/shard_map/ppermute | solution.py:24
  48.3 0.7 %collective-permute-done.14 = f32[4,128]{1,0:T(4,128)S(1)} collective-permute-done((f32[4,128]{1,0:T(4,128)S(1)}, f32[4,128]{1,0:T(4,128)S(1)}, u32[]{:S(2)}, u32[]{:S(2)}) %collective-permute-start.14) | collective-permute-done | bytes 2080 | tf_op jit(solution)/shard_map/ppermute | solution.py:24
  49.5 1.1 %fusion.3 = bf16[4,128,576]{1,2,0:T(8,128)(2,1)} fusion(bf16[4,128,576]{1,2,0:T(8,128)(2,1)S(1)} %copy-done.4, f32[4,128]{1,0:T(4,128)S(1)} %fusion.21, f32[576]{0:T(1024)S(1)} %copy-done.12, f32[4,128]{1,0:T(4,128)S(1)} %add_rsqrt_fusion, f32[512,576]{0,1:T(8,128)S(1)} %get-tuple-element.6), kind=kLoop, calls=%fused_computation.7 | loop fusion | flops 1769472 | bytes 2365696 | tf_op jit(solution)/shard_map/convert_element_type | solution.py:210
  (56 shorter events, 5.8 us)
Async XLA Ops:
  0.0 37.9 %copy-start = (bf16[2048,576]{0,1:T(8,128)(2,1)S(1)}, bf16[2048,576]{0,1:T(8,128)(2,1)}, u32[]{:S(2)}) copy-start(bf16[2048,576]{0,1:T(8,128)(2,1)} %param.18) | copy-start | bytes 7077892
  3.2 21.0 %copy-start.1 = (bf16[128,512]{1,0:T(8,128)(2,1)}, bf16[128,512]{1,0:T(8,128)(2,1)S(1)}, u32[]{:S(2)}) copy-start(bf16[128,512]{1,0:T(8,128)(2,1)S(1)} %select_bitcast_fusion.rest_0_) | copy-start | bytes 393220
  3.2 9.6 %collective-permute-start.3 = (bf16[128,512]{1,0:T(8,128)(2,1)S(1)}, bf16[128,512]{1,0:T(8,128)(2,1)S(1)}, u32[]{:S(2)}, u32[]{:S(2)}) collective-permute-start(bf16[128,512]{1,0:T(8,128)(2,1)S(1)} %select_bitcast_fusion.rest_0_), channel_id=1, source_target_pairs={{0,24},{4,28},{8,16},{12,20},{16,8},{20,12},{24,0},{28,4},{1,25},{... | collective-permute-start | bytes 393224 | tf_op jit(solution)/shard_map/ppermute | solution.py:28
  8.4 7.5 %collective-permute-start = (bf16[128,512]{1,0:T(8,128)(2,1)S(1)}, bf16[128,512]{1,0:T(8,128)(2,1)S(1)}, u32[]{:S(2)}, u32[]{:S(2)}) collective-permute-start(bf16[128,512]{1,0:T(8,128)(2,1)S(1)} %select_bitcast_fusion.rest_0_), channel_id=1, source_target_pairs={{0,4},{4,0},{8,12},{12,8},{16,20},{20,16},{24,28},{28,24},{1,5},{5... | collective-permute-start | bytes 393224 | tf_op jit(solution)/shard_map/ppermute | solution.py:28
  9.9 9.4 %collective-permute-start.1 = (bf16[128,512]{1,0:T(8,128)(2,1)S(1)}, bf16[128,512]{1,0:T(8,128)(2,1)S(1)}, u32[]{:S(2)}, u32[]{:S(2)}) collective-permute-start(bf16[128,512]{1,0:T(8,128)(2,1)S(1)} %select_bitcast_fusion.rest_0_), channel_id=1, source_target_pairs={{0,8},{4,12},{8,0},{12,4},{16,24},{20,28},{24,16},{28,20},{1,9},{5... | collective-permute-start | bytes 393224 | tf_op jit(solution)/shard_map/ppermute | solution.py:28
  9.9 9.4 %collective-permute-start.2 = (bf16[128,512]{1,0:T(8,128)(2,1)S(1)}, bf16[128,512]{1,0:T(8,128)(2,1)S(1)}, u32[]{:S(2)}, u32[]{:S(2)}) collective-permute-start(bf16[128,512]{1,0:T(8,128)(2,1)S(1)} %select_bitcast_fusion.rest_0_), channel_id=1, source_target_pairs={{0,12},{4,8},{8,4},{12,0},{16,28},{20,24},{24,20},{28,16},{1,13},{... | collective-permute-start | bytes 393224 | tf_op jit(solution)/shard_map/ppermute | solution.py:28
  12.8 11.4 %copy-start.5 = (bf16[128,512]{1,0:T(8,128)(2,1)}, bf16[128,512]{1,0:T(8,128)(2,1)S(1)}, u32[]{:S(2)}) copy-start(bf16[128,512]{1,0:T(8,128)(2,1)S(1)} %collective-permute-done.3.rest_4_) | copy-start | bytes 393220
  12.8 7.1 %collective-permute-start.4 = (bf16[128,512]{1,0:T(8,128)(2,1)S(1)}, bf16[128,512]{1,0:T(8,128)(2,1)S(1)}, u32[]{:S(2)}, u32[]{:S(2)}) collective-permute-start(bf16[128,512]{1,0:T(8,128)(2,1)S(1)} %collective-permute-done.3.rest_4_), channel_id=1, source_target_pairs={{0,4},{4,0},{8,12},{12,8},{16,20},{20,16},{24,28},{28,24},{1,5},{5... | collective-permute-start | bytes 393224 | tf_op jit(solution)/shard_map/ppermute | solution.py:28
  14.5 7.4 %collective-permute-start.5 = (bf16[128,512]{1,0:T(8,128)(2,1)S(1)}, bf16[128,512]{1,0:T(8,128)(2,1)S(1)}, u32[]{:S(2)}, u32[]{:S(2)}) collective-permute-start(bf16[128,512]{1,0:T(8,128)(2,1)S(1)} %collective-permute-done.3.rest_4_), channel_id=1, source_target_pairs={{0,8},{4,12},{8,0},{12,4},{16,24},{20,28},{24,16},{28,20},{1,9},{5... | collective-permute-start | bytes 393224 | tf_op jit(solution)/shard_map/ppermute | solution.py:28
  15.9 8.3 %copy-start.6 = (bf16[128,512]{1,0:T(8,128)(2,1)}, bf16[128,512]{1,0:T(8,128)(2,1)S(1)}, u32[]{:S(2)}) copy-start(bf16[128,512]{1,0:T(8,128)(2,1)S(1)} %collective-permute-done.rest_1_) | copy-start | bytes 393220
  15.9 8.3 %collective-permute-start.6 = (bf16[128,512]{1,0:T(8,128)(2,1)S(1)}, bf16[128,512]{1,0:T(8,128)(2,1)S(1)}, u32[]{:S(2)}, u32[]{:S(2)}) collective-permute-start(bf16[128,512]{1,0:T(8,128)(2,1)S(1)} %collective-permute-done.3.rest_4_), channel_id=1, source_target_pairs={{0,12},{4,8},{8,4},{12,0},{16,28},{20,24},{24,20},{28,16},{1,13},{... | collective-permute-start | bytes 393224 | tf_op jit(solution)/shard_map/ppermute | solution.py:28
  28.6 9.3 %collective-permute-start.7 = (bf16[256,512]{1,0:T(8,128)(2,1)}, bf16[256,512]{1,0:T(8,128)(2,1)S(1)}, u32[]{:S(2)}, u32[]{:S(2)}) collective-permute-start(bf16[256,512]{1,0:T(8,128)(2,1)} %bitcast.32), channel_id=1, source_target_pairs={{0,1},{1,0},{2,3},{3,2},{4,5},{5,4},{6,7},{7,6},{8,9},{9,8},{10,11... | collective-permute-start | bytes 786440 | tf_op jit(solution)/shard_map/ppermute | solution.py:28
  28.6 9.3 %collective-permute-start.9 = (bf16[256,512]{1,0:T(8,128)(2,1)}, bf16[256,512]{1,0:T(8,128)(2,1)S(1)}, u32[]{:S(2)}, u32[]{:S(2)}) collective-permute-start(bf16[256,512]{1,0:T(8,128)(2,1)} %bitcast.33), channel_id=1, source_target_pairs={{0,2},{1,3},{2,0},{3,1},{4,6},{5,7},{6,4},{7,5},{8,10},{9,11},{10,... | collective-permute-start | bytes 786440 | tf_op jit(solution)/shard_map/ppermute | solution.py:28
  33.8 5.5 %copy-start.2 = (bf16[2,128,512]{2,1,0:T(8,128)(2,1)S(1)}, bf16[2,128,512]{2,1,0:T(8,128)(2,1)}, u32[]{:S(2)}) copy-start(bf16[2,128,512]{2,1,0:T(8,128)(2,1)} %shard_map.109) | copy-start | bytes 786436
  33.8 5.6 %copy-start.3 = (bf16[2,128,512]{2,1,0:T(8,128)(2,1)S(1)}, bf16[2,128,512]{2,1,0:T(8,128)(2,1)}, u32[]{:S(2)}) copy-start(bf16[2,128,512]{2,1,0:T(8,128)(2,1)} %shard_map.110) | copy-start | bytes 786436
  33.8 4.1 %collective-permute-start.8 = (bf16[256,512]{1,0:T(8,128)(2,1)}, bf16[256,512]{1,0:T(8,128)(2,1)}, u32[]{:S(2)}, u32[]{:S(2)}) collective-permute-start(bf16[256,512]{1,0:T(8,128)(2,1)} %bitcast.35), channel_id=1, source_target_pairs={{0,1},{1,0},{2,3},{3,2},{4,5},{5,4},{6,7},{7,6},{8,9},{9,8},{10,11... | collective-permute-start | bytes 786440 | tf_op jit(solution)/shard_map/ppermute | solution.py:28
  34.1 9.0 %collective-permute-start.10 = (bf16[256,512]{1,0:T(8,128)(2,1)}, bf16[256,512]{1,0:T(8,128)(2,1)S(1)}, u32[]{:S(2)}, u32[]{:S(2)}) collective-permute-start(bf16[256,512]{1,0:T(8,128)(2,1)} %bitcast.36), channel_id=1, source_target_pairs={{0,2},{1,3},{2,0},{3,1},{4,6},{5,7},{6,4},{7,5},{8,10},{9,11},{10,... | collective-permute-start | bytes 786440 | tf_op jit(solution)/shard_map/ppermute | solution.py:28
  37.9 5.8 %collective-permute-start.11 = (bf16[256,512]{1,0:T(8,128)(2,1)S(1)}, bf16[256,512]{1,0:T(8,128)(2,1)S(1)}, u32[]{:S(2)}, u32[]{:S(2)}) collective-permute-start(bf16[256,512]{1,0:T(8,128)(2,1)S(1)} %collective-permute-done.9), channel_id=1, source_target_pairs={{0,1},{1,0},{2,3},{3,2},{4,5},{5,4},{6,7},{7,6},{8,9},{9,8},{10,11... | collective-permute-start | bytes 786440 | tf_op jit(solution)/shard_map/ppermute | solution.py:28
  43.2 1.5 %collective-permute-start.12 = (bf16[256,512]{1,0:T(8,128)(2,1)S(1)}, bf16[256,512]{1,0:T(8,128)(2,1)S(1)}, u32[]{:S(2)}, u32[]{:S(2)}) collective-permute-start(bf16[256,512]{1,0:T(8,128)(2,1)S(1)} %collective-permute-done.10), channel_id=1, source_target_pairs={{0,1},{1,0},{2,3},{3,2},{4,5},{5,4},{6,7},{7,6},{8,9},{9,8},{10,11... | collective-permute-start | bytes 786440 | tf_op jit(solution)/shard_map/ppermute | solution.py:28
  43.7 5.8 %copy-start.4 = (bf16[4,128,576]{1,2,0:T(8,128)(2,1)S(1)}, bf16[4,128,576]{1,2,0:T(8,128)(2,1)}, u32[]{:S(2)}) copy-start(bf16[4,128,576]{1,2,0:T(8,128)(2,1)} %param.11) | copy-start | bytes 1769476
  43.7 5.8 %copy-start.12 = (f32[576]{0:T(1024)S(1)}, f32[576]{0:T(1024)}, u32[]{:S(2)}) copy-start(f32[576]{0:T(1024)} %param.19) | copy-start | bytes 6916
  45.2 3.1 %collective-permute-start.13 = (f32[4,128]{1,0:T(4,128)S(1)}, f32[4,128]{1,0:T(4,128)S(1)}, u32[]{:S(2)}, u32[]{:S(2)}) collective-permute-start(f32[4,128]{1,0:T(4,128)S(1)} %bitcast.38), channel_id=1, source_target_pairs={{0,1},{1,2},{2,3},{3,0},{4,5},{5,6},{6,7},{7,4},{8,9},{9,10},{10,1... | collective-permute-start | bytes 6152 | tf_op jit(solution)/shard_map/ppermute | solution.py:24
  45.4 3.6 %collective-permute-start.14 = (f32[4,128]{1,0:T(4,128)S(1)}, f32[4,128]{1,0:T(4,128)S(1)}, u32[]{:S(2)}, u32[]{:S(2)}) collective-permute-start(f32[4,128]{1,0:T(4,128)S(1)} %bitcast.39), channel_id=1, source_target_pairs={{0,2},{1,3},{2,0},{3,1},{4,6},{5,7},{6,4},{7,5},{8,10},{9,11},{10,... | collective-permute-start | bytes 6152 | tf_op jit(solution)/shard_map/ppermute | solution.py:24
  46.9 2.6 %collective-permute-start.15 = (f32[4,128]{1,0:T(4,128)S(1)}, f32[4,128]{1,0:T(4,128)S(1)}, u32[]{:S(2)}, u32[]{:S(2)}) collective-permute-start(f32[4,128]{1,0:T(4,128)S(1)} %bitcast.40), channel_id=1, source_target_pairs={{0,3},{1,0},{2,1},{3,2},{4,7},{5,4},{6,5},{7,6},{8,11},{9,8},{10,9... | collective-permute-start | bytes 6152 | tf_op jit(solution)/shard_map/ppermute | solution.py:24
  (5 other events, 17.1 us)
